TPU v7x, 32 devices: a whole 2x2x4 slice. The times are simulated.
32 devices in a mesh: groups: 2 (over y), seq: 4 (over z), head: 4 (over x, core).
Axes of the slice: x: 2, y: 2, z: 4, core: 2. Of those that a mesh axis runs over, the one named last changes fastest.
Arguments:
- queries: bfloat16 [1024, 16, 128], P(('groups', 'seq'), 'head'), parts along dimension 0, may hold values from -1.25 to 1.25
- reflect_keys: bfloat16 [1024, 2, 16, 128], P(('groups', 'seq'), None, 'head'), parts along dimension 0, may hold values from -1.25 to 1.25
- write_values: bfloat16 [1024, 2, 16, 128], P(('groups', 'seq'), None, 'head'), parts along dimension 0, may hold values from -2.5 to 2.5
- out_cotangent: bfloat16 [1024, 16, 128], P(('groups', 'seq'), 'head'), parts along dimension 0, may hold values from -4 to 4
Outputs:
- outputs: bfloat16 [1024, 16, 128], P(('groups', 'seq'), 'head'), parts along dimension 0
- grad_queries: bfloat16 [1024, 16, 128], P(('groups', 'seq'), 'head'), parts along dimension 0
- grad_keys: bfloat16 [1024, 2, 16, 128], P(('groups', 'seq'), None, 'head'), parts along dimension 0
- grad_values: bfloat16 [1024, 2, 16, 128], P(('groups', 'seq'), None, 'head'), parts along dimension 0
There are 2 independent parts, one for each index of `groups`. A program takes and returns all parts, laid end to end along the dimension named above; each array names one. Nothing has to cross between parts.
All inputs are finite; a program needn't handle non-finite values.
Results may differ from a plain program's by a relative error of at most 0.0012.
Values sent between devices are 32-bit elements; how exact they have to be, the bound alone decides.
No kernel may reach another device: no remote copies, remote signals or barrier semaphores. Data moves between devices by JAX's collectives and lax.ppermute only.
A program may use at most 128 MiB of HBM per device.

v0:
```python
import jax
import jax.numpy as jnp
from jax import lax
from jax.sharding import PartitionSpec as P

highest = lax.Precision.HIGHEST
LEAF = 16


def mm(spec, *operands):
    return jnp.einsum(spec, *operands, precision=highest)


def unit_rows(tensor):
    scale = lax.rsqrt(jnp.sum(tensor * tensor, axis=-1, keepdims=True) + 1e-06)
    return tensor * scale, scale


def strict_lower(rows, cols):
    return lax.broadcasted_iota(jnp.int32, (rows, cols), 0) > lax.broadcasted_iota(
        jnp.int32, (rows, cols), 1
    )


def tri_inverse(keys):
    heads, rows, size = keys.shape
    leaves = rows // LEAF
    leaf_keys = keys.reshape(heads, leaves, LEAF, size)
    gram = mm("hpid,hpjd->hpij", leaf_keys, leaf_keys)
    power = jnp.where(strict_lower(LEAF, LEAF), -2.0 * gram, 0.0)
    eye = jnp.eye(LEAF, dtype=jnp.float32)
    inverse = eye + power
    reach = 2
    while reach < LEAF:
        power = mm("hpij,hpjk->hpik", power, power)
        inverse = inverse + mm("hpij,hpjk->hpik", inverse, power)
        reach *= 2
    span = LEAF
    while span < rows:
        pairs = rows // (2 * span)
        blocks = inverse.reshape(heads, pairs, 2, span, span)
        upper_inv = blocks[:, :, 0]
        lower_inv = blocks[:, :, 1]
        halves = keys.reshape(heads, pairs, 2, span, size)
        link = 2.0 * mm("hpid,hpjd->hpij", halves[:, :, 1], halves[:, :, 0])
        corner = -mm("hpij,hpjk->hpik", lower_inv, mm("hpij,hpjk->hpik", link, upper_inv))
        top = jnp.concatenate([upper_inv, jnp.zeros_like(upper_inv)], axis=3)
        bottom = jnp.concatenate([corner, lower_inv], axis=3)
        inverse = jnp.concatenate([top, bottom], axis=2)
        span *= 2
    return inverse.reshape(heads, rows, rows)


def scan_seq(transition, offset, local_cot):
    count = lax.axis_size("seq")
    fwd_map, fwd_sum = transition, offset
    bwd_map, bwd_sum = transition, local_cot
    shift = 1
    while shift < count:
        right = [(i, i + shift) for i in range(count - shift)]
        left = [(i + shift, i) for i in range(count - shift)]
        last = 2 * shift >= count
        if last:
            got_sum = lax.ppermute(fwd_sum, "seq", right)
            got_cot = lax.ppermute(bwd_sum, "seq", left)
        else:
            got_map, got_sum = lax.ppermute((fwd_map, fwd_sum), "seq", right)
            got_bmap, got_cot = lax.ppermute((bwd_map, bwd_sum), "seq", left)
        fwd_sum = mm("hij,hjk->hik", fwd_map, got_sum) + fwd_sum
        bwd_sum = mm("hji,hjk->hik", bwd_map, got_cot) + bwd_sum
        if not last:
            fwd_map = mm("hij,hjk->hik", fwd_map, got_map)
            bwd_map = mm("hij,hjk->hik", got_bmap, bwd_map)
        shift *= 2
    state_in = lax.ppermute(fwd_sum, "seq", [(i, i + 1) for i in range(count - 1)])
    end_cot = lax.ppermute(bwd_sum, "seq", [(i + 1, i) for i in range(count - 1)])
    return state_in, end_cot


def local(queries, reflect_keys, write_values, out_cotangent):
    tok_count, heads_here, head_size = queries.shape
    rows = 2 * tok_count
    q_raw = queries.astype(jnp.float32).transpose(1, 0, 2)
    cot = out_cotangent.astype(jnp.float32).transpose(1, 0, 2)
    k_raw = reflect_keys.astype(jnp.float32).reshape(rows, heads_here, head_size).transpose(1, 0, 2)
    vals = write_values.astype(jnp.float32).reshape(rows, heads_here, head_size).transpose(1, 0, 2)
    qn, q_scale = unit_rows(q_raw)
    kn, k_scale = unit_rows(k_raw)

    inverse = tri_inverse(kn)
    proj = mm("hij,hjd->hid", inverse, kn)
    upd_v = mm("hij,hjd->hid", inverse, vals)
    tok_ids = lax.broadcasted_iota(jnp.int32, (tok_count, rows), 0)
    sub_ids = lax.broadcasted_iota(jnp.int32, (tok_count, rows), 1)
    visible = sub_ids <= 2 * tok_ids + 1
    scores = jnp.where(visible, 2.0 * mm("hid,hjd->hij", qn, kn), 0.0)
    read_map = qn - mm("hij,hjd->hid", scores, proj)
    own_out = mm("hij,hjd->hid", scores, upd_v)
    eye = jnp.eye(head_size, dtype=jnp.float32)
    transition = eye - 2.0 * mm("hjd,hjw->hdw", kn, proj)
    offset = 2.0 * mm("hjd,hjw->hdw", kn, upd_v)
    local_cot = mm("hld,hlw->hdw", read_map, cot)

    state_in, end_cot = scan_seq(transition, offset, local_cot)

    produced = mm("hld,hdw->hlw", read_map, state_in) + own_out
    updates = upd_v - mm("hjd,hdw->hjw", proj, state_in)
    d_upd = mm("hij,hiw->hjw", scores, cot) + 2.0 * mm("hjd,hdw->hjw", kn, end_cot)
    d_w = mm("hij,hiw->hjw", inverse, d_upd)
    touch = jnp.where(visible, mm("hiw,hjw->hij", cot, updates), 0.0)
    d_qn = mm("hiw,hdw->hid", cot, state_in) + 2.0 * mm("hij,hjd->hid", touch, kn)
    gram_cot = jnp.where(strict_lower(rows, rows), -2.0 * mm("hiw,hjw->hij", d_w, updates), 0.0)
    d_kn = (
        2.0 * mm("hij,hid->hjd", touch, qn)
        + 2.0 * mm("hjw,hdw->hjd", updates, end_cot)
        - mm("hjw,hdw->hjd", d_w, state_in)
        + mm("hij,hjd->hid", gram_cot, kn)
        + mm("hji,hjd->hid", gram_cot, kn)
    )
    d_q = q_scale * (d_qn - jnp.sum(qn * d_qn, axis=-1, keepdims=True) * qn)
    d_k = k_scale * (d_kn - jnp.sum(kn * d_kn, axis=-1, keepdims=True) * kn)

    def token_major(tensor):
        return tensor.transpose(1, 0, 2).astype(jnp.bfloat16)

    def pair_major(tensor):
        return (
            tensor.reshape(heads_here, tok_count, 2, head_size)
            .transpose(1, 2, 0, 3)
            .astype(jnp.bfloat16)
        )

    return (token_major(produced), token_major(d_q), pair_major(d_k), pair_major(d_w))


def solution(mesh):
    in_specs = (
        P(("groups", "seq"), "head", None),
        P(("groups", "seq"), None, "head", None),
        P(("groups", "seq"), None, "head", None),
        P(("groups", "seq"), "head", None),
    )
    out_specs = (
        P(("groups", "seq"), "head", None),
        P(("groups", "seq"), "head", None),
        P(("groups", "seq"), None, "head", None),
        P(("groups", "seq"), None, "head", None),
    )
    return jax.shard_map(local, mesh=mesh, in_specs=in_specs, out_specs=out_specs, check_vma=False)
```

profile of v0, /device:TPU:0, one launch (start us, length us, event | category | flops | bytes accessed | tf_op | source)
XLA Modules:
  0.0 75.5 jit_solution(14631895159759880879)
XLA Ops:
  0.7 1.2 %copy.9 = f32[128,2,4,128]{3,1,0,2:T(2,128)S(1)} copy(bf16[128,2,4,128]{3,2,1,0:T(4,128)(2,1)} %param.5) | data formatting | bytes 786432 | tf_op jit(solution)/shard_map/transpose | solution.py:85
  2.3 0.9 %fusion.3 = f32[4,16,16,16]{3,2,1,0:T(8,128)S(1)} fusion(f32[4,16,16,128]{3,2,1,0:T(8,128)S(1)} %bitcast.208, pred[16,16]{1,0:T(8,128)(4,1)S(1)} %iota_compare_fusion.7), kind=kOutput, calls=%fused_computation.10 | convolution fusion | flops 25198592 | bytes 590080 | tf_op jit(solution)/shard_map/hpid,hpjd->hpij/dot_general | solution.py:11
  3.3 0.6 fusion.73
  3.9 0.6 fusion.74
  4.5 0.7 convolution_add_fusion.2
  5.2 0.6 fusion.75
  5.9 0.6 convolution_add_fusion.1
  6.5 0.6 convolution_add_fusion
  7.2 0.5 convolution_multiply_fusion.7
  8.1 0.4 convolution_negate_fusion.3
  8.7 0.5 convolution_multiply_fusion.6
  9.2 0.4 fusion.70
  9.6 0.4 convolution_negate_fusion.2
  10.2 0.5 convolution_multiply_fusion.5
  10.7 0.4 fusion.71
  11.1 0.4 convolution_negate_fusion.1
  11.7 0.7 convolution_multiply_fusion.4
  12.4 0.6 fusion.38
  13.0 0.7 fusion.12
  13.6 1.0 %fusion.24 = f32[4,256,128]{2,1,0:T(8,128)S(1)} fusion(f32[4,256,128]{2,1,0:T(8,128)S(1)} %broadcast_multiply_fusion, f32[4,1,128,128]{3,2,0,1:T(8,128)S(1)} %get-tuple-element.9, f32[4,1,128,128]{3,2,0,1:T(8,128)S(1)} %get-tuple-element.8, f32[4,1,128,128]{3,2,0,1:T(8,128)S(1)} %fusion.12), kind=kOutput, calls=%fused_computation.61 | convolution fusion | flops 403701760 | bytes 1835008 | tf_op jit(solution)/shard_map/hij,hjd->hid/dot_general | solution.py:11
  14.7 1.2 %fusion.13 = f32[4,128,128]{2,1,0:T(8,128)S(1)} fusion(f32[4,256,128]{2,1,0:T(8,128)S(1)} %broadcast_multiply_fusion, f32[4,256,128]{2,1,0:T(8,128)S(1)} %fusion.24, f32[128,128]{1,0:T(8,128)S(1)} %fusion.55), kind=kOutput, calls=%fused_computation.42 | convolution fusion | flops 201457664 | bytes 1376256 | tf_op jit(solution)/shard_map/hjd,hjw->hdw/dot_general | solution.py:11
  15.9 4.9 %collective-permute-start = (f32[4,128,128]{2,1,0:T(8,128)S(1)}, f32[4,128,128]{2,1,0:T(8,128)S(1)}, u32[]{:S(2)}, u32[]{:S(2)}) collective-permute-start(f32[4,128,128]{2,1,0:T(8,128)S(1)} %fusion.13), channel_id=1, source_target_pairs={{0,4},{4,8},{8,12},{1,5},{5,9},{9,13},{2,6},{6,10},{10,14},{3,7},{... | collective-permute-start | bytes 786440 | tf_op jit(solution)/shard_map/ppermute | solution.py:67
  20.9 1.3 %collective-permute-start.4 = (f32[4,128,128]{2,1,0:T(8,128)S(1)}, f32[4,128,128]{2,1,0:T(8,128)S(1)}, u32[]{:S(2)}, u32[]{:S(2)}) collective-permute-start(f32[4,128,128]{2,1,0:T(8,128)S(1)} %fusion.13), channel_id=1, source_target_pairs={{4,0},{8,4},{12,8},{5,1},{9,5},{13,9},{6,2},{10,6},{14,10},{7,3},{... | collective-permute-start | bytes 786440 | tf_op jit(solution)/shard_map/ppermute | solution.py:68
  22.2 0.6 fusion.22
  22.8 1.0 %convolution_multiply_fusion.9 = f32[4,128,128]{2,1,0:T(8,128)S(1)} fusion(f32[4,256,128]{2,1,0:T(8,128)S(1)} %broadcast_multiply_fusion, f32[4,256,128]{2,1,0:T(8,128)S(1)} %fusion.22), kind=kOutput, calls=%fused_computation.39 | convolution fusion | flops 201392128 | bytes 1310720 | tf_op jit(solution)/shard_map/hjd,hjw->hdw/dot_general | solution.py:11
  23.8 4.6 %collective-permute-start.1 = (f32[4,128,128]{2,1,0:T(8,128)S(1)}, f32[4,128,128]{2,1,0:T(8,128)S(1)}, u32[]{:S(2)}, u32[]{:S(2)}) collective-permute-start(f32[4,128,128]{2,1,0:T(8,128)S(1)} %convolution_multiply_fusion.9), channel_id=1, source_target_pairs={{0,4},{4,8},{8,12},{1,5},{5,9},{9,13},{2,6},{6,10},{10,14},{3,7},{... | collective-permute-start | bytes 786440 | tf_op jit(solution)/shard_map/ppermute | solution.py:67
  28.7 0.7 fusion.10
  29.3 0.6 convolution_subtract_fusion.2
  30.0 0.4 fusion.48
  30.4 1.3 %collective-permute-start.5 = (f32[4,128,128]{2,1,0:T(8,128)S(1)}, f32[4,128,128]{2,1,0:T(8,128)S(1)}, u32[]{:S(2)}, u32[]{:S(2)}) collective-permute-start(f32[4,128,128]{2,1,0:T(8,128)S(1)} %fusion.48), channel_id=1, source_target_pairs={{4,0},{8,4},{12,8},{5,1},{9,5},{13,9},{6,2},{10,6},{14,10},{7,3},{... | collective-permute-start | bytes 786440 | tf_op jit(solution)/shard_map/ppermute | solution.py:68
  31.7 0.6 fusion.77
  32.3 0.6 fusion.51
  33.0 0.4 collective-permute-done.1
  33.4 0.4 convolution_add_fusion.9
  33.8 5.4 %collective-permute-start.2 = (f32[4,128,128]{2,1,0:T(8,128)S(1)}, f32[4,128,128]{2,1,0:T(8,128)S(1)}, u32[]{:S(2)}, u32[]{:S(2)}) collective-permute-start(f32[4,128,128]{2,1,0:T(8,128)S(1)} %convolution_add_fusion.9), channel_id=1, source_target_pairs={{0,8},{4,12},{1,9},{5,13},{2,10},{6,14},{3,11},{7,15},{16,24},{20,... | collective-permute-start | bytes 786440 | tf_op jit(solution)/shard_map/ppermute | solution.py:64
  39.5 0.6 convolution_add_fusion.6
  40.1 1.3 %collective-permute-start.6 = (f32[4,128,128]{2,1,0:T(8,128)S(1)}, f32[4,128,128]{2,1,0:T(8,128)S(1)}, u32[]{:S(2)}, u32[]{:S(2)}) collective-permute-start(f32[4,128,128]{2,1,0:T(8,128)S(1)} %convolution_add_fusion.6), channel_id=1, source_target_pairs={{8,0},{12,4},{9,1},{13,5},{10,2},{14,6},{11,3},{15,7},{24,16},{28,... | collective-permute-start | bytes 786440 | tf_op jit(solution)/shard_map/ppermute | solution.py:65
  41.4 0.4 fusion.76
  41.8 1.6 %collective-permute-done.2 = f32[4,128,128]{2,1,0:T(8,128)S(1)} collective-permute-done((f32[4,128,128]{2,1,0:T(8,128)S(1)}, f32[4,128,128]{2,1,0:T(8,128)S(1)}, u32[]{:S(2)}, u32[]{:S(2)}) %collective-permute-start.2) | collective-permute-done | bytes 262176 | tf_op jit(solution)/shard_map/ppermute | solution.py:64
  43.4 0.4 convolution_add_fusion.8
  43.8 9.0 %collective-permute-start.3 = (f32[4,128,128]{2,1,0:T(8,128)S(1)}, f32[4,128,128]{2,1,0:T(8,128)S(1)}, u32[]{:S(2)}, u32[]{:S(2)}) collective-permute-start(f32[4,128,128]{2,1,0:T(8,128)S(1)} %convolution_add_fusion.8), channel_id=1, source_target_pairs={{0,4},{4,8},{8,12},{1,5},{5,9},{9,13},{2,6},{6,10},{10,14},{3,7},{... | collective-permute-start | bytes 786440 | tf_op jit(solution)/shard_map/ppermute | solution.py:75
  52.8 0.6 fusion.78
  53.4 1.4 %collective-permute-done.6 = f32[4,128,128]{2,1,0:T(8,128)S(1)} collective-permute-done((f32[4,128,128]{2,1,0:T(8,128)S(1)}, f32[4,128,128]{2,1,0:T(8,128)S(1)}, u32[]{:S(2)}, u32[]{:S(2)}) %collective-permute-start.6) | collective-permute-done | bytes 262176 | tf_op jit(solution)/shard_map/ppermute | solution.py:65
  54.8 0.4 convolution_add_fusion.5
  55.2 1.5 %collective-permute-start.7 = (f32[4,128,128]{2,1,0:T(8,128)S(1)}, f32[4,128,128]{2,1,0:T(8,128)S(1)}, u32[]{:S(2)}, u32[]{:S(2)}) collective-permute-start(f32[4,128,128]{2,1,0:T(8,128)S(1)} %convolution_add_fusion.5), channel_id=1, source_target_pairs={{4,0},{8,4},{12,8},{5,1},{9,5},{13,9},{6,2},{10,6},{14,10},{7,3},{... | collective-permute-start | bytes 786440 | tf_op jit(solution)/shard_map/ppermute | solution.py:76
  56.7 1.8 %collective-permute-done.3 = f32[4,128,128]{2,1,0:T(8,128)S(1)} collective-permute-done((f32[4,128,128]{2,1,0:T(8,128)S(1)}, f32[4,128,128]{2,1,0:T(8,128)S(1)}, u32[]{:S(2)}, u32[]{:S(2)}) %collective-permute-start.3) | collective-permute-done | bytes 262176 | tf_op jit(solution)/shard_map/ppermute | solution.py:75
  58.5 0.6 convolution_subtract_fusion.1
  59.1 0.4 fusion.2
  59.5 0.4 fusion.53
  59.9 0.7 fusion.32
  60.7 0.4 fusion.15
  61.3 0.8 %copy.36 = bf16[128,4,128]{2,1,0:T(4,128)(2,1)} copy(bf16[128,4,128]{2,0,1:T(8,128)(2,1)S(1)} %fusion.15) | data formatting | bytes 262144
  62.0 0.8 %copy.37 = bf16[128,4,128]{2,1,0:T(4,128)(2,1)} copy(bf16[128,4,128]{2,0,1:T(8,128)(2,1)S(1)} %fusion.37) | data formatting | bytes 262144
  62.8 1.1 %fusion.28 = f32[4,256,128]{2,1,0:T(8,128)S(1)} fusion(f32[4,128,256]{2,1,0:T(8,128)S(1)} %fusion.2, f32[4,128]{1,0:T(4,128)S(1)} %get-tuple-element.17, bf16[128,4,128]{2,1,0:T(4,128)(2,1)S(1)} %copy-done.1), kind=kOutput, calls=%fused_computation.66 | convolution fusion | flops 201457664 | bytes 1181696 | tf_op jit(solution)/shard_map/hij,hid->hjd/dot_general | solution.py:11
  64.3 0.6 fusion.8
  64.9 1.5 %fusion.72 = (bf16[4,256,128]{2,1,0:T(8,128)(2,1)S(1)}, f32[4,256,128]{2,1,0:T(8,128)S(1)}) fusion(f32[4,256,128]{2,1,0:T(8,128)S(1)} %fusion.8, f32[4,1,128,128]{3,2,0,1:T(8,128)S(1)} %get-tuple-element.9, f32[4,1,128,128]{3,2,0,1:T(8,128)S(1)} %get-tuple-element.8, f32[4,1,128,128]{3,2,0,1:T(8,128)S(1)} %fusion.12), kind=kOutput, calls=%fused_computation.137 | convolution fusion | flops 403832832 | bytes 2097152 | tf_op jit(solution)/shard_map/hij,hiw->hjw/dot_general | solution.py:11
  66.4 1.0 %fusion.1 = f32[4,256,256]{2,1,0:T(8,128)S(1)} fusion(f32[4,256,128]{2,1,0:T(8,128)S(1)} %get-tuple-element.21, f32[4,256,128]{2,1,0:T(8,128)S(1)} %convolution_subtract_fusion.1, pred[256,256]{1,0:T(8,128)(4,1)S(1)} %iota_compare_fusion.4), kind=kOutput, calls=%fused_computation.2 | convolution fusion | flops 403177472 | bytes 2162688 | tf_op jit(solution)/shard_map/hiw,hjw->hij/dot_general | solution.py:11
  67.4 1.1 %fusion.79 = f32[4,256,128]{2,1,0:T(8,128)S(1)} fusion(f32[4,256,256]{2,1,0:T(8,128)S(1)} %fusion.1, f32[4,256,128]{2,1,0:T(8,128)S(1)} %broadcast_multiply_fusion), kind=kOutput, calls=%fused_computation.144 | convolution fusion | flops 402653184 | bytes 2097152 | tf_op jit(solution)/shard_map/hij,hjd->hid/dot_general | solution.py:11
  68.5 0.6 fusion.9
  69.1 0.6 fusion.7
  69.7 1.9 %convolution_add_fusion.3 = f32[4,256,128]{2,1,0:T(8,128)S(1)} fusion(f32[4,256,128]{2,1,0:T(8,128)S(1)} %fusion.7, f32[4,256,256]{2,1,0:T(8,128)S(1)} %fusion.1, f32[4,256,128]{2,1,0:T(8,128)S(1)} %broadcast_multiply_fusion), kind=kOutput, calls=%fused_computation.6 | convolution fusion | flops 402784256 | bytes 2621440 | tf_op jit(solution)/shard_map/hji,hjd->hid/dot_general | solution.py:11
  71.6 1.8 %fusion.11 = bf16[4,256,128]{2,1,0:T(8,128)(2,1)S(1)} fusion(f32[4,256,128]{2,1,0:T(8,128)S(1)} %convolution_add_fusion.3, f32[4,256,128]{2,1,0:T(8,128)S(1)} %broadcast_multiply_fusion, f32[4,256]{1,0:T(4,128)S(1)} %add_rsqrt_fusion), kind=kOutput, calls=%fused_computation.23 | output fusion | flops 656511 | bytes 1314816 | tf_op jit(solution)/shard_map/mul | solution.py:121
  73.4 1.0 %copy.84 = bf16[4,128,2,128]{3,0,2,1:T(4,128)(2,1)} copy(bf16[4,128,2,128]{3,2,1,0:T(2,128)(2,1)S(1)} %bitcast.224) | data formatting | bytes 524288 | tf_op jit(solution)/shard_map/convert_element_type | solution.py:130
  74.4 1.0 %copy.83 = bf16[4,128,2,128]{3,0,2,1:T(4,128)(2,1)} copy(bf16[4,128,2,128]{3,2,1,0:T(2,128)(2,1)S(1)} %bitcast.225) | data formatting | bytes 524288 | tf_op jit(solution)/shard_map/convert_element_type | solution.py:130
  (30 shorter events, 2.5 us)
Async XLA Ops:
  0.6 29.4 %copy-start = (bf16[128,4,128]{2,1,0:T(4,128)(2,1)S(1)}, bf16[128,4,128]{2,1,0:T(4,128)(2,1)}, u32[]{:S(2)}) copy-start(bf16[128,4,128]{2,1,0:T(4,128)(2,1)} %param.7) | copy-start | bytes 393220
  14.7 7.5 %copy-start.2 = (bf16[128,2,4,128]{3,2,1,0:T(4,128)(2,1)S(1)}, bf16[128,2,4,128]{3,2,1,0:T(4,128)(2,1)}, u32[]{:S(2)}) copy-start(bf16[128,2,4,128]{3,2,1,0:T(4,128)(2,1)} %param.6) | copy-start | bytes 786436
  15.9 25.5 %collective-permute-start = (f32[4,128,128]{2,1,0:T(8,128)S(1)}, f32[4,128,128]{2,1,0:T(8,128)S(1)}, u32[]{:S(2)}, u32[]{:S(2)}) collective-permute-start(f32[4,128,128]{2,1,0:T(8,128)S(1)} %fusion.13), channel_id=1, source_target_pairs={{0,4},{4,8},{8,12},{1,5},{5,9},{9,13},{2,6},{6,10},{10,14},{3,7},{... | collective-permute-start | bytes 786440 | tf_op jit(solution)/shard_map/ppermute | solution.py:67
  20.9 31.9 %collective-permute-start.4 = (f32[4,128,128]{2,1,0:T(8,128)S(1)}, f32[4,128,128]{2,1,0:T(8,128)S(1)}, u32[]{:S(2)}, u32[]{:S(2)}) collective-permute-start(f32[4,128,128]{2,1,0:T(8,128)S(1)} %fusion.13), channel_id=1, source_target_pairs={{4,0},{8,4},{12,8},{5,1},{9,5},{13,9},{6,2},{10,6},{14,10},{7,3},{... | collective-permute-start | bytes 786440 | tf_op jit(solution)/shard_map/ppermute | solution.py:68
  22.8 5.7 %copy-start.1 = (bf16[128,4,128]{2,1,0:T(4,128)(2,1)S(1)}, bf16[128,4,128]{2,1,0:T(4,128)(2,1)}, u32[]{:S(2)}) copy-start(bf16[128,4,128]{2,1,0:T(4,128)(2,1)} %param.4) | copy-start | bytes 393220
  23.8 9.6 %collective-permute-start.1 = (f32[4,128,128]{2,1,0:T(8,128)S(1)}, f32[4,128,128]{2,1,0:T(8,128)S(1)}, u32[]{:S(2)}, u32[]{:S(2)}) collective-permute-start(f32[4,128,128]{2,1,0:T(8,128)S(1)} %convolution_multiply_fusion.9), channel_id=1, source_target_pairs={{0,4},{4,8},{8,12},{1,5},{5,9},{9,13},{2,6},{6,10},{10,14},{3,7},{... | collective-permute-start | bytes 786440 | tf_op jit(solution)/shard_map/ppermute | solution.py:67
  30.4 9.1 %collective-permute-start.5 = (f32[4,128,128]{2,1,0:T(8,128)S(1)}, f32[4,128,128]{2,1,0:T(8,128)S(1)}, u32[]{:S(2)}, u32[]{:S(2)}) collective-permute-start(f32[4,128,128]{2,1,0:T(8,128)S(1)} %fusion.48), channel_id=1, source_target_pairs={{4,0},{8,4},{12,8},{5,1},{9,5},{13,9},{6,2},{10,6},{14,10},{7,3},{... | collective-permute-start | bytes 786440 | tf_op jit(solution)/shard_map/ppermute | solution.py:68
  33.8 9.6 %collective-permute-start.2 = (f32[4,128,128]{2,1,0:T(8,128)S(1)}, f32[4,128,128]{2,1,0:T(8,128)S(1)}, u32[]{:S(2)}, u32[]{:S(2)}) collective-permute-start(f32[4,128,128]{2,1,0:T(8,128)S(1)} %convolution_add_fusion.9), channel_id=1, source_target_pairs={{0,8},{4,12},{1,9},{5,13},{2,10},{6,14},{3,11},{7,15},{16,24},{20,... | collective-permute-start | bytes 786440 | tf_op jit(solution)/shard_map/ppermute | solution.py:64
  40.1 14.7 %collective-permute-start.6 = (f32[4,128,128]{2,1,0:T(8,128)S(1)}, f32[4,128,128]{2,1,0:T(8,128)S(1)}, u32[]{:S(2)}, u32[]{:S(2)}) collective-permute-start(f32[4,128,128]{2,1,0:T(8,128)S(1)} %convolution_add_fusion.6), channel_id=1, source_target_pairs={{8,0},{12,4},{9,1},{13,5},{10,2},{14,6},{11,3},{15,7},{24,16},{28,... | collective-permute-start | bytes 786440 | tf_op jit(solution)/shard_map/ppermute | solution.py:65
  43.8 14.7 %collective-permute-start.3 = (f32[4,128,128]{2,1,0:T(8,128)S(1)}, f32[4,128,128]{2,1,0:T(8,128)S(1)}, u32[]{:S(2)}, u32[]{:S(2)}) collective-permute-start(f32[4,128,128]{2,1,0:T(8,128)S(1)} %convolution_add_fusion.8), channel_id=1, source_target_pairs={{0,4},{4,8},{8,12},{1,5},{5,9},{9,13},{2,6},{6,10},{10,14},{3,7},{... | collective-permute-start | bytes 786440 | tf_op jit(solution)/shard_map/ppermute | solution.py:75
  55.2 9.1 %collective-permute-start.7 = (f32[4,128,128]{2,1,0:T(8,128)S(1)}, f32[4,128,128]{2,1,0:T(8,128)S(1)}, u32[]{:S(2)}, u32[]{:S(2)}) collective-permute-start(f32[4,128,128]{2,1,0:T(8,128)S(1)} %convolution_add_fusion.5), channel_id=1, source_target_pairs={{4,0},{8,4},{12,8},{5,1},{9,5},{13,9},{6,2},{10,6},{14,10},{7,3},{... | collective-permute-start | bytes 786440 | tf_op jit(solution)/shard_map/ppermute | solution.py:76
where the time goes:
time: 75.8 us; the launch traced here: 75.5 us
  matrix products  31.1 us (41%)
  starting transfers between devices  29.2 us (39%)
  waiting for transfers between devices  5.84 us (8%)
  local copies, waits for them, and re-layouts  4.97 us (7%)
  other arithmetic  3.12 us (4%)
  between operations  1.22 us (2%)
    dot_general x47, matrix products, mm(): return jnp.einsum(spec, *operands, precision=highest)  31.1 us
    ppermute x2, starting transfers between devices, scan_seq(): got_map, got_sum = lax.ppermute((fwd_map, fwd_sum), 'seq', right)  9.5 us
    ppermute x1, starting transfers between devices, scan_seq(): lax.ppermute(fwd_sum, 'seq', [(i, i + 1) for i in range(count - 1)])  8.96 us
    ppermute x1, starting transfers between devices, scan_seq(): got_sum = lax.ppermute(fwd_sum, 'seq', right)  5.4 us
    ppermute x2, starting transfers between devices, scan_seq(): got_bmap, got_cot = lax.ppermute((bwd_map, bwd_sum), 'seq', left)  2.58 us
    convert_element_type x2, local copies, waits for them, and re-layouts, pair_major(): return tensor.reshape(heads_here, tok_count, 2, head_size).transpose(1, 2...  2.09 us
    mul x1, other arithmetic, local(): d_k = k_scale * (d_kn - jnp.sum(kn * d_kn, axis=-1, keepdims=True) * kn)  1.79 us
    ppermute x1, waiting for transfers between devices, scan_seq(): lax.ppermute(fwd_sum, 'seq', [(i, i + 1) for i in range(count - 1)])  1.76 us
  transfers between devices with their start and end apart: 8, of which 6 were waited for; matrix products, arithmetic and copies ran while one was open for 17% of the time, Pallas kernels for 0%

commit v1 on v0

--- a/solution.py
+++ b/solution.py
@@ -51,8 +51,26 @@
     return inverse.reshape(heads, rows, rows)
 
 
+def chain_seq(transition, offset, local_cot):
+    count = lax.axis_size("seq")
+    right = [(i, i + 1) for i in range(count - 1)]
+    left = [(i + 1, i) for i in range(count - 1)]
+    fwd_sum, bwd_sum = offset, local_cot
+    for hop in range(count - 1):
+        got_sum = lax.ppermute(fwd_sum, "seq", right)
+        got_cot = lax.ppermute(bwd_sum, "seq", left)
+        if hop == count - 2:
+            return got_sum, got_cot
+        fwd_sum = mm("hij,hjk->hik", transition, got_sum) + offset
+        bwd_sum = mm("hji,hjk->hik", transition, got_cot) + local_cot
+    zero = jnp.zeros_like(offset)
+    return zero, zero
+
+
 def scan_seq(transition, offset, local_cot):
     count = lax.axis_size("seq")
+    if count <= 4:
+        return chain_seq(transition, offset, local_cot)
     fwd_map, fwd_sum = transition, offset
     bwd_map, bwd_sum = transition, local_cot
     shift = 1

time: 75.8 us -> 63 us (0.83)
  starting transfers between devices: 29.2 us -> 18 us
  waiting for transfers between devices: 5.84 us -> 4.92 us
  matrix products: 31.1 us -> 30.3 us
    ppermute x8 -> x6, starting transfers between devices: 29.2 us -> 18 us  [the longest x3 13.9 us: chain_seq(): got_sum = lax.ppermute(fwd_sum, 'seq', right)]
    ppermute x8 -> x6, waiting for transfers between devices: 5.84 us -> 4.92 us  [the longest x3 2.81 us: chain_seq(): got_cot = lax.ppermute(bwd_sum, 'seq', left)]
    dot_general x47 -> x45, matrix products: 31.1 us -> 30.3 us  [mm(): return jnp.einsum(spec, *operands, precision=highest)]
  transfers between devices with their start and end apart: 8 -> 6, of which waited for: 6 -> 5; matrix products, arithmetic and copies ran while one was open for 17% -> 20% of each run, Pallas kernels for 0% -> 0%
where the time goes in v1:
time: 63 us; the launch traced here: 62.8 us
  matrix products  30.3 us (48%)
  starting transfers between devices  18 us (29%)
  local copies, waits for them, and re-layouts  5.24 us (8%)
  waiting for transfers between devices  4.92 us (8%)
  other arithmetic  3.12 us (5%)
  between operations  1.17 us (2%)
    dot_general x45, matrix products, mm(): return jnp.einsum(spec, *operands, precision=highest)  30.3 us
    ppermute x3, starting transfers between devices, chain_seq(): got_sum = lax.ppermute(fwd_sum, 'seq', right)  13.9 us
    ppermute x3, starting transfers between devices, chain_seq(): got_cot = lax.ppermute(bwd_sum, 'seq', left)  4.1 us
    ppermute x3, waiting for transfers between devices, chain_seq(): got_cot = lax.ppermute(bwd_sum, 'seq', left)  2.81 us
    ppermute x3, waiting for transfers between devices, chain_seq(): got_sum = lax.ppermute(fwd_sum, 'seq', right)  2.11 us
    convert_element_type x2, local copies, waits for them, and re-layouts, pair_major(): return tensor.reshape(heads_here, tok_count, 2, head_size).transpose(1, 2...  2.09 us
    unnamed x8, local copies, waits for them, and re-layouts  1.81 us
    mul x1, other arithmetic, local(): d_k = k_scale * (d_kn - jnp.sum(kn * d_kn, axis=-1, keepdims=True) * kn)  1.79 us
  transfers between devices with their start and end apart: 6, of which 5 were waited for; matrix products, arithmetic and copies ran while one was open for 20% of the time, Pallas kernels for 0%

profile of v1, /device:TPU:0, one launch (start us, length us, event | category | flops | bytes accessed | tf_op | source)
XLA Modules:
  0.0 62.8 jit_solution(12845435145265798767)
XLA Ops:
  0.7 1.2 %copy.9 = f32[128,2,4,128]{3,1,0,2:T(2,128)S(1)} copy(bf16[128,2,4,128]{3,2,1,0:T(4,128)(2,1)} %param.5) | data formatting | bytes 786432 | tf_op jit(solution)/shard_map/transpose | solution.py:103
  1.9 0.2 multiply_reduce_fusion
  2.3 0.9 %fusion.3 = f32[4,16,16,16]{3,2,1,0:T(8,128)S(1)} fusion(f32[4,16,16,128]{3,2,1,0:T(8,128)S(1)} %bitcast.204, pred[16,16]{1,0:T(8,128)(4,1)S(1)} %iota_compare_fusion.7), kind=kOutput, calls=%fused_computation.10 | convolution fusion | flops 25198592 | bytes 590080 | tf_op jit(solution)/shard_map/hpid,hpjd->hpij/dot_general | solution.py:11
  3.2 0.6 %fusion.73 = f32[4,16,16,16]{3,2,1,0:T(8,128)S(1)} fusion(f32[4,16,16,16]{3,2,1,0:T(8,128)S(1)} %fusion.3), kind=kOutput, calls=%fused_computation.138 | convolution fusion | flops 3145728 | bytes 131072 | tf_op jit(solution)/shard_map/hpij,hpjk->hpik/dot_general | solution.py:11
  3.9 0.6 %fusion.74 = f32[4,16,16,16]{3,2,1,0:T(8,128)S(1)} fusion(f32[4,16,16,16]{3,2,1,0:T(8,128)S(1)} %fusion.73), kind=kOutput, calls=%fused_computation.139 | convolution fusion | flops 3145728 | bytes 131072 | tf_op jit(solution)/shard_map/hpij,hpjk->hpik/dot_general | solution.py:11
  4.5 0.7 %convolution_add_fusion.2 = f32[4,16,16,16]{3,2,1,0:T(8,128)S(1)} fusion(f32[4,16,16,16]{3,2,1,0:T(8,128)S(1)} %fusion.73, f32[4,16,16,16]{3,2,1,0:T(8,128)S(1)} %fusion.3, f32[16,16]{1,0:T(8,128)S(1)} %fusion.58), kind=kOutput, calls=%fused_computation.5 | convolution fusion | flops 3178496 | bytes 197632 | tf_op jit(solution)/shard_map/hpij,hpjk->hpik/dot_general | solution.py:11
  5.2 0.6 %fusion.75 = f32[4,16,16,16]{3,2,1,0:T(8,128)S(1)} fusion(f32[4,16,16,16]{3,2,1,0:T(8,128)S(1)} %fusion.74), kind=kOutput, calls=%fused_computation.140 | convolution fusion | flops 3145728 | bytes 131072 | tf_op jit(solution)/shard_map/hpij,hpjk->hpik/dot_general | solution.py:11
  5.8 0.6 %convolution_add_fusion.1 = f32[4,16,16,16]{3,2,1,0:T(8,128)S(1)} fusion(f32[4,16,16,16]{3,2,1,0:T(8,128)S(1)} %convolution_add_fusion.2, f32[4,16,16,16]{3,2,1,0:T(8,128)S(1)} %fusion.74), kind=kOutput, calls=%fused_computation.4 | convolution fusion | flops 3162112 | bytes 196608 | tf_op jit(solution)/shard_map/hpij,hpjk->hpik/dot_general | solution.py:11
  6.5 0.6 %convolution_add_fusion = f32[4,16,16,16]{3,2,1,0:T(8,128)S(1)} fusion(f32[4,16,16,16]{3,2,1,0:T(8,128)S(1)} %convolution_add_fusion.1, f32[4,16,16,16]{3,2,1,0:T(8,128)S(1)} %fusion.75), kind=kOutput, calls=%fused_computation.3 | convolution fusion | flops 3162112 | bytes 196608 | tf_op jit(solution)/shard_map/hpij,hpjk->hpik/dot_general | solution.py:11
  7.2 0.5 convolution_multiply_fusion.7
  7.7 0.4 fusion.69
  8.1 0.4 convolution_negate_fusion.3
  8.7 0.5 convolution_multiply_fusion.6
  9.2 0.4 fusion.70
  9.6 0.4 convolution_negate_fusion.2
  10.2 0.5 convolution_multiply_fusion.5
  10.7 0.4 fusion.71
  11.1 0.4 convolution_negate_fusion.1
  11.7 0.7 %convolution_multiply_fusion.4 = f32[4,128,128]{2,1,0:T(8,128)S(1)} fusion(f32[4,1,2,128,128]{4,3,2,0,1:T(8,128)S(1)} %bitcast.208), kind=kOutput, calls=%fused_computation.31 | convolution fusion | flops 100728832 | bytes 786432 | tf_op jit(solution)/shard_map/hpid,hpjd->hpij/dot_general | solution.py:11
  12.4 0.6 fusion.38
  13.0 0.7 %fusion.12 = f32[4,1,128,128]{3,2,0,1:T(8,128)S(1)} fusion(f32[4,128,128]{1,2,0:T(8,128)S(1)} %fusion.38, f32[4,1,2,128,128]{4,3,2,0,1:T(8,128)S(1)} %fusion.17), kind=kOutput, calls=%fused_computation.30 | convolution fusion | flops 100728832 | bytes 786432 | tf_op jit(solution)/shard_map/hpij,hpjk->hpik/dot_general | solution.py:11
  13.6 0.3 copy-done.2
  13.9 0.6 fusion.22
  14.5 1.2 %convolution_multiply_fusion.9 = f32[4,128,128]{2,1,0:T(8,128)S(1)} fusion(f32[4,256,128]{2,1,0:T(8,128)S(1)} %broadcast_multiply_fusion, f32[4,256,128]{2,1,0:T(8,128)S(1)} %fusion.22), kind=kOutput, calls=%fused_computation.39 | convolution fusion | flops 201392128 | bytes 1310720 | tf_op jit(solution)/shard_map/hjd,hjw->hdw/dot_general | solution.py:11
  15.7 4.9 %collective-permute-start = (f32[4,128,128]{2,1,0:T(8,128)S(1)}, f32[4,128,128]{2,1,0:T(8,128)S(1)}, u32[]{:S(2)}, u32[]{:S(2)}) collective-permute-start(f32[4,128,128]{2,1,0:T(8,128)S(1)} %convolution_multiply_fusion.9), channel_id=1, source_target_pairs={{0,4},{4,8},{8,12},{1,5},{5,9},{9,13},{2,6},{6,10},{10,14},{3,7},{... | collective-permute-start | bytes 786440 | tf_op jit(solution)/shard_map/ppermute | solution.py:60
  20.7 1.0 %fusion.24 = f32[4,256,128]{2,1,0:T(8,128)S(1)} fusion(f32[4,256,128]{2,1,0:T(8,128)S(1)} %broadcast_multiply_fusion, f32[4,1,128,128]{3,2,0,1:T(8,128)S(1)} %get-tuple-element.9, f32[4,1,128,128]{3,2,0,1:T(8,128)S(1)} %get-tuple-element.8, f32[4,1,128,128]{3,2,0,1:T(8,128)S(1)} %fusion.12), kind=kOutput, calls=%fused_computation.61 | convolution fusion | flops 403701760 | bytes 1835008 | tf_op jit(solution)/shard_map/hij,hjd->hid/dot_general | solution.py:11
  22.0 0.6 %fusion.10 = f32[4,128,256]{2,1,0:T(8,128)S(1)} fusion(f32[4,256,128]{2,1,0:T(8,128)S(1)} %broadcast_multiply_fusion, pred[128,256]{1,0:T(8,128)(4,1)S(1)} %iota_compare_fusion.5, f32[4,128]{1,0:T(4,128)S(1)} %get-tuple-element.17, bf16[128,4,128]{2,1,0:T(4,128)(2,1)S(1)} %copy-done.1), kind=kOutput, calls=%fused_computation.22 | convolution fusion | flops 201719808 | bytes 1214464 | tf_op jit(solution)/shard_map/hid,hjd->hij/dot_general | solution.py:11
  22.7 0.6 %convolution_subtract_fusion.2 = f32[4,128,128]{2,1,0:T(8,128)S(1)} fusion(f32[4,128,256]{2,1,0:T(8,128)S(1)} %fusion.10, f32[4,256,128]{2,1,0:T(8,128)S(1)} %fusion.24, f32[4,128]{1,0:T(4,128)S(1)} %get-tuple-element.17, bf16[128,4,128]{2,1,0:T(4,128)(2,1)S(1)} %copy-done.1), kind=kOutput, calls=%fused_computation.41 | convolution fusion | flops 201523200 | bytes 1443840 | tf_op jit(solution)/shard_map/hij,hjd->hid/dot_general | solution.py:11
  23.3 0.4 fusion.48
  23.7 1.3 %collective-permute-start.3 = (f32[4,128,128]{2,1,0:T(8,128)S(1)}, f32[4,128,128]{2,1,0:T(8,128)S(1)}, u32[]{:S(2)}, u32[]{:S(2)}) collective-permute-start(f32[4,128,128]{2,1,0:T(8,128)S(1)} %fusion.48), channel_id=1, source_target_pairs={{4,0},{8,4},{12,8},{5,1},{9,5},{13,9},{6,2},{10,6},{14,10},{7,3},{... | collective-permute-start | bytes 786440 | tf_op jit(solution)/shard_map/ppermute | solution.py:61
  25.0 0.6 %fusion.76 = f32[4,128,128]{2,1,0:T(8,128)S(1)} fusion(f32[4,128,256]{2,1,0:T(8,128)S(1)} %fusion.10, f32[4,256,128]{2,1,0:T(8,128)S(1)} %fusion.22), kind=kOutput, calls=%fused_computation.141 | convolution fusion | flops 201326592 | bytes 1310720 | tf_op jit(solution)/shard_map/hij,hjd->hid/dot_general | solution.py:11
  25.7 1.0 %fusion.13 = f32[4,128,128]{2,1,0:T(8,128)S(1)} fusion(f32[4,256,128]{2,1,0:T(8,128)S(1)} %broadcast_multiply_fusion, f32[4,256,128]{2,1,0:T(8,128)S(1)} %fusion.24, f32[128,128]{1,0:T(8,128)S(1)} %fusion.55), kind=kOutput, calls=%fused_computation.42 | convolution fusion | flops 201457664 | bytes 1376256 | tf_op jit(solution)/shard_map/hjd,hjw->hdw/dot_general | solution.py:11
  26.7 0.4 convolution_add_fusion.9
  27.2 4.6 %collective-permute-start.1 = (f32[4,128,128]{2,1,0:T(8,128)S(1)}, f32[4,128,128]{2,1,0:T(8,128)S(1)}, u32[]{:S(2)}, u32[]{:S(2)}) collective-permute-start(f32[4,128,128]{2,1,0:T(8,128)S(1)} %convolution_add_fusion.9), channel_id=1, source_target_pairs={{0,4},{4,8},{8,12},{1,5},{5,9},{9,13},{2,6},{6,10},{10,14},{3,7},{... | collective-permute-start | bytes 786440 | tf_op jit(solution)/shard_map/ppermute | solution.py:60
  31.7 0.6 fusion.51
  32.3 1.0 %collective-permute-done.3 = f32[4,128,128]{2,1,0:T(8,128)S(1)} collective-permute-done((f32[4,128,128]{2,1,0:T(8,128)S(1)}, f32[4,128,128]{2,1,0:T(8,128)S(1)}, u32[]{:S(2)}, u32[]{:S(2)}) %collective-permute-start.3) | collective-permute-done | bytes 262176 | tf_op jit(solution)/shard_map/ppermute | solution.py:61
  33.4 0.6 convolution_add_fusion.6
  34.0 1.3 %collective-permute-start.4 = (f32[4,128,128]{2,1,0:T(8,128)S(1)}, f32[4,128,128]{2,1,0:T(8,128)S(1)}, u32[]{:S(2)}, u32[]{:S(2)}) collective-permute-start(f32[4,128,128]{2,1,0:T(8,128)S(1)} %convolution_add_fusion.6), channel_id=1, source_target_pairs={{4,0},{8,4},{12,8},{5,1},{9,5},{13,9},{6,2},{10,6},{14,10},{7,3},{... | collective-permute-start | bytes 786440 | tf_op jit(solution)/shard_map/ppermute | solution.py:61
  35.3 1.4 %collective-permute-done.1 = f32[4,128,128]{2,1,0:T(8,128)S(1)} collective-permute-done((f32[4,128,128]{2,1,0:T(8,128)S(1)}, f32[4,128,128]{2,1,0:T(8,128)S(1)}, u32[]{:S(2)}, u32[]{:S(2)}) %collective-permute-start.1) | collective-permute-done | bytes 262176 | tf_op jit(solution)/shard_map/ppermute | solution.py:60
  36.7 0.4 convolution_add_fusion.8
  37.1 4.4 %collective-permute-start.2 = (f32[4,128,128]{2,1,0:T(8,128)S(1)}, f32[4,128,128]{2,1,0:T(8,128)S(1)}, u32[]{:S(2)}, u32[]{:S(2)}) collective-permute-start(f32[4,128,128]{2,1,0:T(8,128)S(1)} %convolution_add_fusion.8), channel_id=1, source_target_pairs={{0,4},{4,8},{8,12},{1,5},{5,9},{9,13},{2,6},{6,10},{10,14},{3,7},{... | collective-permute-start | bytes 786440 | tf_op jit(solution)/shard_map/ppermute | solution.py:60
  41.5 1.2 %collective-permute-done.4 = f32[4,128,128]{2,1,0:T(8,128)S(1)} collective-permute-done((f32[4,128,128]{2,1,0:T(8,128)S(1)}, f32[4,128,128]{2,1,0:T(8,128)S(1)}, u32[]{:S(2)}, u32[]{:S(2)}) %collective-permute-start.4) | collective-permute-done | bytes 262176 | tf_op jit(solution)/shard_map/ppermute | solution.py:61
  42.7 0.6 convolution_add_fusion.5
  43.3 1.5 %collective-permute-start.5 = (f32[4,128,128]{2,1,0:T(8,128)S(1)}, f32[4,128,128]{2,1,0:T(8,128)S(1)}, u32[]{:S(2)}, u32[]{:S(2)}) collective-permute-start(f32[4,128,128]{2,1,0:T(8,128)S(1)} %convolution_add_fusion.5), channel_id=1, source_target_pairs={{4,0},{8,4},{12,8},{5,1},{9,5},{13,9},{6,2},{10,6},{14,10},{7,3},{... | collective-permute-start | bytes 786440 | tf_op jit(solution)/shard_map/ppermute | solution.py:61
  44.8 0.7 %collective-permute-done.2 = f32[4,128,128]{2,1,0:T(8,128)S(1)} collective-permute-done((f32[4,128,128]{2,1,0:T(8,128)S(1)}, f32[4,128,128]{2,1,0:T(8,128)S(1)}, u32[]{:S(2)}, u32[]{:S(2)}) %collective-permute-start.2) | collective-permute-done | bytes 262176 | tf_op jit(solution)/shard_map/ppermute | solution.py:60
  45.5 0.6 convolution_subtract_fusion.1
  46.1 0.4 fusion.2
  46.6 0.4 fusion.53
  47.0 0.7 %fusion.32 = (f32[4,128]{1,0:T(4,128)S(1)}, f32[4,128,128]{2,1,0:T(8,128)S(1)}) fusion(f32[4,128,128]{1,2,0:T(8,128)S(1)} %fusion.53, f32[4,128]{1,0:T(4,128)S(1)} %get-tuple-element.17, bf16[128,4,128]{2,1,0:T(4,128)(2,1)S(1)} %copy-done.1, f32[4,128,256]{2,1,0:T(8,128)S(1)} %fusion.2, f32[4,256,128]{2,1,0:T(8,128)S(1)} %broadcast_multiply_fusion), kind=kOutput, calls=%fused_computation.68 | convolution fusion | flops 201719296 | bytes 1708032 | tf_op jit(solution)/shard_map/hij,hjd->hid/dot_general | solution.py:11
  47.7 0.4 fusion.15
  48.3 0.8 %copy.36 = bf16[128,4,128]{2,1,0:T(4,128)(2,1)} copy(bf16[128,4,128]{2,0,1:T(8,128)(2,1)S(1)} %fusion.15) | data formatting | bytes 262144
  49.1 0.8 %copy.37 = bf16[128,4,128]{2,1,0:T(4,128)(2,1)} copy(bf16[128,4,128]{2,0,1:T(8,128)(2,1)S(1)} %fusion.37) | data formatting | bytes 262144
  49.8 1.1 %fusion.28 = f32[4,256,128]{2,1,0:T(8,128)S(1)} fusion(f32[4,128,256]{2,1,0:T(8,128)S(1)} %fusion.2, f32[4,128]{1,0:T(4,128)S(1)} %get-tuple-element.17, bf16[128,4,128]{2,1,0:T(4,128)(2,1)S(1)} %copy-done.1), kind=kOutput, calls=%fused_computation.66 | convolution fusion | flops 201457664 | bytes 1181696 | tf_op jit(solution)/shard_map/hij,hid->hjd/dot_general | solution.py:11
  50.9 0.6 collective-permute-done.5
  51.6 0.6 fusion.8
  52.2 1.5 %fusion.72 = (bf16[4,256,128]{2,1,0:T(8,128)(2,1)S(1)}, f32[4,256,128]{2,1,0:T(8,128)S(1)}) fusion(f32[4,256,128]{2,1,0:T(8,128)S(1)} %fusion.8, f32[4,1,128,128]{3,2,0,1:T(8,128)S(1)} %get-tuple-element.9, f32[4,1,128,128]{3,2,0,1:T(8,128)S(1)} %get-tuple-element.8, f32[4,1,128,128]{3,2,0,1:T(8,128)S(1)} %fusion.12), kind=kOutput, calls=%fused_computation.137 | convolution fusion | flops 403832832 | bytes 2097152 | tf_op jit(solution)/shard_map/hij,hiw->hjw/dot_general | solution.py:11
  53.7 1.0 %fusion.1 = f32[4,256,256]{2,1,0:T(8,128)S(1)} fusion(f32[4,256,128]{2,1,0:T(8,128)S(1)} %get-tuple-element.21, f32[4,256,128]{2,1,0:T(8,128)S(1)} %convolution_subtract_fusion.1, pred[256,256]{1,0:T(8,128)(4,1)S(1)} %iota_compare_fusion.4), kind=kOutput, calls=%fused_computation.2 | convolution fusion | flops 403177472 | bytes 2162688 | tf_op jit(solution)/shard_map/hiw,hjw->hij/dot_general | solution.py:11
  54.7 1.1 %fusion.77 = f32[4,256,128]{2,1,0:T(8,128)S(1)} fusion(f32[4,256,256]{2,1,0:T(8,128)S(1)} %fusion.1, f32[4,256,128]{2,1,0:T(8,128)S(1)} %broadcast_multiply_fusion), kind=kOutput, calls=%fused_computation.142 | convolution fusion | flops 402653184 | bytes 2097152 | tf_op jit(solution)/shard_map/hij,hjd->hid/dot_general | solution.py:11
  55.8 0.6 fusion.9
  56.4 0.6 fusion.7
  57.0 1.9 %convolution_add_fusion.3 = f32[4,256,128]{2,1,0:T(8,128)S(1)} fusion(f32[4,256,128]{2,1,0:T(8,128)S(1)} %fusion.7, f32[4,256,256]{2,1,0:T(8,128)S(1)} %fusion.1, f32[4,256,128]{2,1,0:T(8,128)S(1)} %broadcast_multiply_fusion), kind=kOutput, calls=%fused_computation.6 | convolution fusion | flops 402784256 | bytes 2621440 | tf_op jit(solution)/shard_map/hji,hjd->hid/dot_general | solution.py:11
  58.9 1.8 %fusion.11 = bf16[4,256,128]{2,1,0:T(8,128)(2,1)S(1)} fusion(f32[4,256,128]{2,1,0:T(8,128)S(1)} %convolution_add_fusion.3, f32[4,256,128]{2,1,0:T(8,128)S(1)} %broadcast_multiply_fusion, f32[4,256]{1,0:T(4,128)S(1)} %add_rsqrt_fusion), kind=kOutput, calls=%fused_computation.23 | output fusion | flops 656511 | bytes 1314816 | tf_op jit(solution)/shard_map/mul | solution.py:139
  60.7 1.0 %copy.84 = bf16[4,128,2,128]{3,0,2,1:T(4,128)(2,1)} copy(bf16[4,128,2,128]{3,2,1,0:T(2,128)(2,1)S(1)} %bitcast.220) | data formatting | bytes 524288 | tf_op jit(solution)/shard_map/convert_element_type | solution.py:148
  61.7 1.0 %copy.83 = bf16[4,128,2,128]{3,0,2,1:T(4,128)(2,1)} copy(bf16[4,128,2,128]{3,2,1,0:T(2,128)(2,1)S(1)} %bitcast.221) | data formatting | bytes 524288 | tf_op jit(solution)/shard_map/convert_element_type | solution.py:148
  (24 shorter events, 1.3 us)
Async XLA Ops:
  0.6 22.7 %copy-start = (bf16[128,4,128]{2,1,0:T(4,128)(2,1)S(1)}, bf16[128,4,128]{2,1,0:T(4,128)(2,1)}, u32[]{:S(2)}) copy-start(bf16[128,4,128]{2,1,0:T(4,128)(2,1)} %param.7) | copy-start | bytes 393220
  13.0 1.0 %copy-start.2 = (bf16[128,2,4,128]{3,2,1,0:T(4,128)(2,1)S(1)}, bf16[128,2,4,128]{3,2,1,0:T(4,128)(2,1)}, u32[]{:S(2)}) copy-start(bf16[128,2,4,128]{3,2,1,0:T(4,128)(2,1)} %param.6) | copy-start | bytes 786436
  15.7 11.0 %collective-permute-start = (f32[4,128,128]{2,1,0:T(8,128)S(1)}, f32[4,128,128]{2,1,0:T(8,128)S(1)}, u32[]{:S(2)}, u32[]{:S(2)}) collective-permute-start(f32[4,128,128]{2,1,0:T(8,128)S(1)} %convolution_multiply_fusion.9), channel_id=1, source_target_pairs={{0,4},{4,8},{8,12},{1,5},{5,9},{9,13},{2,6},{6,10},{10,14},{3,7},{... | collective-permute-start | bytes 786440 | tf_op jit(solution)/shard_map/ppermute | solution.py:60
  20.7 1.1 %copy-start.1 = (bf16[128,4,128]{2,1,0:T(4,128)(2,1)S(1)}, bf16[128,4,128]{2,1,0:T(4,128)(2,1)}, u32[]{:S(2)}) copy-start(bf16[128,4,128]{2,1,0:T(4,128)(2,1)} %param.4) | copy-start | bytes 393220
  23.7 9.6 %collective-permute-start.3 = (f32[4,128,128]{2,1,0:T(8,128)S(1)}, f32[4,128,128]{2,1,0:T(8,128)S(1)}, u32[]{:S(2)}, u32[]{:S(2)}) collective-permute-start(f32[4,128,128]{2,1,0:T(8,128)S(1)} %fusion.48), channel_id=1, source_target_pairs={{4,0},{8,4},{12,8},{5,1},{9,5},{13,9},{6,2},{10,6},{14,10},{7,3},{... | collective-permute-start | bytes 786440 | tf_op jit(solution)/shard_map/ppermute | solution.py:61
  27.2 9.5 %collective-permute-start.1 = (f32[4,128,128]{2,1,0:T(8,128)S(1)}, f32[4,128,128]{2,1,0:T(8,128)S(1)}, u32[]{:S(2)}, u32[]{:S(2)}) collective-permute-start(f32[4,128,128]{2,1,0:T(8,128)S(1)} %convolution_add_fusion.9), channel_id=1, source_target_pairs={{0,4},{4,8},{8,12},{1,5},{5,9},{9,13},{2,6},{6,10},{10,14},{3,7},{... | collective-permute-start | bytes 786440 | tf_op jit(solution)/shard_map/ppermute | solution.py:60
  34.0 8.7 %collective-permute-start.4 = (f32[4,128,128]{2,1,0:T(8,128)S(1)}, f32[4,128,128]{2,1,0:T(8,128)S(1)}, u32[]{:S(2)}, u32[]{:S(2)}) collective-permute-start(f32[4,128,128]{2,1,0:T(8,128)S(1)} %convolution_add_fusion.6), channel_id=1, source_target_pairs={{4,0},{8,4},{12,8},{5,1},{9,5},{13,9},{6,2},{10,6},{14,10},{7,3},{... | collective-permute-start | bytes 786440 | tf_op jit(solution)/shard_map/ppermute | solution.py:61
  37.1 8.4 %collective-permute-start.2 = (f32[4,128,128]{2,1,0:T(8,128)S(1)}, f32[4,128,128]{2,1,0:T(8,128)S(1)}, u32[]{:S(2)}, u32[]{:S(2)}) collective-permute-start(f32[4,128,128]{2,1,0:T(8,128)S(1)} %convolution_add_fusion.8), channel_id=1, source_target_pairs={{0,4},{4,8},{8,12},{1,5},{5,9},{9,13},{2,6},{6,10},{10,14},{3,7},{... | collective-permute-start | bytes 786440 | tf_op jit(solution)/shard_map/ppermute | solution.py:60
  43.3 8.3 %collective-permute-start.5 = (f32[4,128,128]{2,1,0:T(8,128)S(1)}, f32[4,128,128]{2,1,0:T(8,128)S(1)}, u32[]{:S(2)}, u32[]{:S(2)}) collective-permute-start(f32[4,128,128]{2,1,0:T(8,128)S(1)} %convolution_add_fusion.5), channel_id=1, source_target_pairs={{4,0},{8,4},{12,8},{5,1},{9,5},{13,9},{6,2},{10,6},{14,10},{7,3},{... | collective-permute-start | bytes 786440 | tf_op jit(solution)/shard_map/ppermute | solution.py:61

commit v2 on v0

--- a/solution.py
+++ b/solution.py
@@ -53,8 +53,12 @@
 
 def scan_seq(transition, offset, local_cot):
     count = lax.axis_size("seq")
+    if count == 1:
+        zero = jnp.zeros_like(offset)
+        return zero, zero
     fwd_map, fwd_sum = transition, offset
     bwd_map, bwd_sum = transition, local_cot
+    ex_map = ex_sum = bx_map = bx_sum = None
     shift = 1
     while shift < count:
         right = [(i, i + shift) for i in range(count - shift)]
@@ -64,17 +68,24 @@
             got_sum = lax.ppermute(fwd_sum, "seq", right)
             got_cot = lax.ppermute(bwd_sum, "seq", left)
         else:
-            got_map, got_sum = lax.ppermute((fwd_map, fwd_sum), "seq", right)
-            got_bmap, got_cot = lax.ppermute((bwd_map, bwd_sum), "seq", left)
-        fwd_sum = mm("hij,hjk->hik", fwd_map, got_sum) + fwd_sum
-        bwd_sum = mm("hji,hjk->hik", bwd_map, got_cot) + bwd_sum
+            got_map, got_sum = lax.ppermute(jnp.stack([fwd_map, fwd_sum]), "seq", right)
+            got_bmap, got_cot = lax.ppermute(jnp.stack([bwd_map, bwd_sum]), "seq", left)
+        if ex_map is None:
+            ex_map, ex_sum = (None if last else got_map), got_sum
+            bx_map, bx_sum = (None if last else got_bmap), got_cot
+        else:
+            ex_sum = mm("hij,hjk->hik", ex_map, got_sum) + ex_sum
+            bx_sum = bx_sum + mm("hji,hjk->hik", bx_map, got_cot)
+            if not last:
+                ex_map = mm("hij,hjk->hik", ex_map, got_map)
+                bx_map = mm("hij,hjk->hik", got_bmap, bx_map)
         if not last:
+            fwd_sum = mm("hij,hjk->hik", fwd_map, got_sum) + fwd_sum
+            bwd_sum = bwd_sum + mm("hji,hjk->hik", bwd_map, got_cot)
             fwd_map = mm("hij,hjk->hik", fwd_map, got_map)
             bwd_map = mm("hij,hjk->hik", got_bmap, bwd_map)
         shift *= 2
-    state_in = lax.ppermute(fwd_sum, "seq", [(i, i + 1) for i in range(count - 1)])
-    end_cot = lax.ppermute(bwd_sum, "seq", [(i + 1, i) for i in range(count - 1)])
-    return state_in, end_cot
+    return ex_sum, bx_sum
 
 
 def local(queries, reflect_keys, write_values, out_cotangent):

time: 75.8 us -> 72.5 us (0.956)
  starting transfers between devices: 29.2 us -> 13 us
  waiting for transfers between devices: 5.84 us -> 19.6 us
  matrix products: 31.1 us -> 30.3 us
    ppermute x6 -> x2, starting transfers between devices: 22.6 us -> 6.26 us  [the longest x1 4.97 us: scan_seq(): got_map, got_sum = lax.ppermute(jnp.stack([fwd_map, fwd_sum]), 'seq', right)]
    ppermute x1, waiting for transfers between devices: 1.43 us -> 8.28 us  [scan_seq(): got_cot = lax.ppermute(bwd_sum, 'seq', left)]
    ppermute x6 -> x2, waiting for transfers between devices: 2.82 us -> 8.57 us  [the longest x1 8.57 us: scan_seq(): got_map, got_sum = lax.ppermute(jnp.stack([fwd_map, fwd_sum]), 'seq', right)]
    ppermute x1, waiting for transfers between devices: 1.59 us -> 2.74 us  [scan_seq(): got_sum = lax.ppermute(fwd_sum, 'seq', right)]
    dot_general x47 -> x45, matrix products: 31.1 us -> 30.3 us  [mm(): return jnp.einsum(spec, *operands, precision=highest)]
  transfers between devices with their start and end apart: 8 -> 4, of which waited for: 6 -> 3; matrix products, arithmetic and copies ran while one was open for 17% -> 7% of each run, Pallas kernels for 0% -> 0%
where the time goes in v2:
time: 72.5 us; the launch traced here: 72.3 us
  matrix products  30.3 us (42%)
  waiting for transfers between devices  19.6 us (27%)
  starting transfers between devices  13 us (18%)
  local copies, waits for them, and re-layouts  4.94 us (7%)
  other arithmetic  3.24 us (4%)
  between operations  1.17 us (2%)
    dot_general x45, matrix products, mm(): return jnp.einsum(spec, *operands, precision=highest)  30.3 us
    ppermute x1, waiting for transfers between devices, scan_seq(): got_map, got_sum = lax.ppermute(jnp.stack([fwd_map, fwd_sum]), 'seq', right)  8.57 us
    ppermute x1, waiting for transfers between devices, scan_seq(): got_cot = lax.ppermute(bwd_sum, 'seq', left)  8.28 us
    ppermute x1, starting transfers between devices, scan_seq(): got_sum = lax.ppermute(fwd_sum, 'seq', right)  5.42 us
    ppermute x1, starting transfers between devices, scan_seq(): got_map, got_sum = lax.ppermute(jnp.stack([fwd_map, fwd_sum]), 'seq', right)  4.97 us
    ppermute x1, waiting for transfers between devices, scan_seq(): got_sum = lax.ppermute(fwd_sum, 'seq', right)  2.74 us
    convert_element_type x2, local copies, waits for them, and re-layouts, pair_major(): return tensor.reshape(heads_here, tok_count, 2, head_size).transpose(1, 2...  2.09 us
    mul x1, other arithmetic, local(): d_k = k_scale * (d_kn - jnp.sum(kn * d_kn, axis=-1, keepdims=True) * kn)  1.79 us
  transfers between devices with their start and end apart: 4, of which 3 were waited for; matrix products, arithmetic and copies ran while one was open for 7% of the time, Pallas kernels for 0%

profile of v2, /device:TPU:0, one launch (start us, length us, event | category | flops | bytes accessed | tf_op | source)
XLA Modules:
  0.0 72.3 jit_solution(10859678410933755812)
XLA Ops:
  0.7 1.2 %copy.9 = f32[128,2,4,128]{3,1,0,2:T(2,128)S(1)} copy(bf16[128,2,4,128]{3,2,1,0:T(4,128)(2,1)} %param.5) | data formatting | bytes 786432 | tf_op jit(solution)/shard_map/transpose | solution.py:96
  1.9 0.2 multiply_reduce_fusion
  2.1 0.2 broadcast_multiply_fusion
  2.3 0.9 %fusion.3 = f32[4,16,16,16]{3,2,1,0:T(8,128)S(1)} fusion(f32[4,16,16,128]{3,2,1,0:T(8,128)S(1)} %bitcast.219, pred[16,16]{1,0:T(8,128)(4,1)S(1)} %iota_compare_fusion.7), kind=kOutput, calls=%fused_computation.10 | convolution fusion | flops 25198592 | bytes 590080 | tf_op jit(solution)/shard_map/hpid,hpjd->hpij/dot_general | solution.py:11
  3.2 0.6 fusion.73
  3.9 0.6 fusion.74
  4.5 0.7 convolution_add_fusion.2
  5.2 0.6 fusion.75
  5.8 0.6 convolution_add_fusion.1
  6.5 0.5 convolution_multiply_fusion.7
  7.0 0.6 convolution_add_fusion
  7.7 0.4 fusion.69
  8.1 0.4 convolution_negate_fusion.3
  8.5 0.5 convolution_multiply_fusion.6
  9.0 0.1 select_maximum_fusion.3
  9.2 0.4 fusion.70
  9.6 0.4 convolution_negate_fusion.2
  10.0 0.5 convolution_multiply_fusion.5
  10.5 0.1 select_maximum_fusion.2
  10.7 0.4 fusion.71
  11.1 0.4 convolution_negate_fusion.1
  11.5 0.7 convolution_multiply_fusion.4
  12.3 0.6 fusion.38
  12.9 0.7 fusion.12
  13.6 1.0 %fusion.24 = f32[4,256,128]{2,1,0:T(8,128)S(1)} fusion(f32[4,256,128]{2,1,0:T(8,128)S(1)} %broadcast_multiply_fusion, f32[4,1,128,128]{3,2,0,1:T(8,128)S(1)} %get-tuple-element.9, f32[4,1,128,128]{3,2,0,1:T(8,128)S(1)} %get-tuple-element.8, f32[4,1,128,128]{3,2,0,1:T(8,128)S(1)} %fusion.12), kind=kOutput, calls=%fused_computation.63 | convolution fusion | flops 403701760 | bytes 1835008 | tf_op jit(solution)/shard_map/hij,hjd->hid/dot_general | solution.py:11
  14.7 0.8 %fusion.22 = f32[4,256,128]{2,1,0:T(8,128)S(1)} fusion(f32[4,1,128,128]{3,2,0,1:T(8,128)S(1)} %get-tuple-element.9, f32[4,1,128,128]{3,2,0,1:T(8,128)S(1)} %get-tuple-element.8, f32[4,1,128,128]{3,2,0,1:T(8,128)S(1)} %fusion.12, bf16[256,4,128]{2,1,0:T(4,128)(2,1)S(1)} %bitcast.243), kind=kOutput, calls=%fused_computation.62 | convolution fusion | flops 403701760 | bytes 1572864 | tf_op jit(solution)/shard_map/hij,hjd->hid/dot_general | solution.py:11
  15.5 1.0 %convolution_multiply_fusion.9 = f32[4,128,128]{2,1,0:T(8,128)S(1)} fusion(f32[4,256,128]{2,1,0:T(8,128)S(1)} %broadcast_multiply_fusion, f32[4,256,128]{2,1,0:T(8,128)S(1)} %fusion.22), kind=kOutput, calls=%fused_computation.39 | convolution fusion | flops 201392128 | bytes 1310720 | tf_op jit(solution)/shard_map/hjd,hjw->hdw/dot_general | solution.py:11
  16.5 0.1 fusion.33
  16.8 1.0 %fusion.13 = f32[4,128,128]{2,1,0:T(8,128)S(1)} fusion(f32[4,256,128]{2,1,0:T(8,128)S(1)} %broadcast_multiply_fusion, f32[4,256,128]{2,1,0:T(8,128)S(1)} %fusion.24, f32[128,128]{1,0:T(8,128)S(1)} %fusion.55), kind=kOutput, calls=%fused_computation.42 | convolution fusion | flops 201457664 | bytes 1376256 | tf_op jit(solution)/shard_map/hjd,hjw->hdw/dot_general | solution.py:11
  17.8 0.6 fusion.10
  18.5 0.6 convolution_subtract_fusion.2
  19.2 0.4 fusion.48
  19.7 5.0 %collective-permute-start = (f32[2,4,128,128]{3,2,1,0:T(8,128)S(1)}, f32[2,4,128,128]{3,2,1,0:T(8,128)S(1)}, u32[]{:S(2)}, u32[]{:S(2)}) collective-permute-start(f32[2,4,128,128]{3,2,1,0:T(8,128)S(1)} %get-tuple-element.17), channel_id=1, source_target_pairs={{0,4},{4,8},{8,12},{1,5},{5,9},{9,13},{2,6},{6,10},{10,14},{3,7},{... | collective-permute-start | bytes 1572872 | tf_op jit(solution)/shard_map/ppermute | solution.py:71
  24.6 1.3 %collective-permute-start.2 = (f32[2,4,128,128]{3,2,1,0:T(8,128)S(1)}, f32[2,4,128,128]{3,2,1,0:T(8,128)S(1)}, u32[]{:S(2)}, u32[]{:S(2)}) collective-permute-start(f32[2,4,128,128]{3,2,1,0:T(8,128)S(1)} %get-tuple-element.16), channel_id=1, source_target_pairs={{4,0},{8,4},{12,8},{5,1},{9,5},{13,9},{6,2},{10,6},{14,10},{7,3},{... | collective-permute-start | bytes 1572872 | tf_op jit(solution)/shard_map/ppermute | solution.py:72
  25.9 0.6 fusion.76
  26.6 0.6 fusion.51
  27.2 8.6 %collective-permute-done = f32[2,4,128,128]{3,2,1,0:T(8,128)S(1)} collective-permute-done((f32[2,4,128,128]{3,2,1,0:T(8,128)S(1)}, f32[2,4,128,128]{3,2,1,0:T(8,128)S(1)}, u32[]{:S(2)}, u32[]{:S(2)}) %collective-permute-start) | collective-permute-done | bytes 524320 | tf_op jit(solution)/shard_map/ppermute | solution.py:71
  35.8 0.4 convolution_add_fusion.9
  36.2 5.4 %collective-permute-start.1 = (f32[4,128,128]{2,1,0:T(8,128)S(1)}, f32[4,128,128]{2,1,0:T(8,128)S(1)}, u32[]{:S(2)}, u32[]{:S(2)}) collective-permute-start(f32[4,128,128]{2,1,0:T(8,128)S(1)} %convolution_add_fusion.9), channel_id=1, source_target_pairs={{0,8},{4,12},{1,9},{5,13},{2,10},{6,14},{3,11},{7,15},{16,24},{20,... | collective-permute-start | bytes 786440 | tf_op jit(solution)/shard_map/ppermute | solution.py:68
  41.6 0.6 convolution_add_fusion.6
  42.3 1.3 %collective-permute-start.3 = (f32[4,128,128]{2,1,0:T(8,128)S(1)}, f32[4,128,128]{2,1,0:T(8,128)S(1)}, u32[]{:S(2)}, u32[]{:S(2)}) collective-permute-start(f32[4,128,128]{2,1,0:T(8,128)S(1)} %convolution_add_fusion.6), channel_id=1, source_target_pairs={{8,0},{12,4},{9,1},{13,5},{10,2},{14,6},{11,3},{15,7},{24,16},{28,... | collective-permute-start | bytes 786440 | tf_op jit(solution)/shard_map/ppermute | solution.py:69
  43.6 2.7 %collective-permute-done.1 = f32[4,128,128]{2,1,0:T(8,128)S(1)} collective-permute-done((f32[4,128,128]{2,1,0:T(8,128)S(1)}, f32[4,128,128]{2,1,0:T(8,128)S(1)}, u32[]{:S(2)}, u32[]{:S(2)}) %collective-permute-start.1) | collective-permute-done | bytes 262176 | tf_op jit(solution)/shard_map/ppermute | solution.py:68
  46.3 0.4 convolution_add_fusion.8
  46.7 0.6 convolution_subtract_fusion.1
  47.3 0.4 fusion.2
  47.7 0.4 fusion.53
  48.1 1.1 %fusion.28 = f32[4,256,128]{2,1,0:T(8,128)S(1)} fusion(f32[4,128,256]{2,1,0:T(8,128)S(1)} %fusion.2, f32[4,128]{1,0:T(4,128)S(1)} %get-tuple-element.19, bf16[128,4,128]{2,1,0:T(4,128)(2,1)S(1)} %copy-done.1), kind=kOutput, calls=%fused_computation.68 | convolution fusion | flops 201457664 | bytes 1181696 | tf_op jit(solution)/shard_map/hij,hid->hjd/dot_general | solution.py:11
  49.3 8.3 %collective-permute-done.3 = f32[4,128,128]{2,1,0:T(8,128)S(1)} collective-permute-done((f32[4,128,128]{2,1,0:T(8,128)S(1)}, f32[4,128,128]{2,1,0:T(8,128)S(1)}, u32[]{:S(2)}, u32[]{:S(2)}) %collective-permute-start.3) | collective-permute-done | bytes 262176 | tf_op jit(solution)/shard_map/ppermute | solution.py:69
  57.6 0.6 convolution_add_fusion.5
  58.2 0.6 fusion.9
  58.8 0.6 fusion.8
  59.4 1.5 %fusion.72 = (bf16[4,256,128]{2,1,0:T(8,128)(2,1)S(1)}, f32[4,256,128]{2,1,0:T(8,128)S(1)}) fusion(f32[4,256,128]{2,1,0:T(8,128)S(1)} %fusion.8, f32[4,1,128,128]{3,2,0,1:T(8,128)S(1)} %get-tuple-element.9, f32[4,1,128,128]{3,2,0,1:T(8,128)S(1)} %get-tuple-element.8, f32[4,1,128,128]{3,2,0,1:T(8,128)S(1)} %fusion.12), kind=kOutput, calls=%fused_computation.143 | convolution fusion | flops 403832832 | bytes 2097152 | tf_op jit(solution)/shard_map/hij,hiw->hjw/dot_general | solution.py:11
  60.9 1.0 %fusion.1 = f32[4,256,256]{2,1,0:T(8,128)S(1)} fusion(f32[4,256,128]{2,1,0:T(8,128)S(1)} %get-tuple-element.23, f32[4,256,128]{2,1,0:T(8,128)S(1)} %convolution_subtract_fusion.1, pred[256,256]{1,0:T(8,128)(4,1)S(1)} %iota_compare_fusion.4), kind=kOutput, calls=%fused_computation.2 | convolution fusion | flops 403177472 | bytes 2162688 | tf_op jit(solution)/shard_map/hiw,hjw->hij/dot_general | solution.py:11
  62.0 1.1 %fusion.77 = f32[4,256,128]{2,1,0:T(8,128)S(1)} fusion(f32[4,256,256]{2,1,0:T(8,128)S(1)} %fusion.1, f32[4,256,128]{2,1,0:T(8,128)S(1)} %broadcast_multiply_fusion), kind=kOutput, calls=%fused_computation.148 | convolution fusion | flops 402653184 | bytes 2097152 | tf_op jit(solution)/shard_map/hij,hjd->hid/dot_general | solution.py:11
  63.0 0.6 fusion.7
  63.6 1.9 %convolution_add_fusion.3 = f32[4,256,128]{2,1,0:T(8,128)S(1)} fusion(f32[4,256,128]{2,1,0:T(8,128)S(1)} %fusion.7, f32[4,256,256]{2,1,0:T(8,128)S(1)} %fusion.1, f32[4,256,128]{2,1,0:T(8,128)S(1)} %broadcast_multiply_fusion), kind=kOutput, calls=%fused_computation.6 | convolution fusion | flops 402784256 | bytes 2621440 | tf_op jit(solution)/shard_map/hji,hjd->hid/dot_general | solution.py:11
  65.5 1.8 %fusion.11 = bf16[4,256,128]{2,1,0:T(8,128)(2,1)S(1)} fusion(f32[4,256,128]{2,1,0:T(8,128)S(1)} %convolution_add_fusion.3, f32[4,256,128]{2,1,0:T(8,128)S(1)} %broadcast_multiply_fusion, f32[4,256]{1,0:T(4,128)S(1)} %add_rsqrt_fusion), kind=kOutput, calls=%fused_computation.23 | output fusion | flops 656511 | bytes 1314816 | tf_op jit(solution)/shard_map/mul | solution.py:132
  67.3 1.0 %copy.84 = bf16[4,128,2,128]{3,0,2,1:T(4,128)(2,1)} copy(bf16[4,128,2,128]{3,2,1,0:T(2,128)(2,1)S(1)} %bitcast.238) | data formatting | bytes 524288 | tf_op jit(solution)/shard_map/convert_element_type | solution.py:141
  68.3 1.0 %copy.83 = bf16[4,128,2,128]{3,0,2,1:T(4,128)(2,1)} copy(bf16[4,128,2,128]{3,2,1,0:T(2,128)(2,1)S(1)} %bitcast.241) | data formatting | bytes 524288 | tf_op jit(solution)/shard_map/convert_element_type | solution.py:141
  69.4 0.7 %fusion.32 = (f32[4,128]{1,0:T(4,128)S(1)}, f32[4,128,128]{2,1,0:T(8,128)S(1)}) fusion(f32[4,128,128]{1,2,0:T(8,128)S(1)} %fusion.53, f32[4,128]{1,0:T(4,128)S(1)} %get-tuple-element.19, bf16[128,4,128]{2,1,0:T(4,128)(2,1)S(1)} %copy-done.1, f32[4,128,256]{2,1,0:T(8,128)S(1)} %fusion.2, f32[4,256,128]{2,1,0:T(8,128)S(1)} %broadcast_multiply_fusion), kind=kOutput, calls=%fused_computation.70 | convolution fusion | flops 201719296 | bytes 1708032 | tf_op jit(solution)/shard_map/hij,hjd->hid/dot_general | solution.py:11
  70.1 0.2 fusion.37
  70.3 0.8 %copy.37 = bf16[128,4,128]{2,1,0:T(4,128)(2,1)} copy(bf16[128,4,128]{2,0,1:T(8,128)(2,1)S(1)} %fusion.37) | data formatting | bytes 262144
  71.1 0.4 fusion.15
  71.5 0.8 %copy.36 = bf16[128,4,128]{2,1,0:T(4,128)(2,1)} copy(bf16[128,4,128]{2,0,1:T(8,128)(2,1)S(1)} %fusion.15) | data formatting | bytes 262144
  (21 shorter events, 0.6 us)
Async XLA Ops:
  0.6 18.5 %copy-start = (bf16[128,4,128]{2,1,0:T(4,128)(2,1)S(1)}, bf16[128,4,128]{2,1,0:T(4,128)(2,1)}, u32[]{:S(2)}) copy-start(bf16[128,4,128]{2,1,0:T(4,128)(2,1)} %param.7) | copy-start | bytes 393220
  13.6 1.0 %copy-start.2 = (bf16[128,2,4,128]{3,2,1,0:T(4,128)(2,1)S(1)}, bf16[128,2,4,128]{3,2,1,0:T(4,128)(2,1)}, u32[]{:S(2)}) copy-start(bf16[128,2,4,128]{3,2,1,0:T(4,128)(2,1)} %param.6) | copy-start | bytes 786436
  15.5 1.1 %copy-start.1 = (bf16[128,4,128]{2,1,0:T(4,128)(2,1)S(1)}, bf16[128,4,128]{2,1,0:T(4,128)(2,1)}, u32[]{:S(2)}) copy-start(bf16[128,4,128]{2,1,0:T(4,128)(2,1)} %param.4) | copy-start | bytes 393220
  19.7 16.1 %collective-permute-start = (f32[2,4,128,128]{3,2,1,0:T(8,128)S(1)}, f32[2,4,128,128]{3,2,1,0:T(8,128)S(1)}, u32[]{:S(2)}, u32[]{:S(2)}) collective-permute-start(f32[2,4,128,128]{3,2,1,0:T(8,128)S(1)} %get-tuple-element.17), channel_id=1, source_target_pairs={{0,4},{4,8},{8,12},{1,5},{5,9},{9,13},{2,6},{6,10},{10,14},{3,7},{... | collective-permute-start | bytes 1572872 | tf_op jit(solution)/shard_map/ppermute | solution.py:71
  24.6 17.0 %collective-permute-start.2 = (f32[2,4,128,128]{3,2,1,0:T(8,128)S(1)}, f32[2,4,128,128]{3,2,1,0:T(8,128)S(1)}, u32[]{:S(2)}, u32[]{:S(2)}) collective-permute-start(f32[2,4,128,128]{3,2,1,0:T(8,128)S(1)} %get-tuple-element.16), channel_id=1, source_target_pairs={{4,0},{8,4},{12,8},{5,1},{9,5},{13,9},{6,2},{10,6},{14,10},{7,3},{... | collective-permute-start | bytes 1572872 | tf_op jit(solution)/shard_map/ppermute | solution.py:72
  36.2 10.1 %collective-permute-start.1 = (f32[4,128,128]{2,1,0:T(8,128)S(1)}, f32[4,128,128]{2,1,0:T(8,128)S(1)}, u32[]{:S(2)}, u32[]{:S(2)}) collective-permute-start(f32[4,128,128]{2,1,0:T(8,128)S(1)} %convolution_add_fusion.9), channel_id=1, source_target_pairs={{0,8},{4,12},{1,9},{5,13},{2,10},{6,14},{3,11},{7,15},{16,24},{20,... | collective-permute-start | bytes 786440 | tf_op jit(solution)/shard_map/ppermute | solution.py:68
  42.3 15.3 %collective-permute-start.3 = (f32[4,128,128]{2,1,0:T(8,128)S(1)}, f32[4,128,128]{2,1,0:T(8,128)S(1)}, u32[]{:S(2)}, u32[]{:S(2)}) collective-permute-start(f32[4,128,128]{2,1,0:T(8,128)S(1)} %convolution_add_fusion.6), channel_id=1, source_target_pairs={{8,0},{12,4},{9,1},{13,5},{10,2},{14,6},{11,3},{15,7},{24,16},{28,... | collective-permute-start | bytes 786440 | tf_op jit(solution)/shard_map/ppermute | solution.py:69

commit v3 on v2

--- a/solution.py
+++ b/solution.py
@@ -1,6 +1,7 @@
 import jax
 import jax.numpy as jnp
 from jax import lax
+from jax.experimental import pallas as pl
 from jax.sharding import PartitionSpec as P
 
 highest = lax.Precision.HIGHEST
@@ -51,11 +52,163 @@
     return inverse.reshape(heads, rows, rows)
 
 
+TILE = 128
+
+
+def dot(left, right, t_left=False, t_right=False):
+    dims = (((0 if t_left else 1,), (1 if t_right else 0,)), ((), ()))
+    return lax.dot_general(
+        left, right, dims, precision=highest, preferred_element_type=jnp.float32
+    )
+
+
+def ids(rows, cols):
+    return (
+        lax.broadcasted_iota(jnp.int32, (rows, cols), 0),
+        lax.broadcasted_iota(jnp.int32, (rows, cols), 1),
+    )
+
+
+def normed(tensor):
+    scale = lax.rsqrt(jnp.sum(tensor * tensor, axis=-1, keepdims=True) + 1e-06)
+    return tensor * scale, scale
+
+
+def tile_inverse(link):
+    row, col = ids(TILE, TILE)
+    eye = jnp.where(row == col, 1.0, 0.0).astype(jnp.float32)
+    power = jnp.where(row // LEAF == col // LEAF, -link, 0.0)
+    inverse = eye + power
+    reach = 2
+    while reach < LEAF:
+        power = dot(power, power)
+        inverse = inverse + dot(inverse, power)
+        reach *= 2
+    span = LEAF
+    while span < TILE:
+        cross = (row // (2 * span) == col // (2 * span)) & (row // span != col // span)
+        inverse = inverse - dot(inverse, dot(jnp.where(cross, link, 0.0), inverse))
+        span *= 2
+    return inverse
+
+
+def front_kernel(q_ref, k_ref, v_ref, c_ref, inv_ref, proj_ref, updv_ref, scores_ref,
+                 rmap_ref, own_ref, trans_ref, off_ref, lc_ref):
+    rows = k_ref.shape[1]
+    size = k_ref.shape[2]
+    toks = q_ref.shape[1]
+    tiles = rows // TILE
+    qn, _ = normed(q_ref[0])
+    kn, _ = normed(k_ref[0])
+    vals = v_ref[0]
+    cot = c_ref[0]
+    row, col = ids(TILE, TILE)
+    key_tiles = [kn[t * TILE:(t + 1) * TILE] for t in range(tiles)]
+    val_tiles = [vals[t * TILE:(t + 1) * TILE] for t in range(tiles)]
+    inv = {}
+    for i in range(tiles):
+        gram = dot(key_tiles[i], key_tiles[i], t_right=True)
+        inv[i, i] = tile_inverse(jnp.where(row > col, 2.0 * gram, 0.0))
+        for j in range(i - 1, -1, -1):
+            acc = None
+            for m in range(j, i):
+                link = 2.0 * dot(key_tiles[i], key_tiles[m], t_right=True)
+                term = dot(link, inv[m, j])
+                acc = term if acc is None else acc + term
+            inv[i, j] = -dot(inv[i, i], acc)
+    zero_tile = jnp.zeros((TILE, TILE), jnp.float32)
+    for i in range(tiles):
+        for j in range(tiles):
+            inv_ref[0, i * TILE:(i + 1) * TILE, j * TILE:(j + 1) * TILE] = inv.get((i, j), zero_tile)
+        proj_i = None
+        updv_i = None
+        for j in range(i + 1):
+            p_term = dot(inv[i, j], key_tiles[j])
+            u_term = dot(inv[i, j], val_tiles[j])
+            proj_i = p_term if proj_i is None else proj_i + p_term
+            updv_i = u_term if updv_i is None else updv_i + u_term
+        proj_ref[0, i * TILE:(i + 1) * TILE, :] = proj_i
+        updv_ref[0, i * TILE:(i + 1) * TILE, :] = updv_i
+    proj = proj_ref[0]
+    updv = updv_ref[0]
+    tok_ids, sub_ids = ids(toks, rows)
+    scores = jnp.where(sub_ids <= 2 * tok_ids + 1, 2.0 * dot(qn, kn, t_right=True), 0.0)
+    scores_ref[0] = scores
+    rmap = qn - dot(scores, proj)
+    rmap_ref[0] = rmap
+    own_ref[0] = dot(scores, updv)
+    er, ec = ids(size, size)
+    trans_ref[0] = jnp.where(er == ec, 1.0, 0.0) - 2.0 * dot(kn, proj, t_left=True)
+    off_ref[0] = 2.0 * dot(kn, updv, t_left=True)
+    lc_ref[0] = dot(rmap, cot, t_left=True)
+
+
+def back_kernel(q_ref, k_ref, c_ref, s0_ref, lam_ref, inv_ref, proj_ref, updv_ref, scores_ref,
+                rmap_ref, own_ref, out_ref, dq_ref, dk_ref, dv_ref):
+    rows = k_ref.shape[1]
+    toks = q_ref.shape[1]
+    qn, q_scale = normed(q_ref[0])
+    kn, k_scale = normed(k_ref[0])
+    cot = c_ref[0]
+    state = s0_ref[0]
+    lam = lam_ref[0]
+    scores = scores_ref[0]
+    out_ref[0] = dot(rmap_ref[0], state) + own_ref[0]
+    updates = updv_ref[0] - dot(proj_ref[0], state)
+    d_upd = dot(scores, cot, t_left=True) + 2.0 * dot(kn, lam)
+    d_w = dot(inv_ref[0], d_upd, t_left=True)
+    dv_ref[0] = d_w
+    tok_ids, sub_ids = ids(toks, rows)
+    touch = jnp.where(sub_ids <= 2 * tok_ids + 1, dot(cot, updates, t_right=True), 0.0)
+    d_qn = dot(cot, state, t_right=True) + 2.0 * dot(touch, kn)
+    dq_ref[0] = q_scale * (d_qn - jnp.sum(qn * d_qn, axis=-1, keepdims=True) * qn)
+    row, col = ids(rows, rows)
+    gram_cot = jnp.where(row > col, -2.0 * dot(d_w, updates, t_right=True), 0.0)
+    d_kn = (
+        2.0 * dot(touch, qn, t_left=True)
+        + 2.0 * dot(updates, lam, t_right=True)
+        - dot(d_w, state, t_right=True)
+        + dot(gram_cot, kn)
+        + dot(gram_cot, kn, t_left=True)
+    )
+    dk_ref[0] = k_scale * (d_kn - jnp.sum(kn * d_kn, axis=-1, keepdims=True) * kn)
+
+
+def per_head(shape):
+    return pl.BlockSpec((1,) + tuple(shape[1:]), lambda h: (h, 0, 0))
+
+
+def run_heads(kernel, operands, out_shapes):
+    heads = operands[0].shape[0]
+    return pl.pallas_call(
+        kernel,
+        grid=(heads,),
+        in_specs=[per_head(x.shape) for x in operands],
+        out_specs=[per_head(s) for s in out_shapes],
+        out_shape=[jax.ShapeDtypeStruct(s, jnp.float32) for s in out_shapes],
+    )(*operands)
+
+
+def chain_seq(transition, offset, local_cot):
+    count = lax.axis_size("seq")
+    right = [(i, i + 1) for i in range(count - 1)]
+    left = [(i + 1, i) for i in range(count - 1)]
+    fwd_sum, bwd_sum = offset, local_cot
+    for hop in range(count - 1):
+        got_sum = lax.ppermute(fwd_sum, "seq", right)
+        got_cot = lax.ppermute(bwd_sum, "seq", left)
+        if hop == count - 2:
+            return got_sum, got_cot
+        fwd_sum = mm("hij,hjk->hik", transition, got_sum) + offset
+        bwd_sum = mm("hji,hjk->hik", transition, got_cot) + local_cot
+    zero = jnp.zeros_like(offset)
+    return zero, zero
+
+
 def scan_seq(transition, offset, local_cot):
     count = lax.axis_size("seq")
-    if count == 1:
-        zero = jnp.zeros_like(offset)
-        return zero, zero
+    if count <= 4:
+        return chain_seq(transition, offset, local_cot)
     fwd_map, fwd_sum = transition, offset
     bwd_map, bwd_sum = transition, local_cot
     ex_map = ex_sum = bx_map = bx_sum = None
@@ -95,41 +248,21 @@
     cot = out_cotangent.astype(jnp.float32).transpose(1, 0, 2)
     k_raw = reflect_keys.astype(jnp.float32).reshape(rows, heads_here, head_size).transpose(1, 0, 2)
     vals = write_values.astype(jnp.float32).reshape(rows, heads_here, head_size).transpose(1, 0, 2)
-    qn, q_scale = unit_rows(q_raw)
-    kn, k_scale = unit_rows(k_raw)
-
-    inverse = tri_inverse(kn)
-    proj = mm("hij,hjd->hid", inverse, kn)
-    upd_v = mm("hij,hjd->hid", inverse, vals)
-    tok_ids = lax.broadcasted_iota(jnp.int32, (tok_count, rows), 0)
-    sub_ids = lax.broadcasted_iota(jnp.int32, (tok_count, rows), 1)
-    visible = sub_ids <= 2 * tok_ids + 1
-    scores = jnp.where(visible, 2.0 * mm("hid,hjd->hij", qn, kn), 0.0)
-    read_map = qn - mm("hij,hjd->hid", scores, proj)
-    own_out = mm("hij,hjd->hid", scores, upd_v)
-    eye = jnp.eye(head_size, dtype=jnp.float32)
-    transition = eye - 2.0 * mm("hjd,hjw->hdw", kn, proj)
-    offset = 2.0 * mm("hjd,hjw->hdw", kn, upd_v)
-    local_cot = mm("hld,hlw->hdw", read_map, cot)
+    h, d = heads_here, head_size
+    inverse, proj, upd_v, scores, read_map, own_out, transition, offset, local_cot = run_heads(
+        front_kernel,
+        (q_raw, k_raw, vals, cot),
+        [(h, rows, rows), (h, rows, d), (h, rows, d), (h, tok_count, rows), (h, tok_count, d),
+         (h, tok_count, d), (h, d, d), (h, d, d), (h, d, d)],
+    )
 
     state_in, end_cot = scan_seq(transition, offset, local_cot)
 
-    produced = mm("hld,hdw->hlw", read_map, state_in) + own_out
-    updates = upd_v - mm("hjd,hdw->hjw", proj, state_in)
-    d_upd = mm("hij,hiw->hjw", scores, cot) + 2.0 * mm("hjd,hdw->hjw", kn, end_cot)
-    d_w = mm("hij,hiw->hjw", inverse, d_upd)
-    touch = jnp.where(visible, mm("hiw,hjw->hij", cot, updates), 0.0)
-    d_qn = mm("hiw,hdw->hid", cot, state_in) + 2.0 * mm("hij,hjd->hid", touch, kn)
-    gram_cot = jnp.where(strict_lower(rows, rows), -2.0 * mm("hiw,hjw->hij", d_w, updates), 0.0)
-    d_kn = (
-        2.0 * mm("hij,hid->hjd", touch, qn)
-        + 2.0 * mm("hjw,hdw->hjd", updates, end_cot)
-        - mm("hjw,hdw->hjd", d_w, state_in)
-        + mm("hij,hjd->hid", gram_cot, kn)
-        + mm("hji,hjd->hid", gram_cot, kn)
-    )
-    d_q = q_scale * (d_qn - jnp.sum(qn * d_qn, axis=-1, keepdims=True) * qn)
-    d_k = k_scale * (d_kn - jnp.sum(kn * d_kn, axis=-1, keepdims=True) * kn)
+    produced, d_q, d_k, d_w = run_heads(
+        back_kernel,
+        (q_raw, k_raw, cot, state_in, end_cot, inverse, proj, upd_v, scores, read_map, own_out),
+        [(h, tok_count, d), (h, tok_count, d), (h, rows, d), (h, rows, d)],
+    )
 
     def token_major(tensor):
         return tensor.transpose(1, 0, 2).astype(jnp.bfloat16)

time: 72.5 us -> 84.3 us (1.16)
  Pallas kernels: 0 us -> 38.9 us
  matrix products: 30.3 us -> 3.08 us
  waiting for transfers between devices: 19.6 us -> 14.2 us
  starting transfers between devices: 13 us -> 17.7 us
  local copies, waits for them, and re-layouts: 4.94 us -> 7.34 us
  other arithmetic: 3.24 us -> 1.93 us
    pallas_call x0 -> x2, Pallas kernels: none -> 38.9 us  [run_heads(): pl.pallas_call(kernel, grid=(heads,), in_specs=[per_head(x.shape) for x i...]
    dot_general x45 -> x4, matrix products: 30.3 us -> 3.08 us  [mm(): return jnp.einsum(spec, *operands, precision=highest)]
    ppermute x4 -> x6, waiting for transfers between devices: 19.6 us -> 14.2 us  [the longest x3 9.18 us: chain_seq(): got_sum = lax.ppermute(fwd_sum, 'seq', right)]
    ppermute x4 -> x6, starting transfers between devices: 13 us -> 17.7 us  [the longest x3 13.8 us: chain_seq(): got_sum = lax.ppermute(fwd_sum, 'seq', right)]
    mul x2 -> x0, other arithmetic: 1.99 us -> none  [the longest x1 1.79 us: local(): d_k = k_scale * (d_kn - jnp.sum(kn * d_kn, axis=-1, keepdims=True) * kn)]
    transpose x0 -> x1, local copies, waits for them, and re-layouts: none -> 0.99 us  [local(): write_values.astype(jnp.float32).reshape(rows, heads_here, head_size)]
    transpose x1, local copies, waits for them, and re-layouts: 1.15 us -> 2.01 us  [local(): reflect_keys.astype(jnp.float32).reshape(rows, heads_here, head_size)]
    unnamed x8 -> x24, local copies, waits for them, and re-layouts: 1.54 us -> 2.25 us
  transfers between devices with their start and end apart: 4 -> 6, of which waited for: 3 -> 4; matrix products, arithmetic and copies ran while one was open for 7% -> 4% of each run, Pallas kernels for 0% -> 0%
where the time goes in v3:
time: 84.3 us; the launch traced here: 84 us
  Pallas kernels  38.9 us (46%)
  starting transfers between devices  17.7 us (21%)
  waiting for transfers between devices  14.2 us (17%)
  local copies, waits for them, and re-layouts  7.34 us (9%)
  matrix products  3.08 us (4%)
  other arithmetic  1.93 us (2%)
    pallas_call x2, Pallas kernels, run_heads(): pl.pallas_call(kernel, grid=(heads,), in_specs=[per_head(x.shape) for x i...  38.9 us
    ppermute x3, starting transfers between devices, chain_seq(): got_sum = lax.ppermute(fwd_sum, 'seq', right)  13.8 us
    ppermute x3, waiting for transfers between devices, chain_seq(): got_sum = lax.ppermute(fwd_sum, 'seq', right)  9.18 us
    ppermute x3, waiting for transfers between devices, chain_seq(): got_cot = lax.ppermute(bwd_sum, 'seq', left)  5.03 us
    ppermute x3, starting transfers between devices, chain_seq(): got_cot = lax.ppermute(bwd_sum, 'seq', left)  3.88 us
    dot_general x4, matrix products, mm(): return jnp.einsum(spec, *operands, precision=highest)  3.08 us
    unnamed x24, local copies, waits for them, and re-layouts  2.25 us
    convert_element_type x2, local copies, waits for them, and re-layouts, pair_major(): return tensor.reshape(heads_here, tok_count, 2, head_size).transpose(1, 2...  2.09 us
  transfers between devices with their start and end apart: 6, of which 4 were waited for; matrix products, arithmetic and copies ran while one was open for 4% of the time, Pallas kernels for 0%

profile of v3, /device:TPU:0, one launch (start us, length us, event | category | flops | bytes accessed | tf_op | source)
XLA Modules:
  0.0 84.0 jit_solution(1913593837581348394)
XLA Ops:
  0.6 0.0 copy-start.5
  0.6 2.0 %copy.9 = f32[128,2,4,128]{3,1,0,2:T(2,128)} copy(bf16[128,2,4,128]{3,2,1,0:T(4,128)(2,1)} %param.5) | data formatting | bytes 786432 | tf_op jit(solution)/shard_map/transpose | solution.py:249
  2.7 0.0 copy-done.5
  2.7 0.0 copy-start.9
  2.7 0.0 copy-start.10
  2.7 1.0 %copy.11 = f32[128,2,4,128]{3,1,0,2:T(2,128)} copy(bf16[128,2,4,128]{3,2,1,0:T(4,128)(2,1)S(1)} %copy-done.5) | data formatting | bytes 786432 | tf_op jit(solution)/shard_map/transpose | solution.py:250
  3.7 0.0 copy-done.9
  3.7 0.0 copy-done.10
  3.7 0.8 convert_bitcast_fusion
  4.5 27.8 %shard_map.75 = (f32[4,256,256]{2,1,0:T(8,128)}, f32[4,256,128]{2,1,0:T(8,128)}, f32[4,256,128]{2,1,0:T(8,128)}, f32[4,128,256]{2,1,0:T(8,128)}, f32[4,128,128]{...) custom-call(f32[4,128,128]{2,1,0:T(8,128)} %get-tuple-element.35.q_r, ...), custom_call_target="tpu_custom_call" | custom-call | tf_op jit(solution)/shard_map/pallas_call | solution.py:183
  32.2 4.9 %collective-permute-start = (f32[4,128,128]{2,1,0:T(8,128)}, f32[4,128,128]{2,1,0:T(8,128)S(1)}, u32[]{:S(2)}, u32[]{:S(2)}) collective-permute-start(f32[4,128,128]{2,1,0:T(8,128)} %get-tuple-element.18), channel_id=1, source_target_pairs={{0,4},{4,8},{8,12},{1,5},{5,9},{9,13},{2,6},{6,10},{10,14},{3,7},{... | collective-permute-start | bytes 786440 | tf_op jit(solution)/shard_map/ppermute | solution.py:198
  37.2 1.3 %collective-permute-start.3 = (f32[4,128,128]{2,1,0:T(8,128)}, f32[4,128,128]{2,1,0:T(8,128)S(1)}, u32[]{:S(2)}, u32[]{:S(2)}) collective-permute-start(f32[4,128,128]{2,1,0:T(8,128)} %get-tuple-element.19), channel_id=1, source_target_pairs={{4,0},{8,4},{12,8},{5,1},{9,5},{13,9},{6,2},{10,6},{14,10},{7,3},{... | collective-permute-start | bytes 786440 | tf_op jit(solution)/shard_map/ppermute | solution.py:199
  38.5 4.5 %collective-permute-done = f32[4,128,128]{2,1,0:T(8,128)S(1)} collective-permute-done((f32[4,128,128]{2,1,0:T(8,128)}, f32[4,128,128]{2,1,0:T(8,128)S(1)}, u32[]{:S(2)}, u32[]{:S(2)}) %collective-permute-start) | collective-permute-done | bytes 262176 | tf_op jit(solution)/shard_map/ppermute | solution.py:198
  43.0 0.0 copy-start
  43.0 0.0 copy-start.1
  43.0 1.5 %convolution_add_fusion.3 = f32[4,128,128]{2,1,0:T(8,128)S(1)} fusion(f32[4,128,128]{2,1,0:T(8,128)} %get-tuple-element.18, f32[4,128,128]{2,1,0:T(8,128)} %get-tuple-element.17, f32[4,128,128]{2,1,0:T(8,128)S(1)} %collective-permute-done), kind=kOutput, calls=%fused_computation.3 | convolution fusion | flops 100728832 | bytes 1048576 | tf_op jit(solution)/shard_map/hij,hjk->hik/dot_general | solution.py:12
  44.5 0.0 copy-start.2
  44.5 4.4 %collective-permute-start.1 = (f32[4,128,128]{2,1,0:T(8,128)S(1)}, f32[4,128,128]{2,1,0:T(8,128)S(1)}, u32[]{:S(2)}, u32[]{:S(2)}) collective-permute-start(f32[4,128,128]{2,1,0:T(8,128)S(1)} %convolution_add_fusion.3), channel_id=1, source_target_pairs={{0,4},{4,8},{8,12},{1,5},{5,9},{9,13},{2,6},{6,10},{10,14},{3,7},{... | collective-permute-start | bytes 786440 | tf_op jit(solution)/shard_map/ppermute | solution.py:198
  49.0 0.0 collective-permute-done.3
  49.0 0.0 copy-done
  49.0 0.0 copy-done.1
  49.0 0.6 convolution_add_fusion.1
  49.6 1.3 %collective-permute-start.4 = (f32[4,128,128]{2,1,0:T(8,128)S(1)}, f32[4,128,128]{2,1,0:T(8,128)S(1)}, u32[]{:S(2)}, u32[]{:S(2)}) collective-permute-start(f32[4,128,128]{2,1,0:T(8,128)S(1)} %convolution_add_fusion.1), channel_id=1, source_target_pairs={{4,0},{8,4},{12,8},{5,1},{9,5},{13,9},{6,2},{10,6},{14,10},{7,3},{... | collective-permute-start | bytes 786440 | tf_op jit(solution)/shard_map/ppermute | solution.py:199
  50.9 2.7 %collective-permute-done.1 = f32[4,128,128]{2,1,0:T(8,128)S(1)} collective-permute-done((f32[4,128,128]{2,1,0:T(8,128)S(1)}, f32[4,128,128]{2,1,0:T(8,128)S(1)}, u32[]{:S(2)}, u32[]{:S(2)}) %collective-permute-start.1) | collective-permute-done | bytes 262176 | tf_op jit(solution)/shard_map/ppermute | solution.py:198
  53.6 0.0 copy-done.2
  53.6 0.4 convolution_add_fusion.2
  54.0 4.4 %collective-permute-start.2 = (f32[4,128,128]{2,1,0:T(8,128)S(1)}, f32[4,128,128]{2,1,0:T(8,128)S(1)}, u32[]{:S(2)}, u32[]{:S(2)}) collective-permute-start(f32[4,128,128]{2,1,0:T(8,128)S(1)} %convolution_add_fusion.2), channel_id=1, source_target_pairs={{0,4},{4,8},{8,12},{1,5},{5,9},{9,13},{2,6},{6,10},{10,14},{3,7},{... | collective-permute-start | bytes 786440 | tf_op jit(solution)/shard_map/ppermute | solution.py:198
  58.4 0.0 collective-permute-done.4
  58.5 0.6 convolution_add_fusion
  59.1 1.3 %collective-permute-start.5 = (f32[4,128,128]{2,1,0:T(8,128)S(1)}, f32[4,128,128]{2,1,0:T(8,128)S(1)}, u32[]{:S(2)}, u32[]{:S(2)}) collective-permute-start(f32[4,128,128]{2,1,0:T(8,128)S(1)} %convolution_add_fusion), channel_id=1, source_target_pairs={{4,0},{8,4},{12,8},{5,1},{9,5},{13,9},{6,2},{10,6},{14,10},{7,3},{... | collective-permute-start | bytes 786440 | tf_op jit(solution)/shard_map/ppermute | solution.py:199
  60.4 1.9 %collective-permute-done.2.s0_ref = f32[4,128,128]{2,1,0:T(8,128)S(1)} collective-permute-done((f32[4,128,128]{2,1,0:T(8,128)S(1)}, f32[4,128,128]{2,1,0:T(8,128)S(1)}, u32[]{:S(2)}, u32[]{:S(2)}) %collective-permute-start.2) | collective-permute-done | bytes 262176 | tf_op jit(solution)/shard_map/ppermute | solution.py:198
  62.3 0.0 copy-start.6
  62.3 5.0 %collective-permute-done.5.lam_ref = f32[4,128,128]{2,1,0:T(8,128)S(1)} collective-permute-done((f32[4,128,128]{2,1,0:T(8,128)S(1)}, f32[4,128,128]{2,1,0:T(8,128)S(1)}, u32[]{:S(2)}, u32[]{:S(2)}) %collective-permute-start.5) | collective-permute-done | bytes 262176 | tf_op jit(solution)/shard_map/ppermute | solution.py:199
  67.3 0.0 copy-start.7
  67.3 0.0 copy-done.6
  67.3 0.7 copy-done.7
  68.0 11.2 %shard_map.76 = (f32[4,128,128]{2,1,0:T(8,128)}, f32[4,128,128]{2,1,0:T(8,128)}, f32[4,256,128]{2,1,0:T(8,128)}, f32[4,256,128]{2,1,0:T(8,128)}) custom-call(f32[4,128,128]{2,1,0:T(8,128)} %get-tuple-element.35.q_ref, f32[4,256,128]{2,1,0:T(8,128)} %bitcast.31, f32[4,128,128]{2,1,0:T(8,128)} %get-tuple-element.34.c_ref, f32[4,128,128]{2,1,0:T(8,128)} %copy-done.6, ...), custom_call_target="tpu_custom_call" | custom-call | tf_op jit(solution)/shard_map/pallas_call | solution.py:183
  79.2 0.0 copy-start.8
  79.2 1.0 %convert_bitcast_fusion.3 = bf16[128,4,128]{2,0,1:T(8,128)(2,1)S(1)} fusion(f32[4,128,128]{2,1,0:T(8,128)} %get-tuple-element.26), kind=kLoop, calls=%fused_computation.9 | loop fusion | flops 65536 | bytes 393216 | tf_op jit(solution)/shard_map/convert_element_type | solution.py:268
  80.2 0.0 copy-start.4
  80.2 0.8 copy.15
  81.0 0.0 copy-done.8
  81.0 0.8 copy.16
  81.8 0.0 copy-done.4
  81.8 0.0 copy-start.3
  81.8 1.0 %copy.23 = bf16[4,128,2,128]{3,0,2,1:T(4,128)(2,1)} copy(bf16[4,128,2,128]{3,2,1,0:T(2,128)(2,1)S(1)} %bitcast.33) | data formatting | bytes 524288 | tf_op jit(solution)/shard_map/convert_element_type | solution.py:274
  82.9 0.0 copy-done.3
  82.9 1.0 %copy.22 = bf16[4,128,2,128]{3,0,2,1:T(4,128)(2,1)} copy(bf16[4,128,2,128]{3,2,1,0:T(2,128)(2,1)S(1)} %bitcast.34) | data formatting | bytes 524288 | tf_op jit(solution)/shard_map/convert_element_type | solution.py:274
  (3 shorter events, 0.1 us)
Async XLA Ops:
  0.6 2.0 %copy-start.5 = (bf16[128,2,4,128]{3,2,1,0:T(4,128)(2,1)S(1)}, bf16[128,2,4,128]{3,2,1,0:T(4,128)(2,1)}, u32[]{:S(2)}) copy-start(bf16[128,2,4,128]{3,2,1,0:T(4,128)(2,1)} %param.6) | copy-start | bytes 786436
  2.7 1.0 %copy-start.9 = (bf16[128,4,128]{2,1,0:T(4,128)(2,1)S(1)}, bf16[128,4,128]{2,1,0:T(4,128)(2,1)}, u32[]{:S(2)}) copy-start(bf16[128,4,128]{2,1,0:T(4,128)(2,1)} %param.7) | copy-start | bytes 393220
  2.7 1.0 %copy-start.10 = (bf16[128,4,128]{2,1,0:T(4,128)(2,1)S(1)}, bf16[128,4,128]{2,1,0:T(4,128)(2,1)}, u32[]{:S(2)}) copy-start(bf16[128,4,128]{2,1,0:T(4,128)(2,1)} %param.4) | copy-start | bytes 393220
  32.2 10.8 %collective-permute-start = (f32[4,128,128]{2,1,0:T(8,128)}, f32[4,128,128]{2,1,0:T(8,128)S(1)}, u32[]{:S(2)}, u32[]{:S(2)}) collective-permute-start(f32[4,128,128]{2,1,0:T(8,128)} %get-tuple-element.18), channel_id=1, source_target_pairs={{0,4},{4,8},{8,12},{1,5},{5,9},{9,13},{2,6},{6,10},{10,14},{3,7},{... | collective-permute-start | bytes 786440 | tf_op jit(solution)/shard_map/ppermute | solution.py:198
  37.2 11.8 %collective-permute-start.3 = (f32[4,128,128]{2,1,0:T(8,128)}, f32[4,128,128]{2,1,0:T(8,128)S(1)}, u32[]{:S(2)}, u32[]{:S(2)}) collective-permute-start(f32[4,128,128]{2,1,0:T(8,128)} %get-tuple-element.19), channel_id=1, source_target_pairs={{4,0},{8,4},{12,8},{5,1},{9,5},{13,9},{6,2},{10,6},{14,10},{7,3},{... | collective-permute-start | bytes 786440 | tf_op jit(solution)/shard_map/ppermute | solution.py:199
  43.0 5.9 %copy-start = (f32[4,128,128]{2,1,0:T(8,128)S(1)}, f32[4,128,128]{2,1,0:T(8,128)}, u32[]{:S(2)}) copy-start(f32[4,128,128]{2,1,0:T(8,128)} %get-tuple-element.17) | copy-start | bytes 786436
  43.0 6.0 %copy-start.1 = (f32[4,128,128]{2,1,0:T(8,128)S(1)}, f32[4,128,128]{2,1,0:T(8,128)}, u32[]{:S(2)}) copy-start(f32[4,128,128]{2,1,0:T(8,128)} %get-tuple-element.19) | copy-start | bytes 786436
  44.5 9.1 %copy-start.2 = (f32[4,128,128]{2,1,0:T(8,128)S(1)}, f32[4,128,128]{2,1,0:T(8,128)}, u32[]{:S(2)}) copy-start(f32[4,128,128]{2,1,0:T(8,128)} %get-tuple-element.18) | copy-start | bytes 786436
  44.5 9.1 %collective-permute-start.1 = (f32[4,128,128]{2,1,0:T(8,128)S(1)}, f32[4,128,128]{2,1,0:T(8,128)S(1)}, u32[]{:S(2)}, u32[]{:S(2)}) collective-permute-start(f32[4,128,128]{2,1,0:T(8,128)S(1)} %convolution_add_fusion.3), channel_id=1, source_target_pairs={{0,4},{4,8},{8,12},{1,5},{5,9},{9,13},{2,6},{6,10},{10,14},{3,7},{... | collective-permute-start | bytes 786440 | tf_op jit(solution)/shard_map/ppermute | solution.py:198
  49.6 8.8 %collective-permute-start.4 = (f32[4,128,128]{2,1,0:T(8,128)S(1)}, f32[4,128,128]{2,1,0:T(8,128)S(1)}, u32[]{:S(2)}, u32[]{:S(2)}) collective-permute-start(f32[4,128,128]{2,1,0:T(8,128)S(1)} %convolution_add_fusion.1), channel_id=1, source_target_pairs={{4,0},{8,4},{12,8},{5,1},{9,5},{13,9},{6,2},{10,6},{14,10},{7,3},{... | collective-permute-start | bytes 786440 | tf_op jit(solution)/shard_map/ppermute | solution.py:199
  54.0 8.3 %collective-permute-start.2 = (f32[4,128,128]{2,1,0:T(8,128)S(1)}, f32[4,128,128]{2,1,0:T(8,128)S(1)}, u32[]{:S(2)}, u32[]{:S(2)}) collective-permute-start(f32[4,128,128]{2,1,0:T(8,128)S(1)} %convolution_add_fusion.2), channel_id=1, source_target_pairs={{0,4},{4,8},{8,12},{1,5},{5,9},{9,13},{2,6},{6,10},{10,14},{3,7},{... | collective-permute-start | bytes 786440 | tf_op jit(solution)/shard_map/ppermute | solution.py:198
  59.1 8.3 %collective-permute-start.5 = (f32[4,128,128]{2,1,0:T(8,128)S(1)}, f32[4,128,128]{2,1,0:T(8,128)S(1)}, u32[]{:S(2)}, u32[]{:S(2)}) collective-permute-start(f32[4,128,128]{2,1,0:T(8,128)S(1)} %convolution_add_fusion), channel_id=1, source_target_pairs={{4,0},{8,4},{12,8},{5,1},{9,5},{13,9},{6,2},{10,6},{14,10},{7,3},{... | collective-permute-start | bytes 786440 | tf_op jit(solution)/shard_map/ppermute | solution.py:199
  62.3 5.0 %copy-start.6 = (f32[4,128,128]{2,1,0:T(8,128)}, f32[4,128,128]{2,1,0:T(8,128)S(1)}, u32[]{:S(2)}) copy-start(f32[4,128,128]{2,1,0:T(8,128)S(1)} %collective-permute-done.2.s0_ref) | copy-start | bytes 786436
  67.3 0.7 copy-start.7
  79.2 1.8 %copy-start.8 = (f32[4,128,128]{2,1,0:T(8,128)S(1)}, f32[4,128,128]{2,1,0:T(8,128)}, u32[]{:S(2)}) copy-start(f32[4,128,128]{2,1,0:T(8,128)} %get-tuple-element.27) | copy-start | bytes 786436
  80.2 1.6 %copy-start.4 = (f32[4,256,128]{2,1,0:T(8,128)S(1)}, f32[4,256,128]{2,1,0:T(8,128)}, u32[]{:S(2)}) copy-start(f32[4,256,128]{2,1,0:T(8,128)} %get-tuple-element.28) | copy-start | bytes 1572868
  81.8 1.1 %copy-start.3 = (f32[4,256,128]{2,1,0:T(8,128)S(1)}, f32[4,256,128]{2,1,0:T(8,128)}, u32[]{:S(2)}) copy-start(f32[4,256,128]{2,1,0:T(8,128)} %get-tuple-element.29) | copy-start | bytes 1572868

commit v4 on v1

--- a/solution.py
+++ b/solution.py
@@ -51,14 +51,29 @@
     return inverse.reshape(heads, rows, rows)
 
 
+def crossing_pairs(count, width, core_goes_right):
+    pairs = []
+    for s in range(count):
+        for h in range(width):
+            target = s + 1 if (h % 2 == 0) == core_goes_right else s - 1
+            if 0 <= target < count:
+                pairs.append((s * width + h, target * width + h))
+    return pairs
+
+
 def chain_seq(transition, offset, local_cot):
     count = lax.axis_size("seq")
-    right = [(i, i + 1) for i in range(count - 1)]
-    left = [(i + 1, i) for i in range(count - 1)]
+    width = lax.axis_size("head")
+    even = lax.axis_index("head") % 2 == 0
+    first = crossing_pairs(count, width, True)
+    second = crossing_pairs(count, width, False)
+    axes = ("seq", "head")
     fwd_sum, bwd_sum = offset, local_cot
     for hop in range(count - 1):
-        got_sum = lax.ppermute(fwd_sum, "seq", right)
-        got_cot = lax.ppermute(bwd_sum, "seq", left)
+        got_first = lax.ppermute(jnp.where(even, fwd_sum, bwd_sum), axes, first)
+        got_second = lax.ppermute(jnp.where(even, bwd_sum, fwd_sum), axes, second)
+        got_sum = jnp.where(even, got_first, got_second)
+        got_cot = jnp.where(even, got_second, got_first)
         if hop == count - 2:
             return got_sum, got_cot
         fwd_sum = mm("hij,hjk->hik", transition, got_sum) + offset

time: 63 us -> 70.5 us (1.12); the launches traced: 62.8 us -> 69.4 us
  waiting for transfers between devices: 4.92 us -> 9.96 us
  starting transfers between devices: 18 us -> 19.5 us
  other arithmetic: 3.12 us -> 4.07 us
  local copies, waits for them, and re-layouts: 5.24 us -> 4.32 us
    ppermute x6, waiting for transfers between devices: 4.92 us -> 9.96 us  [the longest x3 5.03 us: chain_seq(): got_second = lax.ppermute(jnp.where(even, bwd_sum, fwd_sum), axes, second)]
    ppermute x6, starting transfers between devices: 18 us -> 19.5 us  [the longest x3 15.6 us: chain_seq(): got_first = lax.ppermute(jnp.where(even, fwd_sum, bwd_sum), axes, first)]
    reduce_sum x2, other arithmetic: 0.35 us -> 1.26 us  [unit_rows(): scale = lax.rsqrt(jnp.sum(tensor * tensor, axis=-1, keepdims=True) + 1e-06)]
    convert_element_type x2 -> x1, local copies, waits for them, and re-layouts: 2.09 us -> 1.47 us  [pair_major(): return tensor.reshape(heads_here, tok_count, 2, head_size).transpose(1, 2...]
  transfers between devices with their start and end apart: 6 -> 6, of which waited for: 5 -> 6; matrix products, arithmetic and copies ran while one was open for 20% -> 3% of each run, Pallas kernels for 0% -> 0%
where the time goes in v4:
time: 70.5 us; the launch traced here: 69.4 us
  matrix products  30.3 us (43%)
  starting transfers between devices  19.5 us (28%)
  waiting for transfers between devices  9.96 us (14%)
  local copies, waits for them, and re-layouts  4.32 us (6%)
  other arithmetic  4.07 us (6%)
  between operations  1.2 us (2%)
    dot_general x45, matrix products, mm(): return jnp.einsum(spec, *operands, precision=highest)  30.3 us
    ppermute x3, starting transfers between devices, chain_seq(): got_first = lax.ppermute(jnp.where(even, fwd_sum, bwd_sum), axes, first)  15.6 us
    ppermute x3, waiting for transfers between devices, chain_seq(): got_second = lax.ppermute(jnp.where(even, bwd_sum, fwd_sum), axes, second)  5.03 us
    ppermute x3, waiting for transfers between devices, chain_seq(): got_first = lax.ppermute(jnp.where(even, fwd_sum, bwd_sum), axes, first)  4.93 us
    ppermute x3, starting transfers between devices, chain_seq(): got_second = lax.ppermute(jnp.where(even, bwd_sum, fwd_sum), axes, second)  3.88 us
    mul x1, other arithmetic, local(): d_k = k_scale * (d_kn - jnp.sum(kn * d_kn, axis=-1, keepdims=True) * kn)  1.79 us
    unnamed x8, local copies, waits for them, and re-layouts  1.54 us
    convert_element_type x1, local copies, waits for them, and re-layouts, pair_major(): return tensor.reshape(heads_here, tok_count, 2, head_size).transpose(1, 2...  1.47 us
  transfers between devices with their start and end apart: 6, of which 6 were waited for; matrix products, arithmetic and copies ran while one was open for 3% of the time, Pallas kernels for 0%

profile of v4, /device:TPU:0, one launch (start us, length us, event | category | flops | bytes accessed | tf_op | source)
XLA Modules:
  0.0 69.4 jit_solution(3101114992309741132)
XLA Ops:
  0.7 1.0 %fusion.33 = f32[4,128]{1,0:T(4,128)S(1)} fusion(bf16[128,4,128]{2,1,0:T(4,128)(2,1)} %param.4), kind=kLoop, calls=%fused_computation.69 | loop fusion | flops 196096 | bytes 133120 | tf_op jit(solution)/shard_map/reduce_sum | solution.py:15
  1.9 1.2 %copy.9 = f32[128,2,4,128]{3,1,0,2:T(2,128)S(1)} copy(bf16[128,2,4,128]{3,2,1,0:T(4,128)(2,1)} %param.5) | data formatting | bytes 786432 | tf_op jit(solution)/shard_map/transpose | solution.py:118
  3.0 0.2 multiply_reduce_fusion
  3.5 0.5 convolution_multiply_fusion.7
  4.0 0.5 convolution_multiply_fusion.6
  4.5 0.5 convolution_multiply_fusion.5
  5.1 0.7 convolution_multiply_fusion.4
  5.7 0.9 %fusion.3 = f32[4,16,16,16]{3,2,1,0:T(8,128)S(1)} fusion(f32[4,16,16,128]{3,2,1,0:T(8,128)S(1)} %bitcast.200, pred[16,16]{1,0:T(8,128)(4,1)S(1)} %iota_compare_fusion.7), kind=kOutput, calls=%fused_computation.10 | convolution fusion | flops 25198592 | bytes 590080 | tf_op jit(solution)/shard_map/hpid,hpjd->hpij/dot_general | solution.py:11
  6.7 0.6 fusion.81
  7.3 0.6 fusion.82
  8.0 0.7 convolution_add_fusion.2
  8.6 0.6 fusion.83
  9.3 0.6 convolution_add_fusion.1
  9.9 0.6 convolution_add_fusion
  10.6 0.4 fusion.77
  11.0 0.4 convolution_negate_fusion.3
  11.6 0.4 fusion.78
  12.0 0.4 convolution_negate_fusion.2
  12.6 0.4 fusion.79
  12.9 0.4 convolution_negate_fusion.1
  13.5 0.6 fusion.38
  14.1 0.7 fusion.12
  14.8 1.0 %fusion.24 = f32[4,256,128]{2,1,0:T(8,128)S(1)} fusion(f32[4,256,128]{2,1,0:T(8,128)S(1)} %broadcast_multiply_fusion, f32[4,1,128,128]{3,2,0,1:T(8,128)S(1)} %get-tuple-element.15, f32[4,1,128,128]{3,2,0,1:T(8,128)S(1)} %get-tuple-element.14, f32[4,1,128,128]{3,2,0,1:T(8,128)S(1)} %fusion.12), kind=kOutput, calls=%fused_computation.61 | convolution fusion | flops 403701760 | bytes 1835008 | tf_op jit(solution)/shard_map/hij,hjd->hid/dot_general | solution.py:11
  15.8 0.8 %fusion.22 = f32[4,256,128]{2,1,0:T(8,128)S(1)} fusion(f32[4,1,128,128]{3,2,0,1:T(8,128)S(1)} %get-tuple-element.15, f32[4,1,128,128]{3,2,0,1:T(8,128)S(1)} %get-tuple-element.14, f32[4,1,128,128]{3,2,0,1:T(8,128)S(1)} %fusion.12, bf16[256,4,128]{2,1,0:T(4,128)(2,1)S(1)} %bitcast.215), kind=kOutput, calls=%fused_computation.60 | convolution fusion | flops 403701760 | bytes 1572864 | tf_op jit(solution)/shard_map/hij,hjd->hid/dot_general | solution.py:11
  16.7 1.0 %convolution_multiply_fusion.9 = f32[4,128,128]{2,1,0:T(8,128)S(1)} fusion(f32[4,256,128]{2,1,0:T(8,128)S(1)} %broadcast_multiply_fusion, f32[4,256,128]{2,1,0:T(8,128)S(1)} %fusion.22), kind=kOutput, calls=%fused_computation.39 | convolution fusion | flops 201392128 | bytes 1310720 | tf_op jit(solution)/shard_map/hjd,hjw->hdw/dot_general | solution.py:11
  17.7 0.6 fusion.10
  18.4 0.6 convolution_subtract_fusion.2
  19.0 0.4 broadcast_select_fusion.6
  19.4 1.3 %collective-permute-start.1 = (f32[4,128,128]{2,1,0:T(8,128)S(1)}, f32[4,128,128]{2,1,0:T(8,128)S(1)}, u32[]{:S(2)}, u32[]{:S(2)}) collective-permute-start(f32[4,128,128]{2,1,0:T(8,128)S(1)} %get-tuple-element.12), channel_id=1, source_target_pairs={{1,5},{3,7},{4,0},{5,9},{6,2},{7,11},{8,4},{9,13},{10,6},{11,15},{... | collective-permute-start | bytes 786440 | tf_op jit(solution)/shard_map/ppermute | solution.py:74
  20.7 5.6 %collective-permute-start = (f32[4,128,128]{2,1,0:T(8,128)S(1)}, f32[4,128,128]{2,1,0:T(8,128)S(1)}, u32[]{:S(2)}, u32[]{:S(2)}) collective-permute-start(f32[4,128,128]{2,1,0:T(8,128)S(1)} %get-tuple-element.13), channel_id=1, source_target_pairs={{0,4},{2,6},{4,8},{5,1},{6,10},{7,3},{8,12},{9,5},{10,14},{11,7},{... | collective-permute-start | bytes 786440 | tf_op jit(solution)/shard_map/ppermute | solution.py:73
  26.3 1.0 %fusion.13 = f32[4,128,128]{2,1,0:T(8,128)S(1)} fusion(f32[4,256,128]{2,1,0:T(8,128)S(1)} %broadcast_multiply_fusion, f32[4,256,128]{2,1,0:T(8,128)S(1)} %fusion.24, f32[128,128]{1,0:T(8,128)S(1)} %fusion.63), kind=kOutput, calls=%fused_computation.42 | convolution fusion | flops 201457664 | bytes 1376256 | tf_op jit(solution)/shard_map/hjd,hjw->hdw/dot_general | solution.py:11
  27.4 1.5 %collective-permute-done.1 = f32[4,128,128]{2,1,0:T(8,128)S(1)} collective-permute-done((f32[4,128,128]{2,1,0:T(8,128)S(1)}, f32[4,128,128]{2,1,0:T(8,128)S(1)}, u32[]{:S(2)}, u32[]{:S(2)}) %collective-permute-start.1) | collective-permute-done | bytes 262176 | tf_op jit(solution)/shard_map/ppermute | solution.py:74
  28.9 1.3 %collective-permute-done = f32[4,128,128]{2,1,0:T(8,128)S(1)} collective-permute-done((f32[4,128,128]{2,1,0:T(8,128)S(1)}, f32[4,128,128]{2,1,0:T(8,128)S(1)}, u32[]{:S(2)}, u32[]{:S(2)}) %collective-permute-start) | collective-permute-done | bytes 262176 | tf_op jit(solution)/shard_map/ppermute | solution.py:73
  30.2 0.4 convolution_add_fusion.9
  30.6 0.6 broadcast_select_fusion.4
  31.2 1.3 %collective-permute-start.3 = (f32[4,128,128]{2,1,0:T(8,128)S(1)}, f32[4,128,128]{2,1,0:T(8,128)S(1)}, u32[]{:S(2)}, u32[]{:S(2)}) collective-permute-start(f32[4,128,128]{2,1,0:T(8,128)S(1)} %get-tuple-element.10), channel_id=1, source_target_pairs={{1,5},{3,7},{4,0},{5,9},{6,2},{7,11},{8,4},{9,13},{10,6},{11,15},{... | collective-permute-start | bytes 786440 | tf_op jit(solution)/shard_map/ppermute | solution.py:74
  32.5 5.0 %collective-permute-start.2 = (f32[4,128,128]{2,1,0:T(8,128)S(1)}, f32[4,128,128]{2,1,0:T(8,128)S(1)}, u32[]{:S(2)}, u32[]{:S(2)}) collective-permute-start(f32[4,128,128]{2,1,0:T(8,128)S(1)} %get-tuple-element.11), channel_id=1, source_target_pairs={{0,4},{2,6},{4,8},{5,1},{6,10},{7,3},{8,12},{9,5},{10,14},{11,7},{... | collective-permute-start | bytes 786440 | tf_op jit(solution)/shard_map/ppermute | solution.py:73
  37.5 0.6 fusion.59
  38.1 1.8 %collective-permute-done.3 = f32[4,128,128]{2,1,0:T(8,128)S(1)} collective-permute-done((f32[4,128,128]{2,1,0:T(8,128)S(1)}, f32[4,128,128]{2,1,0:T(8,128)S(1)}, u32[]{:S(2)}, u32[]{:S(2)}) %collective-permute-start.3) | collective-permute-done | bytes 262176 | tf_op jit(solution)/shard_map/ppermute | solution.py:74
  39.9 2.1 %collective-permute-done.2 = f32[4,128,128]{2,1,0:T(8,128)S(1)} collective-permute-done((f32[4,128,128]{2,1,0:T(8,128)S(1)}, f32[4,128,128]{2,1,0:T(8,128)S(1)}, u32[]{:S(2)}, u32[]{:S(2)}) %collective-permute-start.2) | collective-permute-done | bytes 262176 | tf_op jit(solution)/shard_map/ppermute | solution.py:73
  42.0 0.4 convolution_add_fusion.7
  42.4 0.6 broadcast_select_fusion.2
  43.0 1.3 %collective-permute-start.5 = (f32[4,128,128]{2,1,0:T(8,128)S(1)}, f32[4,128,128]{2,1,0:T(8,128)S(1)}, u32[]{:S(2)}, u32[]{:S(2)}) collective-permute-start(f32[4,128,128]{2,1,0:T(8,128)S(1)} %get-tuple-element.8), channel_id=1, source_target_pairs={{1,5},{3,7},{4,0},{5,9},{6,2},{7,11},{8,4},{9,13},{10,6},{11,15},{... | collective-permute-start | bytes 786440 | tf_op jit(solution)/shard_map/ppermute | solution.py:74
  44.3 5.0 %collective-permute-start.4 = (f32[4,128,128]{2,1,0:T(8,128)S(1)}, f32[4,128,128]{2,1,0:T(8,128)S(1)}, u32[]{:S(2)}, u32[]{:S(2)}) collective-permute-start(f32[4,128,128]{2,1,0:T(8,128)S(1)} %get-tuple-element.9), channel_id=1, source_target_pairs={{0,4},{2,6},{4,8},{5,1},{6,10},{7,3},{8,12},{9,5},{10,14},{11,7},{... | collective-permute-start | bytes 786440 | tf_op jit(solution)/shard_map/ppermute | solution.py:73
  49.3 0.6 fusion.84
  50.0 1.7 %collective-permute-done.5 = f32[4,128,128]{2,1,0:T(8,128)S(1)} collective-permute-done((f32[4,128,128]{2,1,0:T(8,128)S(1)}, f32[4,128,128]{2,1,0:T(8,128)S(1)}, u32[]{:S(2)}, u32[]{:S(2)}) %collective-permute-start.5) | collective-permute-done | bytes 262176 | tf_op jit(solution)/shard_map/ppermute | solution.py:74
  51.7 1.6 %collective-permute-done.4 = f32[4,128,128]{2,1,0:T(8,128)S(1)} collective-permute-done((f32[4,128,128]{2,1,0:T(8,128)S(1)}, f32[4,128,128]{2,1,0:T(8,128)S(1)}, u32[]{:S(2)}, u32[]{:S(2)}) %collective-permute-start.4) | collective-permute-done | bytes 262176 | tf_op jit(solution)/shard_map/ppermute | solution.py:73
  53.3 0.6 convolution_subtract_fusion.1
  54.0 0.4 fusion.57
  54.4 0.6 fusion.8
  55.0 1.5 %fusion.80 = (bf16[4,256,128]{2,1,0:T(8,128)(2,1)S(1)}, f32[4,256,128]{2,1,0:T(8,128)S(1)}) fusion(f32[4,256,128]{2,1,0:T(8,128)S(1)} %fusion.8, f32[4,1,128,128]{3,2,0,1:T(8,128)S(1)} %get-tuple-element.15, f32[4,1,128,128]{3,2,0,1:T(8,128)S(1)} %get-tuple-element.14, f32[4,1,128,128]{3,2,0,1:T(8,128)S(1)} %fusion.12), kind=kOutput, calls=%fused_computation.153 | convolution fusion | flops 403832832 | bytes 2097152 | tf_op jit(solution)/shard_map/hij,hiw->hjw/dot_general | solution.py:11
  56.5 0.4 fusion.15
  56.9 0.8 %copy.37 = bf16[128,4,128]{2,1,0:T(4,128)(2,1)} copy(bf16[128,4,128]{2,0,1:T(8,128)(2,1)S(1)} %fusion.15) | data formatting | bytes 262144
  57.6 0.4 fusion.2
  58.1 1.1 %fusion.28 = f32[4,256,128]{2,1,0:T(8,128)S(1)} fusion(f32[4,128,256]{2,1,0:T(8,128)S(1)} %fusion.2, f32[4,128]{1,0:T(4,128)S(1)} %get-tuple-element.23, bf16[128,4,128]{2,1,0:T(4,128)(2,1)S(1)} %copy-done.1), kind=kOutput, calls=%fused_computation.66 | convolution fusion | flops 201457664 | bytes 1181696 | tf_op jit(solution)/shard_map/hij,hid->hjd/dot_general | solution.py:11
  59.2 0.7 %fusion.32 = (f32[4,128]{1,0:T(4,128)S(1)}, f32[4,128,128]{2,1,0:T(8,128)S(1)}) fusion(f32[4,128,128]{1,2,0:T(8,128)S(1)} %fusion.57, f32[4,128]{1,0:T(4,128)S(1)} %get-tuple-element.23, bf16[128,4,128]{2,1,0:T(4,128)(2,1)S(1)} %copy-done.1, f32[4,128,256]{2,1,0:T(8,128)S(1)} %fusion.2, f32[4,256,128]{2,1,0:T(8,128)S(1)} %broadcast_multiply_fusion), kind=kOutput, calls=%fused_computation.68 | convolution fusion | flops 201719296 | bytes 1708032 | tf_op jit(solution)/shard_map/hij,hjd->hid/dot_general | solution.py:11
  60.2 0.8 %copy.38 = bf16[128,4,128]{2,1,0:T(4,128)(2,1)} copy(bf16[128,4,128]{2,0,1:T(8,128)(2,1)S(1)} %fusion.37) | data formatting | bytes 262144
  60.9 1.0 %fusion.1 = f32[4,256,256]{2,1,0:T(8,128)S(1)} fusion(f32[4,256,128]{2,1,0:T(8,128)S(1)} %get-tuple-element.28, f32[4,256,128]{2,1,0:T(8,128)S(1)} %convolution_subtract_fusion.1, pred[256,256]{1,0:T(8,128)(4,1)S(1)} %iota_compare_fusion.4), kind=kOutput, calls=%fused_computation.2 | convolution fusion | flops 403177472 | bytes 2162688 | tf_op jit(solution)/shard_map/hiw,hjw->hij/dot_general | solution.py:11
  61.9 1.1 %fusion.85 = f32[4,256,128]{2,1,0:T(8,128)S(1)} fusion(f32[4,256,256]{2,1,0:T(8,128)S(1)} %fusion.1, f32[4,256,128]{2,1,0:T(8,128)S(1)} %broadcast_multiply_fusion), kind=kOutput, calls=%fused_computation.158 | convolution fusion | flops 402653184 | bytes 2097152 | tf_op jit(solution)/shard_map/hij,hjd->hid/dot_general | solution.py:11
  63.0 0.6 fusion.9
  63.6 0.6 fusion.7
  64.3 1.9 %convolution_add_fusion.3 = f32[4,256,128]{2,1,0:T(8,128)S(1)} fusion(f32[4,256,128]{2,1,0:T(8,128)S(1)} %fusion.7, f32[4,256,256]{2,1,0:T(8,128)S(1)} %fusion.1, f32[4,256,128]{2,1,0:T(8,128)S(1)} %broadcast_multiply_fusion), kind=kOutput, calls=%fused_computation.6 | convolution fusion | flops 402784256 | bytes 2621440 | tf_op jit(solution)/shard_map/hji,hjd->hid/dot_general | solution.py:11
  66.1 1.8 %fusion.11 = bf16[4,256,128]{2,1,0:T(8,128)(2,1)S(1)} fusion(f32[4,256,128]{2,1,0:T(8,128)S(1)} %convolution_add_fusion.3, f32[4,256,128]{2,1,0:T(8,128)S(1)} %broadcast_multiply_fusion, f32[4,256]{1,0:T(4,128)S(1)} %add_rsqrt_fusion), kind=kOutput, calls=%fused_computation.23 | output fusion | flops 656511 | bytes 1314816 | tf_op jit(solution)/shard_map/mul | solution.py:154
  67.9 1.5 %copy_bitcast_fusion = (bf16[128,2,4,128]{3,2,1,0:T(4,128)(2,1)}, bf16[128,2,4,128]{3,2,1,0:T(4,128)(2,1)}) fusion(bf16[4,128,2,128]{3,2,1,0:T(2,128)(2,1)S(1)} %bitcast.213, bf16[4,128,2,128]{3,2,1,0:T(2,128)(2,1)S(1)} %bitcast.212), kind=kLoop, calls=%fused_computation.94 | loop fusion | bytes 1048576 | tf_op jit(solution)/shard_map/convert_element_type | solution.py:163
  (24 shorter events, 1.2 us)
Async XLA Ops:
  0.6 18.4 %copy-start = (bf16[128,4,128]{2,1,0:T(4,128)(2,1)S(1)}, bf16[128,4,128]{2,1,0:T(4,128)(2,1)}, u32[]{:S(2)}) copy-start(bf16[128,4,128]{2,1,0:T(4,128)(2,1)} %param.7) | copy-start | bytes 393220
  14.8 1.0 %copy-start.2 = (bf16[128,2,4,128]{3,2,1,0:T(4,128)(2,1)S(1)}, bf16[128,2,4,128]{3,2,1,0:T(4,128)(2,1)}, u32[]{:S(2)}) copy-start(bf16[128,2,4,128]{3,2,1,0:T(4,128)(2,1)} %param.6) | copy-start | bytes 786436
  16.6 1.1 %copy-start.1 = (bf16[128,4,128]{2,1,0:T(4,128)(2,1)S(1)}, bf16[128,4,128]{2,1,0:T(4,128)(2,1)}, u32[]{:S(2)}) copy-start(bf16[128,4,128]{2,1,0:T(4,128)(2,1)} %param.4) | copy-start | bytes 393220
  19.4 9.5 %collective-permute-start.1 = (f32[4,128,128]{2,1,0:T(8,128)S(1)}, f32[4,128,128]{2,1,0:T(8,128)S(1)}, u32[]{:S(2)}, u32[]{:S(2)}) collective-permute-start(f32[4,128,128]{2,1,0:T(8,128)S(1)} %get-tuple-element.12), channel_id=1, source_target_pairs={{1,5},{3,7},{4,0},{5,9},{6,2},{7,11},{8,4},{9,13},{10,6},{11,15},{... | collective-permute-start | bytes 786440 | tf_op jit(solution)/shard_map/ppermute | solution.py:74
  20.7 9.4 %collective-permute-start = (f32[4,128,128]{2,1,0:T(8,128)S(1)}, f32[4,128,128]{2,1,0:T(8,128)S(1)}, u32[]{:S(2)}, u32[]{:S(2)}) collective-permute-start(f32[4,128,128]{2,1,0:T(8,128)S(1)} %get-tuple-element.13), channel_id=1, source_target_pairs={{0,4},{2,6},{4,8},{5,1},{6,10},{7,3},{8,12},{9,5},{10,14},{11,7},{... | collective-permute-start | bytes 786440 | tf_op jit(solution)/shard_map/ppermute | solution.py:73
  31.2 8.7 %collective-permute-start.3 = (f32[4,128,128]{2,1,0:T(8,128)S(1)}, f32[4,128,128]{2,1,0:T(8,128)S(1)}, u32[]{:S(2)}, u32[]{:S(2)}) collective-permute-start(f32[4,128,128]{2,1,0:T(8,128)S(1)} %get-tuple-element.10), channel_id=1, source_target_pairs={{1,5},{3,7},{4,0},{5,9},{6,2},{7,11},{8,4},{9,13},{10,6},{11,15},{... | collective-permute-start | bytes 786440 | tf_op jit(solution)/shard_map/ppermute | solution.py:74
  32.5 9.5 %collective-permute-start.2 = (f32[4,128,128]{2,1,0:T(8,128)S(1)}, f32[4,128,128]{2,1,0:T(8,128)S(1)}, u32[]{:S(2)}, u32[]{:S(2)}) collective-permute-start(f32[4,128,128]{2,1,0:T(8,128)S(1)} %get-tuple-element.11), channel_id=1, source_target_pairs={{0,4},{2,6},{4,8},{5,1},{6,10},{7,3},{8,12},{9,5},{10,14},{11,7},{... | collective-permute-start | bytes 786440 | tf_op jit(solution)/shard_map/ppermute | solution.py:73
  43.0 8.7 %collective-permute-start.5 = (f32[4,128,128]{2,1,0:T(8,128)S(1)}, f32[4,128,128]{2,1,0:T(8,128)S(1)}, u32[]{:S(2)}, u32[]{:S(2)}) collective-permute-start(f32[4,128,128]{2,1,0:T(8,128)S(1)} %get-tuple-element.8), channel_id=1, source_target_pairs={{1,5},{3,7},{4,0},{5,9},{6,2},{7,11},{8,4},{9,13},{10,6},{11,15},{... | collective-permute-start | bytes 786440 | tf_op jit(solution)/shard_map/ppermute | solution.py:74
  44.3 9.0 %collective-permute-start.4 = (f32[4,128,128]{2,1,0:T(8,128)S(1)}, f32[4,128,128]{2,1,0:T(8,128)S(1)}, u32[]{:S(2)}, u32[]{:S(2)}) collective-permute-start(f32[4,128,128]{2,1,0:T(8,128)S(1)} %get-tuple-element.9), channel_id=1, source_target_pairs={{0,4},{2,6},{4,8},{5,1},{6,10},{7,3},{8,12},{9,5},{10,14},{11,7},{... | collective-permute-start | bytes 786440 | tf_op jit(solution)/shard_map/ppermute | solution.py:73

commit v5 on v0

--- a/solution.py
+++ b/solution.py
@@ -51,8 +51,29 @@
     return inverse.reshape(heads, rows, rows)
 
 
+def chain_seq(transition, offset, local_cot):
+    count = lax.axis_size("seq")
+    here = lax.axis_index("seq")
+    state_in = jnp.zeros_like(offset)
+    end_cot = jnp.zeros_like(local_cot)
+    fwd_sum, bwd_sum = offset, local_cot
+    for hop in range(1, count):
+        sender = hop - 1
+        back_sender = count - hop
+        payload = jnp.where(here == sender, fwd_sum, bwd_sum)
+        got = lax.ppermute(payload, "seq", [(sender, hop), (back_sender, back_sender - 1)])
+        state_in = jnp.where(here == hop, got, state_in)
+        end_cot = jnp.where(here == back_sender - 1, got, end_cot)
+        if hop < count - 1:
+            fwd_sum = mm("hij,hjk->hik", transition, state_in) + offset
+            bwd_sum = mm("hji,hjk->hik", transition, end_cot) + local_cot
+    return state_in, end_cot
+
+
 def scan_seq(transition, offset, local_cot):
     count = lax.axis_size("seq")
+    if count <= 4:
+        return chain_seq(transition, offset, local_cot)
     fwd_map, fwd_sum = transition, offset
     bwd_map, bwd_sum = transition, local_cot
     shift = 1

time: 75.8 us -> 68.5 us (0.904)
  starting transfers between devices: 29.2 us -> 6.9 us
  waiting for transfers between devices: 5.84 us -> 17.9 us
  local copies, waits for them, and re-layouts: 4.97 us -> 6.12 us
  other arithmetic: 3.12 us -> 4.13 us
  matrix products: 31.1 us -> 31.9 us
    ppermute x8 -> x3, starting transfers between devices: 29.2 us -> 6.9 us  [chain_seq(): lax.ppermute(payload, 'seq', [(sender, hop), (back_sender, back_sender -...]
    ppermute x8 -> x3, waiting for transfers between devices: 5.84 us -> 17.9 us  [chain_seq(): lax.ppermute(payload, 'seq', [(sender, hop), (back_sender, back_sender -...]
    unnamed x8 -> x30, local copies, waits for them, and re-layouts: 1.54 us -> 3.34 us
    reduce_sum x2, other arithmetic: 0.35 us -> 1.29 us  [unit_rows(): scale = lax.rsqrt(jnp.sum(tensor * tensor, axis=-1, keepdims=True) + 1e-06)]
    dot_general x47 -> x45, matrix products: 31.1 us -> 31.9 us  [mm(): return jnp.einsum(spec, *operands, precision=highest)]
    convert_element_type x2 -> x1, local copies, waits for them, and re-layouts: 2.09 us -> 1.47 us  [pair_major(): return tensor.reshape(heads_here, tok_count, 2, head_size).transpose(1, 2...]
  transfers between devices with their start and end apart: 8 -> 3, of which waited for: 6 -> 2; matrix products, arithmetic and copies ran while one was open for 17% -> 5% of each run, Pallas kernels for 0% -> 0%
where the time goes in v5:
time: 68.5 us; the launch traced here: 68.2 us
  matrix products  31.9 us (47%)
  waiting for transfers between devices  17.9 us (26%)
  starting transfers between devices  6.9 us (10%)
  local copies, waits for them, and re-layouts  6.12 us (9%)
  other arithmetic  4.13 us (6%)
  between operations  1.27 us (2%)
    dot_general x45, matrix products, mm(): return jnp.einsum(spec, *operands, precision=highest)  31.9 us
    ppermute x3, waiting for transfers between devices, chain_seq(): lax.ppermute(payload, 'seq', [(sender, hop), (back_sender, back_sender -...  17.9 us
    ppermute x3, starting transfers between devices, chain_seq(): lax.ppermute(payload, 'seq', [(sender, hop), (back_sender, back_sender -...  6.9 us
    unnamed x30, local copies, waits for them, and re-layouts  3.34 us
    mul x1, other arithmetic, local(): d_k = k_scale * (d_kn - jnp.sum(kn * d_kn, axis=-1, keepdims=True) * kn)  1.79 us
    convert_element_type x1, local copies, waits for them, and re-layouts, pair_major(): return tensor.reshape(heads_here, tok_count, 2, head_size).transpose(1, 2...  1.47 us
  transfers between devices with their start and end apart: 3, of which 2 were waited for; matrix products, arithmetic and copies ran while one was open for 5% of the time, Pallas kernels for 0%

profile of v5, /device:TPU:0, one launch (start us, length us, event | category | flops | bytes accessed | tf_op | source)
XLA Modules:
  0.0 68.2 jit_solution(10916106978276060252)
XLA Ops:
  0.7 1.1 %fusion.35 = f32[4,128]{1,0:T(4,128)S(1)} fusion(bf16[128,4,128]{2,1,0:T(4,128)(2,1)} %param.4), kind=kLoop, calls=%fused_computation.71 | loop fusion | flops 196096 | bytes 133120 | tf_op jit(solution)/shard_map/reduce_sum | solution.py:15
  1.9 1.2 %copy.9 = f32[128,2,4,128]{3,1,0,2:T(2,128)S(1)} copy(bf16[128,2,4,128]{3,2,1,0:T(4,128)(2,1)} %param.5) | data formatting | bytes 786432 | tf_op jit(solution)/shard_map/transpose | solution.py:106
  3.0 0.2 multiply_reduce_fusion
  3.3 0.2 broadcast_multiply_fusion
  3.5 0.5 convolution_multiply_fusion.7
  4.0 0.5 convolution_multiply_fusion.6
  4.5 0.5 convolution_multiply_fusion.5
  5.1 0.7 convolution_multiply_fusion.4
  5.8 0.9 %fusion.3 = f32[4,16,16,16]{3,2,1,0:T(8,128)S(1)} fusion(f32[4,16,16,128]{3,2,1,0:T(8,128)S(1)} %bitcast.201, pred[16,16]{1,0:T(8,128)(4,1)S(1)} %iota_compare_fusion.7), kind=kOutput, calls=%fused_computation.10 | convolution fusion | flops 25198592 | bytes 590080 | tf_op jit(solution)/shard_map/hpid,hpjd->hpij/dot_general | solution.py:11
  6.7 0.7 fusion.84
  7.4 0.7 fusion.85
  8.0 0.7 convolution_add_fusion.2
  8.7 0.6 fusion.86
  9.4 0.6 convolution_add_fusion.1
  10.0 0.6 convolution_add_fusion
  10.7 0.4 fusion.80
  11.1 0.4 convolution_negate_fusion.3
  11.5 0.1 select_maximum_fusion.3
  11.6 0.4 fusion.81
  12.0 0.4 convolution_negate_fusion.2
  12.6 0.4 fusion.82
  13.0 0.4 convolution_negate_fusion.1
  13.6 0.6 fusion.40
  14.2 0.7 fusion.14
  14.9 1.0 %fusion.26 = f32[4,256,128]{2,1,0:T(8,128)S(1)} fusion(f32[4,256,128]{2,1,0:T(8,128)S(1)} %broadcast_multiply_fusion, f32[4,1,128,128]{3,2,0,1:T(8,128)S(1)} %get-tuple-element.9, f32[4,1,128,128]{3,2,0,1:T(8,128)S(1)} %get-tuple-element.8, f32[4,1,128,128]{3,2,0,1:T(8,128)S(1)} %fusion.14), kind=kOutput, calls=%fused_computation.63 | convolution fusion | flops 403701760 | bytes 1835008 | tf_op jit(solution)/shard_map/hij,hjd->hid/dot_general | solution.py:11
  16.0 0.8 %fusion.24 = f32[4,256,128]{2,1,0:T(8,128)S(1)} fusion(f32[4,1,128,128]{3,2,0,1:T(8,128)S(1)} %get-tuple-element.9, f32[4,1,128,128]{3,2,0,1:T(8,128)S(1)} %get-tuple-element.8, f32[4,1,128,128]{3,2,0,1:T(8,128)S(1)} %fusion.14, bf16[256,4,128]{2,1,0:T(4,128)(2,1)S(1)} %bitcast.216), kind=kOutput, calls=%fused_computation.62 | convolution fusion | flops 403701760 | bytes 1572864 | tf_op jit(solution)/shard_map/hij,hjd->hid/dot_general | solution.py:11
  16.9 0.6 fusion.10
  17.5 0.6 convolution_subtract_fusion.2
  18.2 0.4 fusion.61
  18.6 0.3 copy-done.2
  18.9 1.0 %broadcast_select_fusion.1 = (f32[4,128,128]{2,1,0:T(8,128)S(1)}, f32[4,128,128]{2,1,0:T(8,128)S(1)}) fusion(f32[4,128,128]{2,1,0:T(8,128)S(1)} %fusion.61, pred[]{:T(512)S(6)} %eq.36, f32[4,256,128]{2,1,0:T(8,128)S(1)} %broadcast_multiply_fusion, f32[4,256,128]{2,1,0:T(8,128)S(1)} %fusion.24), kind=kOutput, calls=%fused_computation.116 | convolution fusion | flops 201457664 | bytes 1835009 | tf_op jit(solution)/shard_map/hjd,hjw->hdw/dot_general | solution.py:11
  19.9 4.9 %collective-permute-start = (f32[4,128,128]{2,1,0:T(8,128)S(1)}, f32[4,128,128]{2,1,0:T(8,128)S(1)}, u32[]{:S(2)}, u32[]{:S(2)}) collective-permute-start(f32[4,128,128]{2,1,0:T(8,128)S(1)} %get-tuple-element.18), channel_id=1, source_target_pairs={{0,4},{12,8},{1,5},{13,9},{2,6},{14,10},{3,7},{15,11},{16,20},{28,... | collective-permute-start | bytes 786440 | tf_op jit(solution)/shard_map/ppermute | solution.py:64
  24.9 1.1 %fusion.15 = f32[4,128,128]{2,1,0:T(8,128)S(1)} fusion(f32[4,256,128]{2,1,0:T(8,128)S(1)} %broadcast_multiply_fusion, f32[4,256,128]{2,1,0:T(8,128)S(1)} %fusion.26, f32[128,128]{1,0:T(8,128)S(1)} %fusion.63), kind=kOutput, calls=%fused_computation.44 | convolution fusion | flops 201457664 | bytes 1376256 | tf_op jit(solution)/shard_map/hjd,hjw->hdw/dot_general | solution.py:11
  26.0 4.5 %collective-permute-done = f32[4,128,128]{2,1,0:T(8,128)S(1)} collective-permute-done((f32[4,128,128]{2,1,0:T(8,128)S(1)}, f32[4,128,128]{2,1,0:T(8,128)S(1)}, u32[]{:S(2)}, u32[]{:S(2)}) %collective-permute-start) | collective-permute-done | bytes 262176 | tf_op jit(solution)/shard_map/ppermute | solution.py:64
  30.4 0.6 convolution_add_fusion.8
  31.0 0.4 fusion.13
  31.5 0.7 collective-permute-start.1
  32.1 1.4 %fusion.59 = f32[4,256,128]{2,1,0:T(8,128)} fusion(f32[4,128,256]{2,1,0:T(8,128)S(1)} %fusion.10, bf16[4,128,128]{2,0,1:T(4,128)(2,1)S(1)} %bitcast.196), kind=kOutput, calls=%fused_computation.123 | convolution fusion | flops 201326592 | bytes 1179648 | tf_op jit(solution)/shard_map/hij,hiw->hjw/dot_general | solution.py:11
  33.6 0.6 convolution_add_fusion.6
  34.2 0.3 copy-done.5
  34.5 1.1 %fusion.12 = f32[4,128,128]{2,1,0:T(8,128)} fusion(f32[4,128,128]{2,1,0:T(8,128)S(1)} %convolution_add_fusion.6, f32[4,128,128]{2,1,0:T(8,128)S(1)} %copy-done.5, f32[4,128,128]{2,1,0:T(8,128)S(1)} %fusion.15, pred[]{:T(512)S(6)} %eq.33, f32[4,128,128]{2,1,0:T(8,128)S(1)} %collective-permute-done.1, f32[4,128,128]{2,1,0:T(8,128)S(1)} %collective-permute-done, ...), kind=kOutput, calls=%fused_computation.27 | convolution fusion | flops 100925440 | bytes 1572866 | tf_op jit(solution)/shard_map/hij,hjk->hik/dot_general | solution.py:11
  35.6 1.3 %collective-permute-start.2 = (f32[4,128,128]{2,1,0:T(8,128)}, f32[4,128,128]{2,1,0:T(8,128)S(1)}, u32[]{:S(2)}, u32[]{:S(2)}) collective-permute-start(f32[4,128,128]{2,1,0:T(8,128)} %fusion.12), channel_id=1, source_target_pairs={{8,12},{4,0},{9,13},{5,1},{10,14},{6,2},{11,15},{7,3},{24,28},{20,... | collective-permute-start | bytes 786440 | tf_op jit(solution)/shard_map/ppermute | solution.py:64
  37.0 0.6 fusion.87
  37.6 13.5 %collective-permute-done.2 = f32[4,128,128]{2,1,0:T(8,128)S(1)} collective-permute-done((f32[4,128,128]{2,1,0:T(8,128)}, f32[4,128,128]{2,1,0:T(8,128)S(1)}, u32[]{:S(2)}, u32[]{:S(2)}) %collective-permute-start.2) | collective-permute-done | bytes 262176 | tf_op jit(solution)/shard_map/ppermute | solution.py:64
  51.1 0.6 convolution_subtract_fusion.1
  51.8 0.4 fusion.57
  52.2 0.5 copy-done.3
  52.7 0.4 fusion.17
  53.1 0.8 %copy.37 = bf16[128,4,128]{2,1,0:T(4,128)(2,1)} copy(bf16[128,4,128]{2,0,1:T(8,128)(2,1)S(1)} %fusion.17) | data formatting | bytes 262144
  53.9 0.6 fusion.8
  54.5 0.3 copy-done.8
  55.0 1.5 %fusion.83 = (bf16[4,256,128]{2,1,0:T(8,128)(2,1)S(1)}, f32[4,256,128]{2,1,0:T(8,128)S(1)}) fusion(f32[4,256,128]{2,1,0:T(8,128)S(1)} %fusion.8, f32[4,1,128,128]{3,2,0,1:T(8,128)S(1)} %copy-done.12, f32[4,1,128,128]{3,2,0,1:T(8,128)S(1)} %copy-done.10, f32[4,1,128,128]{3,2,0,1:T(8,128)S(1)} %copy-done.8), kind=kOutput, calls=%fused_computation.153 | convolution fusion | flops 403832832 | bytes 2097152 | tf_op jit(solution)/shard_map/hij,hiw->hjw/dot_general | solution.py:11
  56.5 0.4 fusion.2
  56.9 1.1 %fusion.30 = f32[4,256,128]{2,1,0:T(8,128)S(1)} fusion(f32[4,128,256]{2,1,0:T(8,128)S(1)} %fusion.2, f32[4,128]{1,0:T(4,128)S(1)} %get-tuple-element.17, bf16[128,4,128]{2,1,0:T(4,128)(2,1)S(1)} %copy-done.1), kind=kOutput, calls=%fused_computation.68 | convolution fusion | flops 201457664 | bytes 1181696 | tf_op jit(solution)/shard_map/hij,hid->hjd/dot_general | solution.py:11
  58.0 0.7 %fusion.34 = (f32[4,128]{1,0:T(4,128)S(1)}, f32[4,128,128]{2,1,0:T(8,128)S(1)}) fusion(f32[4,128,128]{1,2,0:T(8,128)S(1)} %fusion.57, f32[4,128]{1,0:T(4,128)S(1)} %get-tuple-element.17, bf16[128,4,128]{2,1,0:T(4,128)(2,1)S(1)} %copy-done.1, f32[4,128,256]{2,1,0:T(8,128)S(1)} %fusion.2, f32[4,256,128]{2,1,0:T(8,128)S(1)} %broadcast_multiply_fusion), kind=kOutput, calls=%fused_computation.70 | convolution fusion | flops 201719296 | bytes 1708032 | tf_op jit(solution)/shard_map/hij,hjd->hid/dot_general | solution.py:11
  58.8 0.2 fusion.39
  59.0 0.8 %copy.38 = bf16[128,4,128]{2,1,0:T(4,128)(2,1)} copy(bf16[128,4,128]{2,0,1:T(8,128)(2,1)S(1)} %fusion.39) | data formatting | bytes 262144
  59.7 1.0 %fusion.1 = f32[4,256,256]{2,1,0:T(8,128)S(1)} fusion(f32[4,256,128]{2,1,0:T(8,128)S(1)} %get-tuple-element.23, f32[4,256,128]{2,1,0:T(8,128)S(1)} %convolution_subtract_fusion.1, pred[256,256]{1,0:T(8,128)(4,1)S(1)} %iota_compare_fusion.4), kind=kOutput, calls=%fused_computation.2 | convolution fusion | flops 403177472 | bytes 2162688 | tf_op jit(solution)/shard_map/hiw,hjw->hij/dot_general | solution.py:11
  60.8 1.1 %fusion.88 = f32[4,256,128]{2,1,0:T(8,128)S(1)} fusion(f32[4,256,256]{2,1,0:T(8,128)S(1)} %fusion.1, f32[4,256,128]{2,1,0:T(8,128)S(1)} %broadcast_multiply_fusion), kind=kOutput, calls=%fused_computation.158 | convolution fusion | flops 402653184 | bytes 2097152 | tf_op jit(solution)/shard_map/hij,hjd->hid/dot_general | solution.py:11
  61.8 0.6 fusion.9
  62.5 0.6 fusion.7
  63.1 1.9 %convolution_add_fusion.3 = f32[4,256,128]{2,1,0:T(8,128)S(1)} fusion(f32[4,256,128]{2,1,0:T(8,128)S(1)} %fusion.7, f32[4,256,256]{2,1,0:T(8,128)S(1)} %fusion.1, f32[4,256,128]{2,1,0:T(8,128)S(1)} %broadcast_multiply_fusion), kind=kOutput, calls=%fused_computation.6 | convolution fusion | flops 402784256 | bytes 2621440 | tf_op jit(solution)/shard_map/hji,hjd->hid/dot_general | solution.py:11
  65.0 1.8 %fusion.11 = bf16[4,256,128]{2,1,0:T(8,128)(2,1)S(1)} fusion(f32[4,256,128]{2,1,0:T(8,128)S(1)} %convolution_add_fusion.3, f32[4,256,128]{2,1,0:T(8,128)S(1)} %broadcast_multiply_fusion, f32[4,256]{1,0:T(4,128)S(1)} %add_rsqrt_fusion), kind=kOutput, calls=%fused_computation.23 | output fusion | flops 656511 | bytes 1314816 | tf_op jit(solution)/shard_map/mul | solution.py:142
  66.7 1.5 %copy_bitcast_fusion = (bf16[128,2,4,128]{3,2,1,0:T(4,128)(2,1)}, bf16[128,2,4,128]{3,2,1,0:T(4,128)(2,1)}) fusion(bf16[4,128,2,128]{3,2,1,0:T(2,128)(2,1)S(1)} %bitcast.214, bf16[4,128,2,128]{3,2,1,0:T(2,128)(2,1)S(1)} %bitcast.213), kind=kLoop, calls=%fused_computation.96 | loop fusion | bytes 1048576 | tf_op jit(solution)/shard_map/convert_element_type | solution.py:151
  (41 shorter events, 1.0 us)
Async XLA Ops:
  0.6 17.5 %copy-start = (bf16[128,4,128]{2,1,0:T(4,128)(2,1)S(1)}, bf16[128,4,128]{2,1,0:T(4,128)(2,1)}, u32[]{:S(2)}) copy-start(bf16[128,4,128]{2,1,0:T(4,128)(2,1)} %param.7) | copy-start | bytes 393220
  13.6 2.3 %copy-start.9 = (f32[4,1,128,128]{3,2,0,1:T(8,128)}, f32[4,1,128,128]{3,2,0,1:T(8,128)S(1)}, u32[]{:S(2)}) copy-start(f32[4,1,128,128]{3,2,0,1:T(8,128)S(1)} %get-tuple-element.8) | copy-start | bytes 786436
  13.6 2.3 %copy-start.11 = (f32[4,1,128,128]{3,2,0,1:T(8,128)}, f32[4,1,128,128]{3,2,0,1:T(8,128)S(1)}, u32[]{:S(2)}) copy-start(f32[4,1,128,128]{3,2,0,1:T(8,128)S(1)} %get-tuple-element.9) | copy-start | bytes 786436
  14.9 1.1 %copy-start.7 = (f32[4,1,128,128]{3,2,0,1:T(8,128)}, f32[4,1,128,128]{3,2,0,1:T(8,128)S(1)}, u32[]{:S(2)}) copy-start(f32[4,1,128,128]{3,2,0,1:T(8,128)S(1)} %fusion.14) | copy-start | bytes 786436
  14.9 1.1 %copy-start.13 = (bf16[128,2,4,128]{3,2,1,0:T(4,128)(2,1)S(1)}, bf16[128,2,4,128]{3,2,1,0:T(4,128)(2,1)}, u32[]{:S(2)}) copy-start(bf16[128,2,4,128]{3,2,1,0:T(4,128)(2,1)} %param.6) | copy-start | bytes 786436
  16.0 0.9 %copy-start.1 = (bf16[128,4,128]{2,1,0:T(4,128)(2,1)S(1)}, bf16[128,4,128]{2,1,0:T(4,128)(2,1)}, u32[]{:S(2)}) copy-start(bf16[128,4,128]{2,1,0:T(4,128)(2,1)} %param.4) | copy-start | bytes 393220
  18.2 0.7 %copy-start.2 = (f32[4,128,128]{2,1,0:T(8,128)}, f32[4,128,128]{2,1,0:T(8,128)S(1)}, u32[]{:S(2)}) copy-start(f32[4,128,128]{2,1,0:T(8,128)S(1)} %convolution_subtract_fusion.2) | copy-start | bytes 786436
  19.9 11.1 %copy-start.4 = (f32[4,128,128]{2,1,0:T(8,128)}, f32[4,128,128]{2,1,0:T(8,128)S(1)}, u32[]{:S(2)}) copy-start(f32[4,128,128]{2,1,0:T(8,128)S(1)} %get-tuple-element.19) | copy-start | bytes 786436
  19.9 10.5 %collective-permute-start = (f32[4,128,128]{2,1,0:T(8,128)S(1)}, f32[4,128,128]{2,1,0:T(8,128)S(1)}, u32[]{:S(2)}, u32[]{:S(2)}) collective-permute-start(f32[4,128,128]{2,1,0:T(8,128)S(1)} %get-tuple-element.18), channel_id=1, source_target_pairs={{0,4},{12,8},{1,5},{13,9},{2,6},{14,10},{3,7},{15,11},{16,20},{28,... | collective-permute-start | bytes 786440 | tf_op jit(solution)/shard_map/ppermute | solution.py:64
  31.5 2.1 %collective-permute-start.1 = (f32[4,128,128]{2,1,0:T(8,128)S(1)}, f32[4,128,128]{2,1,0:T(8,128)S(1)}, u32[]{:S(2)}, u32[]{:S(2)}) collective-permute-start(f32[4,128,128]{2,1,0:T(8,128)S(1)} %fusion.13), channel_id=1, source_target_pairs={{4,8},{8,4},{5,9},{9,5},{6,10},{10,6},{7,11},{11,7},{20,24},{24,20... | collective-permute-start | bytes 786440 | tf_op jit(solution)/shard_map/ppermute | solution.py:64
  33.6 1.0 %copy-start.5 = (f32[4,128,128]{2,1,0:T(8,128)S(1)}, f32[4,128,128]{2,1,0:T(8,128)}, u32[]{:S(2)}) copy-start(f32[4,128,128]{2,1,0:T(8,128)} %copy-done.4) | copy-start | bytes 786436
  35.6 15.5 %collective-permute-start.2 = (f32[4,128,128]{2,1,0:T(8,128)}, f32[4,128,128]{2,1,0:T(8,128)S(1)}, u32[]{:S(2)}, u32[]{:S(2)}) collective-permute-start(f32[4,128,128]{2,1,0:T(8,128)} %fusion.12), channel_id=1, source_target_pairs={{8,12},{4,0},{9,13},{5,1},{10,14},{6,2},{11,15},{7,3},{24,28},{20,... | collective-permute-start | bytes 786440 | tf_op jit(solution)/shard_map/ppermute | solution.py:64
  51.7 1.0 %copy-start.3 = (f32[4,128,128]{2,1,0:T(8,128)S(1)}, f32[4,128,128]{2,1,0:T(8,128)}, u32[]{:S(2)}) copy-start(f32[4,128,128]{2,1,0:T(8,128)} %copy-done.2) | copy-start | bytes 786436
  52.7 1.2 %copy-start.6 = (f32[4,256,128]{2,1,0:T(8,128)S(1)}, f32[4,256,128]{2,1,0:T(8,128)}, u32[]{:S(2)}) copy-start(f32[4,256,128]{2,1,0:T(8,128)} %fusion.59) | copy-start | bytes 1572868
  53.9 1.0 %copy-start.8 = (f32[4,1,128,128]{3,2,0,1:T(8,128)S(1)}, f32[4,1,128,128]{3,2,0,1:T(8,128)}, u32[]{:S(2)}) copy-start(f32[4,1,128,128]{3,2,0,1:T(8,128)} %copy-done.7) | copy-start | bytes 786436
  53.9 1.0 %copy-start.10 = (f32[4,1,128,128]{3,2,0,1:T(8,128)S(1)}, f32[4,1,128,128]{3,2,0,1:T(8,128)}, u32[]{:S(2)}) copy-start(f32[4,1,128,128]{3,2,0,1:T(8,128)} %copy-done.9) | copy-start | bytes 786436
  53.9 1.1 %copy-start.12 = (f32[4,1,128,128]{3,2,0,1:T(8,128)S(1)}, f32[4,1,128,128]{3,2,0,1:T(8,128)}, u32[]{:S(2)}) copy-start(f32[4,1,128,128]{3,2,0,1:T(8,128)} %copy-done.11) | copy-start | bytes 786436

commit v6 on v1

--- a/solution.py
+++ b/solution.py
@@ -51,14 +51,20 @@
     return inverse.reshape(heads, rows, rows)
 
 
+def sliced_permute(tensor, pairs):
+    heads = tensor.shape[0]
+    parts = [lax.ppermute(tensor[h:h + 1], "seq", pairs) for h in range(heads)]
+    return jnp.concatenate(parts, axis=0)
+
+
 def chain_seq(transition, offset, local_cot):
     count = lax.axis_size("seq")
     right = [(i, i + 1) for i in range(count - 1)]
     left = [(i + 1, i) for i in range(count - 1)]
     fwd_sum, bwd_sum = offset, local_cot
     for hop in range(count - 1):
-        got_sum = lax.ppermute(fwd_sum, "seq", right)
-        got_cot = lax.ppermute(bwd_sum, "seq", left)
+        got_sum = sliced_permute(fwd_sum, right)
+        got_cot = sliced_permute(bwd_sum, left)
         if hop == count - 2:
             return got_sum, got_cot
         fwd_sum = mm("hij,hjk->hik", transition, got_sum) + offset

time: 63 us -> 108 us (1.71)
  starting transfers between devices: 18 us -> 61.9 us
    ppermute x6 -> x24, starting transfers between devices: 18 us -> 61.9 us  [sliced_permute(): parts = [lax.ppermute(tensor[h:h + 1], 'seq', pairs) for h in range(heads)]]
    ppermute x6 -> x24, waiting for transfers between devices: 4.92 us -> 4.37 us  [sliced_permute(): parts = [lax.ppermute(tensor[h:h + 1], 'seq', pairs) for h in range(heads)]]
  transfers between devices with their start and end apart: 6 -> 24, of which waited for: 5 -> 1; matrix products, arithmetic and copies ran while one was open for 20% -> 9% of each run, Pallas kernels for 0% -> 0%
where the time goes in v6:
time: 108 us; the launch traced here: 107 us
  starting transfers between devices  61.9 us (57%)
  matrix products  30.3 us (28%)
  local copies, waits for them, and re-layouts  5.42 us (5%)
  waiting for transfers between devices  4.37 us (4%)
  other arithmetic  3.13 us (3%)
  between operations  1.59 us (1%)
    ppermute x24, starting transfers between devices, sliced_permute(): parts = [lax.ppermute(tensor[h:h + 1], 'seq', pairs) for h in range(heads)]  61.9 us
    dot_general x45, matrix products, mm(): return jnp.einsum(spec, *operands, precision=highest)  30.3 us
    ppermute x24, waiting for transfers between devices, sliced_permute(): parts = [lax.ppermute(tensor[h:h + 1], 'seq', pairs) for h in range(heads)]  4.37 us
  transfers between devices with their start and end apart: 24, of which 1 were waited for; matrix products, arithmetic and copies ran while one was open for 9% of the time, Pallas kernels for 0%

profile of v6, /device:TPU:0, one launch (start us, length us, event | category | flops | bytes accessed | tf_op | source)
XLA Modules:
  0.0 106.8 jit_solution(11740498452994388553)
XLA Ops:
  0.7 1.2 %copy.9 = f32[128,2,4,128]{3,1,0,2:T(2,128)S(1)} copy(bf16[128,2,4,128]{3,2,1,0:T(4,128)(2,1)} %param.5) | data formatting | bytes 786432 | tf_op jit(solution)/shard_map/transpose | solution.py:109
  2.3 0.5 convolution_multiply_fusion.7
  2.8 0.5 convolution_multiply_fusion.6
  3.4 0.5 convolution_multiply_fusion.5
  3.9 0.7 convolution_multiply_fusion.4
  4.6 0.9 fusion.3
  5.5 0.6 fusion.111
  6.2 0.6 fusion.112
  6.8 0.7 convolution_add_fusion.2
  7.5 0.6 fusion.113
  8.1 0.6 convolution_add_fusion.1
  8.8 0.6 convolution_add_fusion
  12.4 0.6 fusion.66
  13.0 0.7 fusion.12
  13.9 0.6 fusion.22
  14.5 1.2 %convolution_multiply_fusion.9 = f32[4,128,128]{2,1,0:T(8,128)S(1)} fusion(f32[4,256,128]{2,1,0:T(8,128)S(1)} %broadcast_multiply_fusion, f32[4,256,128]{2,1,0:T(8,128)S(1)} %fusion.22), kind=kOutput, calls=%fused_computation.39 | convolution fusion | flops 201392128 | bytes 1310720 | tf_op jit(solution)/shard_map/hjd,hjw->hdw/dot_general | solution.py:11
  15.7 4.9 %collective-permute-start = (f32[1,128,128]{2,1,0:T(8,128)S(1)}, f32[1,128,128]{2,1,0:T(8,128)S(1)}, u32[]{:S(2)}, u32[]{:S(2)}) collective-permute-start(f32[1,128,128]{2,1,0:T(8,128)S(1)} %get-tuple-element.36), channel_id=1, source_target_pairs={{0,4},{4,8},{8,12},{1,5},{5,9},{9,13},{2,6},{6,10},{10,14},{3,7},{... | collective-permute-start | bytes 196616 | tf_op jit(solution)/shard_map/ppermute | solution.py:56
  20.7 3.5 %collective-permute-start.3 = (f32[1,128,128]{2,1,0:T(8,128)S(1)}, f32[1,128,128]{2,1,0:T(8,128)S(1)}, u32[]{:S(2)}, u32[]{:S(2)}) collective-permute-start(f32[1,128,128]{2,1,0:T(8,128)S(1)} %get-tuple-element.37), channel_id=1, source_target_pairs={{0,4},{4,8},{8,12},{1,5},{5,9},{9,13},{2,6},{6,10},{10,14},{3,7},{... | collective-permute-start | bytes 196616 | tf_op jit(solution)/shard_map/ppermute | solution.py:56
  24.2 3.5 %collective-permute-start.2 = (f32[1,128,128]{2,1,0:T(8,128)S(1)}, f32[1,128,128]{2,1,0:T(8,128)S(1)}, u32[]{:S(2)}, u32[]{:S(2)}) collective-permute-start(f32[1,128,128]{2,1,0:T(8,128)S(1)} %get-tuple-element.38), channel_id=1, source_target_pairs={{0,4},{4,8},{8,12},{1,5},{5,9},{9,13},{2,6},{6,10},{10,14},{3,7},{... | collective-permute-start | bytes 196616 | tf_op jit(solution)/shard_map/ppermute | solution.py:56
  27.7 1.9 %collective-permute-start.1 = (f32[1,128,128]{2,1,0:T(8,128)S(1)}, f32[1,128,128]{2,1,0:T(8,128)S(1)}, u32[]{:S(2)}, u32[]{:S(2)}) collective-permute-start(f32[1,128,128]{2,1,0:T(8,128)S(1)} %get-tuple-element.39), channel_id=1, source_target_pairs={{0,4},{4,8},{8,12},{1,5},{5,9},{9,13},{2,6},{6,10},{10,14},{3,7},{... | collective-permute-start | bytes 196616 | tf_op jit(solution)/shard_map/ppermute | solution.py:56
  29.6 1.0 fusion.24
  30.9 0.6 fusion.10
  31.6 0.6 convolution_subtract_fusion.2
  32.7 1.3 %collective-permute-start.12 = (f32[1,128,128]{2,1,0:T(8,128)S(1)}, f32[1,128,128]{2,1,0:T(8,128)S(1)}, u32[]{:S(2)}, u32[]{:S(2)}) collective-permute-start(f32[1,128,128]{2,1,0:T(8,128)S(1)} %get-tuple-element.24), channel_id=1, source_target_pairs={{4,0},{8,4},{12,8},{5,1},{9,5},{13,9},{6,2},{10,6},{14,10},{7,3},{... | collective-permute-start | bytes 196616 | tf_op jit(solution)/shard_map/ppermute | solution.py:56
  34.0 0.6 fusion.114
  34.6 0.6 fusion.79
  35.2 1.1 fusion.13
  36.3 1.3 %collective-permute-start.15 = (f32[1,128,128]{2,1,0:T(8,128)S(1)}, f32[1,128,128]{2,1,0:T(8,128)S(1)}, u32[]{:S(2)}, u32[]{:S(2)}) collective-permute-start(f32[1,128,128]{2,1,0:T(8,128)S(1)} %get-tuple-element.25), channel_id=1, source_target_pairs={{4,0},{8,4},{12,8},{5,1},{9,5},{13,9},{6,2},{10,6},{14,10},{7,3},{... | collective-permute-start | bytes 196616 | tf_op jit(solution)/shard_map/ppermute | solution.py:56
  37.7 1.3 %collective-permute-start.14 = (f32[1,128,128]{2,1,0:T(8,128)S(1)}, f32[1,128,128]{2,1,0:T(8,128)S(1)}, u32[]{:S(2)}, u32[]{:S(2)}) collective-permute-start(f32[1,128,128]{2,1,0:T(8,128)S(1)} %get-tuple-element.26), channel_id=1, source_target_pairs={{4,0},{8,4},{12,8},{5,1},{9,5},{13,9},{6,2},{10,6},{14,10},{7,3},{... | collective-permute-start | bytes 196616 | tf_op jit(solution)/shard_map/ppermute | solution.py:56
  39.0 1.3 %collective-permute-start.13 = (f32[1,128,128]{2,1,0:T(8,128)S(1)}, f32[1,128,128]{2,1,0:T(8,128)S(1)}, u32[]{:S(2)}, u32[]{:S(2)}) collective-permute-start(f32[1,128,128]{2,1,0:T(8,128)S(1)} %get-tuple-element.27), channel_id=1, source_target_pairs={{4,0},{8,4},{12,8},{5,1},{9,5},{13,9},{6,2},{10,6},{14,10},{7,3},{... | collective-permute-start | bytes 196616 | tf_op jit(solution)/shard_map/ppermute | solution.py:56
  40.7 6.4 %collective-permute-start.4 = (f32[1,128,128]{2,1,0:T(8,128)S(1)}, f32[1,128,128]{2,1,0:T(8,128)S(1)}, u32[]{:S(2)}, u32[]{:S(2)}) collective-permute-start(f32[1,128,128]{2,1,0:T(8,128)S(1)} %get-tuple-element.32), channel_id=1, source_target_pairs={{0,4},{4,8},{8,12},{1,5},{5,9},{9,13},{2,6},{6,10},{10,14},{3,7},{... | collective-permute-start | bytes 196616 | tf_op jit(solution)/shard_map/ppermute | solution.py:56
  47.2 3.9 %collective-permute-start.7 = (f32[1,128,128]{2,1,0:T(8,128)S(1)}, f32[1,128,128]{2,1,0:T(8,128)S(1)}, u32[]{:S(2)}, u32[]{:S(2)}) collective-permute-start(f32[1,128,128]{2,1,0:T(8,128)S(1)} %get-tuple-element.33), channel_id=1, source_target_pairs={{0,4},{4,8},{8,12},{1,5},{5,9},{9,13},{2,6},{6,10},{10,14},{3,7},{... | collective-permute-start | bytes 196616 | tf_op jit(solution)/shard_map/ppermute | solution.py:56
  51.1 3.9 %collective-permute-start.6 = (f32[1,128,128]{2,1,0:T(8,128)S(1)}, f32[1,128,128]{2,1,0:T(8,128)S(1)}, u32[]{:S(2)}, u32[]{:S(2)}) collective-permute-start(f32[1,128,128]{2,1,0:T(8,128)S(1)} %get-tuple-element.34), channel_id=1, source_target_pairs={{0,4},{4,8},{8,12},{1,5},{5,9},{9,13},{2,6},{6,10},{10,14},{3,7},{... | collective-permute-start | bytes 196616 | tf_op jit(solution)/shard_map/ppermute | solution.py:56
  55.0 1.9 %collective-permute-start.5 = (f32[1,128,128]{2,1,0:T(8,128)S(1)}, f32[1,128,128]{2,1,0:T(8,128)S(1)}, u32[]{:S(2)}, u32[]{:S(2)}) collective-permute-start(f32[1,128,128]{2,1,0:T(8,128)S(1)} %get-tuple-element.35), channel_id=1, source_target_pairs={{0,4},{4,8},{8,12},{1,5},{5,9},{9,13},{2,6},{6,10},{10,14},{3,7},{... | collective-permute-start | bytes 196616 | tf_op jit(solution)/shard_map/ppermute | solution.py:56
  57.0 0.6 convolution_add_fusion.6
  57.6 1.3 %collective-permute-start.16 = (f32[1,128,128]{2,1,0:T(8,128)S(1)}, f32[1,128,128]{2,1,0:T(8,128)S(1)}, u32[]{:S(2)}, u32[]{:S(2)}) collective-permute-start(f32[1,128,128]{2,1,0:T(8,128)S(1)} %get-tuple-element.20), channel_id=1, source_target_pairs={{4,0},{8,4},{12,8},{5,1},{9,5},{13,9},{6,2},{10,6},{14,10},{7,3},{... | collective-permute-start | bytes 196616 | tf_op jit(solution)/shard_map/ppermute | solution.py:56
  58.9 1.3 %collective-permute-start.19 = (f32[1,128,128]{2,1,0:T(8,128)S(1)}, f32[1,128,128]{2,1,0:T(8,128)S(1)}, u32[]{:S(2)}, u32[]{:S(2)}) collective-permute-start(f32[1,128,128]{2,1,0:T(8,128)S(1)} %get-tuple-element.21), channel_id=1, source_target_pairs={{4,0},{8,4},{12,8},{5,1},{9,5},{13,9},{6,2},{10,6},{14,10},{7,3},{... | collective-permute-start | bytes 196616 | tf_op jit(solution)/shard_map/ppermute | solution.py:56
  60.2 1.3 %collective-permute-start.18 = (f32[1,128,128]{2,1,0:T(8,128)S(1)}, f32[1,128,128]{2,1,0:T(8,128)S(1)}, u32[]{:S(2)}, u32[]{:S(2)}) collective-permute-start(f32[1,128,128]{2,1,0:T(8,128)S(1)} %get-tuple-element.22), channel_id=1, source_target_pairs={{4,0},{8,4},{12,8},{5,1},{9,5},{13,9},{6,2},{10,6},{14,10},{7,3},{... | collective-permute-start | bytes 196616 | tf_op jit(solution)/shard_map/ppermute | solution.py:56
  61.5 1.3 %collective-permute-start.17 = (f32[1,128,128]{2,1,0:T(8,128)S(1)}, f32[1,128,128]{2,1,0:T(8,128)S(1)}, u32[]{:S(2)}, u32[]{:S(2)}) collective-permute-start(f32[1,128,128]{2,1,0:T(8,128)S(1)} %get-tuple-element.23), channel_id=1, source_target_pairs={{4,0},{8,4},{12,8},{5,1},{9,5},{13,9},{6,2},{10,6},{14,10},{7,3},{... | collective-permute-start | bytes 196616 | tf_op jit(solution)/shard_map/ppermute | solution.py:56
  63.3 6.4 %collective-permute-start.11 = (f32[1,128,128]{2,1,0:T(8,128)S(1)}, f32[1,128,128]{2,1,0:T(8,128)S(1)}, u32[]{:S(2)}, u32[]{:S(2)}) collective-permute-start(f32[1,128,128]{2,1,0:T(8,128)S(1)} %get-tuple-element.28), channel_id=1, source_target_pairs={{0,4},{4,8},{8,12},{1,5},{5,9},{9,13},{2,6},{6,10},{10,14},{3,7},{... | collective-permute-start | bytes 196616 | tf_op jit(solution)/shard_map/ppermute | solution.py:56
  69.7 3.9 %collective-permute-start.10 = (f32[1,128,128]{2,1,0:T(8,128)S(1)}, f32[1,128,128]{2,1,0:T(8,128)S(1)}, u32[]{:S(2)}, u32[]{:S(2)}) collective-permute-start(f32[1,128,128]{2,1,0:T(8,128)S(1)} %get-tuple-element.29), channel_id=1, source_target_pairs={{0,4},{4,8},{8,12},{1,5},{5,9},{9,13},{2,6},{6,10},{10,14},{3,7},{... | collective-permute-start | bytes 196616 | tf_op jit(solution)/shard_map/ppermute | solution.py:56
  73.7 3.9 %collective-permute-start.9 = (f32[1,128,128]{2,1,0:T(8,128)S(1)}, f32[1,128,128]{2,1,0:T(8,128)S(1)}, u32[]{:S(2)}, u32[]{:S(2)}) collective-permute-start(f32[1,128,128]{2,1,0:T(8,128)S(1)} %get-tuple-element.30), channel_id=1, source_target_pairs={{0,4},{4,8},{8,12},{1,5},{5,9},{9,13},{2,6},{6,10},{10,14},{3,7},{... | collective-permute-start | bytes 196616 | tf_op jit(solution)/shard_map/ppermute | solution.py:56
  77.6 1.9 %collective-permute-start.8 = (f32[1,128,128]{2,1,0:T(8,128)S(1)}, f32[1,128,128]{2,1,0:T(8,128)S(1)}, u32[]{:S(2)}, u32[]{:S(2)}) collective-permute-start(f32[1,128,128]{2,1,0:T(8,128)S(1)} %get-tuple-element.31), channel_id=1, source_target_pairs={{0,4},{4,8},{8,12},{1,5},{5,9},{9,13},{2,6},{6,10},{10,14},{3,7},{... | collective-permute-start | bytes 196616 | tf_op jit(solution)/shard_map/ppermute | solution.py:56
  79.6 0.6 convolution_add_fusion.5
  80.2 1.3 %collective-permute-start.23 = (f32[1,128,128]{2,1,0:T(8,128)S(1)}, f32[1,128,128]{2,1,0:T(8,128)S(1)}, u32[]{:S(2)}, u32[]{:S(2)}) collective-permute-start(f32[1,128,128]{2,1,0:T(8,128)S(1)} %get-tuple-element.16), channel_id=1, source_target_pairs={{4,0},{8,4},{12,8},{5,1},{9,5},{13,9},{6,2},{10,6},{14,10},{7,3},{... | collective-permute-start | bytes 196616 | tf_op jit(solution)/shard_map/ppermute | solution.py:56
  81.5 1.3 %collective-permute-start.22 = (f32[1,128,128]{2,1,0:T(8,128)S(1)}, f32[1,128,128]{2,1,0:T(8,128)S(1)}, u32[]{:S(2)}, u32[]{:S(2)}) collective-permute-start(f32[1,128,128]{2,1,0:T(8,128)S(1)} %get-tuple-element.17), channel_id=1, source_target_pairs={{4,0},{8,4},{12,8},{5,1},{9,5},{13,9},{6,2},{10,6},{14,10},{7,3},{... | collective-permute-start | bytes 196616 | tf_op jit(solution)/shard_map/ppermute | solution.py:56
  82.8 1.3 %collective-permute-start.21 = (f32[1,128,128]{2,1,0:T(8,128)S(1)}, f32[1,128,128]{2,1,0:T(8,128)S(1)}, u32[]{:S(2)}, u32[]{:S(2)}) collective-permute-start(f32[1,128,128]{2,1,0:T(8,128)S(1)} %get-tuple-element.18), channel_id=1, source_target_pairs={{4,0},{8,4},{12,8},{5,1},{9,5},{13,9},{6,2},{10,6},{14,10},{7,3},{... | collective-permute-start | bytes 196616 | tf_op jit(solution)/shard_map/ppermute | solution.py:56
  84.2 1.5 %collective-permute-start.20 = (f32[1,128,128]{2,1,0:T(8,128)S(1)}, f32[1,128,128]{2,1,0:T(8,128)S(1)}, u32[]{:S(2)}, u32[]{:S(2)}) collective-permute-start(f32[1,128,128]{2,1,0:T(8,128)S(1)} %get-tuple-element.19), channel_id=1, source_target_pairs={{4,0},{8,4},{12,8},{5,1},{9,5},{13,9},{6,2},{10,6},{14,10},{7,3},{... | collective-permute-start | bytes 196616 | tf_op jit(solution)/shard_map/ppermute | solution.py:56
  85.7 0.6 convolution_subtract_fusion.1
  87.1 0.8 copy.37
  87.9 4.3 %collective-permute-done.20 = f32[1,128,128]{2,1,0:T(8,128)S(1)} collective-permute-done((f32[1,128,128]{2,1,0:T(8,128)S(1)}, f32[1,128,128]{2,1,0:T(8,128)S(1)}, u32[]{:S(2)}, u32[]{:S(2)}) %collective-permute-start.20) | collective-permute-done | bytes 65568 | tf_op jit(solution)/shard_map/ppermute | solution.py:56
  92.3 0.6 fusion.8
  92.9 1.5 %fusion.110 = (bf16[4,256,128]{2,1,0:T(8,128)(2,1)S(1)}, f32[4,256,128]{2,1,0:T(8,128)S(1)}) fusion(f32[4,256,128]{2,1,0:T(8,128)S(1)} %fusion.8, f32[4,1,128,128]{3,2,0,1:T(8,128)S(1)} %get-tuple-element.9, f32[4,1,128,128]{3,2,0,1:T(8,128)S(1)} %get-tuple-element.8, f32[4,1,128,128]{3,2,0,1:T(8,128)S(1)} %fusion.12), kind=kOutput, calls=%fused_computation.183 | convolution fusion | flops 403832832 | bytes 2097152 | tf_op jit(solution)/shard_map/hij,hiw->hjw/dot_general | solution.py:11
  94.4 1.0 copy.85
  95.9 1.1 %fusion.28 = f32[4,256,128]{2,1,0:T(8,128)S(1)} fusion(f32[4,128,256]{2,1,0:T(8,128)S(1)} %fusion.2, f32[4,128]{1,0:T(4,128)S(1)} %get-tuple-element.41, bf16[128,4,128]{2,1,0:T(4,128)(2,1)S(1)} %copy-done.1), kind=kOutput, calls=%fused_computation.66 | convolution fusion | flops 201457664 | bytes 1181696 | tf_op jit(solution)/shard_map/hij,hid->hjd/dot_general | solution.py:11
  97.0 0.7 fusion.32
  97.8 0.6 fusion.9
  98.6 0.8 copy.38
  99.3 1.0 fusion.1
  100.4 1.1 fusion.115
  101.4 0.6 fusion.7
  102.1 1.9 %convolution_add_fusion.3 = f32[4,256,128]{2,1,0:T(8,128)S(1)} fusion(f32[4,256,128]{2,1,0:T(8,128)S(1)} %fusion.7, f32[4,256,256]{2,1,0:T(8,128)S(1)} %fusion.1, f32[4,256,128]{2,1,0:T(8,128)S(1)} %broadcast_multiply_fusion), kind=kOutput, calls=%fused_computation.6 | convolution fusion | flops 402784256 | bytes 2621440 | tf_op jit(solution)/shard_map/hji,hjd->hid/dot_general | solution.py:11
  103.9 1.8 %fusion.11 = bf16[4,256,128]{2,1,0:T(8,128)(2,1)S(1)} fusion(f32[4,256,128]{2,1,0:T(8,128)S(1)} %convolution_add_fusion.3, f32[4,256,128]{2,1,0:T(8,128)S(1)} %broadcast_multiply_fusion, f32[4,256]{1,0:T(4,128)S(1)} %add_rsqrt_fusion), kind=kOutput, calls=%fused_computation.23 | output fusion | flops 656511 | bytes 1314816 | tf_op jit(solution)/shard_map/mul | solution.py:145
  105.7 1.0 copy.86
  (74 shorter events, 6.7 us)
Async XLA Ops:
  0.6 31.6 %copy-start = (bf16[128,4,128]{2,1,0:T(4,128)(2,1)S(1)}, bf16[128,4,128]{2,1,0:T(4,128)(2,1)}, u32[]{:S(2)}) copy-start(bf16[128,4,128]{2,1,0:T(4,128)(2,1)} %param.7) | copy-start | bytes 393220
  13.0 1.0 copy-start.2
  15.7 20.6 %collective-permute-start = (f32[1,128,128]{2,1,0:T(8,128)S(1)}, f32[1,128,128]{2,1,0:T(8,128)S(1)}, u32[]{:S(2)}, u32[]{:S(2)}) collective-permute-start(f32[1,128,128]{2,1,0:T(8,128)S(1)} %get-tuple-element.36), channel_id=1, source_target_pairs={{0,4},{4,8},{8,12},{1,5},{5,9},{9,13},{2,6},{6,10},{10,14},{3,7},{... | collective-permute-start | bytes 196616 | tf_op jit(solution)/shard_map/ppermute | solution.py:56
  20.7 17.0 %collective-permute-start.3 = (f32[1,128,128]{2,1,0:T(8,128)S(1)}, f32[1,128,128]{2,1,0:T(8,128)S(1)}, u32[]{:S(2)}, u32[]{:S(2)}) collective-permute-start(f32[1,128,128]{2,1,0:T(8,128)S(1)} %get-tuple-element.37), channel_id=1, source_target_pairs={{0,4},{4,8},{8,12},{1,5},{5,9},{9,13},{2,6},{6,10},{10,14},{3,7},{... | collective-permute-start | bytes 196616 | tf_op jit(solution)/shard_map/ppermute | solution.py:56
  24.2 14.8 %collective-permute-start.2 = (f32[1,128,128]{2,1,0:T(8,128)S(1)}, f32[1,128,128]{2,1,0:T(8,128)S(1)}, u32[]{:S(2)}, u32[]{:S(2)}) collective-permute-start(f32[1,128,128]{2,1,0:T(8,128)S(1)} %get-tuple-element.38), channel_id=1, source_target_pairs={{0,4},{4,8},{8,12},{1,5},{5,9},{9,13},{2,6},{6,10},{10,14},{3,7},{... | collective-permute-start | bytes 196616 | tf_op jit(solution)/shard_map/ppermute | solution.py:56
  27.7 12.6 %collective-permute-start.1 = (f32[1,128,128]{2,1,0:T(8,128)S(1)}, f32[1,128,128]{2,1,0:T(8,128)S(1)}, u32[]{:S(2)}, u32[]{:S(2)}) collective-permute-start(f32[1,128,128]{2,1,0:T(8,128)S(1)} %get-tuple-element.39), channel_id=1, source_target_pairs={{0,4},{4,8},{8,12},{1,5},{5,9},{9,13},{2,6},{6,10},{10,14},{3,7},{... | collective-permute-start | bytes 196616 | tf_op jit(solution)/shard_map/ppermute | solution.py:56
  29.6 1.0 copy-start.1
  32.7 14.5 %collective-permute-start.12 = (f32[1,128,128]{2,1,0:T(8,128)S(1)}, f32[1,128,128]{2,1,0:T(8,128)S(1)}, u32[]{:S(2)}, u32[]{:S(2)}) collective-permute-start(f32[1,128,128]{2,1,0:T(8,128)S(1)} %get-tuple-element.24), channel_id=1, source_target_pairs={{4,0},{8,4},{12,8},{5,1},{9,5},{13,9},{6,2},{10,6},{14,10},{7,3},{... | collective-permute-start | bytes 196616 | tf_op jit(solution)/shard_map/ppermute | solution.py:56
  36.3 14.7 %collective-permute-start.15 = (f32[1,128,128]{2,1,0:T(8,128)S(1)}, f32[1,128,128]{2,1,0:T(8,128)S(1)}, u32[]{:S(2)}, u32[]{:S(2)}) collective-permute-start(f32[1,128,128]{2,1,0:T(8,128)S(1)} %get-tuple-element.25), channel_id=1, source_target_pairs={{4,0},{8,4},{12,8},{5,1},{9,5},{13,9},{6,2},{10,6},{14,10},{7,3},{... | collective-permute-start | bytes 196616 | tf_op jit(solution)/shard_map/ppermute | solution.py:56
  37.7 17.4 %collective-permute-start.14 = (f32[1,128,128]{2,1,0:T(8,128)S(1)}, f32[1,128,128]{2,1,0:T(8,128)S(1)}, u32[]{:S(2)}, u32[]{:S(2)}) collective-permute-start(f32[1,128,128]{2,1,0:T(8,128)S(1)} %get-tuple-element.26), channel_id=1, source_target_pairs={{4,0},{8,4},{12,8},{5,1},{9,5},{13,9},{6,2},{10,6},{14,10},{7,3},{... | collective-permute-start | bytes 196616 | tf_op jit(solution)/shard_map/ppermute | solution.py:56
  39.0 18.0 %collective-permute-start.13 = (f32[1,128,128]{2,1,0:T(8,128)S(1)}, f32[1,128,128]{2,1,0:T(8,128)S(1)}, u32[]{:S(2)}, u32[]{:S(2)}) collective-permute-start(f32[1,128,128]{2,1,0:T(8,128)S(1)} %get-tuple-element.27), channel_id=1, source_target_pairs={{4,0},{8,4},{12,8},{5,1},{9,5},{13,9},{6,2},{10,6},{14,10},{7,3},{... | collective-permute-start | bytes 196616 | tf_op jit(solution)/shard_map/ppermute | solution.py:56
  40.7 18.2 %collective-permute-start.4 = (f32[1,128,128]{2,1,0:T(8,128)S(1)}, f32[1,128,128]{2,1,0:T(8,128)S(1)}, u32[]{:S(2)}, u32[]{:S(2)}) collective-permute-start(f32[1,128,128]{2,1,0:T(8,128)S(1)} %get-tuple-element.32), channel_id=1, source_target_pairs={{0,4},{4,8},{8,12},{1,5},{5,9},{9,13},{2,6},{6,10},{10,14},{3,7},{... | collective-permute-start | bytes 196616 | tf_op jit(solution)/shard_map/ppermute | solution.py:56
  47.2 13.1 %collective-permute-start.7 = (f32[1,128,128]{2,1,0:T(8,128)S(1)}, f32[1,128,128]{2,1,0:T(8,128)S(1)}, u32[]{:S(2)}, u32[]{:S(2)}) collective-permute-start(f32[1,128,128]{2,1,0:T(8,128)S(1)} %get-tuple-element.33), channel_id=1, source_target_pairs={{0,4},{4,8},{8,12},{1,5},{5,9},{9,13},{2,6},{6,10},{10,14},{3,7},{... | collective-permute-start | bytes 196616 | tf_op jit(solution)/shard_map/ppermute | solution.py:56
  51.1 10.4 %collective-permute-start.6 = (f32[1,128,128]{2,1,0:T(8,128)S(1)}, f32[1,128,128]{2,1,0:T(8,128)S(1)}, u32[]{:S(2)}, u32[]{:S(2)}) collective-permute-start(f32[1,128,128]{2,1,0:T(8,128)S(1)} %get-tuple-element.34), channel_id=1, source_target_pairs={{0,4},{4,8},{8,12},{1,5},{5,9},{9,13},{2,6},{6,10},{10,14},{3,7},{... | collective-permute-start | bytes 196616 | tf_op jit(solution)/shard_map/ppermute | solution.py:56
  55.0 7.8 %collective-permute-start.5 = (f32[1,128,128]{2,1,0:T(8,128)S(1)}, f32[1,128,128]{2,1,0:T(8,128)S(1)}, u32[]{:S(2)}, u32[]{:S(2)}) collective-permute-start(f32[1,128,128]{2,1,0:T(8,128)S(1)} %get-tuple-element.35), channel_id=1, source_target_pairs={{0,4},{4,8},{8,12},{1,5},{5,9},{9,13},{2,6},{6,10},{10,14},{3,7},{... | collective-permute-start | bytes 196616 | tf_op jit(solution)/shard_map/ppermute | solution.py:56
  57.6 12.1 %collective-permute-start.16 = (f32[1,128,128]{2,1,0:T(8,128)S(1)}, f32[1,128,128]{2,1,0:T(8,128)S(1)}, u32[]{:S(2)}, u32[]{:S(2)}) collective-permute-start(f32[1,128,128]{2,1,0:T(8,128)S(1)} %get-tuple-element.20), channel_id=1, source_target_pairs={{4,0},{8,4},{12,8},{5,1},{9,5},{13,9},{6,2},{10,6},{14,10},{7,3},{... | collective-permute-start | bytes 196616 | tf_op jit(solution)/shard_map/ppermute | solution.py:56
  58.9 14.7 %collective-permute-start.19 = (f32[1,128,128]{2,1,0:T(8,128)S(1)}, f32[1,128,128]{2,1,0:T(8,128)S(1)}, u32[]{:S(2)}, u32[]{:S(2)}) collective-permute-start(f32[1,128,128]{2,1,0:T(8,128)S(1)} %get-tuple-element.21), channel_id=1, source_target_pairs={{4,0},{8,4},{12,8},{5,1},{9,5},{13,9},{6,2},{10,6},{14,10},{7,3},{... | collective-permute-start | bytes 196616 | tf_op jit(solution)/shard_map/ppermute | solution.py:56
  60.2 17.4 %collective-permute-start.18 = (f32[1,128,128]{2,1,0:T(8,128)S(1)}, f32[1,128,128]{2,1,0:T(8,128)S(1)}, u32[]{:S(2)}, u32[]{:S(2)}) collective-permute-start(f32[1,128,128]{2,1,0:T(8,128)S(1)} %get-tuple-element.22), channel_id=1, source_target_pairs={{4,0},{8,4},{12,8},{5,1},{9,5},{13,9},{6,2},{10,6},{14,10},{7,3},{... | collective-permute-start | bytes 196616 | tf_op jit(solution)/shard_map/ppermute | solution.py:56
  61.5 18.0 %collective-permute-start.17 = (f32[1,128,128]{2,1,0:T(8,128)S(1)}, f32[1,128,128]{2,1,0:T(8,128)S(1)}, u32[]{:S(2)}, u32[]{:S(2)}) collective-permute-start(f32[1,128,128]{2,1,0:T(8,128)S(1)} %get-tuple-element.23), channel_id=1, source_target_pairs={{4,0},{8,4},{12,8},{5,1},{9,5},{13,9},{6,2},{10,6},{14,10},{7,3},{... | collective-permute-start | bytes 196616 | tf_op jit(solution)/shard_map/ppermute | solution.py:56
  63.3 22.4 %collective-permute-start.11 = (f32[1,128,128]{2,1,0:T(8,128)S(1)}, f32[1,128,128]{2,1,0:T(8,128)S(1)}, u32[]{:S(2)}, u32[]{:S(2)}) collective-permute-start(f32[1,128,128]{2,1,0:T(8,128)S(1)} %get-tuple-element.28), channel_id=1, source_target_pairs={{0,4},{4,8},{8,12},{1,5},{5,9},{9,13},{2,6},{6,10},{10,14},{3,7},{... | collective-permute-start | bytes 196616 | tf_op jit(solution)/shard_map/ppermute | solution.py:56
  69.7 14.4 %collective-permute-start.10 = (f32[1,128,128]{2,1,0:T(8,128)S(1)}, f32[1,128,128]{2,1,0:T(8,128)S(1)}, u32[]{:S(2)}, u32[]{:S(2)}) collective-permute-start(f32[1,128,128]{2,1,0:T(8,128)S(1)} %get-tuple-element.29), channel_id=1, source_target_pairs={{0,4},{4,8},{8,12},{1,5},{5,9},{9,13},{2,6},{6,10},{10,14},{3,7},{... | collective-permute-start | bytes 196616 | tf_op jit(solution)/shard_map/ppermute | solution.py:56
  73.7 9.1 %collective-permute-start.9 = (f32[1,128,128]{2,1,0:T(8,128)S(1)}, f32[1,128,128]{2,1,0:T(8,128)S(1)}, u32[]{:S(2)}, u32[]{:S(2)}) collective-permute-start(f32[1,128,128]{2,1,0:T(8,128)S(1)} %get-tuple-element.30), channel_id=1, source_target_pairs={{0,4},{4,8},{8,12},{1,5},{5,9},{9,13},{2,6},{6,10},{10,14},{3,7},{... | collective-permute-start | bytes 196616 | tf_op jit(solution)/shard_map/ppermute | solution.py:56
  77.6 3.9 %collective-permute-start.8 = (f32[1,128,128]{2,1,0:T(8,128)S(1)}, f32[1,128,128]{2,1,0:T(8,128)S(1)}, u32[]{:S(2)}, u32[]{:S(2)}) collective-permute-start(f32[1,128,128]{2,1,0:T(8,128)S(1)} %get-tuple-element.31), channel_id=1, source_target_pairs={{0,4},{4,8},{8,12},{1,5},{5,9},{9,13},{2,6},{6,10},{10,14},{3,7},{... | collective-permute-start | bytes 196616 | tf_op jit(solution)/shard_map/ppermute | solution.py:56
  80.2 12.1 %collective-permute-start.23 = (f32[1,128,128]{2,1,0:T(8,128)S(1)}, f32[1,128,128]{2,1,0:T(8,128)S(1)}, u32[]{:S(2)}, u32[]{:S(2)}) collective-permute-start(f32[1,128,128]{2,1,0:T(8,128)S(1)} %get-tuple-element.16), channel_id=1, source_target_pairs={{4,0},{8,4},{12,8},{5,1},{9,5},{13,9},{6,2},{10,6},{14,10},{7,3},{... | collective-permute-start | bytes 196616 | tf_op jit(solution)/shard_map/ppermute | solution.py:56
  81.5 10.7 %collective-permute-start.22 = (f32[1,128,128]{2,1,0:T(8,128)S(1)}, f32[1,128,128]{2,1,0:T(8,128)S(1)}, u32[]{:S(2)}, u32[]{:S(2)}) collective-permute-start(f32[1,128,128]{2,1,0:T(8,128)S(1)} %get-tuple-element.17), channel_id=1, source_target_pairs={{4,0},{8,4},{12,8},{5,1},{9,5},{13,9},{6,2},{10,6},{14,10},{7,3},{... | collective-permute-start | bytes 196616 | tf_op jit(solution)/shard_map/ppermute | solution.py:56
  82.8 9.4 %collective-permute-start.21 = (f32[1,128,128]{2,1,0:T(8,128)S(1)}, f32[1,128,128]{2,1,0:T(8,128)S(1)}, u32[]{:S(2)}, u32[]{:S(2)}) collective-permute-start(f32[1,128,128]{2,1,0:T(8,128)S(1)} %get-tuple-element.18), channel_id=1, source_target_pairs={{4,0},{8,4},{12,8},{5,1},{9,5},{13,9},{6,2},{10,6},{14,10},{7,3},{... | collective-permute-start | bytes 196616 | tf_op jit(solution)/shard_map/ppermute | solution.py:56
  84.2 8.0 %collective-permute-start.20 = (f32[1,128,128]{2,1,0:T(8,128)S(1)}, f32[1,128,128]{2,1,0:T(8,128)S(1)}, u32[]{:S(2)}, u32[]{:S(2)}) collective-permute-start(f32[1,128,128]{2,1,0:T(8,128)S(1)} %get-tuple-element.19), channel_id=1, source_target_pairs={{4,0},{8,4},{12,8},{5,1},{9,5},{13,9},{6,2},{10,6},{14,10},{7,3},{... | collective-permute-start | bytes 196616 | tf_op jit(solution)/shard_map/ppermute | solution.py:56

commit v7 on v1

--- a/solution.py
+++ b/solution.py
@@ -9,6 +9,10 @@
 
 def mm(spec, *operands):
     return jnp.einsum(spec, *operands, precision=highest)
+
+
+def mh(spec, *operands):
+    return jnp.einsum(spec, *operands, precision=lax.Precision.HIGH)
 
 
 def unit_rows(tensor):
@@ -106,34 +110,34 @@
     kn, k_scale = unit_rows(k_raw)
 
     inverse = tri_inverse(kn)
-    proj = mm("hij,hjd->hid", inverse, kn)
-    upd_v = mm("hij,hjd->hid", inverse, vals)
+    proj = mh("hij,hjd->hid", inverse, kn)
+    upd_v = mh("hij,hjd->hid", inverse, vals)
     tok_ids = lax.broadcasted_iota(jnp.int32, (tok_count, rows), 0)
     sub_ids = lax.broadcasted_iota(jnp.int32, (tok_count, rows), 1)
     visible = sub_ids <= 2 * tok_ids + 1
-    scores = jnp.where(visible, 2.0 * mm("hid,hjd->hij", qn, kn), 0.0)
-    read_map = qn - mm("hij,hjd->hid", scores, proj)
-    own_out = mm("hij,hjd->hid", scores, upd_v)
+    scores = jnp.where(visible, 2.0 * mh("hid,hjd->hij", qn, kn), 0.0)
+    read_map = qn - mh("hij,hjd->hid", scores, proj)
+    own_out = mh("hij,hjd->hid", scores, upd_v)
     eye = jnp.eye(head_size, dtype=jnp.float32)
-    transition = eye - 2.0 * mm("hjd,hjw->hdw", kn, proj)
-    offset = 2.0 * mm("hjd,hjw->hdw", kn, upd_v)
-    local_cot = mm("hld,hlw->hdw", read_map, cot)
+    transition = eye - 2.0 * mh("hjd,hjw->hdw", kn, proj)
+    offset = 2.0 * mh("hjd,hjw->hdw", kn, upd_v)
+    local_cot = mh("hld,hlw->hdw", read_map, cot)
 
     state_in, end_cot = scan_seq(transition, offset, local_cot)
 
-    produced = mm("hld,hdw->hlw", read_map, state_in) + own_out
-    updates = upd_v - mm("hjd,hdw->hjw", proj, state_in)
-    d_upd = mm("hij,hiw->hjw", scores, cot) + 2.0 * mm("hjd,hdw->hjw", kn, end_cot)
-    d_w = mm("hij,hiw->hjw", inverse, d_upd)
-    touch = jnp.where(visible, mm("hiw,hjw->hij", cot, updates), 0.0)
-    d_qn = mm("hiw,hdw->hid", cot, state_in) + 2.0 * mm("hij,hjd->hid", touch, kn)
-    gram_cot = jnp.where(strict_lower(rows, rows), -2.0 * mm("hiw,hjw->hij", d_w, updates), 0.0)
+    produced = mh("hld,hdw->hlw", read_map, state_in) + own_out
+    updates = upd_v - mh("hjd,hdw->hjw", proj, state_in)
+    d_upd = mh("hij,hiw->hjw", scores, cot) + 2.0 * mh("hjd,hdw->hjw", kn, end_cot)
+    d_w = mh("hij,hiw->hjw", inverse, d_upd)
+    touch = jnp.where(visible, mh("hiw,hjw->hij", cot, updates), 0.0)
+    d_qn = mh("hiw,hdw->hid", cot, state_in) + 2.0 * mh("hij,hjd->hid", touch, kn)
+    gram_cot = jnp.where(strict_lower(rows, rows), -2.0 * mh("hiw,hjw->hij", d_w, updates), 0.0)
     d_kn = (
-        2.0 * mm("hij,hid->hjd", touch, qn)
-        + 2.0 * mm("hjw,hdw->hjd", updates, end_cot)
-        - mm("hjw,hdw->hjd", d_w, state_in)
-        + mm("hij,hjd->hid", gram_cot, kn)
-        + mm("hji,hjd->hid", gram_cot, kn)
+        2.0 * mh("hij,hid->hjd", touch, qn)
+        + 2.0 * mh("hjw,hdw->hjd", updates, end_cot)
+        - mh("hjw,hdw->hjd", d_w, state_in)
+        + mh("hij,hjd->hid", gram_cot, kn)
+        + mh("hji,hjd->hid", gram_cot, kn)
     )
     d_q = q_scale * (d_qn - jnp.sum(qn * d_qn, axis=-1, keepdims=True) * qn)
     d_k = k_scale * (d_kn - jnp.sum(kn * d_kn, axis=-1, keepdims=True) * kn)

time: 63 us -> 58.7 us (0.932)
  matrix products: 30.3 us -> 23.5 us
  waiting for transfers between devices: 4.92 us -> 7.43 us
    dot_general x45 -> x23, matrix products: 30.3 us -> 12.6 us  [mm(): return jnp.einsum(spec, *operands, precision=highest)]
    dot_general x0 -> x22, matrix products: none -> 10.9 us  [mh(): return jnp.einsum(spec, *operands, precision=lax.Precision.HIGH)]
    ppermute x3, waiting for transfers between devices: 2.81 us -> 5.33 us  [chain_seq(): got_cot = lax.ppermute(bwd_sum, 'seq', left)]
  transfers between devices with their start and end apart: 6 -> 6, of which waited for: 5 -> 6; matrix products, arithmetic and copies ran while one was open for 20% -> 16% of each run, Pallas kernels for 0% -> 0%
where the time goes in v7:
time: 58.7 us; the launch traced here: 58.4 us
  matrix products  23.5 us (40%)
  starting transfers between devices  17.8 us (30%)
  waiting for transfers between devices  7.43 us (13%)
  local copies, waits for them, and re-layouts  5.45 us (9%)
  other arithmetic  3.12 us (5%)
  between operations  1.15 us (2%)
    ppermute x3, starting transfers between devices, chain_seq(): got_sum = lax.ppermute(fwd_sum, 'seq', right)  13.9 us
    dot_general x23, matrix products, mm(): return jnp.einsum(spec, *operands, precision=highest)  12.6 us
    dot_general x22, matrix products, mh(): return jnp.einsum(spec, *operands, precision=lax.Precision.HIGH)  10.9 us
    ppermute x3, waiting for transfers between devices, chain_seq(): got_cot = lax.ppermute(bwd_sum, 'seq', left)  5.33 us
    ppermute x3, starting transfers between devices, chain_seq(): got_cot = lax.ppermute(bwd_sum, 'seq', left)  3.88 us
    ppermute x3, waiting for transfers between devices, chain_seq(): got_sum = lax.ppermute(fwd_sum, 'seq', right)  2.1 us
    convert_element_type x2, local copies, waits for them, and re-layouts, pair_major(): return tensor.reshape(heads_here, tok_count, 2, head_size).transpose(1, 2...  2.09 us
    unnamed x8, local copies, waits for them, and re-layouts  2.02 us
  transfers between devices with their start and end apart: 6, of which 6 were waited for; matrix products, arithmetic and copies ran while one was open for 16% of the time, Pallas kernels for 0%

profile of v7, /device:TPU:0, one launch (start us, length us, event | category | flops | bytes accessed | tf_op | source)
XLA Modules:
  0.0 58.4 jit_solution(18054667563364053368)
XLA Ops:
  0.7 1.2 %copy.9 = f32[128,2,4,128]{3,1,0,2:T(2,128)S(1)} copy(bf16[128,2,4,128]{3,2,1,0:T(4,128)(2,1)} %param.5) | data formatting | bytes 786432 | tf_op jit(solution)/shard_map/transpose | solution.py:107
  2.3 0.9 %fusion.3 = f32[4,16,16,16]{3,2,1,0:T(8,128)S(1)} fusion(f32[4,16,16,128]{3,2,1,0:T(8,128)S(1)} %bitcast.204, pred[16,16]{1,0:T(8,128)(4,1)S(1)} %iota_compare_fusion.7), kind=kOutput, calls=%fused_computation.10 | convolution fusion | flops 25198592 | bytes 590080 | tf_op jit(solution)/shard_map/hpid,hpjd->hpij/dot_general | solution.py:11
  3.2 0.6 %fusion.73 = f32[4,16,16,16]{3,2,1,0:T(8,128)S(1)} fusion(f32[4,16,16,16]{3,2,1,0:T(8,128)S(1)} %fusion.3), kind=kOutput, calls=%fused_computation.138 | convolution fusion | flops 3145728 | bytes 131072 | tf_op jit(solution)/shard_map/hpij,hpjk->hpik/dot_general | solution.py:11
  3.9 0.6 %fusion.74 = f32[4,16,16,16]{3,2,1,0:T(8,128)S(1)} fusion(f32[4,16,16,16]{3,2,1,0:T(8,128)S(1)} %fusion.73), kind=kOutput, calls=%fused_computation.139 | convolution fusion | flops 3145728 | bytes 131072 | tf_op jit(solution)/shard_map/hpij,hpjk->hpik/dot_general | solution.py:11
  4.5 0.7 %convolution_add_fusion.2 = f32[4,16,16,16]{3,2,1,0:T(8,128)S(1)} fusion(f32[4,16,16,16]{3,2,1,0:T(8,128)S(1)} %fusion.73, f32[4,16,16,16]{3,2,1,0:T(8,128)S(1)} %fusion.3, f32[16,16]{1,0:T(8,128)S(1)} %fusion.58), kind=kOutput, calls=%fused_computation.5 | convolution fusion | flops 3178496 | bytes 197632 | tf_op jit(solution)/shard_map/hpij,hpjk->hpik/dot_general | solution.py:11
  5.2 0.6 %fusion.75 = f32[4,16,16,16]{3,2,1,0:T(8,128)S(1)} fusion(f32[4,16,16,16]{3,2,1,0:T(8,128)S(1)} %fusion.74), kind=kOutput, calls=%fused_computation.140 | convolution fusion | flops 3145728 | bytes 131072 | tf_op jit(solution)/shard_map/hpij,hpjk->hpik/dot_general | solution.py:11
  5.8 0.6 %convolution_add_fusion.1 = f32[4,16,16,16]{3,2,1,0:T(8,128)S(1)} fusion(f32[4,16,16,16]{3,2,1,0:T(8,128)S(1)} %convolution_add_fusion.2, f32[4,16,16,16]{3,2,1,0:T(8,128)S(1)} %fusion.74), kind=kOutput, calls=%fused_computation.4 | convolution fusion | flops 3162112 | bytes 196608 | tf_op jit(solution)/shard_map/hpij,hpjk->hpik/dot_general | solution.py:11
  6.5 0.6 %convolution_add_fusion = f32[4,16,16,16]{3,2,1,0:T(8,128)S(1)} fusion(f32[4,16,16,16]{3,2,1,0:T(8,128)S(1)} %convolution_add_fusion.1, f32[4,16,16,16]{3,2,1,0:T(8,128)S(1)} %fusion.75), kind=kOutput, calls=%fused_computation.3 | convolution fusion | flops 3162112 | bytes 196608 | tf_op jit(solution)/shard_map/hpij,hpjk->hpik/dot_general | solution.py:11
  7.2 0.5 convolution_multiply_fusion.7
  7.7 0.4 fusion.69
  8.1 0.4 convolution_negate_fusion.3
  8.7 0.5 convolution_multiply_fusion.6
  9.2 0.4 fusion.70
  9.6 0.4 convolution_negate_fusion.2
  10.2 0.5 convolution_multiply_fusion.5
  10.7 0.4 fusion.71
  11.1 0.4 convolution_negate_fusion.1
  11.7 0.7 %convolution_multiply_fusion.4 = f32[4,128,128]{2,1,0:T(8,128)S(1)} fusion(f32[4,1,2,128,128]{4,3,2,0,1:T(8,128)S(1)} %bitcast.208), kind=kOutput, calls=%fused_computation.31 | convolution fusion | flops 100728832 | bytes 786432 | tf_op jit(solution)/shard_map/hpid,hpjd->hpij/dot_general | solution.py:11
  12.4 0.6 %fusion.38 = f32[4,128,128]{1,2,0:T(8,128)S(1)} fusion(f32[4,128,128]{2,1,0:T(8,128)S(1)} %convolution_multiply_fusion.4, f32[4,1,2,128,128]{4,3,2,0,1:T(8,128)S(1)} %fusion.17), kind=kOutput, calls=%fused_computation.88 | convolution fusion | flops 100663296 | bytes 786432 | tf_op jit(solution)/shard_map/hpij,hpjk->hpik/dot_general | solution.py:11
  13.0 0.7 %fusion.12 = f32[4,1,128,128]{3,2,0,1:T(8,128)S(1)} fusion(f32[4,128,128]{1,2,0:T(8,128)S(1)} %fusion.38, f32[4,1,2,128,128]{4,3,2,0,1:T(8,128)S(1)} %fusion.17), kind=kOutput, calls=%fused_computation.30 | convolution fusion | flops 100728832 | bytes 786432 | tf_op jit(solution)/shard_map/hpij,hpjk->hpik/dot_general | solution.py:11
  13.6 0.3 copy-done.2
  13.9 0.4 fusion.22
  14.4 0.6 %convolution_multiply_fusion.9 = f32[4,128,128]{2,1,0:T(8,128)S(1)} fusion(f32[4,256,128]{2,1,0:T(8,128)S(1)} %broadcast_multiply_fusion, f32[4,256,128]{2,1,0:T(8,128)S(1)} %fusion.22), kind=kOutput, calls=%fused_computation.39 | convolution fusion | flops 100728832 | bytes 1310720 | tf_op jit(solution)/shard_map/hjd,hjw->hdw/dot_general | solution.py:15
  15.0 5.1 %collective-permute-start = (f32[4,128,128]{2,1,0:T(8,128)S(1)}, f32[4,128,128]{2,1,0:T(8,128)S(1)}, u32[]{:S(2)}, u32[]{:S(2)}) collective-permute-start(f32[4,128,128]{2,1,0:T(8,128)S(1)} %convolution_multiply_fusion.9), channel_id=1, source_target_pairs={{0,4},{4,8},{8,12},{1,5},{5,9},{9,13},{2,6},{6,10},{10,14},{3,7},{... | collective-permute-start | bytes 786440 | tf_op jit(solution)/shard_map/ppermute | solution.py:64
  20.2 0.6 fusion.24
  21.2 0.4 fusion.10
  21.7 0.4 convolution_subtract_fusion.2
  22.1 0.3 fusion.48
  22.4 1.3 %collective-permute-start.3 = (f32[4,128,128]{2,1,0:T(8,128)S(1)}, f32[4,128,128]{2,1,0:T(8,128)S(1)}, u32[]{:S(2)}, u32[]{:S(2)}) collective-permute-start(f32[4,128,128]{2,1,0:T(8,128)S(1)} %fusion.48), channel_id=1, source_target_pairs={{4,0},{8,4},{12,8},{5,1},{9,5},{13,9},{6,2},{10,6},{14,10},{7,3},{... | collective-permute-start | bytes 786440 | tf_op jit(solution)/shard_map/ppermute | solution.py:65
  23.7 0.4 fusion.76
  24.1 0.6 %fusion.13 = f32[4,128,128]{2,1,0:T(8,128)S(1)} fusion(f32[4,256,128]{2,1,0:T(8,128)S(1)} %broadcast_multiply_fusion, f32[4,256,128]{2,1,0:T(8,128)S(1)} %fusion.24, f32[128,128]{1,0:T(8,128)S(1)} %fusion.55), kind=kOutput, calls=%fused_computation.42 | convolution fusion | flops 100794368 | bytes 1376256 | tf_op jit(solution)/shard_map/hjd,hjw->hdw/dot_general | solution.py:15
  24.7 0.8 %collective-permute-done = f32[4,128,128]{2,1,0:T(8,128)S(1)} collective-permute-done((f32[4,128,128]{2,1,0:T(8,128)S(1)}, f32[4,128,128]{2,1,0:T(8,128)S(1)}, u32[]{:S(2)}, u32[]{:S(2)}) %collective-permute-start) | collective-permute-done | bytes 262176 | tf_op jit(solution)/shard_map/ppermute | solution.py:64
  25.5 0.4 convolution_add_fusion.9
  25.9 4.4 %collective-permute-start.1 = (f32[4,128,128]{2,1,0:T(8,128)S(1)}, f32[4,128,128]{2,1,0:T(8,128)S(1)}, u32[]{:S(2)}, u32[]{:S(2)}) collective-permute-start(f32[4,128,128]{2,1,0:T(8,128)S(1)} %convolution_add_fusion.9), channel_id=1, source_target_pairs={{0,4},{4,8},{8,12},{1,5},{5,9},{9,13},{2,6},{6,10},{10,14},{3,7},{... | collective-permute-start | bytes 786440 | tf_op jit(solution)/shard_map/ppermute | solution.py:64
  30.3 0.5 fusion.51
  30.8 1.3 %collective-permute-done.3 = f32[4,128,128]{2,1,0:T(8,128)S(1)} collective-permute-done((f32[4,128,128]{2,1,0:T(8,128)S(1)}, f32[4,128,128]{2,1,0:T(8,128)S(1)}, u32[]{:S(2)}, u32[]{:S(2)}) %collective-permute-start.3) | collective-permute-done | bytes 262176 | tf_op jit(solution)/shard_map/ppermute | solution.py:65
  32.0 0.6 %convolution_add_fusion.6 = f32[4,128,128]{2,1,0:T(8,128)S(1)} fusion(f32[4,128,128]{2,1,0:T(8,128)S(1)} %fusion.48, f32[4,128,128]{2,1,0:T(8,128)S(1)} %fusion.13, f32[4,128,128]{2,1,0:T(8,128)S(1)} %collective-permute-done.3), kind=kOutput, calls=%fused_computation.25 | convolution fusion | flops 100728832 | bytes 1048576 | tf_op jit(solution)/shard_map/hji,hjk->hik/dot_general | solution.py:11
  32.6 1.3 %collective-permute-start.4 = (f32[4,128,128]{2,1,0:T(8,128)S(1)}, f32[4,128,128]{2,1,0:T(8,128)S(1)}, u32[]{:S(2)}, u32[]{:S(2)}) collective-permute-start(f32[4,128,128]{2,1,0:T(8,128)S(1)} %convolution_add_fusion.6), channel_id=1, source_target_pairs={{4,0},{8,4},{12,8},{5,1},{9,5},{13,9},{6,2},{10,6},{14,10},{7,3},{... | collective-permute-start | bytes 786440 | tf_op jit(solution)/shard_map/ppermute | solution.py:65
  33.9 1.0 %collective-permute-done.1 = f32[4,128,128]{2,1,0:T(8,128)S(1)} collective-permute-done((f32[4,128,128]{2,1,0:T(8,128)S(1)}, f32[4,128,128]{2,1,0:T(8,128)S(1)}, u32[]{:S(2)}, u32[]{:S(2)}) %collective-permute-start.1) | collective-permute-done | bytes 262176 | tf_op jit(solution)/shard_map/ppermute | solution.py:64
  34.9 0.4 convolution_add_fusion.8
  35.3 4.4 %collective-permute-start.2 = (f32[4,128,128]{2,1,0:T(8,128)S(1)}, f32[4,128,128]{2,1,0:T(8,128)S(1)}, u32[]{:S(2)}, u32[]{:S(2)}) collective-permute-start(f32[4,128,128]{2,1,0:T(8,128)S(1)} %convolution_add_fusion.8), channel_id=1, source_target_pairs={{0,4},{4,8},{8,12},{1,5},{5,9},{9,13},{2,6},{6,10},{10,14},{3,7},{... | collective-permute-start | bytes 786440 | tf_op jit(solution)/shard_map/ppermute | solution.py:64
  39.8 1.6 %collective-permute-done.4 = f32[4,128,128]{2,1,0:T(8,128)S(1)} collective-permute-done((f32[4,128,128]{2,1,0:T(8,128)S(1)}, f32[4,128,128]{2,1,0:T(8,128)S(1)}, u32[]{:S(2)}, u32[]{:S(2)}) %collective-permute-start.4) | collective-permute-done | bytes 262176 | tf_op jit(solution)/shard_map/ppermute | solution.py:65
  41.4 0.6 %convolution_add_fusion.5 = f32[4,128,128]{2,1,0:T(8,128)S(1)} fusion(f32[4,128,128]{2,1,0:T(8,128)S(1)} %fusion.48, f32[4,128,128]{2,1,0:T(8,128)S(1)} %fusion.13, f32[4,128,128]{2,1,0:T(8,128)S(1)} %collective-permute-done.4), kind=kOutput, calls=%fused_computation.24 | convolution fusion | flops 100728832 | bytes 1048576 | tf_op jit(solution)/shard_map/hji,hjk->hik/dot_general | solution.py:11
  42.0 1.3 %collective-permute-start.5 = (f32[4,128,128]{2,1,0:T(8,128)S(1)}, f32[4,128,128]{2,1,0:T(8,128)S(1)}, u32[]{:S(2)}, u32[]{:S(2)}) collective-permute-start(f32[4,128,128]{2,1,0:T(8,128)S(1)} %convolution_add_fusion.5), channel_id=1, source_target_pairs={{4,0},{8,4},{12,8},{5,1},{9,5},{13,9},{6,2},{10,6},{14,10},{7,3},{... | collective-permute-start | bytes 786440 | tf_op jit(solution)/shard_map/ppermute | solution.py:65
  43.3 0.3 collective-permute-done.2
  43.6 0.4 convolution_subtract_fusion.1
  44.0 0.3 fusion.2
  44.3 0.3 fusion.53
  44.6 0.5 fusion.32
  45.1 0.3 fusion.15
  45.6 0.8 %copy.36 = bf16[128,4,128]{2,1,0:T(4,128)(2,1)} copy(bf16[128,4,128]{2,0,1:T(8,128)(2,1)S(1)} %fusion.15) | data formatting | bytes 262144
  46.3 0.8 %copy.37 = bf16[128,4,128]{2,1,0:T(4,128)(2,1)} copy(bf16[128,4,128]{2,0,1:T(8,128)(2,1)S(1)} %fusion.37) | data formatting | bytes 262144
  47.1 0.7 %fusion.28 = f32[4,256,128]{2,1,0:T(8,128)S(1)} fusion(f32[4,128,256]{2,1,0:T(8,128)S(1)} %fusion.2, f32[4,128]{1,0:T(4,128)S(1)} %get-tuple-element.17, bf16[128,4,128]{2,1,0:T(4,128)(2,1)S(1)} %copy-done.1), kind=kOutput, calls=%fused_computation.66 | convolution fusion | flops 100794368 | bytes 1181696 | tf_op jit(solution)/shard_map/hij,hid->hjd/dot_general | solution.py:15
  47.8 2.5 %collective-permute-done.5 = f32[4,128,128]{2,1,0:T(8,128)S(1)} collective-permute-done((f32[4,128,128]{2,1,0:T(8,128)S(1)}, f32[4,128,128]{2,1,0:T(8,128)S(1)}, u32[]{:S(2)}, u32[]{:S(2)}) %collective-permute-start.5) | collective-permute-done | bytes 262176 | tf_op jit(solution)/shard_map/ppermute | solution.py:65
  50.2 0.4 fusion.8
  50.6 0.9 %fusion.72 = (bf16[4,256,128]{2,1,0:T(8,128)(2,1)S(1)}, f32[4,256,128]{2,1,0:T(8,128)S(1)}) fusion(f32[4,256,128]{2,1,0:T(8,128)S(1)} %fusion.8, f32[4,1,128,128]{3,2,0,1:T(8,128)S(1)} %get-tuple-element.9, f32[4,1,128,128]{3,2,0,1:T(8,128)S(1)} %get-tuple-element.8, f32[4,1,128,128]{3,2,0,1:T(8,128)S(1)} %fusion.12), kind=kOutput, calls=%fused_computation.137 | convolution fusion | flops 202506240 | bytes 2097152 | tf_op jit(solution)/shard_map/hij,hiw->hjw/dot_general | solution.py:15
  51.5 0.6 %fusion.1 = f32[4,256,256]{2,1,0:T(8,128)S(1)} fusion(f32[4,256,128]{2,1,0:T(8,128)S(1)} %get-tuple-element.21, f32[4,256,128]{2,1,0:T(8,128)S(1)} %convolution_subtract_fusion.1, pred[256,256]{1,0:T(8,128)(4,1)S(1)} %iota_compare_fusion.4), kind=kOutput, calls=%fused_computation.2 | convolution fusion | flops 201850880 | bytes 2162688 | tf_op jit(solution)/shard_map/hiw,hjw->hij/dot_general | solution.py:15
  52.1 0.6 %fusion.77 = f32[4,256,128]{2,1,0:T(8,128)S(1)} fusion(f32[4,256,256]{2,1,0:T(8,128)S(1)} %fusion.1, f32[4,256,128]{2,1,0:T(8,128)S(1)} %broadcast_multiply_fusion), kind=kOutput, calls=%fused_computation.142 | convolution fusion | flops 201326592 | bytes 2097152 | tf_op jit(solution)/shard_map/hij,hjd->hid/dot_general | solution.py:15
  52.7 0.4 fusion.9
  53.1 0.4 fusion.7
  53.5 1.0 %convolution_add_fusion.3 = f32[4,256,128]{2,1,0:T(8,128)S(1)} fusion(f32[4,256,128]{2,1,0:T(8,128)S(1)} %fusion.7, f32[4,256,256]{2,1,0:T(8,128)S(1)} %fusion.1, f32[4,256,128]{2,1,0:T(8,128)S(1)} %broadcast_multiply_fusion), kind=kOutput, calls=%fused_computation.6 | convolution fusion | flops 201457664 | bytes 2621440 | tf_op jit(solution)/shard_map/hji,hjd->hid/dot_general | solution.py:15
  54.6 1.8 %fusion.11 = bf16[4,256,128]{2,1,0:T(8,128)(2,1)S(1)} fusion(f32[4,256,128]{2,1,0:T(8,128)S(1)} %convolution_add_fusion.3, f32[4,256,128]{2,1,0:T(8,128)S(1)} %broadcast_multiply_fusion, f32[4,256]{1,0:T(4,128)S(1)} %add_rsqrt_fusion), kind=kOutput, calls=%fused_computation.23 | output fusion | flops 656511 | bytes 1314816 | tf_op jit(solution)/shard_map/mul | solution.py:143
  56.3 1.0 %copy.84 = bf16[4,128,2,128]{3,0,2,1:T(4,128)(2,1)} copy(bf16[4,128,2,128]{3,2,1,0:T(2,128)(2,1)S(1)} %bitcast.220) | data formatting | bytes 524288 | tf_op jit(solution)/shard_map/convert_element_type | solution.py:152
  57.4 1.0 %copy.83 = bf16[4,128,2,128]{3,0,2,1:T(4,128)(2,1)} copy(bf16[4,128,2,128]{3,2,1,0:T(2,128)(2,1)S(1)} %bitcast.221) | data formatting | bytes 524288 | tf_op jit(solution)/shard_map/convert_element_type | solution.py:152
  (24 shorter events, 1.7 us)
Async XLA Ops:
  0.6 21.4 %copy-start = (bf16[128,4,128]{2,1,0:T(4,128)(2,1)S(1)}, bf16[128,4,128]{2,1,0:T(4,128)(2,1)}, u32[]{:S(2)}) copy-start(bf16[128,4,128]{2,1,0:T(4,128)(2,1)} %param.7) | copy-start | bytes 393220
  13.0 1.0 %copy-start.2 = (bf16[128,2,4,128]{3,2,1,0:T(4,128)(2,1)S(1)}, bf16[128,2,4,128]{3,2,1,0:T(4,128)(2,1)}, u32[]{:S(2)}) copy-start(bf16[128,2,4,128]{3,2,1,0:T(4,128)(2,1)} %param.6) | copy-start | bytes 786436
  15.0 10.5 %collective-permute-start = (f32[4,128,128]{2,1,0:T(8,128)S(1)}, f32[4,128,128]{2,1,0:T(8,128)S(1)}, u32[]{:S(2)}, u32[]{:S(2)}) collective-permute-start(f32[4,128,128]{2,1,0:T(8,128)S(1)} %convolution_multiply_fusion.9), channel_id=1, source_target_pairs={{0,4},{4,8},{8,12},{1,5},{5,9},{9,13},{2,6},{6,10},{10,14},{3,7},{... | collective-permute-start | bytes 786440 | tf_op jit(solution)/shard_map/ppermute | solution.py:64
  20.2 0.9 %copy-start.1 = (bf16[128,4,128]{2,1,0:T(4,128)(2,1)S(1)}, bf16[128,4,128]{2,1,0:T(4,128)(2,1)}, u32[]{:S(2)}) copy-start(bf16[128,4,128]{2,1,0:T(4,128)(2,1)} %param.4) | copy-start | bytes 393220
  22.4 9.7 %collective-permute-start.3 = (f32[4,128,128]{2,1,0:T(8,128)S(1)}, f32[4,128,128]{2,1,0:T(8,128)S(1)}, u32[]{:S(2)}, u32[]{:S(2)}) collective-permute-start(f32[4,128,128]{2,1,0:T(8,128)S(1)} %fusion.48), channel_id=1, source_target_pairs={{4,0},{8,4},{12,8},{5,1},{9,5},{13,9},{6,2},{10,6},{14,10},{7,3},{... | collective-permute-start | bytes 786440 | tf_op jit(solution)/shard_map/ppermute | solution.py:65
  25.9 9.1 %collective-permute-start.1 = (f32[4,128,128]{2,1,0:T(8,128)S(1)}, f32[4,128,128]{2,1,0:T(8,128)S(1)}, u32[]{:S(2)}, u32[]{:S(2)}) collective-permute-start(f32[4,128,128]{2,1,0:T(8,128)S(1)} %convolution_add_fusion.9), channel_id=1, source_target_pairs={{0,4},{4,8},{8,12},{1,5},{5,9},{9,13},{2,6},{6,10},{10,14},{3,7},{... | collective-permute-start | bytes 786440 | tf_op jit(solution)/shard_map/ppermute | solution.py:64
  32.6 8.7 %collective-permute-start.4 = (f32[4,128,128]{2,1,0:T(8,128)S(1)}, f32[4,128,128]{2,1,0:T(8,128)S(1)}, u32[]{:S(2)}, u32[]{:S(2)}) collective-permute-start(f32[4,128,128]{2,1,0:T(8,128)S(1)} %convolution_add_fusion.6), channel_id=1, source_target_pairs={{4,0},{8,4},{12,8},{5,1},{9,5},{13,9},{6,2},{10,6},{14,10},{7,3},{... | collective-permute-start | bytes 786440 | tf_op jit(solution)/shard_map/ppermute | solution.py:65
  35.3 8.3 %collective-permute-start.2 = (f32[4,128,128]{2,1,0:T(8,128)S(1)}, f32[4,128,128]{2,1,0:T(8,128)S(1)}, u32[]{:S(2)}, u32[]{:S(2)}) collective-permute-start(f32[4,128,128]{2,1,0:T(8,128)S(1)} %convolution_add_fusion.8), channel_id=1, source_target_pairs={{0,4},{4,8},{8,12},{1,5},{5,9},{9,13},{2,6},{6,10},{10,14},{3,7},{... | collective-permute-start | bytes 786440 | tf_op jit(solution)/shard_map/ppermute | solution.py:64
  42.0 8.3 %collective-permute-start.5 = (f32[4,128,128]{2,1,0:T(8,128)S(1)}, f32[4,128,128]{2,1,0:T(8,128)S(1)}, u32[]{:S(2)}, u32[]{:S(2)}) collective-permute-start(f32[4,128,128]{2,1,0:T(8,128)S(1)} %convolution_add_fusion.5), channel_id=1, source_target_pairs={{4,0},{8,4},{12,8},{5,1},{9,5},{13,9},{6,2},{10,6},{14,10},{7,3},{... | collective-permute-start | bytes 786440 | tf_op jit(solution)/shard_map/ppermute | solution.py:65

commit v8 on v7

--- a/solution.py
+++ b/solution.py
@@ -57,18 +57,21 @@
 
 def chain_seq(transition, offset, local_cot):
     count = lax.axis_size("seq")
-    right = [(i, i + 1) for i in range(count - 1)]
-    left = [(i + 1, i) for i in range(count - 1)]
+    here = lax.axis_index("seq")
+    state_in = jnp.zeros_like(offset)
+    end_cot = jnp.zeros_like(local_cot)
     fwd_sum, bwd_sum = offset, local_cot
-    for hop in range(count - 1):
-        got_sum = lax.ppermute(fwd_sum, "seq", right)
-        got_cot = lax.ppermute(bwd_sum, "seq", left)
-        if hop == count - 2:
-            return got_sum, got_cot
-        fwd_sum = mm("hij,hjk->hik", transition, got_sum) + offset
-        bwd_sum = mm("hji,hjk->hik", transition, got_cot) + local_cot
-    zero = jnp.zeros_like(offset)
-    return zero, zero
+    for hop in range(1, count):
+        sender = hop - 1
+        back_sender = count - hop
+        payload = jnp.where(here == sender, fwd_sum, bwd_sum)
+        got = lax.ppermute(payload, "seq", [(sender, hop), (back_sender, back_sender - 1)])
+        state_in = jnp.where(here == hop, got, state_in)
+        end_cot = jnp.where(here == back_sender - 1, got, end_cot)
+        if hop < count - 1:
+            fwd_sum = mm("hij,hjk->hik", transition, state_in) + offset
+            bwd_sum = mm("hji,hjk->hik", transition, end_cot) + local_cot
+    return state_in, end_cot
 
 
 def scan_seq(transition, offset, local_cot):

time: 58.7 us -> 63.9 us (1.089)
  waiting for transfers between devices: 7.43 us -> 18.8 us
  starting transfers between devices: 17.8 us -> 6.89 us
  local copies, waits for them, and re-layouts: 5.45 us -> 7.28 us
  matrix products: 23.5 us -> 25.2 us
  other arithmetic: 3.12 us -> 4.13 us
    ppermute x6 -> x3, waiting for transfers between devices: 7.43 us -> 18.8 us  [chain_seq(): lax.ppermute(payload, 'seq', [(sender, hop), (back_sender, back_sender -...]
    ppermute x6 -> x3, starting transfers between devices: 17.8 us -> 6.89 us  [chain_seq(): lax.ppermute(payload, 'seq', [(sender, hop), (back_sender, back_sender -...]
    unnamed x8 -> x30, local copies, waits for them, and re-layouts: 2.02 us -> 4.5 us
    dot_general x22, matrix products: 10.9 us -> 11.9 us  [mh(): return jnp.einsum(spec, *operands, precision=lax.Precision.HIGH)]
    reduce_sum x2, other arithmetic: 0.35 us -> 1.29 us  [unit_rows(): scale = lax.rsqrt(jnp.sum(tensor * tensor, axis=-1, keepdims=True) + 1e-06)]
    dot_general x23, matrix products: 12.6 us -> 13.3 us  [mm(): return jnp.einsum(spec, *operands, precision=highest)]
    convert_element_type x2 -> x1, local copies, waits for them, and re-layouts: 2.09 us -> 1.47 us  [pair_major(): return tensor.reshape(heads_here, tok_count, 2, head_size).transpose(1, 2...]
  transfers between devices with their start and end apart: 6 -> 3, of which waited for: 6 -> 2; matrix products, arithmetic and copies ran while one was open for 16% -> 4% of each run, Pallas kernels for 0% -> 0%
where the time goes in v8:
time: 63.9 us; the launch traced here: 63.5 us
  matrix products  25.2 us (39%)
  waiting for transfers between devices  18.8 us (29%)
  local copies, waits for them, and re-layouts  7.28 us (11%)
  starting transfers between devices  6.89 us (11%)
  other arithmetic  4.13 us (6%)
  between operations  1.24 us (2%)
    ppermute x3, waiting for transfers between devices, chain_seq(): lax.ppermute(payload, 'seq', [(sender, hop), (back_sender, back_sender -...  18.8 us
    dot_general x23, matrix products, mm(): return jnp.einsum(spec, *operands, precision=highest)  13.3 us
    dot_general x22, matrix products, mh(): return jnp.einsum(spec, *operands, precision=lax.Precision.HIGH)  11.9 us
    ppermute x3, starting transfers between devices, chain_seq(): lax.ppermute(payload, 'seq', [(sender, hop), (back_sender, back_sender -...  6.89 us
    unnamed x30, local copies, waits for them, and re-layouts  4.5 us
    mul x1, other arithmetic, local(): d_k = k_scale * (d_kn - jnp.sum(kn * d_kn, axis=-1, keepdims=True) * kn)  1.79 us
    convert_element_type x1, local copies, waits for them, and re-layouts, pair_major(): return tensor.reshape(heads_here, tok_count, 2, head_size).transpose(1, 2...  1.47 us
    reduce_sum x2, other arithmetic, unit_rows(): scale = lax.rsqrt(jnp.sum(tensor * tensor, axis=-1, keepdims=True) + 1e-06)  1.29 us
  transfers between devices with their start and end apart: 3, of which 2 were waited for; matrix products, arithmetic and copies ran while one was open for 4% of the time, Pallas kernels for 0%

profile of v8, /device:TPU:0, one launch (start us, length us, event | category | flops | bytes accessed | tf_op | source)
XLA Modules:
  0.0 63.5 jit_solution(13419630867000626487)
XLA Ops:
  0.7 1.1 %fusion.35 = f32[4,128]{1,0:T(4,128)S(1)} fusion(bf16[128,4,128]{2,1,0:T(4,128)(2,1)} %param.4), kind=kLoop, calls=%fused_computation.71 | loop fusion | flops 196096 | bytes 133120 | tf_op jit(solution)/shard_map/reduce_sum | solution.py:19
  1.9 1.2 %copy.9 = f32[128,2,4,128]{3,1,0,2:T(2,128)S(1)} copy(bf16[128,2,4,128]{3,2,1,0:T(4,128)(2,1)} %param.5) | data formatting | bytes 786432 | tf_op jit(solution)/shard_map/transpose | solution.py:110
  3.0 0.2 multiply_reduce_fusion
  3.5 0.5 convolution_multiply_fusion.7
  4.0 0.5 convolution_multiply_fusion.6
  4.5 0.5 convolution_multiply_fusion.5
  5.1 0.7 %convolution_multiply_fusion.4 = f32[4,128,128]{2,1,0:T(8,128)S(1)} fusion(f32[4,1,2,128,128]{4,3,2,0,1:T(8,128)S(1)} %bitcast.200), kind=kOutput, calls=%fused_computation.33 | convolution fusion | flops 100728832 | bytes 786432 | tf_op jit(solution)/shard_map/hpid,hpjd->hpij/dot_general | solution.py:11
  5.8 0.9 %fusion.3 = f32[4,16,16,16]{3,2,1,0:T(8,128)S(1)} fusion(f32[4,16,16,128]{3,2,1,0:T(8,128)S(1)} %bitcast.201, pred[16,16]{1,0:T(8,128)(4,1)S(1)} %iota_compare_fusion.7), kind=kOutput, calls=%fused_computation.10 | convolution fusion | flops 25198592 | bytes 590080 | tf_op jit(solution)/shard_map/hpid,hpjd->hpij/dot_general | solution.py:11
  6.7 0.7 %fusion.84 = f32[4,16,16,16]{3,2,1,0:T(8,128)S(1)} fusion(f32[4,16,16,16]{3,2,1,0:T(8,128)S(1)} %fusion.3), kind=kOutput, calls=%fused_computation.154 | convolution fusion | flops 3145728 | bytes 131072 | tf_op jit(solution)/shard_map/hpij,hpjk->hpik/dot_general | solution.py:11
  7.4 0.7 %fusion.85 = f32[4,16,16,16]{3,2,1,0:T(8,128)S(1)} fusion(f32[4,16,16,16]{3,2,1,0:T(8,128)S(1)} %fusion.84), kind=kOutput, calls=%fused_computation.155 | convolution fusion | flops 3145728 | bytes 131072 | tf_op jit(solution)/shard_map/hpij,hpjk->hpik/dot_general | solution.py:11
  8.0 0.7 %convolution_add_fusion.2 = f32[4,16,16,16]{3,2,1,0:T(8,128)S(1)} fusion(f32[4,16,16,16]{3,2,1,0:T(8,128)S(1)} %fusion.84, f32[4,16,16,16]{3,2,1,0:T(8,128)S(1)} %fusion.3, f32[16,16]{1,0:T(8,128)S(1)} %fusion.66), kind=kOutput, calls=%fused_computation.5 | convolution fusion | flops 3178496 | bytes 197632 | tf_op jit(solution)/shard_map/hpij,hpjk->hpik/dot_general | solution.py:11
  8.7 0.6 %fusion.86 = f32[4,16,16,16]{3,2,1,0:T(8,128)S(1)} fusion(f32[4,16,16,16]{3,2,1,0:T(8,128)S(1)} %fusion.85), kind=kOutput, calls=%fused_computation.156 | convolution fusion | flops 3145728 | bytes 131072 | tf_op jit(solution)/shard_map/hpij,hpjk->hpik/dot_general | solution.py:11
  9.4 0.6 convolution_add_fusion.1
  10.0 0.6 convolution_add_fusion
  10.7 0.4 fusion.80
  11.1 0.4 convolution_negate_fusion.3
  11.6 0.4 fusion.81
  12.0 0.4 convolution_negate_fusion.2
  12.6 0.4 fusion.82
  13.0 0.4 convolution_negate_fusion.1
  13.6 0.6 fusion.40
  14.2 0.7 %fusion.14 = f32[4,1,128,128]{3,2,0,1:T(8,128)S(1)} fusion(f32[4,128,128]{1,2,0:T(8,128)S(1)} %fusion.40, f32[4,1,2,128,128]{4,3,2,0,1:T(8,128)S(1)} %fusion.19), kind=kOutput, calls=%fused_computation.32 | convolution fusion | flops 100728832 | bytes 786432 | tf_op jit(solution)/shard_map/hpij,hpjk->hpik/dot_general | solution.py:11
  14.9 0.6 fusion.26
  15.6 0.3 copy-done.13
  15.9 0.4 fusion.24
  16.4 0.4 copy-done.1
  16.8 0.6 fusion.10
  17.4 0.4 convolution_subtract_fusion.2
  17.9 0.3 fusion.61
  18.2 0.4 copy-done.2
  18.5 0.6 %broadcast_select_fusion.1 = (f32[4,128,128]{2,1,0:T(8,128)S(1)}, f32[4,128,128]{2,1,0:T(8,128)S(1)}) fusion(f32[4,128,128]{2,1,0:T(8,128)S(1)} %fusion.61, pred[]{:T(512)S(6)} %eq.36, f32[4,256,128]{2,1,0:T(8,128)S(1)} %broadcast_multiply_fusion, f32[4,256,128]{2,1,0:T(8,128)S(1)} %fusion.24), kind=kOutput, calls=%fused_computation.116 | convolution fusion | flops 100794368 | bytes 1835009 | tf_op jit(solution)/shard_map/hjd,hjw->hdw/dot_general | solution.py:15
  19.2 4.9 %collective-permute-start = (f32[4,128,128]{2,1,0:T(8,128)S(1)}, f32[4,128,128]{2,1,0:T(8,128)S(1)}, u32[]{:S(2)}, u32[]{:S(2)}) collective-permute-start(f32[4,128,128]{2,1,0:T(8,128)S(1)} %get-tuple-element.18), channel_id=1, source_target_pairs={{0,4},{12,8},{1,5},{13,9},{2,6},{14,10},{3,7},{15,11},{16,20},{28,... | collective-permute-start | bytes 786440 | tf_op jit(solution)/shard_map/ppermute | solution.py:68
  24.2 0.6 %fusion.15 = f32[4,128,128]{2,1,0:T(8,128)S(1)} fusion(f32[4,256,128]{2,1,0:T(8,128)S(1)} %broadcast_multiply_fusion, f32[4,256,128]{2,1,0:T(8,128)S(1)} %fusion.26, f32[128,128]{1,0:T(8,128)S(1)} %fusion.63), kind=kOutput, calls=%fused_computation.44 | convolution fusion | flops 100794368 | bytes 1376256 | tf_op jit(solution)/shard_map/hjd,hjw->hdw/dot_general | solution.py:15
  24.8 4.9 %collective-permute-done = f32[4,128,128]{2,1,0:T(8,128)S(1)} collective-permute-done((f32[4,128,128]{2,1,0:T(8,128)S(1)}, f32[4,128,128]{2,1,0:T(8,128)S(1)}, u32[]{:S(2)}, u32[]{:S(2)}) %collective-permute-start) | collective-permute-done | bytes 262176 | tf_op jit(solution)/shard_map/ppermute | solution.py:68
  29.7 0.6 convolution_add_fusion.8
  30.3 0.4 fusion.13
  30.7 0.7 %collective-permute-start.1 = (f32[4,128,128]{2,1,0:T(8,128)S(1)}, f32[4,128,128]{2,1,0:T(8,128)S(1)}, u32[]{:S(2)}, u32[]{:S(2)}) collective-permute-start(f32[4,128,128]{2,1,0:T(8,128)S(1)} %fusion.13), channel_id=1, source_target_pairs={{4,8},{8,4},{5,9},{9,5},{6,10},{10,6},{7,11},{11,7},{20,24},{24,20... | collective-permute-start | bytes 786440 | tf_op jit(solution)/shard_map/ppermute | solution.py:68
  31.4 1.2 %fusion.59 = f32[4,256,128]{2,1,0:T(8,128)} fusion(f32[4,128,256]{2,1,0:T(8,128)S(1)} %fusion.10, bf16[4,128,128]{2,0,1:T(4,128)(2,1)S(1)} %bitcast.196), kind=kOutput, calls=%fused_computation.123 | convolution fusion | flops 100663296 | bytes 1179648 | tf_op jit(solution)/shard_map/hij,hiw->hjw/dot_general | solution.py:15
  32.7 0.6 convolution_add_fusion.6
  33.3 0.3 copy-done.5
  33.6 1.1 %fusion.12 = f32[4,128,128]{2,1,0:T(8,128)} fusion(f32[4,128,128]{2,1,0:T(8,128)S(1)} %convolution_add_fusion.6, f32[4,128,128]{2,1,0:T(8,128)S(1)} %copy-done.5, f32[4,128,128]{2,1,0:T(8,128)S(1)} %fusion.15, pred[]{:T(512)S(6)} %eq.33, f32[4,128,128]{2,1,0:T(8,128)S(1)} %collective-permute-done.1, f32[4,128,128]{2,1,0:T(8,128)S(1)} %collective-permute-done, ...), kind=kOutput, calls=%fused_computation.27 | convolution fusion | flops 100925440 | bytes 1572866 | tf_op jit(solution)/shard_map/hij,hjk->hik/dot_general | solution.py:11
  34.7 1.3 %collective-permute-start.2 = (f32[4,128,128]{2,1,0:T(8,128)}, f32[4,128,128]{2,1,0:T(8,128)S(1)}, u32[]{:S(2)}, u32[]{:S(2)}) collective-permute-start(f32[4,128,128]{2,1,0:T(8,128)} %fusion.12), channel_id=1, source_target_pairs={{8,12},{4,0},{9,13},{5,1},{10,14},{6,2},{11,15},{7,3},{24,28},{20,... | collective-permute-start | bytes 786440 | tf_op jit(solution)/shard_map/ppermute | solution.py:68
  36.1 0.4 fusion.87
  36.5 13.9 %collective-permute-done.2 = f32[4,128,128]{2,1,0:T(8,128)S(1)} collective-permute-done((f32[4,128,128]{2,1,0:T(8,128)}, f32[4,128,128]{2,1,0:T(8,128)S(1)}, u32[]{:S(2)}, u32[]{:S(2)}) %collective-permute-start.2) | collective-permute-done | bytes 262176 | tf_op jit(solution)/shard_map/ppermute | solution.py:68
  50.4 0.4 convolution_subtract_fusion.1
  50.8 0.3 fusion.57
  51.1 0.6 copy-done.3
  51.7 0.3 fusion.17
  52.0 0.8 %copy.37 = bf16[128,4,128]{2,1,0:T(4,128)(2,1)} copy(bf16[128,4,128]{2,0,1:T(8,128)(2,1)S(1)} %fusion.17) | data formatting | bytes 262144
  52.8 0.4 fusion.8
  53.1 0.6 copy-done.8
  53.9 0.9 %fusion.83 = (bf16[4,256,128]{2,1,0:T(8,128)(2,1)S(1)}, f32[4,256,128]{2,1,0:T(8,128)S(1)}) fusion(f32[4,256,128]{2,1,0:T(8,128)S(1)} %fusion.8, f32[4,1,128,128]{3,2,0,1:T(8,128)S(1)} %copy-done.12, f32[4,1,128,128]{3,2,0,1:T(8,128)S(1)} %copy-done.10, f32[4,1,128,128]{3,2,0,1:T(8,128)S(1)} %copy-done.8), kind=kOutput, calls=%fused_computation.153 | convolution fusion | flops 202506240 | bytes 2097152 | tf_op jit(solution)/shard_map/hij,hiw->hjw/dot_general | solution.py:15
  54.8 0.3 fusion.2
  55.1 0.7 %fusion.30 = f32[4,256,128]{2,1,0:T(8,128)S(1)} fusion(f32[4,128,256]{2,1,0:T(8,128)S(1)} %fusion.2, f32[4,128]{1,0:T(4,128)S(1)} %get-tuple-element.17, bf16[128,4,128]{2,1,0:T(4,128)(2,1)S(1)} %copy-done.1), kind=kOutput, calls=%fused_computation.68 | convolution fusion | flops 100794368 | bytes 1181696 | tf_op jit(solution)/shard_map/hij,hid->hjd/dot_general | solution.py:15
  55.8 0.5 fusion.34
  56.2 0.2 fusion.39
  56.5 0.8 %copy.38 = bf16[128,4,128]{2,1,0:T(4,128)(2,1)} copy(bf16[128,4,128]{2,0,1:T(8,128)(2,1)S(1)} %fusion.39) | data formatting | bytes 262144
  57.2 0.6 fusion.1
  57.8 0.6 fusion.88
  58.4 0.4 fusion.9
  58.8 0.4 fusion.7
  59.2 1.0 %convolution_add_fusion.3 = f32[4,256,128]{2,1,0:T(8,128)S(1)} fusion(f32[4,256,128]{2,1,0:T(8,128)S(1)} %fusion.7, f32[4,256,256]{2,1,0:T(8,128)S(1)} %fusion.1, f32[4,256,128]{2,1,0:T(8,128)S(1)} %broadcast_multiply_fusion), kind=kOutput, calls=%fused_computation.6 | convolution fusion | flops 201457664 | bytes 2621440 | tf_op jit(solution)/shard_map/hji,hjd->hid/dot_general | solution.py:15
  60.3 1.8 %fusion.11 = bf16[4,256,128]{2,1,0:T(8,128)(2,1)S(1)} fusion(f32[4,256,128]{2,1,0:T(8,128)S(1)} %convolution_add_fusion.3, f32[4,256,128]{2,1,0:T(8,128)S(1)} %broadcast_multiply_fusion, f32[4,256]{1,0:T(4,128)S(1)} %add_rsqrt_fusion), kind=kOutput, calls=%fused_computation.23 | output fusion | flops 656511 | bytes 1314816 | tf_op jit(solution)/shard_map/mul | solution.py:146
  62.1 1.5 %copy_bitcast_fusion = (bf16[128,2,4,128]{3,2,1,0:T(4,128)(2,1)}, bf16[128,2,4,128]{3,2,1,0:T(4,128)(2,1)}) fusion(bf16[4,128,2,128]{3,2,1,0:T(2,128)(2,1)S(1)} %bitcast.214, bf16[4,128,2,128]{3,2,1,0:T(2,128)(2,1)S(1)} %bitcast.213), kind=kLoop, calls=%fused_computation.96 | loop fusion | bytes 1048576 | tf_op jit(solution)/shard_map/convert_element_type | solution.py:155
  (41 shorter events, 1.3 us)
Async XLA Ops:
  0.6 17.2 %copy-start = (bf16[128,4,128]{2,1,0:T(4,128)(2,1)S(1)}, bf16[128,4,128]{2,1,0:T(4,128)(2,1)}, u32[]{:S(2)}) copy-start(bf16[128,4,128]{2,1,0:T(4,128)(2,1)} %param.7) | copy-start | bytes 393220
  13.6 1.9 %copy-start.9 = (f32[4,1,128,128]{3,2,0,1:T(8,128)}, f32[4,1,128,128]{3,2,0,1:T(8,128)S(1)}, u32[]{:S(2)}) copy-start(f32[4,1,128,128]{3,2,0,1:T(8,128)S(1)} %get-tuple-element.8) | copy-start | bytes 786436
  13.6 1.9 %copy-start.11 = (f32[4,1,128,128]{3,2,0,1:T(8,128)}, f32[4,1,128,128]{3,2,0,1:T(8,128)S(1)}, u32[]{:S(2)}) copy-start(f32[4,1,128,128]{3,2,0,1:T(8,128)S(1)} %get-tuple-element.9) | copy-start | bytes 786436
  14.9 0.7 %copy-start.7 = (f32[4,1,128,128]{3,2,0,1:T(8,128)}, f32[4,1,128,128]{3,2,0,1:T(8,128)S(1)}, u32[]{:S(2)}) copy-start(f32[4,1,128,128]{3,2,0,1:T(8,128)S(1)} %fusion.14) | copy-start | bytes 786436
  14.9 1.0 %copy-start.13 = (bf16[128,2,4,128]{3,2,1,0:T(4,128)(2,1)S(1)}, bf16[128,2,4,128]{3,2,1,0:T(4,128)(2,1)}, u32[]{:S(2)}) copy-start(bf16[128,2,4,128]{3,2,1,0:T(4,128)(2,1)} %param.6) | copy-start | bytes 786436
  15.9 0.9 %copy-start.1 = (bf16[128,4,128]{2,1,0:T(4,128)(2,1)S(1)}, bf16[128,4,128]{2,1,0:T(4,128)(2,1)}, u32[]{:S(2)}) copy-start(bf16[128,4,128]{2,1,0:T(4,128)(2,1)} %param.4) | copy-start | bytes 393220
  17.8 0.7 %copy-start.2 = (f32[4,128,128]{2,1,0:T(8,128)}, f32[4,128,128]{2,1,0:T(8,128)S(1)}, u32[]{:S(2)}) copy-start(f32[4,128,128]{2,1,0:T(8,128)S(1)} %convolution_subtract_fusion.2) | copy-start | bytes 786436
  19.2 11.1 %copy-start.4 = (f32[4,128,128]{2,1,0:T(8,128)}, f32[4,128,128]{2,1,0:T(8,128)S(1)}, u32[]{:S(2)}) copy-start(f32[4,128,128]{2,1,0:T(8,128)S(1)} %get-tuple-element.19) | copy-start | bytes 786436
  19.2 10.5 %collective-permute-start = (f32[4,128,128]{2,1,0:T(8,128)S(1)}, f32[4,128,128]{2,1,0:T(8,128)S(1)}, u32[]{:S(2)}, u32[]{:S(2)}) collective-permute-start(f32[4,128,128]{2,1,0:T(8,128)S(1)} %get-tuple-element.18), channel_id=1, source_target_pairs={{0,4},{12,8},{1,5},{13,9},{2,6},{14,10},{3,7},{15,11},{16,20},{28,... | collective-permute-start | bytes 786440 | tf_op jit(solution)/shard_map/ppermute | solution.py:68
  30.7 1.9 %collective-permute-start.1 = (f32[4,128,128]{2,1,0:T(8,128)S(1)}, f32[4,128,128]{2,1,0:T(8,128)S(1)}, u32[]{:S(2)}, u32[]{:S(2)}) collective-permute-start(f32[4,128,128]{2,1,0:T(8,128)S(1)} %fusion.13), channel_id=1, source_target_pairs={{4,8},{8,4},{5,9},{9,5},{6,10},{10,6},{7,11},{11,7},{20,24},{24,20... | collective-permute-start | bytes 786440 | tf_op jit(solution)/shard_map/ppermute | solution.py:68
  32.7 1.0 %copy-start.5 = (f32[4,128,128]{2,1,0:T(8,128)S(1)}, f32[4,128,128]{2,1,0:T(8,128)}, u32[]{:S(2)}) copy-start(f32[4,128,128]{2,1,0:T(8,128)} %copy-done.4) | copy-start | bytes 786436
  34.7 15.6 %collective-permute-start.2 = (f32[4,128,128]{2,1,0:T(8,128)}, f32[4,128,128]{2,1,0:T(8,128)S(1)}, u32[]{:S(2)}, u32[]{:S(2)}) collective-permute-start(f32[4,128,128]{2,1,0:T(8,128)} %fusion.12), channel_id=1, source_target_pairs={{8,12},{4,0},{9,13},{5,1},{10,14},{6,2},{11,15},{7,3},{24,28},{20,... | collective-permute-start | bytes 786440 | tf_op jit(solution)/shard_map/ppermute | solution.py:68
  50.8 1.0 %copy-start.3 = (f32[4,128,128]{2,1,0:T(8,128)S(1)}, f32[4,128,128]{2,1,0:T(8,128)}, u32[]{:S(2)}) copy-start(f32[4,128,128]{2,1,0:T(8,128)} %copy-done.2) | copy-start | bytes 786436
  51.7 1.0 %copy-start.6 = (f32[4,256,128]{2,1,0:T(8,128)S(1)}, f32[4,256,128]{2,1,0:T(8,128)}, u32[]{:S(2)}) copy-start(f32[4,256,128]{2,1,0:T(8,128)} %fusion.59) | copy-start | bytes 1572868
  52.8 0.9 %copy-start.8 = (f32[4,1,128,128]{3,2,0,1:T(8,128)S(1)}, f32[4,1,128,128]{3,2,0,1:T(8,128)}, u32[]{:S(2)}) copy-start(f32[4,1,128,128]{3,2,0,1:T(8,128)} %copy-done.7) | copy-start | bytes 786436
  52.8 1.0 %copy-start.10 = (f32[4,1,128,128]{3,2,0,1:T(8,128)S(1)}, f32[4,1,128,128]{3,2,0,1:T(8,128)}, u32[]{:S(2)}) copy-start(f32[4,1,128,128]{3,2,0,1:T(8,128)} %copy-done.9) | copy-start | bytes 786436
  52.8 1.1 %copy-start.12 = (f32[4,1,128,128]{3,2,0,1:T(8,128)S(1)}, f32[4,1,128,128]{3,2,0,1:T(8,128)}, u32[]{:S(2)}) copy-start(f32[4,1,128,128]{3,2,0,1:T(8,128)} %copy-done.11) | copy-start | bytes 786436

commit v9 on v7

--- a/solution.py
+++ b/solution.py
@@ -28,31 +28,42 @@
 
 def tri_inverse(keys):
     heads, rows, size = keys.shape
-    leaves = rows // LEAF
-    leaf_keys = keys.reshape(heads, leaves, LEAF, size)
-    gram = mm("hpid,hpjd->hpij", leaf_keys, leaf_keys)
-    power = jnp.where(strict_lower(LEAF, LEAF), -2.0 * gram, 0.0)
-    eye = jnp.eye(LEAF, dtype=jnp.float32)
+    tile = min(rows, 128)
+    tiles = rows // tile
+    tile_keys = keys.reshape(heads, tiles, tile, size)
+    row = lax.broadcasted_iota(jnp.int32, (tile, tile), 0)
+    col = lax.broadcasted_iota(jnp.int32, (tile, tile), 1)
+    link = jnp.where(row > col, 2.0 * mm("htid,htjd->htij", tile_keys, tile_keys), 0.0)
+    eye = jnp.eye(tile, dtype=jnp.float32)
+    power = jnp.where(row // LEAF == col // LEAF, -link, 0.0)
     inverse = eye + power
     reach = 2
     while reach < LEAF:
-        power = mm("hpij,hpjk->hpik", power, power)
-        inverse = inverse + mm("hpij,hpjk->hpik", inverse, power)
+        power = mm("htij,htjk->htik", power, power)
+        inverse = inverse + mm("htij,htjk->htik", inverse, power)
         reach *= 2
     span = LEAF
-    while span < rows:
-        pairs = rows // (2 * span)
-        blocks = inverse.reshape(heads, pairs, 2, span, span)
-        upper_inv = blocks[:, :, 0]
-        lower_inv = blocks[:, :, 1]
-        halves = keys.reshape(heads, pairs, 2, span, size)
-        link = 2.0 * mm("hpid,hpjd->hpij", halves[:, :, 1], halves[:, :, 0])
-        corner = -mm("hpij,hpjk->hpik", lower_inv, mm("hpij,hpjk->hpik", link, upper_inv))
-        top = jnp.concatenate([upper_inv, jnp.zeros_like(upper_inv)], axis=3)
-        bottom = jnp.concatenate([corner, lower_inv], axis=3)
-        inverse = jnp.concatenate([top, bottom], axis=2)
+    while span < tile:
+        cross = (row // (2 * span) == col // (2 * span)) & (row // span != col // span)
+        inverse = inverse - mm(
+            "htij,htjk->htik", inverse, mm("htij,htjk->htik", jnp.where(cross, link, 0.0), inverse)
+        )
         span *= 2
-    return inverse.reshape(heads, rows, rows)
+    if tiles == 1:
+        return inverse.reshape(heads, rows, rows)
+    blocks = {}
+    for i in range(tiles):
+        blocks[i, i] = inverse[:, i]
+        for j in range(i - 1, -1, -1):
+            acc = None
+            for m in range(j, i):
+                cross_link = 2.0 * mm("hid,hjd->hij", tile_keys[:, i], tile_keys[:, m])
+                term = mm("hij,hjk->hik", cross_link, blocks[m, j])
+                acc = term if acc is None else acc + term
+            blocks[i, j] = -mm("hij,hjk->hik", blocks[i, i], acc)
+    zero = jnp.zeros((heads, tile, tile), jnp.float32)
+    band = [jnp.concatenate([blocks.get((i, j), zero) for j in range(tiles)], axis=2) for i in range(tiles)]
+    return jnp.concatenate(band, axis=1)
 
 
 def chain_seq(transition, offset, local_cot):

time: 58.7 us -> 59.1 us (level)
  local copies, waits for them, and re-layouts: 5.45 us -> 4.1 us
  other arithmetic: 3.12 us -> 3.93 us
  starting transfers between devices: 17.8 us -> 18.5 us
    ppermute x3, waiting for transfers between devices: 2.1 us -> 0.11 us  [chain_seq(): got_sum = lax.ppermute(fwd_sum, 'seq', right)]
    ppermute x3, waiting for transfers between devices: 5.33 us -> 7.03 us  [chain_seq(): got_cot = lax.ppermute(bwd_sum, 'seq', left)]
    transpose x1, local copies, waits for them, and re-layouts: 1.19 us -> 0.2 us  [local(): reflect_keys.astype(jnp.float32).reshape(rows, heads_here, head_size)]
    reduce_sum x2, other arithmetic: 0.35 us -> 1.26 us  [unit_rows(): scale = lax.rsqrt(jnp.sum(tensor * tensor, axis=-1, keepdims=True) + 1e-06)]
    ppermute x3, starting transfers between devices: 13.9 us -> 14.6 us  [chain_seq(): got_sum = lax.ppermute(fwd_sum, 'seq', right)]
    dot_general x23 -> x20, matrix products: 12.6 us -> 12.9 us  [mm(): return jnp.einsum(spec, *operands, precision=highest)]
    unnamed x8 -> x10, local copies, waits for them, and re-layouts: 2.02 us -> 1.77 us
  transfers between devices with their start and end apart: 6 -> 6, of which waited for: 6 -> 4; matrix products, arithmetic and copies ran while one was open for 16% -> 12% of each run, Pallas kernels for 0% -> 0%
where the time goes in v9:
time: 59.1 us; the launch traced here: 58.8 us
  matrix products  24 us (41%)
  starting transfers between devices  18.5 us (31%)
  waiting for transfers between devices  7.14 us (12%)
  local copies, waits for them, and re-layouts  4.1 us (7%)
  other arithmetic  3.93 us (7%)
  between operations  1.19 us (2%)
    ppermute x3, starting transfers between devices, chain_seq(): got_sum = lax.ppermute(fwd_sum, 'seq', right)  14.6 us
    dot_general x20, matrix products, mm(): return jnp.einsum(spec, *operands, precision=highest)  12.9 us
    dot_general x22, matrix products, mh(): return jnp.einsum(spec, *operands, precision=lax.Precision.HIGH)  11.1 us
    ppermute x3, waiting for transfers between devices, chain_seq(): got_cot = lax.ppermute(bwd_sum, 'seq', left)  7.03 us
    ppermute x3, starting transfers between devices, chain_seq(): got_cot = lax.ppermute(bwd_sum, 'seq', left)  3.88 us
    convert_element_type x2, local copies, waits for them, and re-layouts, pair_major(): return tensor.reshape(heads_here, tok_count, 2, head_size).transpose(1, 2...  2.09 us
    mul x1, other arithmetic, local(): d_k = k_scale * (d_kn - jnp.sum(kn * d_kn, axis=-1, keepdims=True) * kn)  1.79 us
    unnamed x10, local copies, waits for them, and re-layouts  1.77 us
  transfers between devices with their start and end apart: 6, of which 4 were waited for; matrix products, arithmetic and copies ran while one was open for 12% of the time, Pallas kernels for 0%

profile of v9, /device:TPU:0, one launch (start us, length us, event | category | flops | bytes accessed | tf_op | source)
XLA Modules:
  0.0 58.8 jit_solution(100853187707130773)
XLA Ops:
  0.8 1.0 %fusion.34 = f32[4,128]{1,0:T(4,128)S(1)} fusion(bf16[128,4,128]{2,1,0:T(4,128)(2,1)} %param.4), kind=kLoop, calls=%fused_computation.65 | loop fusion | flops 196096 | bytes 133120 | tf_op jit(solution)/shard_map/reduce_sum | solution.py:19
  1.9 0.2 copy.9
  2.2 0.2 multiply_reduce_fusion
  2.4 0.2 broadcast_multiply_fusion
  2.6 0.7 %convolution_multiply_fusion.4 = f32[4,128,128]{2,1,0:T(8,128)S(1)} fusion(f32[4,2,128,128]{3,2,1,0:T(8,128)S(1)} %bitcast.134), kind=kOutput, calls=%fused_computation.33 | convolution fusion | flops 100728832 | bytes 786432 | tf_op jit(solution)/shard_map/hid,hjd->hij/dot_general | solution.py:11
  3.3 1.2 %fusion.3 = f32[4,2,128,128]{3,2,1,0:T(8,128)S(1)} fusion(f32[4,2,128,128]{3,2,1,0:T(8,128)S(1)} %bitcast.135, pred[128,128]{1,0:T(8,128)(4,1)S(1)} %iota_compare_fusion.3), kind=kOutput, calls=%fused_computation.13 | convolution fusion | flops 201588736 | bytes 1064960 | tf_op jit(solution)/shard_map/htid,htjd->htij/dot_general | solution.py:11
  4.5 0.3 fusion.61
  4.8 0.6 %fusion.23 = f32[4,2,128,128]{3,2,1,0:T(8,128)S(1)} fusion(f32[4,2,128,128]{3,2,1,0:T(8,128)S(1)} %fusion.3, pred[128,128]{1,0:T(8,128)(4,1)S(1)} %get-tuple-element.15), kind=kOutput, calls=%fused_computation.54 | convolution fusion | flops 201588736 | bytes 1064960 | tf_op jit(solution)/shard_map/htij,htjk->htik/dot_general | solution.py:11
  5.4 0.6 %fusion.85 = f32[4,2,128,128]{3,2,1,0:T(8,128)S(1)} fusion(f32[4,2,128,128]{3,2,1,0:T(8,128)S(1)} %fusion.23), kind=kOutput, calls=%fused_computation.156 | convolution fusion | flops 201326592 | bytes 1048576 | tf_op jit(solution)/shard_map/htij,htjk->htik/dot_general | solution.py:11
  6.0 0.7 %convolution_add_fusion.2 = f32[4,2,128,128]{3,2,1,0:T(8,128)S(1)} fusion(f32[4,2,128,128]{3,2,1,0:T(8,128)S(1)} %fusion.23, f32[4,2,128,128]{3,2,1,0:T(8,128)S(1)} %fusion.3, f32[128,128]{1,0:T(8,128)S(1)} %fusion.64, pred[128,128]{1,0:T(8,128)(4,1)S(1)} %get-tuple-element.15), kind=kOutput, calls=%fused_computation.8 | convolution fusion | flops 201850880 | bytes 1654784 | tf_op jit(solution)/shard_map/htij,htjk->htik/dot_general | solution.py:11
  6.7 0.6 %fusion.86 = f32[4,2,128,128]{3,2,1,0:T(8,128)S(1)} fusion(f32[4,2,128,128]{3,2,1,0:T(8,128)S(1)} %fusion.85), kind=kOutput, calls=%fused_computation.157 | convolution fusion | flops 201326592 | bytes 1048576 | tf_op jit(solution)/shard_map/htij,htjk->htik/dot_general | solution.py:11
  7.3 0.6 %convolution_add_fusion.1 = f32[4,2,128,128]{3,2,1,0:T(8,128)S(1)} fusion(f32[4,2,128,128]{3,2,1,0:T(8,128)S(1)} %convolution_add_fusion.2, f32[4,2,128,128]{3,2,1,0:T(8,128)S(1)} %fusion.85), kind=kOutput, calls=%fused_computation.7 | convolution fusion | flops 201457664 | bytes 1572864 | tf_op jit(solution)/shard_map/htij,htjk->htik/dot_general | solution.py:11
  8.0 0.6 %convolution_add_fusion = f32[4,2,128,128]{3,2,1,0:T(8,128)S(1)} fusion(f32[4,2,128,128]{3,2,1,0:T(8,128)S(1)} %convolution_add_fusion.1, f32[4,2,128,128]{3,2,1,0:T(8,128)S(1)} %fusion.86), kind=kOutput, calls=%fused_computation.6 | convolution fusion | flops 201457664 | bytes 1572864 | tf_op jit(solution)/shard_map/htij,htjk->htik/dot_general | solution.py:11
  8.7 0.7 %fusion.19 = f32[4,2,128,128]{3,2,1,0:T(8,128)S(1)} fusion(f32[4,2,128,128]{3,2,1,0:T(8,128)S(1)} %convolution_add_fusion, f32[4,2,128,128]{3,2,1,0:T(8,128)S(1)} %fusion.3, pred[128,128]{1,0:T(8,128)(4,1)S(1)} %get-tuple-element.14), kind=kOutput, calls=%fused_computation.47 | convolution fusion | flops 201457664 | bytes 1589248 | tf_op jit(solution)/shard_map/htij,htjk->htik/dot_general | solution.py:11
  9.3 0.6 %convolution_subtract_fusion.2 = f32[4,2,128,128]{3,2,1,0:T(8,128)S(1)} fusion(f32[4,2,128,128]{3,2,1,0:T(8,128)S(1)} %convolution_add_fusion, f32[4,2,128,128]{3,2,1,0:T(8,128)S(1)} %fusion.19), kind=kOutput, calls=%fused_computation.5 | convolution fusion | flops 201457664 | bytes 1572864 | tf_op jit(solution)/shard_map/htij,htjk->htik/dot_general | solution.py:11
  10.0 0.7 %fusion.17 = f32[4,2,128,128]{3,2,1,0:T(8,128)S(1)} fusion(f32[4,2,128,128]{3,2,1,0:T(8,128)S(1)} %convolution_subtract_fusion.2, f32[4,2,128,128]{3,2,1,0:T(8,128)S(1)} %fusion.3, pred[128,128]{1,0:T(8,128)(4,1)S(1)} %get-tuple-element.13), kind=kOutput, calls=%fused_computation.45 | convolution fusion | flops 201457664 | bytes 1589248 | tf_op jit(solution)/shard_map/htij,htjk->htik/dot_general | solution.py:11
  10.6 0.6 %convolution_subtract_fusion.1 = f32[4,2,128,128]{3,2,1,0:T(8,128)S(1)} fusion(f32[4,2,128,128]{3,2,1,0:T(8,128)S(1)} %convolution_subtract_fusion.2, f32[4,2,128,128]{3,2,1,0:T(8,128)S(1)} %fusion.17), kind=kOutput, calls=%fused_computation.4 | convolution fusion | flops 201457664 | bytes 1572864 | tf_op jit(solution)/shard_map/htij,htjk->htik/dot_general | solution.py:11
  11.3 0.7 %fusion.15 = f32[4,2,128,128]{3,2,1,0:T(8,128)S(1)} fusion(f32[4,2,128,128]{3,2,1,0:T(8,128)S(1)} %convolution_subtract_fusion.1, f32[4,2,128,128]{3,2,1,0:T(8,128)S(1)} %fusion.3, pred[128,128]{1,0:T(8,128)(4,1)S(1)} %get-tuple-element.12), kind=kOutput, calls=%fused_computation.43 | convolution fusion | flops 201457664 | bytes 1589248 | tf_op jit(solution)/shard_map/htij,htjk->htik/dot_general | solution.py:11
  12.0 0.6 %convolution_subtract_fusion = f32[4,2,128,128]{3,2,1,0:T(8,128)S(1)} fusion(f32[4,2,128,128]{3,2,1,0:T(8,128)S(1)} %convolution_subtract_fusion.1, f32[4,2,128,128]{3,2,1,0:T(8,128)S(1)} %fusion.15), kind=kOutput, calls=%fused_computation.3 | convolution fusion | flops 201457664 | bytes 1572864 | tf_op jit(solution)/shard_map/htij,htjk->htik/dot_general | solution.py:11
  12.7 0.6 %fusion.83 = f32[4,128,128]{1,2,0:T(8,128)S(1)} fusion(f32[4,128,128]{2,1,0:T(8,128)S(1)} %convolution_multiply_fusion.4, f32[4,2,128,128]{3,2,1,0:T(8,128)S(1)} %convolution_subtract_fusion), kind=kOutput, calls=%fused_computation.154 | convolution fusion | flops 100663296 | bytes 786432 | tf_op jit(solution)/shard_map/hij,hjk->hik/dot_general | solution.py:11
  13.3 0.7 %convolution_negate_fusion = f32[4,128,128]{2,1,0:T(8,128)S(1)} fusion(f32[4,128,128]{1,2,0:T(8,128)S(1)} %fusion.83, f32[4,2,128,128]{3,2,1,0:T(8,128)S(1)} %convolution_subtract_fusion), kind=kOutput, calls=%fused_computation.32 | convolution fusion | flops 100728832 | bytes 786432 | tf_op jit(solution)/shard_map/hij,hjk->hik/dot_general | solution.py:11
  13.9 0.2 copy-done.1
  14.2 0.4 fusion.10
  14.6 0.8 %fusion.26 = f32[4,256,128]{2,1,0:T(8,128)S(1)} fusion(f32[4,256,128]{2,1,0:T(8,128)S(1)} %broadcast_multiply_fusion, f32[4,128,128]{2,1,0:T(8,128)S(1)} %get-tuple-element.9, f32[4,128,128]{2,1,0:T(8,128)S(1)} %get-tuple-element.8, f32[4,128,128]{2,1,0:T(8,128)S(1)} %convolution_negate_fusion), kind=kOutput, calls=%fused_computation.57 | convolution fusion | flops 202375168 | bytes 1835008 | tf_op jit(solution)/shard_map/hij,hjd->hid/dot_general | solution.py:15
  15.4 0.4 convolution_subtract_fusion.5
  15.8 0.3 fusion.54
  16.1 1.3 %collective-permute-start.3 = (f32[4,128,128]{2,1,0:T(8,128)S(1)}, f32[4,128,128]{2,1,0:T(8,128)S(1)}, u32[]{:S(2)}, u32[]{:S(2)}) collective-permute-start(f32[4,128,128]{2,1,0:T(8,128)S(1)} %fusion.54), channel_id=1, source_target_pairs={{4,0},{8,4},{12,8},{5,1},{9,5},{13,9},{6,2},{10,6},{14,10},{7,3},{... | collective-permute-start | bytes 786440 | tf_op jit(solution)/shard_map/ppermute | solution.py:76
  17.4 0.4 fusion.25
  17.9 0.6 %convolution_multiply_fusion.6 = f32[4,128,128]{2,1,0:T(8,128)S(1)} fusion(f32[4,256,128]{2,1,0:T(8,128)S(1)} %broadcast_multiply_fusion, f32[4,256,128]{2,1,0:T(8,128)S(1)} %fusion.25), kind=kOutput, calls=%fused_computation.35 | convolution fusion | flops 100728832 | bytes 1310720 | tf_op jit(solution)/shard_map/hjd,hjw->hdw/dot_general | solution.py:15
  18.5 5.6 %collective-permute-start = (f32[4,128,128]{2,1,0:T(8,128)S(1)}, f32[4,128,128]{2,1,0:T(8,128)S(1)}, u32[]{:S(2)}, u32[]{:S(2)}) collective-permute-start(f32[4,128,128]{2,1,0:T(8,128)S(1)} %convolution_multiply_fusion.6), channel_id=1, source_target_pairs={{0,4},{4,8},{8,12},{1,5},{5,9},{9,13},{2,6},{6,10},{10,14},{3,7},{... | collective-permute-start | bytes 786440 | tf_op jit(solution)/shard_map/ppermute | solution.py:75
  24.1 0.4 fusion.87
  24.5 0.6 %fusion.12 = f32[4,128,128]{2,1,0:T(8,128)S(1)} fusion(f32[4,256,128]{2,1,0:T(8,128)S(1)} %broadcast_multiply_fusion, f32[4,256,128]{2,1,0:T(8,128)S(1)} %fusion.26, f32[128,128]{1,0:T(8,128)S(1)} %fusion.64), kind=kOutput, calls=%fused_computation.38 | convolution fusion | flops 100794368 | bytes 1376256 | tf_op jit(solution)/shard_map/hjd,hjw->hdw/dot_general | solution.py:15
  25.1 2.2 %collective-permute-done.3 = f32[4,128,128]{2,1,0:T(8,128)S(1)} collective-permute-done((f32[4,128,128]{2,1,0:T(8,128)S(1)}, f32[4,128,128]{2,1,0:T(8,128)S(1)}, u32[]{:S(2)}, u32[]{:S(2)}) %collective-permute-start.3) | collective-permute-done | bytes 262176 | tf_op jit(solution)/shard_map/ppermute | solution.py:76
  27.3 0.6 %convolution_add_fusion.6 = f32[4,128,128]{2,1,0:T(8,128)S(1)} fusion(f32[4,128,128]{2,1,0:T(8,128)S(1)} %fusion.54, f32[4,128,128]{2,1,0:T(8,128)S(1)} %fusion.12, f32[4,128,128]{2,1,0:T(8,128)S(1)} %collective-permute-done.3), kind=kOutput, calls=%fused_computation.28 | convolution fusion | flops 100728832 | bytes 1048576 | tf_op jit(solution)/shard_map/hji,hjk->hik/dot_general | solution.py:11
  28.0 1.3 %collective-permute-start.4 = (f32[4,128,128]{2,1,0:T(8,128)S(1)}, f32[4,128,128]{2,1,0:T(8,128)S(1)}, u32[]{:S(2)}, u32[]{:S(2)}) collective-permute-start(f32[4,128,128]{2,1,0:T(8,128)S(1)} %convolution_add_fusion.6), channel_id=1, source_target_pairs={{4,0},{8,4},{12,8},{5,1},{9,5},{13,9},{6,2},{10,6},{14,10},{7,3},{... | collective-permute-start | bytes 786440 | tf_op jit(solution)/shard_map/ppermute | solution.py:76
  29.3 0.5 fusion.57
  29.7 0.4 convolution_add_fusion.9
  30.1 4.6 %collective-permute-start.1 = (f32[4,128,128]{2,1,0:T(8,128)S(1)}, f32[4,128,128]{2,1,0:T(8,128)S(1)}, u32[]{:S(2)}, u32[]{:S(2)}) collective-permute-start(f32[4,128,128]{2,1,0:T(8,128)S(1)} %convolution_add_fusion.9), channel_id=1, source_target_pairs={{0,4},{4,8},{8,12},{1,5},{5,9},{9,13},{2,6},{6,10},{10,14},{3,7},{... | collective-permute-start | bytes 786440 | tf_op jit(solution)/shard_map/ppermute | solution.py:75
  34.7 2.7 %collective-permute-done.4 = f32[4,128,128]{2,1,0:T(8,128)S(1)} collective-permute-done((f32[4,128,128]{2,1,0:T(8,128)S(1)}, f32[4,128,128]{2,1,0:T(8,128)S(1)}, u32[]{:S(2)}, u32[]{:S(2)}) %collective-permute-start.4) | collective-permute-done | bytes 262176 | tf_op jit(solution)/shard_map/ppermute | solution.py:76
  37.4 0.6 %convolution_add_fusion.5 = f32[4,128,128]{2,1,0:T(8,128)S(1)} fusion(f32[4,128,128]{2,1,0:T(8,128)S(1)} %fusion.54, f32[4,128,128]{2,1,0:T(8,128)S(1)} %fusion.12, f32[4,128,128]{2,1,0:T(8,128)S(1)} %collective-permute-done.4), kind=kOutput, calls=%fused_computation.27 | convolution fusion | flops 100728832 | bytes 1048576 | tf_op jit(solution)/shard_map/hji,hjk->hik/dot_general | solution.py:11
  38.0 1.3 %collective-permute-start.5 = (f32[4,128,128]{2,1,0:T(8,128)S(1)}, f32[4,128,128]{2,1,0:T(8,128)S(1)}, u32[]{:S(2)}, u32[]{:S(2)}) collective-permute-start(f32[4,128,128]{2,1,0:T(8,128)S(1)} %convolution_add_fusion.5), channel_id=1, source_target_pairs={{4,0},{8,4},{12,8},{5,1},{9,5},{13,9},{6,2},{10,6},{14,10},{7,3},{... | collective-permute-start | bytes 786440 | tf_op jit(solution)/shard_map/ppermute | solution.py:76
  39.3 0.1 collective-permute-done.1
  39.4 0.4 convolution_add_fusion.8
  39.8 4.5 %collective-permute-start.2 = (f32[4,128,128]{2,1,0:T(8,128)S(1)}, f32[4,128,128]{2,1,0:T(8,128)S(1)}, u32[]{:S(2)}, u32[]{:S(2)}) collective-permute-start(f32[4,128,128]{2,1,0:T(8,128)S(1)} %convolution_add_fusion.8), channel_id=1, source_target_pairs={{0,4},{4,8},{8,12},{1,5},{5,9},{9,13},{2,6},{6,10},{10,14},{3,7},{... | collective-permute-start | bytes 786440 | tf_op jit(solution)/shard_map/ppermute | solution.py:75
  44.3 2.2 %collective-permute-done.5 = f32[4,128,128]{2,1,0:T(8,128)S(1)} collective-permute-done((f32[4,128,128]{2,1,0:T(8,128)S(1)}, f32[4,128,128]{2,1,0:T(8,128)S(1)}, u32[]{:S(2)}, u32[]{:S(2)}) %collective-permute-start.5) | collective-permute-done | bytes 262176 | tf_op jit(solution)/shard_map/ppermute | solution.py:76
  46.4 0.4 fusion.8
  46.8 0.9 %fusion.84 = (bf16[4,256,128]{2,1,0:T(8,128)(2,1)S(1)}, f32[4,256,128]{2,1,0:T(8,128)S(1)}) fusion(f32[4,256,128]{2,1,0:T(8,128)S(1)} %fusion.8, f32[4,128,128]{2,1,0:T(8,128)S(1)} %get-tuple-element.9, f32[4,128,128]{2,1,0:T(8,128)S(1)} %get-tuple-element.8, f32[4,128,128]{2,1,0:T(8,128)S(1)} %convolution_negate_fusion), kind=kOutput, calls=%fused_computation.155 | convolution fusion | flops 202506240 | bytes 2097152 | tf_op jit(solution)/shard_map/hij,hiw->hjw/dot_general | solution.py:15
  47.7 1.0 %copy.71 = bf16[4,128,2,128]{3,0,2,1:T(4,128)(2,1)} copy(bf16[4,128,2,128]{3,2,1,0:T(2,128)(2,1)S(1)} %bitcast.141) | data formatting | bytes 524288 | tf_op jit(solution)/shard_map/convert_element_type | solution.py:163
  48.8 0.3 fusion.14
  49.0 0.8 %copy.30 = bf16[128,4,128]{2,1,0:T(4,128)(2,1)} copy(bf16[128,4,128]{2,0,1:T(8,128)(2,1)S(1)} %fusion.14) | data formatting | bytes 262144
  49.8 0.4 convolution_subtract_fusion.4
  50.2 0.3 fusion.2
  50.5 0.7 %fusion.29 = f32[4,256,128]{2,1,0:T(8,128)S(1)} fusion(f32[4,128,256]{2,1,0:T(8,128)S(1)} %fusion.2, f32[4,128]{1,0:T(4,128)S(1)} %get-tuple-element.11, bf16[128,4,128]{2,1,0:T(4,128)(2,1)S(1)} %copy-done.1), kind=kOutput, calls=%fused_computation.62 | convolution fusion | flops 100794368 | bytes 1181696 | tf_op jit(solution)/shard_map/hij,hid->hjd/dot_general | solution.py:15
  51.2 0.3 fusion.59
  51.5 0.5 fusion.33
  52.0 0.2 fusion.38
  52.2 0.8 %copy.31 = bf16[128,4,128]{2,1,0:T(4,128)(2,1)} copy(bf16[128,4,128]{2,0,1:T(8,128)(2,1)S(1)} %fusion.38) | data formatting | bytes 262144
  52.9 0.6 %fusion.1 = f32[4,256,256]{2,1,0:T(8,128)S(1)} fusion(f32[4,256,128]{2,1,0:T(8,128)S(1)} %get-tuple-element.19, f32[4,256,128]{2,1,0:T(8,128)S(1)} %convolution_subtract_fusion.4, pred[256,256]{1,0:T(8,128)(4,1)S(1)} %iota_compare_fusion.1), kind=kOutput, calls=%fused_computation.2 | convolution fusion | flops 201850880 | bytes 2162688 | tf_op jit(solution)/shard_map/hiw,hjw->hij/dot_general | solution.py:15
  53.6 0.6 fusion.88
  54.2 0.4 fusion.9
  54.5 0.4 fusion.7
  54.9 1.0 %convolution_add_fusion.3 = f32[4,256,128]{2,1,0:T(8,128)S(1)} fusion(f32[4,256,128]{2,1,0:T(8,128)S(1)} %fusion.7, f32[4,256,256]{2,1,0:T(8,128)S(1)} %fusion.1, f32[4,256,128]{2,1,0:T(8,128)S(1)} %broadcast_multiply_fusion), kind=kOutput, calls=%fused_computation.9 | convolution fusion | flops 201457664 | bytes 2621440 | tf_op jit(solution)/shard_map/hji,hjd->hid/dot_general | solution.py:15
  56.0 1.8 %fusion.11 = bf16[4,256,128]{2,1,0:T(8,128)(2,1)S(1)} fusion(f32[4,256,128]{2,1,0:T(8,128)S(1)} %convolution_add_fusion.3, f32[4,256,128]{2,1,0:T(8,128)S(1)} %broadcast_multiply_fusion, f32[4,256]{1,0:T(4,128)S(1)} %add_rsqrt_fusion), kind=kOutput, calls=%fused_computation.26 | output fusion | flops 656511 | bytes 1314816 | tf_op jit(solution)/shard_map/mul | solution.py:154
  57.8 1.0 %copy.72 = bf16[4,128,2,128]{3,0,2,1:T(4,128)(2,1)} copy(bf16[4,128,2,128]{3,2,1,0:T(2,128)(2,1)S(1)} %bitcast.138) | data formatting | bytes 524288 | tf_op jit(solution)/shard_map/convert_element_type | solution.py:163
  (23 shorter events, 0.3 us)
Async XLA Ops:
  0.6 15.1 %copy-start = (bf16[128,4,128]{2,1,0:T(4,128)(2,1)S(1)}, bf16[128,4,128]{2,1,0:T(4,128)(2,1)}, u32[]{:S(2)}) copy-start(bf16[128,4,128]{2,1,0:T(4,128)(2,1)} %param.7) | copy-start | bytes 393220
  0.6 1.3 %copy-start.2 = (bf16[128,2,4,128]{3,2,1,0:T(4,128)(2,1)S(1)}, bf16[128,2,4,128]{3,2,1,0:T(4,128)(2,1)}, u32[]{:S(2)}) copy-start(bf16[128,2,4,128]{3,2,1,0:T(4,128)(2,1)} %param.5) | copy-start | bytes 786436
  13.3 0.9 %copy-start.1 = (bf16[128,4,128]{2,1,0:T(4,128)(2,1)S(1)}, bf16[128,4,128]{2,1,0:T(4,128)(2,1)}, u32[]{:S(2)}) copy-start(bf16[128,4,128]{2,1,0:T(4,128)(2,1)} %param.4) | copy-start | bytes 393220
  15.8 1.6 %copy-start.3 = (bf16[128,2,4,128]{3,2,1,0:T(4,128)(2,1)S(1)}, bf16[128,2,4,128]{3,2,1,0:T(4,128)(2,1)}, u32[]{:S(2)}) copy-start(bf16[128,2,4,128]{3,2,1,0:T(4,128)(2,1)} %param.6) | copy-start | bytes 786436
  16.1 11.2 %collective-permute-start.3 = (f32[4,128,128]{2,1,0:T(8,128)S(1)}, f32[4,128,128]{2,1,0:T(8,128)S(1)}, u32[]{:S(2)}, u32[]{:S(2)}) collective-permute-start(f32[4,128,128]{2,1,0:T(8,128)S(1)} %fusion.54), channel_id=1, source_target_pairs={{4,0},{8,4},{12,8},{5,1},{9,5},{13,9},{6,2},{10,6},{14,10},{7,3},{... | collective-permute-start | bytes 786440 | tf_op jit(solution)/shard_map/ppermute | solution.py:76
  18.5 11.2 %collective-permute-start = (f32[4,128,128]{2,1,0:T(8,128)S(1)}, f32[4,128,128]{2,1,0:T(8,128)S(1)}, u32[]{:S(2)}, u32[]{:S(2)}) collective-permute-start(f32[4,128,128]{2,1,0:T(8,128)S(1)} %convolution_multiply_fusion.6), channel_id=1, source_target_pairs={{0,4},{4,8},{8,12},{1,5},{5,9},{9,13},{2,6},{6,10},{10,14},{3,7},{... | collective-permute-start | bytes 786440 | tf_op jit(solution)/shard_map/ppermute | solution.py:75
  28.0 9.4 %collective-permute-start.4 = (f32[4,128,128]{2,1,0:T(8,128)S(1)}, f32[4,128,128]{2,1,0:T(8,128)S(1)}, u32[]{:S(2)}, u32[]{:S(2)}) collective-permute-start(f32[4,128,128]{2,1,0:T(8,128)S(1)} %convolution_add_fusion.6), channel_id=1, source_target_pairs={{4,0},{8,4},{12,8},{5,1},{9,5},{13,9},{6,2},{10,6},{14,10},{7,3},{... | collective-permute-start | bytes 786440 | tf_op jit(solution)/shard_map/ppermute | solution.py:76
  30.1 9.3 %collective-permute-start.1 = (f32[4,128,128]{2,1,0:T(8,128)S(1)}, f32[4,128,128]{2,1,0:T(8,128)S(1)}, u32[]{:S(2)}, u32[]{:S(2)}) collective-permute-start(f32[4,128,128]{2,1,0:T(8,128)S(1)} %convolution_add_fusion.9), channel_id=1, source_target_pairs={{0,4},{4,8},{8,12},{1,5},{5,9},{9,13},{2,6},{6,10},{10,14},{3,7},{... | collective-permute-start | bytes 786440 | tf_op jit(solution)/shard_map/ppermute | solution.py:75
  38.0 8.5 %collective-permute-start.5 = (f32[4,128,128]{2,1,0:T(8,128)S(1)}, f32[4,128,128]{2,1,0:T(8,128)S(1)}, u32[]{:S(2)}, u32[]{:S(2)}) collective-permute-start(f32[4,128,128]{2,1,0:T(8,128)S(1)} %convolution_add_fusion.5), channel_id=1, source_target_pairs={{4,0},{8,4},{12,8},{5,1},{9,5},{13,9},{6,2},{10,6},{14,10},{7,3},{... | collective-permute-start | bytes 786440 | tf_op jit(solution)/shard_map/ppermute | solution.py:76
  39.8 8.9 %collective-permute-start.2 = (f32[4,128,128]{2,1,0:T(8,128)S(1)}, f32[4,128,128]{2,1,0:T(8,128)S(1)}, u32[]{:S(2)}, u32[]{:S(2)}) collective-permute-start(f32[4,128,128]{2,1,0:T(8,128)S(1)} %convolution_add_fusion.8), channel_id=1, source_target_pairs={{0,4},{4,8},{8,12},{1,5},{5,9},{9,13},{2,6},{6,10},{10,14},{3,7},{... | collective-permute-start | bytes 786440 | tf_op jit(solution)/shard_map/ppermute | solution.py:75

commit v10 on v7

--- a/solution.py
+++ b/solution.py
@@ -110,17 +110,20 @@
     kn, k_scale = unit_rows(k_raw)
 
     inverse = tri_inverse(kn)
-    proj = mh("hij,hjd->hid", inverse, kn)
-    upd_v = mh("hij,hjd->hid", inverse, vals)
+    solved = mh("hij,hjd->hid", inverse, jnp.concatenate([kn, vals], axis=2))
+    proj = solved[:, :, :head_size]
+    upd_v = solved[:, :, head_size:]
     tok_ids = lax.broadcasted_iota(jnp.int32, (tok_count, rows), 0)
     sub_ids = lax.broadcasted_iota(jnp.int32, (tok_count, rows), 1)
     visible = sub_ids <= 2 * tok_ids + 1
     scores = jnp.where(visible, 2.0 * mh("hid,hjd->hij", qn, kn), 0.0)
-    read_map = qn - mh("hij,hjd->hid", scores, proj)
-    own_out = mh("hij,hjd->hid", scores, upd_v)
+    seen = mh("hij,hjd->hid", scores, solved)
+    read_map = qn - seen[:, :, :head_size]
+    own_out = seen[:, :, head_size:]
     eye = jnp.eye(head_size, dtype=jnp.float32)
-    transition = eye - 2.0 * mh("hjd,hjw->hdw", kn, proj)
-    offset = 2.0 * mh("hjd,hjw->hdw", kn, upd_v)
+    moved = 2.0 * mh("hjd,hjw->hdw", kn, solved)
+    transition = eye - moved[:, :, :head_size]
+    offset = moved[:, :, head_size:]
     local_cot = mh("hld,hlw->hdw", read_map, cot)
 
     state_in, end_cot = scan_seq(transition, offset, local_cot)
@@ -136,8 +139,7 @@
         2.0 * mh("hij,hid->hjd", touch, qn)
         + 2.0 * mh("hjw,hdw->hjd", updates, end_cot)
         - mh("hjw,hdw->hjd", d_w, state_in)
-        + mh("hij,hjd->hid", gram_cot, kn)
-        + mh("hji,hjd->hid", gram_cot, kn)
+        + mh("hij,hjd->hid", gram_cot + gram_cot.transpose(0, 2, 1), kn)
     )
     d_q = q_scale * (d_qn - jnp.sum(qn * d_qn, axis=-1, keepdims=True) * qn)
     d_k = k_scale * (d_kn - jnp.sum(kn * d_kn, axis=-1, keepdims=True) * kn)

time: 58.7 us -> 64.6 us (1.10)
  waiting for transfers between devices: 7.43 us -> 10.9 us
  local copies, waits for them, and re-layouts: 5.45 us -> 6.78 us
  other arithmetic: 3.12 us -> 3.8 us
    ppermute x3, waiting for transfers between devices: 2.1 us -> 4.31 us  [chain_seq(): got_sum = lax.ppermute(fwd_sum, 'seq', right)]
    ppermute x3, waiting for transfers between devices: 5.33 us -> 6.55 us  [chain_seq(): got_cot = lax.ppermute(bwd_sum, 'seq', left)]
    unnamed x8 -> x18, local copies, waits for them, and re-layouts: 2.02 us -> 2.8 us
    gt x2, other arithmetic: 0.03 us -> 0.71 us  [strict_lower(): lax.broadcasted_iota(jnp.int32, (rows, cols), 0)]
    dot_general x22 -> x18, matrix products: 10.9 us -> 11.2 us  [mh(): return jnp.einsum(spec, *operands, precision=lax.Precision.HIGH)]
  transfers between devices with their start and end apart: 6 -> 6, of which waited for: 6 -> 6; matrix products, arithmetic and copies ran while one was open for 16% -> 9% of each run, Pallas kernels for 0% -> 0%
where the time goes in v10:
time: 64.6 us; the launch traced here: 64.2 us
  matrix products  23.8 us (37%)
  starting transfers between devices  17.8 us (28%)
  waiting for transfers between devices  10.9 us (17%)
  local copies, waits for them, and re-layouts  6.78 us (10%)
  other arithmetic  3.8 us (6%)
  between operations  1.2 us (2%)
    ppermute x3, starting transfers between devices, chain_seq(): got_sum = lax.ppermute(fwd_sum, 'seq', right)  13.9 us
    dot_general x23, matrix products, mm(): return jnp.einsum(spec, *operands, precision=highest)  12.6 us
    dot_general x18, matrix products, mh(): return jnp.einsum(spec, *operands, precision=lax.Precision.HIGH)  11.2 us
    ppermute x3, waiting for transfers between devices, chain_seq(): got_cot = lax.ppermute(bwd_sum, 'seq', left)  6.55 us
    ppermute x3, waiting for transfers between devices, chain_seq(): got_sum = lax.ppermute(fwd_sum, 'seq', right)  4.31 us
    ppermute x3, starting transfers between devices, chain_seq(): got_cot = lax.ppermute(bwd_sum, 'seq', left)  3.88 us
    unnamed x18, local copies, waits for them, and re-layouts  2.8 us
    convert_element_type x2, local copies, waits for them, and re-layouts, pair_major(): return tensor.reshape(heads_here, tok_count, 2, head_size).transpose(1, 2...  2.09 us
  transfers between devices with their start and end apart: 6, of which 6 were waited for; matrix products, arithmetic and copies ran while one was open for 9% of the time, Pallas kernels for 0%

profile of v10, /device:TPU:0, one launch (start us, length us, event | category | flops | bytes accessed | tf_op | source)
XLA Modules:
  0.0 64.2 jit_solution(13115431338443452809)
XLA Ops:
  0.7 1.2 %copy.9 = f32[128,2,4,128]{3,1,0,2:T(2,128)S(1)} copy(bf16[128,2,4,128]{3,2,1,0:T(4,128)(2,1)} %param.5) | data formatting | bytes 786432 | tf_op jit(solution)/shard_map/transpose | solution.py:107
  2.3 0.5 convolution_multiply_fusion.8
  2.8 0.5 convolution_multiply_fusion.7
  3.4 0.5 convolution_multiply_fusion.6
  3.9 0.7 %convolution_multiply_fusion.5 = f32[4,128,128]{2,1,0:T(8,128)S(1)} fusion(f32[4,1,2,128,128]{4,3,2,0,1:T(8,128)S(1)} %bitcast.197), kind=kOutput, calls=%fused_computation.30 | convolution fusion | flops 100728832 | bytes 786432 | tf_op jit(solution)/shard_map/hpid,hpjd->hpij/dot_general | solution.py:11
  4.6 0.9 %fusion.2 = f32[4,16,16,16]{3,2,1,0:T(8,128)S(1)} fusion(f32[4,16,16,128]{3,2,1,0:T(8,128)S(1)} %bitcast.198, pred[16,16]{1,0:T(8,128)(4,1)S(1)} %iota_compare_fusion.8), kind=kOutput, calls=%fused_computation.9 | convolution fusion | flops 25198592 | bytes 590080 | tf_op jit(solution)/shard_map/hpid,hpjd->hpij/dot_general | solution.py:11
  5.5 0.7 %fusion.91 = f32[4,16,16,16]{3,2,1,0:T(8,128)S(1)} fusion(f32[4,16,16,16]{3,2,1,0:T(8,128)S(1)} %fusion.2), kind=kOutput, calls=%fused_computation.154 | convolution fusion | flops 3145728 | bytes 131072 | tf_op jit(solution)/shard_map/hpij,hpjk->hpik/dot_general | solution.py:11
  6.2 0.7 %fusion.92 = f32[4,16,16,16]{3,2,1,0:T(8,128)S(1)} fusion(f32[4,16,16,16]{3,2,1,0:T(8,128)S(1)} %fusion.91), kind=kOutput, calls=%fused_computation.155 | convolution fusion | flops 3145728 | bytes 131072 | tf_op jit(solution)/shard_map/hpij,hpjk->hpik/dot_general | solution.py:11
  6.8 0.7 %convolution_add_fusion.2 = f32[4,16,16,16]{3,2,1,0:T(8,128)S(1)} fusion(f32[4,16,16,16]{3,2,1,0:T(8,128)S(1)} %fusion.91, f32[4,16,16,16]{3,2,1,0:T(8,128)S(1)} %fusion.2, f32[16,16]{1,0:T(8,128)S(1)} %fusion.78), kind=kOutput, calls=%fused_computation.4 | convolution fusion | flops 3178496 | bytes 197632 | tf_op jit(solution)/shard_map/hpij,hpjk->hpik/dot_general | solution.py:11
  7.5 0.6 fusion.93
  8.2 0.6 convolution_add_fusion.1
  8.8 0.6 convolution_add_fusion
  9.5 0.4 fusion.87
  9.9 0.4 convolution_negate_fusion.3
  10.5 0.4 fusion.88
  10.9 0.4 convolution_negate_fusion.2
  11.4 0.4 fusion.89
  11.8 0.4 convolution_negate_fusion.1
  12.4 0.6 fusion.50
  13.0 0.7 %fusion.11 = f32[4,1,128,128]{3,2,0,1:T(8,128)S(1)} fusion(f32[4,128,128]{1,2,0:T(8,128)S(1)} %fusion.50, f32[4,1,2,128,128]{4,3,2,0,1:T(8,128)S(1)} %fusion.31), kind=kOutput, calls=%fused_computation.29 | convolution fusion | flops 100728832 | bytes 786432 | tf_op jit(solution)/shard_map/hpij,hpjk->hpik/dot_general | solution.py:11
  13.7 0.3 copy-done.7
  14.2 0.7 %fusion.15 = f32[4,256,256]{2,1,0:T(8,128)S(1)} fusion(f32[4,256,128]{2,1,0:T(8,128)S(1)} %bitcast.211, f32[4,256,128]{2,1,0:T(8,128)S(1)} %broadcast_multiply_fusion, f32[4,1,128,128]{3,2,0,1:T(8,128)S(1)} %get-tuple-element.9, f32[4,1,128,128]{3,2,0,1:T(8,128)S(1)} %get-tuple-element.8, f32[4,1,128,128]{3,2,0,1:T(8,128)S(1)} %fusion.11), kind=kOutput, calls=%fused_computation.43 | convolution fusion | flops 403963904 | bytes 2883584 | tf_op jit(solution)/shard_map/hij,hjd->hid/dot_general | solution.py:15
  14.8 0.8 %convolution_multiply_fusion.1 = f32[4,128,256]{2,1,0:T(8,128)S(1)} fusion(f32[4,256,128]{2,1,0:T(8,128)S(1)} %broadcast_multiply_fusion, f32[4,256,256]{2,1,0:T(8,128)S(1)} %fusion.15), kind=kOutput, calls=%fused_computation.5 | convolution fusion | flops 201457664 | bytes 2097152 | tf_op jit(solution)/shard_map/hjd,hjw->hdw/dot_general | solution.py:15
  15.7 5.1 %collective-permute-start = (f32[4,128,128]{2,1,0:T(8,128)S(1)}, f32[4,128,128]{2,1,0:T(8,128)S(1)}, u32[]{:S(2)}, u32[]{:S(2)}) collective-permute-start(f32[4,128,128]{2,1,0:T(8,128)S(1)} %slice.106), channel_id=1, source_target_pairs={{0,4},{4,8},{8,12},{1,5},{5,9},{9,13},{2,6},{6,10},{10,14},{3,7},{... | collective-permute-start | bytes 786440 | tf_op jit(solution)/shard_map/ppermute | solution.py:64
  21.1 0.4 fusion.9
  21.5 0.5 fusion.94
  22.0 0.4 fusion.56
  22.4 1.3 %collective-permute-start.3 = (f32[4,128,128]{2,1,0:T(8,128)S(1)}, f32[4,128,128]{2,1,0:T(8,128)S(1)}, u32[]{:S(2)}, u32[]{:S(2)}) collective-permute-start(f32[4,128,128]{2,1,0:T(8,128)S(1)} %fusion.56), channel_id=1, source_target_pairs={{4,0},{8,4},{12,8},{5,1},{9,5},{13,9},{6,2},{10,6},{14,10},{7,3},{... | collective-permute-start | bytes 786440 | tf_op jit(solution)/shard_map/ppermute | solution.py:65
  23.8 2.6 %collective-permute-done = f32[4,128,128]{2,1,0:T(8,128)S(1)} collective-permute-done((f32[4,128,128]{2,1,0:T(8,128)S(1)}, f32[4,128,128]{2,1,0:T(8,128)S(1)}, u32[]{:S(2)}, u32[]{:S(2)}) %collective-permute-start) | collective-permute-done | bytes 262176 | tf_op jit(solution)/shard_map/ppermute | solution.py:64
  26.3 0.4 convolution_add_fusion.8
  26.7 4.4 %collective-permute-start.1 = (f32[4,128,128]{2,1,0:T(8,128)S(1)}, f32[4,128,128]{2,1,0:T(8,128)S(1)}, u32[]{:S(2)}, u32[]{:S(2)}) collective-permute-start(f32[4,128,128]{2,1,0:T(8,128)S(1)} %convolution_add_fusion.8), channel_id=1, source_target_pairs={{0,4},{4,8},{8,12},{1,5},{5,9},{9,13},{2,6},{6,10},{10,14},{3,7},{... | collective-permute-start | bytes 786440 | tf_op jit(solution)/shard_map/ppermute | solution.py:64
  31.1 1.0 %collective-permute-done.3 = f32[4,128,128]{2,1,0:T(8,128)S(1)} collective-permute-done((f32[4,128,128]{2,1,0:T(8,128)S(1)}, f32[4,128,128]{2,1,0:T(8,128)S(1)}, u32[]{:S(2)}, u32[]{:S(2)}) %collective-permute-start.3) | collective-permute-done | bytes 262176 | tf_op jit(solution)/shard_map/ppermute | solution.py:65
  32.1 0.6 convolution_add_fusion.5
  32.7 1.3 %collective-permute-start.4 = (f32[4,128,128]{2,1,0:T(8,128)S(1)}, f32[4,128,128]{2,1,0:T(8,128)S(1)}, u32[]{:S(2)}, u32[]{:S(2)}) collective-permute-start(f32[4,128,128]{2,1,0:T(8,128)S(1)} %convolution_add_fusion.5), channel_id=1, source_target_pairs={{4,0},{8,4},{12,8},{5,1},{9,5},{13,9},{6,2},{10,6},{14,10},{7,3},{... | collective-permute-start | bytes 786440 | tf_op jit(solution)/shard_map/ppermute | solution.py:65
  34.0 0.5 fusion.69
  34.5 1.3 %collective-permute-done.1 = f32[4,128,128]{2,1,0:T(8,128)S(1)} collective-permute-done((f32[4,128,128]{2,1,0:T(8,128)S(1)}, f32[4,128,128]{2,1,0:T(8,128)S(1)}, u32[]{:S(2)}, u32[]{:S(2)}) %collective-permute-start.1) | collective-permute-done | bytes 262176 | tf_op jit(solution)/shard_map/ppermute | solution.py:64
  35.8 0.4 convolution_add_fusion.7
  36.2 4.4 %collective-permute-start.2 = (f32[4,128,128]{2,1,0:T(8,128)S(1)}, f32[4,128,128]{2,1,0:T(8,128)S(1)}, u32[]{:S(2)}, u32[]{:S(2)}) collective-permute-start(f32[4,128,128]{2,1,0:T(8,128)S(1)} %convolution_add_fusion.7), channel_id=1, source_target_pairs={{0,4},{4,8},{8,12},{1,5},{5,9},{9,13},{2,6},{6,10},{10,14},{3,7},{... | collective-permute-start | bytes 786440 | tf_op jit(solution)/shard_map/ppermute | solution.py:64
  40.6 0.8 %collective-permute-done.4 = f32[4,128,128]{2,1,0:T(8,128)S(1)} collective-permute-done((f32[4,128,128]{2,1,0:T(8,128)S(1)}, f32[4,128,128]{2,1,0:T(8,128)S(1)}, u32[]{:S(2)}, u32[]{:S(2)}) %collective-permute-start.4) | collective-permute-done | bytes 262176 | tf_op jit(solution)/shard_map/ppermute | solution.py:65
  41.5 0.6 convolution_add_fusion.4
  42.1 1.3 %collective-permute-start.5 = (f32[4,128,128]{2,1,0:T(8,128)S(1)}, f32[4,128,128]{2,1,0:T(8,128)S(1)}, u32[]{:S(2)}, u32[]{:S(2)}) collective-permute-start(f32[4,128,128]{2,1,0:T(8,128)S(1)} %convolution_add_fusion.4), channel_id=1, source_target_pairs={{4,0},{8,4},{12,8},{5,1},{9,5},{13,9},{6,2},{10,6},{14,10},{7,3},{... | collective-permute-start | bytes 786440 | tf_op jit(solution)/shard_map/ppermute | solution.py:65
  43.4 0.7 %iota_compare_fusion.4 = (pred[256,256]{0,1:T(8,128)(4,1)}, pred[256,256]{0,1:T(8,128)(4,1)}) fusion(), kind=kLoop, calls=%fused_computation.106 | loop fusion | flops 131072 | bytes 131072 | tf_op jit(solution)/shard_map/gt | solution.py:24
  44.1 0.4 collective-permute-done.2
  44.5 0.3 fusion.13
  44.8 0.8 %copy.36 = bf16[128,4,128]{2,1,0:T(4,128)(2,1)} copy(bf16[128,4,128]{2,0,1:T(8,128)(2,1)S(1)} %fusion.13) | data formatting | bytes 262144
  45.6 4.8 %collective-permute-done.5 = f32[4,128,128]{2,1,0:T(8,128)S(1)} collective-permute-done((f32[4,128,128]{2,1,0:T(8,128)S(1)}, f32[4,128,128]{2,1,0:T(8,128)S(1)}, u32[]{:S(2)}, u32[]{:S(2)}) %collective-permute-start.5) | collective-permute-done | bytes 262176 | tf_op jit(solution)/shard_map/ppermute | solution.py:65
  50.3 0.4 fusion.7
  50.7 0.3 copy-done.5
  51.0 0.9 %fusion.90 = (bf16[4,256,128]{2,1,0:T(8,128)(2,1)S(1)}, f32[4,256,128]{2,1,0:T(8,128)S(1)}) fusion(f32[4,256,128]{2,1,0:T(8,128)S(1)} %fusion.7, f32[4,1,128,128]{3,2,0,1:T(8,128)S(1)} %get-tuple-element.9, f32[4,1,128,128]{3,2,0,1:T(8,128)S(1)} %get-tuple-element.8, f32[4,1,128,128]{3,2,0,1:T(8,128)S(1)} %fusion.11), kind=kOutput, calls=%fused_computation.153 | convolution fusion | flops 202506240 | bytes 2097152 | tf_op jit(solution)/shard_map/hij,hiw->hjw/dot_general | solution.py:15
  51.9 1.0 %copy.85 = bf16[4,128,2,128]{3,0,2,1:T(4,128)(2,1)} copy(bf16[4,128,2,128]{3,2,1,0:T(2,128)(2,1)S(1)} %bitcast.214) | data formatting | bytes 524288 | tf_op jit(solution)/shard_map/convert_element_type | solution.py:154
  53.0 0.4 convolution_subtract_fusion.1
  53.4 0.3 fusion.1
  53.7 1.5 %fusion.39 = f32[4,256,128]{2,1,0:T(8,128)} fusion(f32[4,128,256]{2,1,0:T(8,128)S(1)} %fusion.1, f32[4,128]{1,0:T(4,128)S(1)} %get-tuple-element.17, bf16[128,4,128]{2,1,0:T(4,128)(2,1)S(1)} %copy-done.1), kind=kOutput, calls=%fused_computation.75 | convolution fusion | flops 100794368 | bytes 1181696 | tf_op jit(solution)/shard_map/hij,hid->hjd/dot_general | solution.py:15
  55.2 0.3 fusion.71
  55.5 0.5 fusion.44
  56.2 0.8 %copy.37 = bf16[128,4,128]{2,1,0:T(4,128)(2,1)} copy(bf16[128,4,128]{2,0,1:T(8,128)(2,1)S(1)} %fusion.49) | data formatting | bytes 262144
  56.9 0.6 convolution_multiply_fusion
  57.5 0.3 copy.32
  57.9 2.0 %fusion.20 = f32[4,256,128]{2,1,0:T(8,128)S(1)} fusion(f32[4,256,128]{2,1,0:T(8,128)S(1)} %broadcast_multiply_fusion, f32[4,256,256]{2,1,0:T(8,128)S(1)} %convolution_multiply_fusion, f32[4,256,256]{1,2,0:T(8,128)S(1)} %copy.32, pred[256,256]{0,1:T(8,128)(4,1)} %get-tuple-element.22, pred[256,256]{0,1:T(8,128)(4,1)} %get-tuple-element.23), kind=kOutput, calls=%fused_computation.49 | convolution fusion | flops 202113024 | bytes 3276800 | tf_op jit(solution)/shard_map/hij,hjd->hid/dot_general | solution.py:15
  59.9 0.4 fusion.8
  60.3 0.6 copy-done.4
  61.0 0.4 fusion.6
  61.4 1.8 %fusion.10 = bf16[4,256,128]{2,1,0:T(8,128)(2,1)S(1)} fusion(f32[4,256,128]{2,1,0:T(8,128)S(1)} %fusion.6, f32[4,256,128]{2,1,0:T(8,128)S(1)} %broadcast_multiply_fusion, f32[4,256]{1,0:T(4,128)S(1)} %add_rsqrt_fusion), kind=kOutput, calls=%fused_computation.22 | output fusion | flops 656511 | bytes 1314816 | tf_op jit(solution)/shard_map/mul | solution.py:145
  63.2 1.0 %copy.86 = bf16[4,128,2,128]{3,0,2,1:T(4,128)(2,1)} copy(bf16[4,128,2,128]{3,2,1,0:T(2,128)(2,1)S(1)} %bitcast.210) | data formatting | bytes 524288 | tf_op jit(solution)/shard_map/convert_element_type | solution.py:154
  (33 shorter events, 1.7 us)
Async XLA Ops:
  0.6 21.4 %copy-start = (bf16[128,4,128]{2,1,0:T(4,128)(2,1)S(1)}, bf16[128,4,128]{2,1,0:T(4,128)(2,1)}, u32[]{:S(2)}) copy-start(bf16[128,4,128]{2,1,0:T(4,128)(2,1)} %param.7) | copy-start | bytes 393220
  13.0 1.0 %copy-start.7 = (bf16[128,2,4,128]{3,2,1,0:T(4,128)(2,1)S(1)}, bf16[128,2,4,128]{3,2,1,0:T(4,128)(2,1)}, u32[]{:S(2)}) copy-start(bf16[128,2,4,128]{3,2,1,0:T(4,128)(2,1)} %param.6) | copy-start | bytes 786436
  15.7 5.1 %copy-start.1 = (bf16[128,4,128]{2,1,0:T(4,128)(2,1)S(1)}, bf16[128,4,128]{2,1,0:T(4,128)(2,1)}, u32[]{:S(2)}) copy-start(bf16[128,4,128]{2,1,0:T(4,128)(2,1)} %param.4) | copy-start | bytes 393220
  15.7 10.6 %collective-permute-start = (f32[4,128,128]{2,1,0:T(8,128)S(1)}, f32[4,128,128]{2,1,0:T(8,128)S(1)}, u32[]{:S(2)}, u32[]{:S(2)}) collective-permute-start(f32[4,128,128]{2,1,0:T(8,128)S(1)} %slice.106), channel_id=1, source_target_pairs={{0,4},{4,8},{8,12},{1,5},{5,9},{9,13},{2,6},{6,10},{10,14},{3,7},{... | collective-permute-start | bytes 786440 | tf_op jit(solution)/shard_map/ppermute | solution.py:64
  22.4 9.7 %collective-permute-start.3 = (f32[4,128,128]{2,1,0:T(8,128)S(1)}, f32[4,128,128]{2,1,0:T(8,128)S(1)}, u32[]{:S(2)}, u32[]{:S(2)}) collective-permute-start(f32[4,128,128]{2,1,0:T(8,128)S(1)} %fusion.56), channel_id=1, source_target_pairs={{4,0},{8,4},{12,8},{5,1},{9,5},{13,9},{6,2},{10,6},{14,10},{7,3},{... | collective-permute-start | bytes 786440 | tf_op jit(solution)/shard_map/ppermute | solution.py:65
  26.7 9.1 %collective-permute-start.1 = (f32[4,128,128]{2,1,0:T(8,128)S(1)}, f32[4,128,128]{2,1,0:T(8,128)S(1)}, u32[]{:S(2)}, u32[]{:S(2)}) collective-permute-start(f32[4,128,128]{2,1,0:T(8,128)S(1)} %convolution_add_fusion.8), channel_id=1, source_target_pairs={{0,4},{4,8},{8,12},{1,5},{5,9},{9,13},{2,6},{6,10},{10,14},{3,7},{... | collective-permute-start | bytes 786440 | tf_op jit(solution)/shard_map/ppermute | solution.py:64
  32.7 8.7 %collective-permute-start.4 = (f32[4,128,128]{2,1,0:T(8,128)S(1)}, f32[4,128,128]{2,1,0:T(8,128)S(1)}, u32[]{:S(2)}, u32[]{:S(2)}) collective-permute-start(f32[4,128,128]{2,1,0:T(8,128)S(1)} %convolution_add_fusion.5), channel_id=1, source_target_pairs={{4,0},{8,4},{12,8},{5,1},{9,5},{13,9},{6,2},{10,6},{14,10},{7,3},{... | collective-permute-start | bytes 786440 | tf_op jit(solution)/shard_map/ppermute | solution.py:65
  36.2 8.3 %collective-permute-start.2 = (f32[4,128,128]{2,1,0:T(8,128)S(1)}, f32[4,128,128]{2,1,0:T(8,128)S(1)}, u32[]{:S(2)}, u32[]{:S(2)}) collective-permute-start(f32[4,128,128]{2,1,0:T(8,128)S(1)} %convolution_add_fusion.7), channel_id=1, source_target_pairs={{0,4},{4,8},{8,12},{1,5},{5,9},{9,13},{2,6},{6,10},{10,14},{3,7},{... | collective-permute-start | bytes 786440 | tf_op jit(solution)/shard_map/ppermute | solution.py:64
  42.1 8.3 %collective-permute-start.5 = (f32[4,128,128]{2,1,0:T(8,128)S(1)}, f32[4,128,128]{2,1,0:T(8,128)S(1)}, u32[]{:S(2)}, u32[]{:S(2)}) collective-permute-start(f32[4,128,128]{2,1,0:T(8,128)S(1)} %convolution_add_fusion.4), channel_id=1, source_target_pairs={{4,0},{8,4},{12,8},{5,1},{9,5},{13,9},{6,2},{10,6},{14,10},{7,3},{... | collective-permute-start | bytes 786440 | tf_op jit(solution)/shard_map/ppermute | solution.py:65
  50.3 0.7 %copy-start.5 = (f32[4,128,128]{2,1,0:T(8,128)}, f32[4,128,128]{2,1,0:T(8,128)S(1)}, u32[]{:S(2)}) copy-start(f32[4,128,128]{2,1,0:T(8,128)S(1)} %collective-permute-done.5) | copy-start | bytes 786436
  51.9 5.0 %copy-start.3 = (f32[4,256,128]{2,1,0:T(8,128)}, f32[4,256,128]{2,1,0:T(8,128)S(1)}, u32[]{:S(2)}) copy-start(f32[4,256,128]{2,1,0:T(8,128)S(1)} %get-tuple-element.21) | copy-start | bytes 1572868
  57.8 2.1 %copy-start.2 = (f32[4,256,128]{2,1,0:T(8,128)S(1)}, f32[4,256,128]{2,1,0:T(8,128)}, u32[]{:S(2)}) copy-start(f32[4,256,128]{2,1,0:T(8,128)} %fusion.39) | copy-start | bytes 1572868
  57.8 2.1 %copy-start.6 = (f32[4,128,128]{2,1,0:T(8,128)S(1)}, f32[4,128,128]{2,1,0:T(8,128)}, u32[]{:S(2)}) copy-start(f32[4,128,128]{2,1,0:T(8,128)} %copy-done.5) | copy-start | bytes 786436
  59.9 1.0 %copy-start.4 = (f32[4,256,128]{2,1,0:T(8,128)S(1)}, f32[4,256,128]{2,1,0:T(8,128)}, u32[]{:S(2)}) copy-start(f32[4,256,128]{2,1,0:T(8,128)} %copy-done.3) | copy-start | bytes 1572868

commit v11 on v7

--- a/solution.py
+++ b/solution.py
@@ -1,6 +1,7 @@
 import jax
 import jax.numpy as jnp
 from jax import lax
+from jax.experimental import pallas as pl
 from jax.sharding import PartitionSpec as P
 
 highest = lax.Precision.HIGHEST
@@ -26,33 +27,61 @@
     )
 
 
+TILE = 128
+
+
+def dot(left, right, t_right=False):
+    dims = (((1,), (1 if t_right else 0,)), ((), ()))
+    return lax.dot_general(left, right, dims, precision=highest, preferred_element_type=jnp.float32)
+
+
+def inverse_kernel(k_ref, inv_ref):
+    heads, rows, size = k_ref.shape
+    tiles = rows // TILE
+    row = lax.broadcasted_iota(jnp.int32, (TILE, TILE), 0)
+    col = lax.broadcasted_iota(jnp.int32, (TILE, TILE), 1)
+    eye = jnp.where(row == col, 1.0, 0.0).astype(jnp.float32)
+    chains = [(h, t) for h in range(heads) for t in range(tiles)]
+    keys = {(h, t): k_ref[h, t * TILE:(t + 1) * TILE, :] for h, t in chains}
+    link = {c: jnp.where(row > col, 2.0 * dot(keys[c], keys[c], t_right=True), 0.0) for c in chains}
+    power = {c: jnp.where(row // LEAF == col // LEAF, -link[c], 0.0) for c in chains}
+    inverse = {c: eye + power[c] for c in chains}
+    reach = 2
+    while reach < LEAF:
+        power = {c: dot(power[c], power[c]) for c in chains}
+        inverse = {c: inverse[c] + dot(inverse[c], power[c]) for c in chains}
+        reach *= 2
+    span = LEAF
+    while span < TILE:
+        cross = (row // (2 * span) == col // (2 * span)) & (row // span != col // span)
+        inner = {c: dot(jnp.where(cross, link[c], 0.0), inverse[c]) for c in chains}
+        inverse = {c: inverse[c] - dot(inverse[c], inner[c]) for c in chains}
+        span *= 2
+    blocks = {}
+    for h in range(heads):
+        for t in range(tiles):
+            blocks[h, t, t] = inverse[h, t]
+    for i in range(tiles):
+        for j in range(i - 1, -1, -1):
+            for h in range(heads):
+                acc = None
+                for m in range(j, i):
+                    term = dot(2.0 * dot(keys[h, i], keys[h, m], t_right=True), blocks[h, m, j])
+                    acc = term if acc is None else acc + term
+                blocks[h, i, j] = -dot(blocks[h, i, i], acc)
+    zero = jnp.zeros((TILE, TILE), jnp.float32)
+    for h in range(heads):
+        for i in range(tiles):
+            for j in range(tiles):
+                inv_ref[h, i * TILE:(i + 1) * TILE, j * TILE:(j + 1) * TILE] = blocks.get((h, i, j), zero)
+
+
 def tri_inverse(keys):
     heads, rows, size = keys.shape
-    leaves = rows // LEAF
-    leaf_keys = keys.reshape(heads, leaves, LEAF, size)
-    gram = mm("hpid,hpjd->hpij", leaf_keys, leaf_keys)
-    power = jnp.where(strict_lower(LEAF, LEAF), -2.0 * gram, 0.0)
-    eye = jnp.eye(LEAF, dtype=jnp.float32)
-    inverse = eye + power
-    reach = 2
-    while reach < LEAF:
-        power = mm("hpij,hpjk->hpik", power, power)
-        inverse = inverse + mm("hpij,hpjk->hpik", inverse, power)
-        reach *= 2
-    span = LEAF
-    while span < rows:
-        pairs = rows // (2 * span)
-        blocks = inverse.reshape(heads, pairs, 2, span, span)
-        upper_inv = blocks[:, :, 0]
-        lower_inv = blocks[:, :, 1]
-        halves = keys.reshape(heads, pairs, 2, span, size)
-        link = 2.0 * mm("hpid,hpjd->hpij", halves[:, :, 1], halves[:, :, 0])
-        corner = -mm("hpij,hpjk->hpik", lower_inv, mm("hpij,hpjk->hpik", link, upper_inv))
-        top = jnp.concatenate([upper_inv, jnp.zeros_like(upper_inv)], axis=3)
-        bottom = jnp.concatenate([corner, lower_inv], axis=3)
-        inverse = jnp.concatenate([top, bottom], axis=2)
-        span *= 2
-    return inverse.reshape(heads, rows, rows)
+    return pl.pallas_call(
+        inverse_kernel,
+        out_shape=jax.ShapeDtypeStruct((heads, rows, rows), jnp.float32),
+    )(keys)
 
 
 def chain_seq(transition, offset, local_cot):

time: 58.7 us -> 59.9 us (1.020)
  Pallas kernels: 0 us -> 10.6 us
  matrix products: 23.5 us -> 14.4 us
    pallas_call x0 -> x1, Pallas kernels: none -> 10.6 us  [tri_inverse(): pl.pallas_call(inverse_kernel, out_shape=jax.ShapeDtypeStruct((heads, row...]
    dot_general x23 -> x4, matrix products: 12.6 us -> 1.99 us  [mm(): return jnp.einsum(spec, *operands, precision=highest)]
    dot_general x22, matrix products: 10.9 us -> 12.4 us  [mh(): return jnp.einsum(spec, *operands, precision=lax.Precision.HIGH)]
    mul x1, other arithmetic: 0.2 us -> 1 us  [unit_rows(): return (tensor * scale, scale)]
    unnamed x8 -> x12, local copies, waits for them, and re-layouts: 2.02 us -> 1.75 us
where the time goes in v11:
time: 59.9 us; the launch traced here: 59.6 us
  starting transfers between devices  17.8 us (30%)
  matrix products  14.4 us (24%)
  Pallas kernels  10.6 us (18%)
  waiting for transfers between devices  7.26 us (12%)
  local copies, waits for them, and re-layouts  5.03 us (8%)
  other arithmetic  3.49 us (6%)
  between operations  0.98 us (2%)
    ppermute x3, starting transfers between devices, chain_seq(): got_sum = lax.ppermute(fwd_sum, 'seq', right)  13.7 us
    dot_general x22, matrix products, mh(): return jnp.einsum(spec, *operands, precision=lax.Precision.HIGH)  12.4 us
    pallas_call x1, Pallas kernels, tri_inverse(): pl.pallas_call(inverse_kernel, out_shape=jax.ShapeDtypeStruct((heads, row...  10.6 us
    ppermute x3, waiting for transfers between devices, chain_seq(): got_cot = lax.ppermute(bwd_sum, 'seq', left)  4.83 us
    ppermute x3, starting transfers between devices, chain_seq(): got_cot = lax.ppermute(bwd_sum, 'seq', left)  4.06 us
    ppermute x3, waiting for transfers between devices, chain_seq(): got_sum = lax.ppermute(fwd_sum, 'seq', right)  2.43 us
    convert_element_type x2, local copies, waits for them, and re-layouts, pair_major(): return tensor.reshape(heads_here, tok_count, 2, head_size).transpose(1, 2...  2.09 us
    dot_general x4, matrix products, mm(): return jnp.einsum(spec, *operands, precision=highest)  1.99 us
  transfers between devices with their start and end apart: 6, of which 6 were waited for; matrix products, arithmetic and copies ran while one was open for 16% of the time, Pallas kernels for 0%

profile of v11, /device:TPU:0, one launch (start us, length us, event | category | flops | bytes accessed | tf_op | source)
XLA Modules:
  0.0 59.6 jit_solution(15388598159566917500)
XLA Ops:
  0.6 0.0 copy-start
  0.6 1.2 %copy.9 = f32[128,2,4,128]{3,1,0,2:T(2,128)S(1)} copy(bf16[128,2,4,128]{3,2,1,0:T(4,128)(2,1)} %param.5) | data formatting | bytes 786432 | tf_op jit(solution)/shard_map/transpose | solution.py:136
  1.8 0.2 multiply_reduce_fusion
  2.1 1.0 %broadcast_multiply_fusion.k_ref = f32[4,256,128]{2,1,0:T(8,128)} fusion(f32[4,256,128]{2,1,0:T(8,128)S(1)} %bitcast.101, f32[4,256]{1,0:T(4,128)S(1)} %add_rsqrt_fusion), kind=kLoop, calls=%fused_computation.54 | loop fusion | flops 131072 | bytes 1052672 | tf_op jit(solution)/shard_map/mul | solution.py:21
  3.1 0.0 copy-start.4
  3.1 10.6 %shard_map.75 = f32[4,256,256]{2,1,0:T(8,128)} custom-call(f32[4,256,128]{2,1,0:T(8,128)} %broadcast_multiply_fusion.k_ref), custom_call_target="tpu_custom_call" | custom-call | tf_op jit(solution)/shard_map/pallas_call | solution.py:81
  13.7 0.0 copy-done.4
  13.7 0.0 copy-start.1
  13.7 1.7 %fusion.27 = f32[4,256,128]{2,1,0:T(8,128)S(1)} fusion(f32[4,256,256]{2,1,0:T(8,128)} %shard_map.75, bf16[256,4,128]{2,1,0:T(4,128)(2,1)S(1)} %bitcast.104), kind=kOutput, calls=%fused_computation.48 | convolution fusion | flops 201326592 | bytes 1835008 | tf_op jit(solution)/shard_map/hij,hjd->hid/dot_general | solution.py:16
  15.4 0.0 copy-done.1
  15.4 0.0 copy-start.2
  15.5 0.6 %convolution_multiply_fusion.4 = f32[4,128,128]{2,1,0:T(8,128)S(1)} fusion(f32[4,256,128]{2,1,0:T(8,128)S(1)} %copy-done.1, f32[4,256,128]{2,1,0:T(8,128)S(1)} %fusion.27), kind=kOutput, calls=%fused_computation.25 | convolution fusion | flops 100728832 | bytes 1310720 | tf_op jit(solution)/shard_map/hjd,hjw->hdw/dot_general | solution.py:16
  16.1 4.9 %collective-permute-start = (f32[4,128,128]{2,1,0:T(8,128)S(1)}, f32[4,128,128]{2,1,0:T(8,128)S(1)}, u32[]{:S(2)}, u32[]{:S(2)}) collective-permute-start(f32[4,128,128]{2,1,0:T(8,128)S(1)} %convolution_multiply_fusion.4), channel_id=1, source_target_pairs={{0,4},{4,8},{8,12},{1,5},{5,9},{9,13},{2,6},{6,10},{10,14},{3,7},{... | collective-permute-start | bytes 786440 | tf_op jit(solution)/shard_map/ppermute | solution.py:93
  21.1 0.0 copy-done.2
  21.1 0.0 copy-start.3
  21.1 0.6 fusion.44
  21.7 0.1 iota_compare_fusion.1
  21.8 0.2 copy-done.3
  22.0 0.1 fusion.22
  22.1 0.4 fusion.9
  22.6 0.4 convolution_subtract_fusion.2
  23.0 0.0 copy-done
  23.0 0.3 fusion.32
  23.3 1.5 %collective-permute-start.3 = (f32[4,128,128]{2,1,0:T(8,128)S(1)}, f32[4,128,128]{2,1,0:T(8,128)S(1)}, u32[]{:S(2)}, u32[]{:S(2)}) collective-permute-start(f32[4,128,128]{2,1,0:T(8,128)S(1)} %fusion.32), channel_id=1, source_target_pairs={{4,0},{8,4},{12,8},{5,1},{9,5},{13,9},{6,2},{10,6},{14,10},{7,3},{... | collective-permute-start | bytes 786440 | tf_op jit(solution)/shard_map/ppermute | solution.py:94
  24.8 0.4 fusion.45
  25.2 0.6 %fusion.11 = f32[4,128,128]{2,1,0:T(8,128)S(1)} fusion(f32[4,256,128]{2,1,0:T(8,128)S(1)} %copy-done.1, f32[4,256,128]{2,1,0:T(8,128)S(1)} %fusion.44, f32[128,128]{1,0:T(8,128)S(1)} %fusion.39), kind=kOutput, calls=%fused_computation.28 | convolution fusion | flops 100794368 | bytes 1376256 | tf_op jit(solution)/shard_map/hjd,hjw->hdw/dot_general | solution.py:16
  25.8 0.8 %collective-permute-done = f32[4,128,128]{2,1,0:T(8,128)S(1)} collective-permute-done((f32[4,128,128]{2,1,0:T(8,128)S(1)}, f32[4,128,128]{2,1,0:T(8,128)S(1)}, u32[]{:S(2)}, u32[]{:S(2)}) %collective-permute-start) | collective-permute-done | bytes 262176 | tf_op jit(solution)/shard_map/ppermute | solution.py:93
  26.6 0.4 convolution_add_fusion.6
  27.0 4.4 %collective-permute-start.1 = (f32[4,128,128]{2,1,0:T(8,128)S(1)}, f32[4,128,128]{2,1,0:T(8,128)S(1)}, u32[]{:S(2)}, u32[]{:S(2)}) collective-permute-start(f32[4,128,128]{2,1,0:T(8,128)S(1)} %convolution_add_fusion.6), channel_id=1, source_target_pairs={{0,4},{4,8},{8,12},{1,5},{5,9},{9,13},{2,6},{6,10},{10,14},{3,7},{... | collective-permute-start | bytes 786440 | tf_op jit(solution)/shard_map/ppermute | solution.py:93
  31.4 0.5 fusion.35
  31.9 1.1 %collective-permute-done.3 = f32[4,128,128]{2,1,0:T(8,128)S(1)} collective-permute-done((f32[4,128,128]{2,1,0:T(8,128)S(1)}, f32[4,128,128]{2,1,0:T(8,128)S(1)}, u32[]{:S(2)}, u32[]{:S(2)}) %collective-permute-start.3) | collective-permute-done | bytes 262176 | tf_op jit(solution)/shard_map/ppermute | solution.py:94
  33.0 0.6 %convolution_add_fusion.3 = f32[4,128,128]{2,1,0:T(8,128)S(1)} fusion(f32[4,128,128]{2,1,0:T(8,128)S(1)} %fusion.32, f32[4,128,128]{2,1,0:T(8,128)S(1)} %fusion.11, f32[4,128,128]{2,1,0:T(8,128)S(1)} %collective-permute-done.3), kind=kOutput, calls=%fused_computation.20 | convolution fusion | flops 100728832 | bytes 1048576 | tf_op jit(solution)/shard_map/hji,hjk->hik/dot_general | solution.py:12
  33.6 1.3 %collective-permute-start.4 = (f32[4,128,128]{2,1,0:T(8,128)S(1)}, f32[4,128,128]{2,1,0:T(8,128)S(1)}, u32[]{:S(2)}, u32[]{:S(2)}) collective-permute-start(f32[4,128,128]{2,1,0:T(8,128)S(1)} %convolution_add_fusion.3), channel_id=1, source_target_pairs={{4,0},{8,4},{12,8},{5,1},{9,5},{13,9},{6,2},{10,6},{14,10},{7,3},{... | collective-permute-start | bytes 786440 | tf_op jit(solution)/shard_map/ppermute | solution.py:94
  34.9 1.2 %collective-permute-done.1 = f32[4,128,128]{2,1,0:T(8,128)S(1)} collective-permute-done((f32[4,128,128]{2,1,0:T(8,128)S(1)}, f32[4,128,128]{2,1,0:T(8,128)S(1)}, u32[]{:S(2)}, u32[]{:S(2)}) %collective-permute-start.1) | collective-permute-done | bytes 262176 | tf_op jit(solution)/shard_map/ppermute | solution.py:93
  36.1 0.4 convolution_add_fusion.5
  36.5 4.4 %collective-permute-start.2 = (f32[4,128,128]{2,1,0:T(8,128)S(1)}, f32[4,128,128]{2,1,0:T(8,128)S(1)}, u32[]{:S(2)}, u32[]{:S(2)}) collective-permute-start(f32[4,128,128]{2,1,0:T(8,128)S(1)} %convolution_add_fusion.5), channel_id=1, source_target_pairs={{0,4},{4,8},{8,12},{1,5},{5,9},{9,13},{2,6},{6,10},{10,14},{3,7},{... | collective-permute-start | bytes 786440 | tf_op jit(solution)/shard_map/ppermute | solution.py:93
  40.9 1.4 %collective-permute-done.4 = f32[4,128,128]{2,1,0:T(8,128)S(1)} collective-permute-done((f32[4,128,128]{2,1,0:T(8,128)S(1)}, f32[4,128,128]{2,1,0:T(8,128)S(1)}, u32[]{:S(2)}, u32[]{:S(2)}) %collective-permute-start.4) | collective-permute-done | bytes 262176 | tf_op jit(solution)/shard_map/ppermute | solution.py:94
  42.3 0.6 %convolution_add_fusion.2 = f32[4,128,128]{2,1,0:T(8,128)S(1)} fusion(f32[4,128,128]{2,1,0:T(8,128)S(1)} %fusion.32, f32[4,128,128]{2,1,0:T(8,128)S(1)} %fusion.11, f32[4,128,128]{2,1,0:T(8,128)S(1)} %collective-permute-done.4), kind=kOutput, calls=%fused_computation.19 | convolution fusion | flops 100728832 | bytes 1048576 | tf_op jit(solution)/shard_map/hji,hjk->hik/dot_general | solution.py:12
  42.9 1.3 %collective-permute-start.5 = (f32[4,128,128]{2,1,0:T(8,128)S(1)}, f32[4,128,128]{2,1,0:T(8,128)S(1)}, u32[]{:S(2)}, u32[]{:S(2)}) collective-permute-start(f32[4,128,128]{2,1,0:T(8,128)S(1)} %convolution_add_fusion.2), channel_id=1, source_target_pairs={{4,0},{8,4},{12,8},{5,1},{9,5},{13,9},{6,2},{10,6},{14,10},{7,3},{... | collective-permute-start | bytes 786440 | tf_op jit(solution)/shard_map/ppermute | solution.py:94
  44.2 0.5 collective-permute-done.2
  44.7 0.4 convolution_subtract_fusion.1
  45.1 0.3 fusion.2
  45.4 0.3 fusion.37
  45.7 0.5 fusion.21
  46.2 0.3 fusion.13
  46.5 0.2 fusion.26
  46.7 0.8 %copy.28 = bf16[128,4,128]{2,1,0:T(4,128)(2,1)} copy(bf16[128,4,128]{2,0,1:T(8,128)(2,1)S(1)} %fusion.13) | data formatting | bytes 262144
  47.5 0.8 %copy.29 = bf16[128,4,128]{2,1,0:T(4,128)(2,1)} copy(bf16[128,4,128]{2,0,1:T(8,128)(2,1)S(1)} %fusion.26) | data formatting | bytes 262144
  48.2 0.7 %fusion.17 = f32[4,256,128]{2,1,0:T(8,128)S(1)} fusion(f32[4,128,256]{2,1,0:T(8,128)S(1)} %fusion.2, f32[4,128]{1,0:T(4,128)S(1)} %get-tuple-element.9, bf16[128,4,128]{2,1,0:T(4,128)(2,1)S(1)} %copy-done.3), kind=kOutput, calls=%fused_computation.38 | convolution fusion | flops 100794368 | bytes 1181696 | tf_op jit(solution)/shard_map/hij,hid->hjd/dot_general | solution.py:16
  48.9 2.3 %collective-permute-done.5 = f32[4,128,128]{2,1,0:T(8,128)S(1)} collective-permute-done((f32[4,128,128]{2,1,0:T(8,128)S(1)}, f32[4,128,128]{2,1,0:T(8,128)S(1)}, u32[]{:S(2)}, u32[]{:S(2)}) %collective-permute-start.5) | collective-permute-done | bytes 262176 | tf_op jit(solution)/shard_map/ppermute | solution.py:94
  51.2 0.4 fusion.7
  51.6 1.0 %fusion.43 = (bf16[4,256,128]{2,1,0:T(8,128)(2,1)S(1)}, f32[4,256,128]{2,1,0:T(8,128)S(1)}) fusion(f32[4,256,256]{2,1,0:T(8,128)S(1)} %copy-done.2, f32[4,256,128]{2,1,0:T(8,128)S(1)} %fusion.7), kind=kOutput, calls=%fused_computation.73 | convolution fusion | flops 201457664 | bytes 2359296 | tf_op jit(solution)/shard_map/hij,hiw->hjw/dot_general | solution.py:16
  52.6 0.6 %fusion.1 = f32[4,256,256]{2,1,0:T(8,128)S(1)} fusion(f32[4,256,128]{2,1,0:T(8,128)S(1)} %get-tuple-element.13, f32[4,256,128]{2,1,0:T(8,128)S(1)} %convolution_subtract_fusion.1, pred[256,256]{1,0:T(8,128)(4,1)S(1)} %iota_compare_fusion), kind=kOutput, calls=%fused_computation.2 | convolution fusion | flops 201850880 | bytes 2162688 | tf_op jit(solution)/shard_map/hiw,hjw->hij/dot_general | solution.py:16
  53.2 0.6 fusion.46
  53.8 0.4 fusion.8
  54.2 0.4 fusion.6
  54.6 1.0 %convolution_add_fusion = f32[4,256,128]{2,1,0:T(8,128)S(1)} fusion(f32[4,256,128]{2,1,0:T(8,128)S(1)} %fusion.6, f32[4,256,256]{2,1,0:T(8,128)S(1)} %fusion.1, f32[4,256,128]{2,1,0:T(8,128)S(1)} %copy-done.1), kind=kOutput, calls=%fused_computation.3 | convolution fusion | flops 201457664 | bytes 2621440 | tf_op jit(solution)/shard_map/hji,hjd->hid/dot_general | solution.py:16
  55.7 1.8 %fusion.10 = bf16[4,256,128]{2,1,0:T(8,128)(2,1)S(1)} fusion(f32[4,256,128]{2,1,0:T(8,128)S(1)} %convolution_add_fusion, f32[4,256,128]{2,1,0:T(8,128)S(1)} %copy-done.1, f32[4,256]{1,0:T(4,128)S(1)} %add_rsqrt_fusion), kind=kOutput, calls=%fused_computation.18 | output fusion | flops 656511 | bytes 1314816 | tf_op jit(solution)/shard_map/mul | solution.py:172
  57.5 1.0 %copy.68 = bf16[4,128,2,128]{3,0,2,1:T(4,128)(2,1)} copy(bf16[4,128,2,128]{3,2,1,0:T(2,128)(2,1)S(1)} %bitcast.103) | data formatting | bytes 524288 | tf_op jit(solution)/shard_map/convert_element_type | solution.py:181
  58.5 1.0 %copy.67 = bf16[4,128,2,128]{3,0,2,1:T(4,128)(2,1)} copy(bf16[4,128,2,128]{3,2,1,0:T(2,128)(2,1)S(1)} %bitcast.102) | data formatting | bytes 524288 | tf_op jit(solution)/shard_map/convert_element_type | solution.py:181
  (5 shorter events, 0.1 us)
Async XLA Ops:
  0.6 22.3 %copy-start = (bf16[128,4,128]{2,1,0:T(4,128)(2,1)S(1)}, bf16[128,4,128]{2,1,0:T(4,128)(2,1)}, u32[]{:S(2)}) copy-start(bf16[128,4,128]{2,1,0:T(4,128)(2,1)} %param.7) | copy-start | bytes 393220
  3.1 10.6 %copy-start.4 = (bf16[128,2,4,128]{3,2,1,0:T(4,128)(2,1)S(1)}, bf16[128,2,4,128]{3,2,1,0:T(4,128)(2,1)}, u32[]{:S(2)}) copy-start(bf16[128,2,4,128]{3,2,1,0:T(4,128)(2,1)} %param.6) | copy-start | bytes 786436
  13.7 1.7 %copy-start.1 = (f32[4,256,128]{2,1,0:T(8,128)S(1)}, f32[4,256,128]{2,1,0:T(8,128)}, u32[]{:S(2)}) copy-start(f32[4,256,128]{2,1,0:T(8,128)} %broadcast_multiply_fusion.k_ref) | copy-start | bytes 1572868
  15.4 5.6 %copy-start.2 = (f32[4,256,256]{2,1,0:T(8,128)S(1)}, f32[4,256,256]{2,1,0:T(8,128)}, u32[]{:S(2)}) copy-start(f32[4,256,256]{2,1,0:T(8,128)} %shard_map.75) | copy-start | bytes 3145732
  16.1 10.5 %collective-permute-start = (f32[4,128,128]{2,1,0:T(8,128)S(1)}, f32[4,128,128]{2,1,0:T(8,128)S(1)}, u32[]{:S(2)}, u32[]{:S(2)}) collective-permute-start(f32[4,128,128]{2,1,0:T(8,128)S(1)} %convolution_multiply_fusion.4), channel_id=1, source_target_pairs={{0,4},{4,8},{8,12},{1,5},{5,9},{9,13},{2,6},{6,10},{10,14},{3,7},{... | collective-permute-start | bytes 786440 | tf_op jit(solution)/shard_map/ppermute | solution.py:93
  21.1 0.9 %copy-start.3 = (bf16[128,4,128]{2,1,0:T(4,128)(2,1)S(1)}, bf16[128,4,128]{2,1,0:T(4,128)(2,1)}, u32[]{:S(2)}) copy-start(bf16[128,4,128]{2,1,0:T(4,128)(2,1)} %param.4) | copy-start | bytes 393220
  23.3 9.7 %collective-permute-start.3 = (f32[4,128,128]{2,1,0:T(8,128)S(1)}, f32[4,128,128]{2,1,0:T(8,128)S(1)}, u32[]{:S(2)}, u32[]{:S(2)}) collective-permute-start(f32[4,128,128]{2,1,0:T(8,128)S(1)} %fusion.32), channel_id=1, source_target_pairs={{4,0},{8,4},{12,8},{5,1},{9,5},{13,9},{6,2},{10,6},{14,10},{7,3},{... | collective-permute-start | bytes 786440 | tf_op jit(solution)/shard_map/ppermute | solution.py:94
  27.0 9.1 %collective-permute-start.1 = (f32[4,128,128]{2,1,0:T(8,128)S(1)}, f32[4,128,128]{2,1,0:T(8,128)S(1)}, u32[]{:S(2)}, u32[]{:S(2)}) collective-permute-start(f32[4,128,128]{2,1,0:T(8,128)S(1)} %convolution_add_fusion.6), channel_id=1, source_target_pairs={{0,4},{4,8},{8,12},{1,5},{5,9},{9,13},{2,6},{6,10},{10,14},{3,7},{... | collective-permute-start | bytes 786440 | tf_op jit(solution)/shard_map/ppermute | solution.py:93
  33.6 8.8 %collective-permute-start.4 = (f32[4,128,128]{2,1,0:T(8,128)S(1)}, f32[4,128,128]{2,1,0:T(8,128)S(1)}, u32[]{:S(2)}, u32[]{:S(2)}) collective-permute-start(f32[4,128,128]{2,1,0:T(8,128)S(1)} %convolution_add_fusion.3), channel_id=1, source_target_pairs={{4,0},{8,4},{12,8},{5,1},{9,5},{13,9},{6,2},{10,6},{14,10},{7,3},{... | collective-permute-start | bytes 786440 | tf_op jit(solution)/shard_map/ppermute | solution.py:94
  36.5 8.3 %collective-permute-start.2 = (f32[4,128,128]{2,1,0:T(8,128)S(1)}, f32[4,128,128]{2,1,0:T(8,128)S(1)}, u32[]{:S(2)}, u32[]{:S(2)}) collective-permute-start(f32[4,128,128]{2,1,0:T(8,128)S(1)} %convolution_add_fusion.5), channel_id=1, source_target_pairs={{0,4},{4,8},{8,12},{1,5},{5,9},{9,13},{2,6},{6,10},{10,14},{3,7},{... | collective-permute-start | bytes 786440 | tf_op jit(solution)/shard_map/ppermute | solution.py:93
  42.9 8.3 %collective-permute-start.5 = (f32[4,128,128]{2,1,0:T(8,128)S(1)}, f32[4,128,128]{2,1,0:T(8,128)S(1)}, u32[]{:S(2)}, u32[]{:S(2)}) collective-permute-start(f32[4,128,128]{2,1,0:T(8,128)S(1)} %convolution_add_fusion.2), channel_id=1, source_target_pairs={{4,0},{8,4},{12,8},{5,1},{9,5},{13,9},{6,2},{10,6},{14,10},{7,3},{... | collective-permute-start | bytes 786440 | tf_op jit(solution)/shard_map/ppermute | solution.py:94

commit v12 on v7

--- a/solution.py
+++ b/solution.py
@@ -59,6 +59,7 @@
     count = lax.axis_size("seq")
     right = [(i, i + 1) for i in range(count - 1)]
     left = [(i + 1, i) for i in range(count - 1)]
+    offset, local_cot = lax.optimization_barrier((offset, local_cot))
     fwd_sum, bwd_sum = offset, local_cot
     for hop in range(count - 1):
         got_sum = lax.ppermute(fwd_sum, "seq", right)

time: 58.7 us -> 63.6 us (1.083)
  waiting for transfers between devices: 7.43 us -> 11.4 us
  other arithmetic: 3.12 us -> 4.06 us
    ppermute x3, waiting for transfers between devices: 2.1 us -> 7.37 us  [chain_seq(): got_sum = lax.ppermute(fwd_sum, 'seq', right)]
    ppermute x3, waiting for transfers between devices: 5.33 us -> 3.99 us  [chain_seq(): got_cot = lax.ppermute(bwd_sum, 'seq', left)]
    reduce_sum x2, other arithmetic: 0.35 us -> 1.29 us  [unit_rows(): scale = lax.rsqrt(jnp.sum(tensor * tensor, axis=-1, keepdims=True) + 1e-06)]
  transfers between devices with their start and end apart: 6 -> 6, of which waited for: 6 -> 4; matrix products, arithmetic and copies ran while one was open for 16% -> 7% of each run, Pallas kernels for 0% -> 0%
where the time goes in v12:
time: 63.6 us; the launch traced here: 63.2 us
  matrix products  23.6 us (37%)
  starting transfers between devices  17.6 us (28%)
  waiting for transfers between devices  11.4 us (18%)
  local copies, waits for them, and re-layouts  5.36 us (8%)
  other arithmetic  4.06 us (6%)
  between operations  1.17 us (2%)
    ppermute x3, starting transfers between devices, chain_seq(): got_sum = lax.ppermute(fwd_sum, 'seq', right)  13.7 us
    dot_general x23, matrix products, mm(): return jnp.einsum(spec, *operands, precision=highest)  12.6 us
    dot_general x22, matrix products, mh(): return jnp.einsum(spec, *operands, precision=lax.Precision.HIGH)  11.1 us
    ppermute x3, waiting for transfers between devices, chain_seq(): got_sum = lax.ppermute(fwd_sum, 'seq', right)  7.37 us
    ppermute x3, waiting for transfers between devices, chain_seq(): got_cot = lax.ppermute(bwd_sum, 'seq', left)  3.99 us
    ppermute x3, starting transfers between devices, chain_seq(): got_cot = lax.ppermute(bwd_sum, 'seq', left)  3.88 us
    convert_element_type x2, local copies, waits for them, and re-layouts, pair_major(): return tensor.reshape(heads_here, tok_count, 2, head_size).transpose(1, 2...  2.09 us
    unnamed x8, local copies, waits for them, and re-layouts  1.96 us
  transfers between devices with their start and end apart: 6, of which 4 were waited for; matrix products, arithmetic and copies ran while one was open for 7% of the time, Pallas kernels for 0%

profile of v12, /device:TPU:0, one launch (start us, length us, event | category | flops | bytes accessed | tf_op | source)
XLA Modules:
  0.0 63.2 jit_solution(12982306942772184308)
XLA Ops:
  0.7 1.1 %fusion.33 = f32[4,128]{1,0:T(4,128)S(1)} fusion(bf16[128,4,128]{2,1,0:T(4,128)(2,1)} %param.4), kind=kLoop, calls=%fused_computation.69 | loop fusion | flops 196096 | bytes 133120 | tf_op jit(solution)/shard_map/reduce_sum | solution.py:19
  1.9 1.2 %copy.9 = f32[128,2,4,128]{3,1,0,2:T(2,128)S(1)} copy(bf16[128,2,4,128]{3,2,1,0:T(4,128)(2,1)} %param.5) | data formatting | bytes 786432 | tf_op jit(solution)/shard_map/transpose | solution.py:108
  3.0 0.2 multiply_reduce_fusion
  3.5 0.5 convolution_multiply_fusion.7
  4.0 0.5 convolution_multiply_fusion.6
  4.5 0.5 convolution_multiply_fusion.5
  5.1 0.7 %convolution_multiply_fusion.4 = f32[4,128,128]{2,1,0:T(8,128)S(1)} fusion(f32[4,1,2,128,128]{4,3,2,0,1:T(8,128)S(1)} %bitcast.207), kind=kOutput, calls=%fused_computation.31 | convolution fusion | flops 100728832 | bytes 786432 | tf_op jit(solution)/shard_map/hpid,hpjd->hpij/dot_general | solution.py:11
  5.8 0.9 %fusion.3 = f32[4,16,16,16]{3,2,1,0:T(8,128)S(1)} fusion(f32[4,16,16,128]{3,2,1,0:T(8,128)S(1)} %bitcast.208, pred[16,16]{1,0:T(8,128)(4,1)S(1)} %iota_compare_fusion.7), kind=kOutput, calls=%fused_computation.10 | convolution fusion | flops 25198592 | bytes 590080 | tf_op jit(solution)/shard_map/hpid,hpjd->hpij/dot_general | solution.py:11
  6.7 0.6 %fusion.73 = f32[4,16,16,16]{3,2,1,0:T(8,128)S(1)} fusion(f32[4,16,16,16]{3,2,1,0:T(8,128)S(1)} %fusion.3), kind=kOutput, calls=%fused_computation.138 | convolution fusion | flops 3145728 | bytes 131072 | tf_op jit(solution)/shard_map/hpij,hpjk->hpik/dot_general | solution.py:11
  7.3 0.6 %fusion.74 = f32[4,16,16,16]{3,2,1,0:T(8,128)S(1)} fusion(f32[4,16,16,16]{3,2,1,0:T(8,128)S(1)} %fusion.73), kind=kOutput, calls=%fused_computation.139 | convolution fusion | flops 3145728 | bytes 131072 | tf_op jit(solution)/shard_map/hpij,hpjk->hpik/dot_general | solution.py:11
  8.0 0.7 %convolution_add_fusion.2 = f32[4,16,16,16]{3,2,1,0:T(8,128)S(1)} fusion(f32[4,16,16,16]{3,2,1,0:T(8,128)S(1)} %fusion.73, f32[4,16,16,16]{3,2,1,0:T(8,128)S(1)} %fusion.3, f32[16,16]{1,0:T(8,128)S(1)} %fusion.58), kind=kOutput, calls=%fused_computation.5 | convolution fusion | flops 3178496 | bytes 197632 | tf_op jit(solution)/shard_map/hpij,hpjk->hpik/dot_general | solution.py:11
  8.7 0.6 %fusion.75 = f32[4,16,16,16]{3,2,1,0:T(8,128)S(1)} fusion(f32[4,16,16,16]{3,2,1,0:T(8,128)S(1)} %fusion.74), kind=kOutput, calls=%fused_computation.140 | convolution fusion | flops 3145728 | bytes 131072 | tf_op jit(solution)/shard_map/hpij,hpjk->hpik/dot_general | solution.py:11
  9.3 0.6 %convolution_add_fusion.1 = f32[4,16,16,16]{3,2,1,0:T(8,128)S(1)} fusion(f32[4,16,16,16]{3,2,1,0:T(8,128)S(1)} %convolution_add_fusion.2, f32[4,16,16,16]{3,2,1,0:T(8,128)S(1)} %fusion.74), kind=kOutput, calls=%fused_computation.4 | convolution fusion | flops 3162112 | bytes 196608 | tf_op jit(solution)/shard_map/hpij,hpjk->hpik/dot_general | solution.py:11
  9.9 0.6 %convolution_add_fusion = f32[4,16,16,16]{3,2,1,0:T(8,128)S(1)} fusion(f32[4,16,16,16]{3,2,1,0:T(8,128)S(1)} %convolution_add_fusion.1, f32[4,16,16,16]{3,2,1,0:T(8,128)S(1)} %fusion.75), kind=kOutput, calls=%fused_computation.3 | convolution fusion | flops 3162112 | bytes 196608 | tf_op jit(solution)/shard_map/hpij,hpjk->hpik/dot_general | solution.py:11
  10.6 0.4 fusion.69
  11.0 0.4 convolution_negate_fusion.3
  11.6 0.4 fusion.70
  12.0 0.4 convolution_negate_fusion.2
  12.6 0.4 fusion.71
  13.0 0.4 convolution_negate_fusion.1
  13.5 0.6 fusion.38
  14.1 0.7 %fusion.12 = f32[4,1,128,128]{3,2,0,1:T(8,128)S(1)} fusion(f32[4,128,128]{1,2,0:T(8,128)S(1)} %fusion.38, f32[4,1,2,128,128]{4,3,2,0,1:T(8,128)S(1)} %fusion.17), kind=kOutput, calls=%fused_computation.30 | convolution fusion | flops 100728832 | bytes 786432 | tf_op jit(solution)/shard_map/hpij,hpjk->hpik/dot_general | solution.py:11
  14.8 0.6 fusion.24
  15.4 0.4 copy-done.2
  15.7 0.4 fusion.22
  16.2 0.8 %convolution_multiply_fusion.9 = f32[4,128,128]{2,1,0:T(8,128)S(1)} fusion(f32[4,256,128]{2,1,0:T(8,128)S(1)} %broadcast_multiply_fusion, f32[4,256,128]{2,1,0:T(8,128)S(1)} %fusion.22), kind=kOutput, calls=%fused_computation.39 | convolution fusion | flops 100728832 | bytes 1310720 | tf_op jit(solution)/shard_map/hjd,hjw->hdw/dot_general | solution.py:15
  17.1 0.4 fusion.10
  17.5 0.4 convolution_subtract_fusion.2
  17.9 0.3 fusion.53
  18.3 4.9 %collective-permute-start = (f32[4,128,128]{2,1,0:T(8,128)S(1)}, f32[4,128,128]{2,1,0:T(8,128)S(1)}, u32[]{:S(2)}, u32[]{:S(2)}) collective-permute-start(f32[4,128,128]{2,1,0:T(8,128)S(1)} %convolution_multiply_fusion.9), channel_id=1, source_target_pairs={{0,4},{4,8},{8,12},{1,5},{5,9},{9,13},{2,6},{6,10},{10,14},{3,7},{... | collective-permute-start | bytes 786440 | tf_op jit(solution)/shard_map/ppermute | solution.py:65
  23.2 1.3 %collective-permute-start.3 = (f32[4,128,128]{2,1,0:T(8,128)S(1)}, f32[4,128,128]{2,1,0:T(8,128)S(1)}, u32[]{:S(2)}, u32[]{:S(2)}) collective-permute-start(f32[4,128,128]{2,1,0:T(8,128)S(1)} %fusion.53), channel_id=1, source_target_pairs={{4,0},{8,4},{12,8},{5,1},{9,5},{13,9},{6,2},{10,6},{14,10},{7,3},{... | collective-permute-start | bytes 786440 | tf_op jit(solution)/shard_map/ppermute | solution.py:66
  24.5 0.6 %fusion.13 = f32[4,128,128]{2,1,0:T(8,128)S(1)} fusion(f32[4,256,128]{2,1,0:T(8,128)S(1)} %broadcast_multiply_fusion, f32[4,256,128]{2,1,0:T(8,128)S(1)} %fusion.24, f32[128,128]{1,0:T(8,128)S(1)} %fusion.55), kind=kOutput, calls=%fused_computation.42 | convolution fusion | flops 100794368 | bytes 1376256 | tf_op jit(solution)/shard_map/hjd,hjw->hdw/dot_general | solution.py:15
  25.2 0.4 fusion.76
  25.6 3.2 %collective-permute-done = f32[4,128,128]{2,1,0:T(8,128)S(1)} collective-permute-done((f32[4,128,128]{2,1,0:T(8,128)S(1)}, f32[4,128,128]{2,1,0:T(8,128)S(1)}, u32[]{:S(2)}, u32[]{:S(2)}) %collective-permute-start) | collective-permute-done | bytes 262176 | tf_op jit(solution)/shard_map/ppermute | solution.py:65
  28.7 0.4 convolution_add_fusion.9
  29.1 4.4 %collective-permute-start.1 = (f32[4,128,128]{2,1,0:T(8,128)S(1)}, f32[4,128,128]{2,1,0:T(8,128)S(1)}, u32[]{:S(2)}, u32[]{:S(2)}) collective-permute-start(f32[4,128,128]{2,1,0:T(8,128)S(1)} %convolution_add_fusion.9), channel_id=1, source_target_pairs={{0,4},{4,8},{8,12},{1,5},{5,9},{9,13},{2,6},{6,10},{10,14},{3,7},{... | collective-permute-start | bytes 786440 | tf_op jit(solution)/shard_map/ppermute | solution.py:65
  33.6 0.6 convolution_add_fusion.6
  34.2 1.3 %collective-permute-start.4 = (f32[4,128,128]{2,1,0:T(8,128)S(1)}, f32[4,128,128]{2,1,0:T(8,128)S(1)}, u32[]{:S(2)}, u32[]{:S(2)}) collective-permute-start(f32[4,128,128]{2,1,0:T(8,128)S(1)} %convolution_add_fusion.6), channel_id=1, source_target_pairs={{4,0},{8,4},{12,8},{5,1},{9,5},{13,9},{6,2},{10,6},{14,10},{7,3},{... | collective-permute-start | bytes 786440 | tf_op jit(solution)/shard_map/ppermute | solution.py:66
  35.5 0.5 fusion.51
  35.9 2.3 %collective-permute-done.1 = f32[4,128,128]{2,1,0:T(8,128)S(1)} collective-permute-done((f32[4,128,128]{2,1,0:T(8,128)S(1)}, f32[4,128,128]{2,1,0:T(8,128)S(1)}, u32[]{:S(2)}, u32[]{:S(2)}) %collective-permute-start.1) | collective-permute-done | bytes 262176 | tf_op jit(solution)/shard_map/ppermute | solution.py:65
  38.2 0.4 convolution_add_fusion.8
  38.6 4.4 %collective-permute-start.2 = (f32[4,128,128]{2,1,0:T(8,128)S(1)}, f32[4,128,128]{2,1,0:T(8,128)S(1)}, u32[]{:S(2)}, u32[]{:S(2)}) collective-permute-start(f32[4,128,128]{2,1,0:T(8,128)S(1)} %convolution_add_fusion.8), channel_id=1, source_target_pairs={{0,4},{4,8},{8,12},{1,5},{5,9},{9,13},{2,6},{6,10},{10,14},{3,7},{... | collective-permute-start | bytes 786440 | tf_op jit(solution)/shard_map/ppermute | solution.py:65
  43.0 0.6 convolution_add_fusion.5
  43.6 1.3 %collective-permute-start.5 = (f32[4,128,128]{2,1,0:T(8,128)S(1)}, f32[4,128,128]{2,1,0:T(8,128)S(1)}, u32[]{:S(2)}, u32[]{:S(2)}) collective-permute-start(f32[4,128,128]{2,1,0:T(8,128)S(1)} %convolution_add_fusion.5), channel_id=1, source_target_pairs={{4,0},{8,4},{12,8},{5,1},{9,5},{13,9},{6,2},{10,6},{14,10},{7,3},{... | collective-permute-start | bytes 786440 | tf_op jit(solution)/shard_map/ppermute | solution.py:66
  45.0 1.9 %collective-permute-done.2 = f32[4,128,128]{2,1,0:T(8,128)S(1)} collective-permute-done((f32[4,128,128]{2,1,0:T(8,128)S(1)}, f32[4,128,128]{2,1,0:T(8,128)S(1)}, u32[]{:S(2)}, u32[]{:S(2)}) %collective-permute-start.2) | collective-permute-done | bytes 262176 | tf_op jit(solution)/shard_map/ppermute | solution.py:65
  46.9 0.3 fusion.15
  47.2 0.8 %copy.36 = bf16[128,4,128]{2,1,0:T(4,128)(2,1)} copy(bf16[128,4,128]{2,0,1:T(8,128)(2,1)S(1)} %fusion.15) | data formatting | bytes 262144
  47.9 4.0 %collective-permute-done.5 = f32[4,128,128]{2,1,0:T(8,128)S(1)} collective-permute-done((f32[4,128,128]{2,1,0:T(8,128)S(1)}, f32[4,128,128]{2,1,0:T(8,128)S(1)}, u32[]{:S(2)}, u32[]{:S(2)}) %collective-permute-start.5) | collective-permute-done | bytes 262176 | tf_op jit(solution)/shard_map/ppermute | solution.py:66
  51.9 0.4 fusion.8
  52.3 0.9 %fusion.72 = (bf16[4,256,128]{2,1,0:T(8,128)(2,1)S(1)}, f32[4,256,128]{2,1,0:T(8,128)S(1)}) fusion(f32[4,256,128]{2,1,0:T(8,128)S(1)} %fusion.8, f32[4,1,128,128]{3,2,0,1:T(8,128)S(1)} %get-tuple-element.13, f32[4,1,128,128]{3,2,0,1:T(8,128)S(1)} %get-tuple-element.12, f32[4,1,128,128]{3,2,0,1:T(8,128)S(1)} %fusion.12), kind=kOutput, calls=%fused_computation.137 | convolution fusion | flops 202506240 | bytes 2097152 | tf_op jit(solution)/shard_map/hij,hiw->hjw/dot_general | solution.py:15
  53.2 1.0 %copy.83 = bf16[4,128,2,128]{3,0,2,1:T(4,128)(2,1)} copy(bf16[4,128,2,128]{3,2,1,0:T(2,128)(2,1)S(1)} %bitcast.223) | data formatting | bytes 524288 | tf_op jit(solution)/shard_map/convert_element_type | solution.py:153
  54.2 0.4 convolution_subtract_fusion.1
  54.6 0.3 fusion.2
  54.9 0.7 %fusion.28 = f32[4,256,128]{2,1,0:T(8,128)S(1)} fusion(f32[4,128,256]{2,1,0:T(8,128)S(1)} %fusion.2, f32[4,128]{1,0:T(4,128)S(1)} %get-tuple-element.21, bf16[128,4,128]{2,1,0:T(4,128)(2,1)S(1)} %copy-done.1), kind=kOutput, calls=%fused_computation.66 | convolution fusion | flops 100794368 | bytes 1181696 | tf_op jit(solution)/shard_map/hij,hid->hjd/dot_general | solution.py:15
  55.6 0.3 fusion.49
  55.9 0.5 fusion.32
  56.6 0.8 %copy.37 = bf16[128,4,128]{2,1,0:T(4,128)(2,1)} copy(bf16[128,4,128]{2,0,1:T(8,128)(2,1)S(1)} %fusion.37) | data formatting | bytes 262144
  57.3 0.6 fusion.1
  58.0 0.6 fusion.77
  58.6 0.4 fusion.9
  59.0 0.4 fusion.7
  59.3 1.0 %convolution_add_fusion.3 = f32[4,256,128]{2,1,0:T(8,128)S(1)} fusion(f32[4,256,128]{2,1,0:T(8,128)S(1)} %fusion.7, f32[4,256,256]{2,1,0:T(8,128)S(1)} %fusion.1, f32[4,256,128]{2,1,0:T(8,128)S(1)} %broadcast_multiply_fusion), kind=kOutput, calls=%fused_computation.6 | convolution fusion | flops 201457664 | bytes 2621440 | tf_op jit(solution)/shard_map/hji,hjd->hid/dot_general | solution.py:15
  60.4 1.8 %fusion.11 = bf16[4,256,128]{2,1,0:T(8,128)(2,1)S(1)} fusion(f32[4,256,128]{2,1,0:T(8,128)S(1)} %convolution_add_fusion.3, f32[4,256,128]{2,1,0:T(8,128)S(1)} %broadcast_multiply_fusion, f32[4,256]{1,0:T(4,128)S(1)} %add_rsqrt_fusion), kind=kOutput, calls=%fused_computation.23 | output fusion | flops 656511 | bytes 1314816 | tf_op jit(solution)/shard_map/mul | solution.py:144
  62.2 1.0 %copy.84 = bf16[4,128,2,128]{3,0,2,1:T(4,128)(2,1)} copy(bf16[4,128,2,128]{3,2,1,0:T(2,128)(2,1)S(1)} %bitcast.220) | data formatting | bytes 524288 | tf_op jit(solution)/shard_map/convert_element_type | solution.py:153
  (24 shorter events, 1.2 us)
Async XLA Ops:
  0.6 17.3 %copy-start = (bf16[128,4,128]{2,1,0:T(4,128)(2,1)S(1)}, bf16[128,4,128]{2,1,0:T(4,128)(2,1)}, u32[]{:S(2)}) copy-start(bf16[128,4,128]{2,1,0:T(4,128)(2,1)} %param.7) | copy-start | bytes 393220
  14.8 1.0 %copy-start.2 = (bf16[128,2,4,128]{3,2,1,0:T(4,128)(2,1)S(1)}, bf16[128,2,4,128]{3,2,1,0:T(4,128)(2,1)}, u32[]{:S(2)}) copy-start(bf16[128,2,4,128]{3,2,1,0:T(4,128)(2,1)} %param.6) | copy-start | bytes 786436
  16.2 0.9 %copy-start.1 = (bf16[128,4,128]{2,1,0:T(4,128)(2,1)S(1)}, bf16[128,4,128]{2,1,0:T(4,128)(2,1)}, u32[]{:S(2)}) copy-start(bf16[128,4,128]{2,1,0:T(4,128)(2,1)} %param.4) | copy-start | bytes 393220
  18.3 10.5 %collective-permute-start = (f32[4,128,128]{2,1,0:T(8,128)S(1)}, f32[4,128,128]{2,1,0:T(8,128)S(1)}, u32[]{:S(2)}, u32[]{:S(2)}) collective-permute-start(f32[4,128,128]{2,1,0:T(8,128)S(1)} %convolution_multiply_fusion.9), channel_id=1, source_target_pairs={{0,4},{4,8},{8,12},{1,5},{5,9},{9,13},{2,6},{6,10},{10,14},{3,7},{... | collective-permute-start | bytes 786440 | tf_op jit(solution)/shard_map/ppermute | solution.py:65
  23.2 10.3 %collective-permute-start.3 = (f32[4,128,128]{2,1,0:T(8,128)S(1)}, f32[4,128,128]{2,1,0:T(8,128)S(1)}, u32[]{:S(2)}, u32[]{:S(2)}) collective-permute-start(f32[4,128,128]{2,1,0:T(8,128)S(1)} %fusion.53), channel_id=1, source_target_pairs={{4,0},{8,4},{12,8},{5,1},{9,5},{13,9},{6,2},{10,6},{14,10},{7,3},{... | collective-permute-start | bytes 786440 | tf_op jit(solution)/shard_map/ppermute | solution.py:66
  29.1 9.1 %collective-permute-start.1 = (f32[4,128,128]{2,1,0:T(8,128)S(1)}, f32[4,128,128]{2,1,0:T(8,128)S(1)}, u32[]{:S(2)}, u32[]{:S(2)}) collective-permute-start(f32[4,128,128]{2,1,0:T(8,128)S(1)} %convolution_add_fusion.9), channel_id=1, source_target_pairs={{0,4},{4,8},{8,12},{1,5},{5,9},{9,13},{2,6},{6,10},{10,14},{3,7},{... | collective-permute-start | bytes 786440 | tf_op jit(solution)/shard_map/ppermute | solution.py:65
  34.2 8.9 %collective-permute-start.4 = (f32[4,128,128]{2,1,0:T(8,128)S(1)}, f32[4,128,128]{2,1,0:T(8,128)S(1)}, u32[]{:S(2)}, u32[]{:S(2)}) collective-permute-start(f32[4,128,128]{2,1,0:T(8,128)S(1)} %convolution_add_fusion.6), channel_id=1, source_target_pairs={{4,0},{8,4},{12,8},{5,1},{9,5},{13,9},{6,2},{10,6},{14,10},{7,3},{... | collective-permute-start | bytes 786440 | tf_op jit(solution)/shard_map/ppermute | solution.py:66
  38.6 8.3 %collective-permute-start.2 = (f32[4,128,128]{2,1,0:T(8,128)S(1)}, f32[4,128,128]{2,1,0:T(8,128)S(1)}, u32[]{:S(2)}, u32[]{:S(2)}) collective-permute-start(f32[4,128,128]{2,1,0:T(8,128)S(1)} %convolution_add_fusion.8), channel_id=1, source_target_pairs={{0,4},{4,8},{8,12},{1,5},{5,9},{9,13},{2,6},{6,10},{10,14},{3,7},{... | collective-permute-start | bytes 786440 | tf_op jit(solution)/shard_map/ppermute | solution.py:65
  43.6 8.3 %collective-permute-start.5 = (f32[4,128,128]{2,1,0:T(8,128)S(1)}, f32[4,128,128]{2,1,0:T(8,128)S(1)}, u32[]{:S(2)}, u32[]{:S(2)}) collective-permute-start(f32[4,128,128]{2,1,0:T(8,128)S(1)} %convolution_add_fusion.5), channel_id=1, source_target_pairs={{4,0},{8,4},{12,8},{5,1},{9,5},{13,9},{6,2},{10,6},{14,10},{7,3},{... | collective-permute-start | bytes 786440 | tf_op jit(solution)/shard_map/ppermute | solution.py:66

commit v13 on v7

--- a/solution.py
+++ b/solution.py
@@ -127,8 +127,9 @@
 
     produced = mh("hld,hdw->hlw", read_map, state_in) + own_out
     updates = upd_v - mh("hjd,hdw->hjw", proj, state_in)
-    d_upd = mh("hij,hiw->hjw", scores, cot) + 2.0 * mh("hjd,hdw->hjw", kn, end_cot)
-    d_w = mh("hij,hiw->hjw", inverse, d_upd)
+    w_cot = mh("hij,hiw->hjw", inverse, mh("hij,hiw->hjw", scores, cot))
+    w_key = 2.0 * mh("hij,hid->hjd", inverse, kn)
+    d_w = w_cot + mh("hjd,hdw->hjw", w_key, end_cot)
     touch = jnp.where(visible, mh("hiw,hjw->hij", cot, updates), 0.0)
     d_qn = mh("hiw,hdw->hid", cot, state_in) + 2.0 * mh("hij,hjd->hid", touch, kn)
     gram_cot = jnp.where(strict_lower(rows, rows), -2.0 * mh("hiw,hjw->hij", d_w, updates), 0.0)

time: 58.7 us -> 63 us (1.073)
  waiting for transfers between devices: 7.43 us -> 10.3 us
  matrix products: 23.5 us -> 24.3 us
    ppermute x3, waiting for transfers between devices: 5.33 us -> 8.91 us  [chain_seq(): got_cot = lax.ppermute(bwd_sum, 'seq', left)]
    dot_general x22 -> x23, matrix products: 10.9 us -> 11.8 us  [mh(): return jnp.einsum(spec, *operands, precision=lax.Precision.HIGH)]
    ppermute x3, waiting for transfers between devices: 2.1 us -> 1.39 us  [chain_seq(): got_sum = lax.ppermute(fwd_sum, 'seq', right)]
  transfers between devices with their start and end apart: 6 -> 6, of which waited for: 6 -> 5; matrix products, arithmetic and copies ran while one was open for 16% -> 14% of each run, Pallas kernels for 0% -> 0%
where the time goes in v13:
time: 63 us; the launch traced here: 62.7 us
  matrix products  24.3 us (39%)
  starting transfers between devices  18.2 us (29%)
  waiting for transfers between devices  10.3 us (16%)
  local copies, waits for them, and re-layouts  5.55 us (9%)
  other arithmetic  3.13 us (5%)
  between operations  1.18 us (2%)
    ppermute x3, starting transfers between devices, chain_seq(): got_sum = lax.ppermute(fwd_sum, 'seq', right)  14.3 us
    dot_general x23, matrix products, mm(): return jnp.einsum(spec, *operands, precision=highest)  12.5 us
    dot_general x23, matrix products, mh(): return jnp.einsum(spec, *operands, precision=lax.Precision.HIGH)  11.8 us
    ppermute x3, waiting for transfers between devices, chain_seq(): got_cot = lax.ppermute(bwd_sum, 'seq', left)  8.91 us
    ppermute x3, starting transfers between devices, chain_seq(): got_cot = lax.ppermute(bwd_sum, 'seq', left)  3.88 us
    unnamed x8, local copies, waits for them, and re-layouts  2.11 us
    convert_element_type x2, local copies, waits for them, and re-layouts, pair_major(): return tensor.reshape(heads_here, tok_count, 2, head_size).transpose(1, 2...  2.09 us
    mul x1, other arithmetic, local(): d_k = k_scale * (d_kn - jnp.sum(kn * d_kn, axis=-1, keepdims=True) * kn)  1.79 us
  transfers between devices with their start and end apart: 6, of which 5 were waited for; matrix products, arithmetic and copies ran while one was open for 14% of the time, Pallas kernels for 0%

profile of v13, /device:TPU:0, one launch (start us, length us, event | category | flops | bytes accessed | tf_op | source)
XLA Modules:
  0.0 62.7 jit_solution(8596418843744737743)
XLA Ops:
  0.7 1.2 %copy.9 = f32[128,2,4,128]{3,1,0,2:T(2,128)S(1)} copy(bf16[128,2,4,128]{3,2,1,0:T(4,128)(2,1)} %param.5) | data formatting | bytes 786432 | tf_op jit(solution)/shard_map/transpose | solution.py:107
  2.3 0.5 convolution_multiply_fusion.7
  2.8 0.5 convolution_multiply_fusion.6
  3.4 0.5 convolution_multiply_fusion.5
  3.9 0.7 %convolution_multiply_fusion.4 = f32[4,128,128]{2,1,0:T(8,128)S(1)} fusion(f32[4,1,2,128,128]{4,3,2,0,1:T(8,128)S(1)} %bitcast.207), kind=kOutput, calls=%fused_computation.31 | convolution fusion | flops 100728832 | bytes 786432 | tf_op jit(solution)/shard_map/hpid,hpjd->hpij/dot_general | solution.py:11
  4.6 0.9 %fusion.3 = f32[4,16,16,16]{3,2,1,0:T(8,128)S(1)} fusion(f32[4,16,16,128]{3,2,1,0:T(8,128)S(1)} %bitcast.208, pred[16,16]{1,0:T(8,128)(4,1)S(1)} %iota_compare_fusion.7), kind=kOutput, calls=%fused_computation.11 | convolution fusion | flops 25198592 | bytes 590080 | tf_op jit(solution)/shard_map/hpid,hpjd->hpij/dot_general | solution.py:11
  5.5 0.6 %fusion.76 = f32[4,16,16,16]{3,2,1,0:T(8,128)S(1)} fusion(f32[4,16,16,16]{3,2,1,0:T(8,128)S(1)} %fusion.3), kind=kOutput, calls=%fused_computation.141 | convolution fusion | flops 3145728 | bytes 131072 | tf_op jit(solution)/shard_map/hpij,hpjk->hpik/dot_general | solution.py:11
  6.2 0.6 %fusion.77 = f32[4,16,16,16]{3,2,1,0:T(8,128)S(1)} fusion(f32[4,16,16,16]{3,2,1,0:T(8,128)S(1)} %fusion.76), kind=kOutput, calls=%fused_computation.142 | convolution fusion | flops 3145728 | bytes 131072 | tf_op jit(solution)/shard_map/hpij,hpjk->hpik/dot_general | solution.py:11
  6.8 0.7 %convolution_add_fusion.2 = f32[4,16,16,16]{3,2,1,0:T(8,128)S(1)} fusion(f32[4,16,16,16]{3,2,1,0:T(8,128)S(1)} %fusion.76, f32[4,16,16,16]{3,2,1,0:T(8,128)S(1)} %fusion.3, f32[16,16]{1,0:T(8,128)S(1)} %fusion.58), kind=kOutput, calls=%fused_computation.5 | convolution fusion | flops 3178496 | bytes 197632 | tf_op jit(solution)/shard_map/hpij,hpjk->hpik/dot_general | solution.py:11
  7.5 0.6 %fusion.78 = f32[4,16,16,16]{3,2,1,0:T(8,128)S(1)} fusion(f32[4,16,16,16]{3,2,1,0:T(8,128)S(1)} %fusion.77), kind=kOutput, calls=%fused_computation.143 | convolution fusion | flops 3145728 | bytes 131072 | tf_op jit(solution)/shard_map/hpij,hpjk->hpik/dot_general | solution.py:11
  8.1 0.6 %convolution_add_fusion.1 = f32[4,16,16,16]{3,2,1,0:T(8,128)S(1)} fusion(f32[4,16,16,16]{3,2,1,0:T(8,128)S(1)} %convolution_add_fusion.2, f32[4,16,16,16]{3,2,1,0:T(8,128)S(1)} %fusion.77), kind=kOutput, calls=%fused_computation.4 | convolution fusion | flops 3162112 | bytes 196608 | tf_op jit(solution)/shard_map/hpij,hpjk->hpik/dot_general | solution.py:11
  8.8 0.6 %convolution_add_fusion = f32[4,16,16,16]{3,2,1,0:T(8,128)S(1)} fusion(f32[4,16,16,16]{3,2,1,0:T(8,128)S(1)} %convolution_add_fusion.1, f32[4,16,16,16]{3,2,1,0:T(8,128)S(1)} %fusion.78), kind=kOutput, calls=%fused_computation.3 | convolution fusion | flops 3162112 | bytes 196608 | tf_op jit(solution)/shard_map/hpij,hpjk->hpik/dot_general | solution.py:11
  9.5 0.4 fusion.72
  9.9 0.4 convolution_negate_fusion.3
  10.4 0.4 fusion.73
  10.8 0.4 convolution_negate_fusion.2
  11.4 0.4 fusion.74
  11.8 0.4 convolution_negate_fusion.1
  12.4 0.6 fusion.31
  13.0 0.7 %fusion.11 = f32[4,1,128,128]{3,2,0,1:T(8,128)S(1)} fusion(f32[4,128,128]{1,2,0:T(8,128)S(1)} %fusion.31, f32[4,1,2,128,128]{4,3,2,0,1:T(8,128)S(1)} %fusion.16), kind=kOutput, calls=%fused_computation.30 | convolution fusion | flops 100728832 | bytes 786432 | tf_op jit(solution)/shard_map/hpij,hpjk->hpik/dot_general | solution.py:11
  13.6 0.3 copy-done.2
  13.9 0.4 fusion.33
  14.4 0.6 %convolution_multiply_fusion.9 = f32[4,128,128]{2,1,0:T(8,128)S(1)} fusion(f32[4,256,128]{2,1,0:T(8,128)S(1)} %broadcast_multiply_fusion, f32[4,256,128]{2,1,0:T(8,128)S(1)} %fusion.33), kind=kOutput, calls=%fused_computation.39 | convolution fusion | flops 100728832 | bytes 1310720 | tf_op jit(solution)/shard_map/hjd,hjw->hdw/dot_general | solution.py:15
  15.0 5.1 %collective-permute-start = (f32[4,128,128]{2,1,0:T(8,128)S(1)}, f32[4,128,128]{2,1,0:T(8,128)S(1)}, u32[]{:S(2)}, u32[]{:S(2)}) collective-permute-start(f32[4,128,128]{2,1,0:T(8,128)S(1)} %convolution_multiply_fusion.9), channel_id=1, source_target_pairs={{0,4},{4,8},{8,12},{1,5},{5,9},{9,13},{2,6},{6,10},{10,14},{3,7},{... | collective-permute-start | bytes 786440 | tf_op jit(solution)/shard_map/ppermute | solution.py:64
  20.2 0.6 fusion.44
  20.7 0.3 copy-done.1
  21.3 0.4 fusion.9
  21.7 0.4 convolution_subtract_fusion.2
  22.1 0.3 fusion.48
  22.5 1.3 %collective-permute-start.3 = (f32[4,128,128]{2,1,0:T(8,128)S(1)}, f32[4,128,128]{2,1,0:T(8,128)S(1)}, u32[]{:S(2)}, u32[]{:S(2)}) collective-permute-start(f32[4,128,128]{2,1,0:T(8,128)S(1)} %fusion.48), channel_id=1, source_target_pairs={{4,0},{8,4},{12,8},{5,1},{9,5},{13,9},{6,2},{10,6},{14,10},{7,3},{... | collective-permute-start | bytes 786440 | tf_op jit(solution)/shard_map/ppermute | solution.py:65
  23.8 0.4 fusion.79
  24.1 0.5 fusion.51
  24.6 0.9 %convolution_multiply_fusion.1 = f32[4,256,128]{2,1,0:T(8,128)S(1)} fusion(f32[4,256,128]{2,1,0:T(8,128)S(1)} %broadcast_multiply_fusion, f32[4,1,128,128]{3,2,0,1:T(8,128)S(1)} %get-tuple-element.9, f32[4,1,128,128]{3,2,0,1:T(8,128)S(1)} %get-tuple-element.8, f32[4,1,128,128]{3,2,0,1:T(8,128)S(1)} %fusion.11), kind=kOutput, calls=%fused_computation.7 | convolution fusion | flops 202506240 | bytes 1835008 | tf_op jit(solution)/shard_map/hij,hid->hjd/dot_general | solution.py:15
  25.5 0.6 %fusion.12 = f32[4,128,128]{2,1,0:T(8,128)S(1)} fusion(f32[4,256,128]{2,1,0:T(8,128)S(1)} %broadcast_multiply_fusion, f32[4,256,128]{2,1,0:T(8,128)S(1)} %fusion.44, f32[128,128]{1,0:T(8,128)S(1)} %fusion.55), kind=kOutput, calls=%fused_computation.42 | convolution fusion | flops 100794368 | bytes 1376256 | tf_op jit(solution)/shard_map/hjd,hjw->hdw/dot_general | solution.py:15
  26.2 6.0 %collective-permute-done.3 = f32[4,128,128]{2,1,0:T(8,128)S(1)} collective-permute-done((f32[4,128,128]{2,1,0:T(8,128)S(1)}, f32[4,128,128]{2,1,0:T(8,128)S(1)}, u32[]{:S(2)}, u32[]{:S(2)}) %collective-permute-start.3) | collective-permute-done | bytes 262176 | tf_op jit(solution)/shard_map/ppermute | solution.py:65
  32.1 0.6 convolution_add_fusion.7
  32.7 1.3 %collective-permute-start.4 = (f32[4,128,128]{2,1,0:T(8,128)S(1)}, f32[4,128,128]{2,1,0:T(8,128)S(1)}, u32[]{:S(2)}, u32[]{:S(2)}) collective-permute-start(f32[4,128,128]{2,1,0:T(8,128)S(1)} %convolution_add_fusion.7), channel_id=1, source_target_pairs={{4,0},{8,4},{12,8},{5,1},{9,5},{13,9},{6,2},{10,6},{14,10},{7,3},{... | collective-permute-start | bytes 786440 | tf_op jit(solution)/shard_map/ppermute | solution.py:65
  34.0 0.9 %fusion.41 = f32[4,256,128]{2,1,0:T(8,128)S(1)} fusion(f32[4,256,128]{2,1,0:T(8,128)S(1)} %fusion.51, f32[4,1,128,128]{3,2,0,1:T(8,128)S(1)} %get-tuple-element.9, f32[4,1,128,128]{3,2,0,1:T(8,128)S(1)} %get-tuple-element.8, f32[4,1,128,128]{3,2,0,1:T(8,128)S(1)} %fusion.11), kind=kOutput, calls=%fused_computation.102 | convolution fusion | flops 202375168 | bytes 1835008 | tf_op jit(solution)/shard_map/hij,hiw->hjw/dot_general | solution.py:15
  34.9 0.4 convolution_add_fusion.10
  35.3 4.6 %collective-permute-start.1 = (f32[4,128,128]{2,1,0:T(8,128)S(1)}, f32[4,128,128]{2,1,0:T(8,128)S(1)}, u32[]{:S(2)}, u32[]{:S(2)}) collective-permute-start(f32[4,128,128]{2,1,0:T(8,128)S(1)} %convolution_add_fusion.10), channel_id=1, source_target_pairs={{0,4},{4,8},{8,12},{1,5},{5,9},{9,13},{2,6},{6,10},{10,14},{3,7},{... | collective-permute-start | bytes 786440 | tf_op jit(solution)/shard_map/ppermute | solution.py:64
  39.9 1.6 %collective-permute-done.4 = f32[4,128,128]{2,1,0:T(8,128)S(1)} collective-permute-done((f32[4,128,128]{2,1,0:T(8,128)S(1)}, f32[4,128,128]{2,1,0:T(8,128)S(1)}, u32[]{:S(2)}, u32[]{:S(2)}) %collective-permute-start.4) | collective-permute-done | bytes 262176 | tf_op jit(solution)/shard_map/ppermute | solution.py:65
  41.5 0.6 convolution_add_fusion.6
  42.1 1.3 %collective-permute-start.5 = (f32[4,128,128]{2,1,0:T(8,128)S(1)}, f32[4,128,128]{2,1,0:T(8,128)S(1)}, u32[]{:S(2)}, u32[]{:S(2)}) collective-permute-start(f32[4,128,128]{2,1,0:T(8,128)S(1)} %convolution_add_fusion.6), channel_id=1, source_target_pairs={{4,0},{8,4},{12,8},{5,1},{9,5},{13,9},{6,2},{10,6},{14,10},{7,3},{... | collective-permute-start | bytes 786440 | tf_op jit(solution)/shard_map/ppermute | solution.py:65
  43.4 0.5 collective-permute-done.1
  43.9 0.4 convolution_add_fusion.9
  44.3 4.6 %collective-permute-start.2 = (f32[4,128,128]{2,1,0:T(8,128)S(1)}, f32[4,128,128]{2,1,0:T(8,128)S(1)}, u32[]{:S(2)}, u32[]{:S(2)}) collective-permute-start(f32[4,128,128]{2,1,0:T(8,128)S(1)} %convolution_add_fusion.9), channel_id=1, source_target_pairs={{0,4},{4,8},{8,12},{1,5},{5,9},{9,13},{2,6},{6,10},{10,14},{3,7},{... | collective-permute-start | bytes 786440 | tf_op jit(solution)/shard_map/ppermute | solution.py:64
  49.0 1.4 %collective-permute-done.5 = f32[4,128,128]{2,1,0:T(8,128)S(1)} collective-permute-done((f32[4,128,128]{2,1,0:T(8,128)S(1)}, f32[4,128,128]{2,1,0:T(8,128)S(1)}, u32[]{:S(2)}, u32[]{:S(2)}) %collective-permute-start.5) | collective-permute-done | bytes 262176 | tf_op jit(solution)/shard_map/ppermute | solution.py:65
  50.3 0.4 fusion.75
  50.7 1.0 %copy.83 = bf16[4,128,2,128]{3,0,2,1:T(4,128)(2,1)} copy(bf16[4,128,2,128]{3,2,1,0:T(2,128)(2,1)S(1)} %bitcast.221) | data formatting | bytes 524288 | tf_op jit(solution)/shard_map/convert_element_type | solution.py:153
  51.7 0.9 %collective-permute-done.2 = f32[4,128,128]{2,1,0:T(8,128)S(1)} collective-permute-done((f32[4,128,128]{2,1,0:T(8,128)S(1)}, f32[4,128,128]{2,1,0:T(8,128)S(1)}, u32[]{:S(2)}, u32[]{:S(2)}) %collective-permute-start.2) | collective-permute-done | bytes 262176 | tf_op jit(solution)/shard_map/ppermute | solution.py:64
  52.9 0.8 %copy.36 = bf16[128,4,128]{2,1,0:T(4,128)(2,1)} copy(bf16[128,4,128]{2,0,1:T(8,128)(2,1)S(1)} %fusion.14) | data formatting | bytes 262144
  53.6 0.4 convolution_subtract_fusion.1
  54.0 0.3 fusion.2
  54.3 0.7 %fusion.21 = f32[4,256,128]{2,1,0:T(8,128)S(1)} fusion(f32[4,128,256]{2,1,0:T(8,128)S(1)} %fusion.2, f32[4,128]{1,0:T(4,128)S(1)} %get-tuple-element.17, bf16[128,4,128]{2,1,0:T(4,128)(2,1)S(1)} %copy-done.1), kind=kOutput, calls=%fused_computation.63 | convolution fusion | flops 100794368 | bytes 1181696 | tf_op jit(solution)/shard_map/hij,hid->hjd/dot_general | solution.py:15
  55.0 0.3 fusion.53
  55.3 0.5 fusion.25
  56.0 0.8 %copy.37 = bf16[128,4,128]{2,1,0:T(4,128)(2,1)} copy(bf16[128,4,128]{2,0,1:T(8,128)(2,1)S(1)} %fusion.30) | data formatting | bytes 262144
  56.8 0.6 fusion.1
  57.4 0.6 fusion.80
  58.0 0.4 fusion.8
  58.4 0.4 fusion.7
  58.8 1.0 %convolution_add_fusion.3 = f32[4,256,128]{2,1,0:T(8,128)S(1)} fusion(f32[4,256,128]{2,1,0:T(8,128)S(1)} %fusion.7, f32[4,256,256]{2,1,0:T(8,128)S(1)} %fusion.1, f32[4,256,128]{2,1,0:T(8,128)S(1)} %broadcast_multiply_fusion), kind=kOutput, calls=%fused_computation.6 | convolution fusion | flops 201457664 | bytes 2621440 | tf_op jit(solution)/shard_map/hji,hjd->hid/dot_general | solution.py:15
  59.8 1.8 %fusion.10 = bf16[4,256,128]{2,1,0:T(8,128)(2,1)S(1)} fusion(f32[4,256,128]{2,1,0:T(8,128)S(1)} %convolution_add_fusion.3, f32[4,256,128]{2,1,0:T(8,128)S(1)} %broadcast_multiply_fusion, f32[4,256]{1,0:T(4,128)S(1)} %add_rsqrt_fusion), kind=kOutput, calls=%fused_computation.23 | output fusion | flops 656511 | bytes 1314816 | tf_op jit(solution)/shard_map/mul | solution.py:144
  61.6 1.0 %copy.84 = bf16[4,128,2,128]{3,0,2,1:T(4,128)(2,1)} copy(bf16[4,128,2,128]{3,2,1,0:T(2,128)(2,1)S(1)} %bitcast.220) | data formatting | bytes 524288 | tf_op jit(solution)/shard_map/convert_element_type | solution.py:153
  (25 shorter events, 1.8 us)
Async XLA Ops:
  0.6 21.5 %copy-start = (bf16[128,4,128]{2,1,0:T(4,128)(2,1)S(1)}, bf16[128,4,128]{2,1,0:T(4,128)(2,1)}, u32[]{:S(2)}) copy-start(bf16[128,4,128]{2,1,0:T(4,128)(2,1)} %param.7) | copy-start | bytes 393220
  13.0 1.0 %copy-start.2 = (bf16[128,2,4,128]{3,2,1,0:T(4,128)(2,1)S(1)}, bf16[128,2,4,128]{3,2,1,0:T(4,128)(2,1)}, u32[]{:S(2)}) copy-start(bf16[128,2,4,128]{3,2,1,0:T(4,128)(2,1)} %param.6) | copy-start | bytes 786436
  15.0 19.9 %collective-permute-start = (f32[4,128,128]{2,1,0:T(8,128)S(1)}, f32[4,128,128]{2,1,0:T(8,128)S(1)}, u32[]{:S(2)}, u32[]{:S(2)}) collective-permute-start(f32[4,128,128]{2,1,0:T(8,128)S(1)} %convolution_multiply_fusion.9), channel_id=1, source_target_pairs={{0,4},{4,8},{8,12},{1,5},{5,9},{9,13},{2,6},{6,10},{10,14},{3,7},{... | collective-permute-start | bytes 786440 | tf_op jit(solution)/shard_map/ppermute | solution.py:64
  20.1 0.9 %copy-start.1 = (bf16[128,4,128]{2,1,0:T(4,128)(2,1)S(1)}, bf16[128,4,128]{2,1,0:T(4,128)(2,1)}, u32[]{:S(2)}) copy-start(bf16[128,4,128]{2,1,0:T(4,128)(2,1)} %param.4) | copy-start | bytes 393220
  22.5 9.7 %collective-permute-start.3 = (f32[4,128,128]{2,1,0:T(8,128)S(1)}, f32[4,128,128]{2,1,0:T(8,128)S(1)}, u32[]{:S(2)}, u32[]{:S(2)}) collective-permute-start(f32[4,128,128]{2,1,0:T(8,128)S(1)} %fusion.48), channel_id=1, source_target_pairs={{4,0},{8,4},{12,8},{5,1},{9,5},{13,9},{6,2},{10,6},{14,10},{7,3},{... | collective-permute-start | bytes 786440 | tf_op jit(solution)/shard_map/ppermute | solution.py:65
  32.7 8.7 %collective-permute-start.4 = (f32[4,128,128]{2,1,0:T(8,128)S(1)}, f32[4,128,128]{2,1,0:T(8,128)S(1)}, u32[]{:S(2)}, u32[]{:S(2)}) collective-permute-start(f32[4,128,128]{2,1,0:T(8,128)S(1)} %convolution_add_fusion.7), channel_id=1, source_target_pairs={{4,0},{8,4},{12,8},{5,1},{9,5},{13,9},{6,2},{10,6},{14,10},{7,3},{... | collective-permute-start | bytes 786440 | tf_op jit(solution)/shard_map/ppermute | solution.py:65
  35.3 8.6 %collective-permute-start.1 = (f32[4,128,128]{2,1,0:T(8,128)S(1)}, f32[4,128,128]{2,1,0:T(8,128)S(1)}, u32[]{:S(2)}, u32[]{:S(2)}) collective-permute-start(f32[4,128,128]{2,1,0:T(8,128)S(1)} %convolution_add_fusion.10), channel_id=1, source_target_pairs={{0,4},{4,8},{8,12},{1,5},{5,9},{9,13},{2,6},{6,10},{10,14},{3,7},{... | collective-permute-start | bytes 786440 | tf_op jit(solution)/shard_map/ppermute | solution.py:64
  42.1 8.3 %collective-permute-start.5 = (f32[4,128,128]{2,1,0:T(8,128)S(1)}, f32[4,128,128]{2,1,0:T(8,128)S(1)}, u32[]{:S(2)}, u32[]{:S(2)}) collective-permute-start(f32[4,128,128]{2,1,0:T(8,128)S(1)} %convolution_add_fusion.6), channel_id=1, source_target_pairs={{4,0},{8,4},{12,8},{5,1},{9,5},{13,9},{6,2},{10,6},{14,10},{7,3},{... | collective-permute-start | bytes 786440 | tf_op jit(solution)/shard_map/ppermute | solution.py:65
  44.3 8.3 %collective-permute-start.2 = (f32[4,128,128]{2,1,0:T(8,128)S(1)}, f32[4,128,128]{2,1,0:T(8,128)S(1)}, u32[]{:S(2)}, u32[]{:S(2)}) collective-permute-start(f32[4,128,128]{2,1,0:T(8,128)S(1)} %convolution_add_fusion.9), channel_id=1, source_target_pairs={{0,4},{4,8},{8,12},{1,5},{5,9},{9,13},{2,6},{6,10},{10,14},{3,7},{... | collective-permute-start | bytes 786440 | tf_op jit(solution)/shard_map/ppermute | solution.py:64

commit v14 on v7

--- a/solution.py
+++ b/solution.py
@@ -125,34 +125,34 @@
 
     state_in, end_cot = scan_seq(transition, offset, local_cot)
 
-    produced = mh("hld,hdw->hlw", read_map, state_in) + own_out
+    produced = mh("hld,hdw->lhw", read_map, state_in) + own_out.transpose(1, 0, 2)
     updates = upd_v - mh("hjd,hdw->hjw", proj, state_in)
     d_upd = mh("hij,hiw->hjw", scores, cot) + 2.0 * mh("hjd,hdw->hjw", kn, end_cot)
-    d_w = mh("hij,hiw->hjw", inverse, d_upd)
+    d_w = mh("hij,hiw->jhw", inverse, d_upd)
     touch = jnp.where(visible, mh("hiw,hjw->hij", cot, updates), 0.0)
-    d_qn = mh("hiw,hdw->hid", cot, state_in) + 2.0 * mh("hij,hjd->hid", touch, kn)
-    gram_cot = jnp.where(strict_lower(rows, rows), -2.0 * mh("hiw,hjw->hij", d_w, updates), 0.0)
+    d_qn = mh("hiw,hdw->ihd", cot, state_in) + 2.0 * mh("hij,hjd->ihd", touch, kn)
+    gram_cot = jnp.where(strict_lower(rows, rows), -2.0 * mh("ihw,hjw->hij", d_w, updates), 0.0)
     d_kn = (
-        2.0 * mh("hij,hid->hjd", touch, qn)
-        + 2.0 * mh("hjw,hdw->hjd", updates, end_cot)
-        - mh("hjw,hdw->hjd", d_w, state_in)
-        + mh("hij,hjd->hid", gram_cot, kn)
-        + mh("hji,hjd->hid", gram_cot, kn)
+        2.0 * mh("hij,hid->jhd", touch, qn)
+        + 2.0 * mh("hjw,hdw->jhd", updates, end_cot)
+        - mh("jhw,hdw->jhd", d_w, state_in)
+        + mh("hij,hjd->ihd", gram_cot, kn)
+        + mh("hji,hjd->ihd", gram_cot, kn)
     )
-    d_q = q_scale * (d_qn - jnp.sum(qn * d_qn, axis=-1, keepdims=True) * qn)
-    d_k = k_scale * (d_kn - jnp.sum(kn * d_kn, axis=-1, keepdims=True) * kn)
-
-    def token_major(tensor):
-        return tensor.transpose(1, 0, 2).astype(jnp.bfloat16)
+    qn_t, q_scale_t = qn.transpose(1, 0, 2), q_scale.transpose(1, 0, 2)
+    kn_t, k_scale_t = kn.transpose(1, 0, 2), k_scale.transpose(1, 0, 2)
+    d_q = q_scale_t * (d_qn - jnp.sum(qn_t * d_qn, axis=-1, keepdims=True) * qn_t)
+    d_k = k_scale_t * (d_kn - jnp.sum(kn_t * d_kn, axis=-1, keepdims=True) * kn_t)
 
     def pair_major(tensor):
-        return (
-            tensor.reshape(heads_here, tok_count, 2, head_size)
-            .transpose(1, 2, 0, 3)
-            .astype(jnp.bfloat16)
-        )
+        return tensor.reshape(tok_count, 2, heads_here, head_size).astype(jnp.bfloat16)
 
-    return (token_major(produced), token_major(d_q), pair_major(d_k), pair_major(d_w))
+    return (
+        produced.astype(jnp.bfloat16),
+        d_q.astype(jnp.bfloat16),
+        pair_major(d_k),
+        pair_major(d_w),
+    )
 
 
 def solution(mesh):

time: 58.7 us -> 62.2 us (1.060)
  matrix products: 23.5 us -> 28.7 us
  waiting for transfers between devices: 7.43 us -> 4.09 us
  local copies, waits for them, and re-layouts: 5.45 us -> 7.78 us
  other arithmetic: 3.12 us -> 1.27 us
  starting transfers between devices: 17.8 us -> 18.7 us
    dot_general x23, matrix products: 12.6 us -> 16.7 us  [mm(): return jnp.einsum(spec, *operands, precision=highest)]
    unnamed x8 -> x29, local copies, waits for them, and re-layouts: 2.02 us -> 5.1 us
    ppermute x3, waiting for transfers between devices: 5.33 us -> 2.85 us  [chain_seq(): got_cot = lax.ppermute(bwd_sum, 'seq', left)]
    reshape x0 -> x2, local copies, waits for them, and re-layouts: none -> 2.19 us  [local(): reflect_keys.astype(jnp.float32).reshape(rows, heads_here, head_size)]
    convert_element_type x2, local copies, waits for them, and re-layouts: 2.09 us -> 0.34 us  [pair_major(): tensor.reshape(tok_count, 2, heads_here, head_size).astype(jnp.bfloat16)]
    mul x1 -> x4, other arithmetic: 1.79 us -> 0.25 us  [the longest x1 0.15 us: local(): jnp.sum(kn_t * d_kn, axis=-1, keepdims=True) * kn_t]
    transpose x1 -> x0, local copies, waits for them, and re-layouts: 1.19 us -> none  [local(): reflect_keys.astype(jnp.float32).reshape(rows, heads_here, head_size)]
    dot_general x22, matrix products: 10.9 us -> 12.1 us  [mh(): return jnp.einsum(spec, *operands, precision=lax.Precision.HIGH)]
  transfers between devices with their start and end apart: 6 -> 6, of which waited for: 6 -> 3; matrix products, arithmetic and copies ran while one was open for 16% -> 26% of each run, Pallas kernels for 0% -> 0%
where the time goes in v14:
time: 62.2 us; the launch traced here: 61.8 us
  matrix products  28.7 us (46%)
  starting transfers between devices  18.7 us (30%)
  local copies, waits for them, and re-layouts  7.78 us (13%)
  waiting for transfers between devices  4.09 us (7%)
  other arithmetic  1.27 us (2%)
  between operations  1.24 us (2%)
    dot_general x23, matrix products, mm(): return jnp.einsum(spec, *operands, precision=highest)  16.7 us
    ppermute x3, starting transfers between devices, chain_seq(): got_sum = lax.ppermute(fwd_sum, 'seq', right)  14.6 us
    dot_general x22, matrix products, mh(): return jnp.einsum(spec, *operands, precision=lax.Precision.HIGH)  12.1 us
    unnamed x29, local copies, waits for them, and re-layouts  5.1 us
    ppermute x3, starting transfers between devices, chain_seq(): got_cot = lax.ppermute(bwd_sum, 'seq', left)  4.07 us
    ppermute x3, waiting for transfers between devices, chain_seq(): got_cot = lax.ppermute(bwd_sum, 'seq', left)  2.85 us
    reshape x2, local copies, waits for them, and re-layouts, local(): reflect_keys.astype(jnp.float32).reshape(rows, heads_here, head_size)  2.19 us
  transfers between devices with their start and end apart: 6, of which 3 were waited for; matrix products, arithmetic and copies ran while one was open for 26% of the time, Pallas kernels for 0%

profile of v14, /device:TPU:0, one launch (start us, length us, event | category | flops | bytes accessed | tf_op | source)
XLA Modules:
  0.0 61.8 jit_solution(1570932303841752701)
XLA Ops:
  0.7 1.2 %copy.39 = f32[128,2,4,128]{3,1,0,2:T(2,128)S(1)} copy(bf16[128,2,4,128]{3,2,1,0:T(4,128)(2,1)} %param.5) | data formatting | bytes 786432 | tf_op jit(solution)/shard_map/reshape | solution.py:107
  2.3 0.9 %fusion.5 = f32[4,16,16,16]{3,2,1,0:T(8,128)S(1)} fusion(f32[4,16,16,128]{3,2,1,0:T(8,128)S(1)} %bitcast.207, pred[16,16]{1,0:T(8,128)(4,1)S(1)} %iota_compare_fusion.7), kind=kOutput, calls=%fused_computation.13 | convolution fusion | flops 25198592 | bytes 590080 | tf_op jit(solution)/shard_map/hpid,hpjd->hpij/dot_general | solution.py:11
  3.2 0.7 %fusion.77 = f32[4,16,16,16]{3,2,1,0:T(8,128)S(1)} fusion(f32[4,16,16,16]{3,2,1,0:T(8,128)S(1)} %fusion.5), kind=kOutput, calls=%fused_computation.140 | convolution fusion | flops 3145728 | bytes 131072 | tf_op jit(solution)/shard_map/hpij,hpjk->hpik/dot_general | solution.py:11
  3.9 0.7 %fusion.78 = f32[4,16,16,16]{3,2,1,0:T(8,128)S(1)} fusion(f32[4,16,16,16]{3,2,1,0:T(8,128)S(1)} %fusion.77), kind=kOutput, calls=%fused_computation.141 | convolution fusion | flops 3145728 | bytes 131072 | tf_op jit(solution)/shard_map/hpij,hpjk->hpik/dot_general | solution.py:11
  4.6 0.7 %convolution_add_fusion.2 = f32[4,16,16,16]{3,2,1,0:T(8,128)S(1)} fusion(f32[4,16,16,16]{3,2,1,0:T(8,128)S(1)} %fusion.77, f32[4,16,16,16]{3,2,1,0:T(8,128)S(1)} %fusion.5, f32[16,16]{1,0:T(8,128)S(1)} %fusion.61), kind=kOutput, calls=%fused_computation.6 | convolution fusion | flops 3178496 | bytes 197632 | tf_op jit(solution)/shard_map/hpij,hpjk->hpik/dot_general | solution.py:11
  5.2 0.6 %fusion.79 = f32[4,16,16,16]{3,2,1,0:T(8,128)S(1)} fusion(f32[4,16,16,16]{3,2,1,0:T(8,128)S(1)} %fusion.78), kind=kOutput, calls=%fused_computation.142 | convolution fusion | flops 3145728 | bytes 131072 | tf_op jit(solution)/shard_map/hpij,hpjk->hpik/dot_general | solution.py:11
  5.9 0.6 %convolution_add_fusion.1 = f32[4,16,16,16]{3,2,1,0:T(8,128)S(1)} fusion(f32[4,16,16,16]{3,2,1,0:T(8,128)S(1)} %convolution_add_fusion.2, f32[4,16,16,16]{3,2,1,0:T(8,128)S(1)} %fusion.78), kind=kOutput, calls=%fused_computation.5 | convolution fusion | flops 3162112 | bytes 196608 | tf_op jit(solution)/shard_map/hpij,hpjk->hpik/dot_general | solution.py:11
  6.5 0.6 %convolution_add_fusion = f32[4,16,16,16]{3,2,1,0:T(8,128)S(1)} fusion(f32[4,16,16,16]{3,2,1,0:T(8,128)S(1)} %convolution_add_fusion.1, f32[4,16,16,16]{3,2,1,0:T(8,128)S(1)} %fusion.79), kind=kOutput, calls=%fused_computation.4 | convolution fusion | flops 3162112 | bytes 196608 | tf_op jit(solution)/shard_map/hpij,hpjk->hpik/dot_general | solution.py:11
  7.2 0.5 convolution_multiply_fusion.7
  7.8 0.4 fusion.73
  8.1 0.4 convolution_negate_fusion.3
  8.7 0.5 convolution_multiply_fusion.6
  9.3 0.4 fusion.74
  9.7 0.4 convolution_negate_fusion.2
  10.2 0.5 convolution_multiply_fusion.5
  10.8 0.4 fusion.75
  11.2 0.4 convolution_negate_fusion.1
  11.8 0.7 %convolution_multiply_fusion.4 = f32[4,128,128]{2,1,0:T(8,128)S(1)} fusion(f32[4,1,2,128,128]{4,3,2,0,1:T(8,128)S(1)} %bitcast.211), kind=kOutput, calls=%fused_computation.41 | convolution fusion | flops 100728832 | bytes 786432 | tf_op jit(solution)/shard_map/hpid,hpjd->hpij/dot_general | solution.py:11
  12.5 0.6 fusion.42
  13.1 0.7 %fusion.19 = f32[4,1,128,128]{3,2,0,1:T(8,128)S(1)} fusion(f32[4,128,128]{1,2,0:T(8,128)S(1)} %fusion.42, f32[4,1,2,128,128]{4,3,2,0,1:T(8,128)S(1)} %fusion.24), kind=kOutput, calls=%fused_computation.40 | convolution fusion | flops 100728832 | bytes 786432 | tf_op jit(solution)/shard_map/hpij,hpjk->hpik/dot_general | solution.py:11
  13.8 0.3 copy-done.11
  14.0 0.4 fusion.29
  14.5 0.6 %convolution_multiply_fusion.9 = f32[4,128,128]{2,1,0:T(8,128)S(1)} fusion(f32[4,256,128]{2,1,0:T(8,128)S(1)} %broadcast_multiply_fusion, f32[4,256,128]{2,1,0:T(8,128)S(1)} %fusion.29), kind=kOutput, calls=%fused_computation.50 | convolution fusion | flops 100728832 | bytes 1310720 | tf_op jit(solution)/shard_map/hjd,hjw->hdw/dot_general | solution.py:15
  15.1 5.6 %collective-permute-start = (f32[4,128,128]{2,1,0:T(8,128)S(1)}, f32[4,128,128]{2,1,0:T(8,128)}, u32[]{:S(2)}, u32[]{:S(2)}) collective-permute-start(f32[4,128,128]{2,1,0:T(8,128)S(1)} %convolution_multiply_fusion.9), channel_id=1, source_target_pairs={{0,4},{4,8},{8,12},{1,5},{5,9},{9,13},{2,6},{6,10},{10,14},{3,7},{... | collective-permute-start | bytes 786440 | tf_op jit(solution)/shard_map/ppermute | solution.py:64
  20.8 0.6 fusion.31
  21.4 0.3 copy-done.10
  22.0 0.4 fusion.12
  22.4 0.6 %convolution_subtract_fusion.2 = f32[4,128,128]{1,2,0:T(8,128)S(1)} fusion(f32[4,128,256]{2,1,0:T(8,128)S(1)} %fusion.12, f32[4,256,128]{2,1,0:T(8,128)S(1)} %fusion.31, bf16[128,4,128]{0,2,1:T(8,128)(2,1)S(1)} %copy.51, f32[4,128]{1,0:T(4,128)S(1)} %get-tuple-element.23), kind=kOutput, calls=%fused_computation.49 | convolution fusion | flops 100859904 | bytes 1443840 | tf_op jit(solution)/shard_map/hij,hjd->hid/dot_general | solution.py:15
  23.1 0.2 fusion.54
  23.3 1.3 %collective-permute-start.3 = (f32[4,128,128]{2,1,0:T(8,128)S(1)}, f32[4,128,128]{2,1,0:T(8,128)S(1)}, u32[]{:S(2)}, u32[]{:S(2)}) collective-permute-start(f32[4,128,128]{2,1,0:T(8,128)S(1)} %fusion.54), channel_id=1, source_target_pairs={{4,0},{8,4},{12,8},{5,1},{9,5},{13,9},{6,2},{10,6},{14,10},{7,3},{... | collective-permute-start | bytes 786440 | tf_op jit(solution)/shard_map/ppermute | solution.py:65
  24.6 1.3 %convolution_bitcast_fusion.2 = f32[128,4,128]{0,2,1:T(8,128)} fusion(f32[4,128,256]{2,1,0:T(8,128)S(1)} %fusion.12, f32[4,256,128]{2,1,0:T(8,128)S(1)} %fusion.29), kind=kOutput, calls=%fused_computation.34 | convolution fusion | flops 100663296 | bytes 1310720 | tf_op jit(solution)/shard_map/hij,hjd->hid/dot_general | solution.py:15
  26.0 0.6 %fusion.20 = f32[4,128,128]{2,1,0:T(8,128)S(1)} fusion(f32[4,256,128]{2,1,0:T(8,128)S(1)} %broadcast_multiply_fusion, f32[4,256,128]{2,1,0:T(8,128)S(1)} %fusion.31, f32[128,128]{1,0:T(8,128)S(1)} %fusion.60), kind=kOutput, calls=%fused_computation.52 | convolution fusion | flops 100794368 | bytes 1376256 | tf_op jit(solution)/shard_map/hjd,hjw->hdw/dot_general | solution.py:15
  26.6 1.3 %convolution_add_fusion.9 = f32[4,128,128]{2,1,0:T(8,128)S(1)} fusion(f32[4,128,128]{2,1,0:T(8,128)S(1)} %convolution_multiply_fusion.9, f32[4,128,128]{2,1,0:T(8,128)S(1)} %fusion.20, f32[4,128,128]{2,1,0:T(8,128)} %collective-permute-done), kind=kOutput, calls=%fused_computation.38 | convolution fusion | flops 100728832 | bytes 1048576 | tf_op jit(solution)/shard_map/hij,hjk->hik/dot_general | solution.py:11
  28.0 4.6 %collective-permute-start.1 = (f32[4,128,128]{2,1,0:T(8,128)S(1)}, f32[4,128,128]{2,1,0:T(8,128)S(1)}, u32[]{:S(2)}, u32[]{:S(2)}) collective-permute-start(f32[4,128,128]{2,1,0:T(8,128)S(1)} %convolution_add_fusion.9), channel_id=1, source_target_pairs={{0,4},{4,8},{8,12},{1,5},{5,9},{9,13},{2,6},{6,10},{10,14},{3,7},{... | collective-permute-start | bytes 786440 | tf_op jit(solution)/shard_map/ppermute | solution.py:64
  32.6 1.1 %fusion.57 = f32[4,256,128]{1,2,0:T(8,128)} fusion(f32[4,128,256]{2,1,0:T(8,128)S(1)} %fusion.12, bf16[4,128,128]{2,0,1:T(4,128)(2,1)S(1)} %bitcast.206), kind=kOutput, calls=%fused_computation.114 | convolution fusion | flops 100663296 | bytes 1179648 | tf_op jit(solution)/shard_map/hij,hiw->hjw/dot_general | solution.py:15
  33.7 1.3 %convolution_add_fusion.6 = f32[4,128,128]{2,1,0:T(8,128)} fusion(f32[4,128,128]{2,1,0:T(8,128)S(1)} %fusion.54, f32[4,128,128]{2,1,0:T(8,128)S(1)} %fusion.20, f32[4,128,128]{2,1,0:T(8,128)S(1)} %collective-permute-done.3), kind=kOutput, calls=%fused_computation.31 | convolution fusion | flops 100728832 | bytes 1048576 | tf_op jit(solution)/shard_map/hji,hjk->hik/dot_general | solution.py:11
  35.0 1.3 %collective-permute-start.4 = (f32[4,128,128]{2,1,0:T(8,128)}, f32[4,128,128]{2,1,0:T(8,128)}, u32[]{:S(2)}, u32[]{:S(2)}) collective-permute-start(f32[4,128,128]{2,1,0:T(8,128)} %convolution_add_fusion.6), channel_id=1, source_target_pairs={{4,0},{8,4},{12,8},{5,1},{9,5},{13,9},{6,2},{10,6},{14,10},{7,3},{... | collective-permute-start | bytes 786440 | tf_op jit(solution)/shard_map/ppermute | solution.py:65
  36.3 1.2 %collective-permute-done.1 = f32[4,128,128]{2,1,0:T(8,128)S(1)} collective-permute-done((f32[4,128,128]{2,1,0:T(8,128)S(1)}, f32[4,128,128]{2,1,0:T(8,128)S(1)}, u32[]{:S(2)}, u32[]{:S(2)}) %collective-permute-start.1) | collective-permute-done | bytes 262176 | tf_op jit(solution)/shard_map/ppermute | solution.py:64
  37.5 1.1 %convolution_add_fusion.8 = f32[4,128,128]{2,1,0:T(8,128)} fusion(f32[4,128,128]{2,1,0:T(8,128)S(1)} %convolution_multiply_fusion.9, f32[4,128,128]{2,1,0:T(8,128)S(1)} %fusion.20, f32[4,128,128]{2,1,0:T(8,128)S(1)} %collective-permute-done.1), kind=kOutput, calls=%fused_computation.37 | convolution fusion | flops 100728832 | bytes 1048576 | tf_op jit(solution)/shard_map/hij,hjk->hik/dot_general | solution.py:11
  38.6 4.4 %collective-permute-start.2 = (f32[4,128,128]{2,1,0:T(8,128)}, f32[4,128,128]{2,1,0:T(8,128)S(1)}, u32[]{:S(2)}, u32[]{:S(2)}) collective-permute-start(f32[4,128,128]{2,1,0:T(8,128)} %convolution_add_fusion.8), channel_id=1, source_target_pairs={{0,4},{4,8},{8,12},{1,5},{5,9},{9,13},{2,6},{6,10},{10,14},{3,7},{... | collective-permute-start | bytes 786440 | tf_op jit(solution)/shard_map/ppermute | solution.py:64
  43.1 1.0 %copy.67 = f32[256,4,128]{0,2,1:T(8,128)} copy(f32[256,4,128]{2,0,1:T(8,128)S(1)} %bitcast.214) | data formatting | bytes 1048576 | tf_op jit(solution)/shard_map/reshape | solution.py:107
  44.1 0.3 collective-permute-done.4
  44.4 2.2 %convolution_add_fusion.5 = f32[4,128,128]{2,1,0:T(8,128)} fusion(f32[4,128,128]{2,1,0:T(8,128)S(1)} %fusion.54, f32[4,128,128]{2,1,0:T(8,128)S(1)} %fusion.20, f32[4,128,128]{2,1,0:T(8,128)} %collective-permute-done.4), kind=kOutput, calls=%fused_computation.30 | convolution fusion | flops 100728832 | bytes 1048576 | tf_op jit(solution)/shard_map/hji,hjk->hik/dot_general | solution.py:11
  46.6 1.5 %collective-permute-start.5 = (f32[4,128,128]{2,1,0:T(8,128)}, f32[4,128,128]{2,1,0:T(8,128)S(1)}, u32[]{:S(2)}, u32[]{:S(2)}) collective-permute-start(f32[4,128,128]{2,1,0:T(8,128)} %convolution_add_fusion.5), channel_id=1, source_target_pairs={{4,0},{8,4},{12,8},{5,1},{9,5},{13,9},{6,2},{10,6},{14,10},{7,3},{... | collective-permute-start | bytes 786440 | tf_op jit(solution)/shard_map/ppermute | solution.py:65
  48.2 0.4 convolution_subtract_fusion.1
  48.5 0.3 fusion.4
  48.9 0.6 %convolution_multiply_fusion.8 = f32[4,128,128]{2,1,0:T(8,128)S(1)} fusion(f32[4,256,128]{2,1,0:T(8,128)S(1)} %broadcast_multiply_fusion, f32[4,128,256]{2,1,0:T(8,128)S(1)} %fusion.4), kind=kOutput, calls=%fused_computation.48 | convolution fusion | flops 100728832 | bytes 1310720 | tf_op jit(solution)/shard_map/hij,hjd->ihd/dot_general | solution.py:15
  49.5 0.3 copy-done.3
  49.8 0.4 fusion.21
  50.2 0.3 fusion.17
  50.6 0.8 %copy.70 = bf16[128,4,128]{2,1,0:T(4,128)(2,1)} copy(bf16[128,4,128]{0,2,1:T(8,128)(2,1)S(1)} %fusion.21) | data formatting | bytes 262144
  51.4 0.8 %copy.71 = bf16[128,4,128]{2,1,0:T(4,128)(2,1)} copy(bf16[128,4,128]{0,2,1:T(8,128)(2,1)S(1)} %fusion.22) | data formatting | bytes 262144
  52.2 0.4 fusion.35
  52.6 2.5 %collective-permute-done.5 = f32[4,128,128]{2,1,0:T(8,128)S(1)} collective-permute-done((f32[4,128,128]{2,1,0:T(8,128)}, f32[4,128,128]{2,1,0:T(8,128)S(1)}, u32[]{:S(2)}, u32[]{:S(2)}) %collective-permute-start.5) | collective-permute-done | bytes 262176 | tf_op jit(solution)/shard_map/ppermute | solution.py:65
  55.1 0.4 fusion.10
  55.6 0.4 fusion.76
  56.0 0.7 %fusion.2 = f32[4,256,256]{2,1,0:T(8,128)S(1)} fusion(f32[256,4,128]{0,2,1:T(8,128)S(1)} %get-tuple-element.25, f32[4,256,128]{2,1,0:T(8,128)S(1)} %convolution_subtract_fusion.1, pred[256,256]{1,0:T(8,128)(4,1)S(1)} %iota_compare_fusion.4), kind=kOutput, calls=%fused_computation.3 | convolution fusion | flops 201850880 | bytes 2162688 | tf_op jit(solution)/shard_map/ihw,hjw->hij/dot_general | solution.py:15
  56.6 0.7 %fusion.80 = f32[4,128,256]{2,1,0:T(8,128)S(1)} fusion(f32[4,256,128]{2,1,0:T(8,128)S(1)} %broadcast_multiply_fusion, f32[4,256,256]{2,1,0:T(8,128)S(1)} %fusion.2), kind=kOutput, calls=%fused_computation.143 | convolution fusion | flops 201326592 | bytes 2097152 | tf_op jit(solution)/shard_map/hij,hjd->ihd/dot_general | solution.py:15
  57.3 0.4 fusion.11
  57.7 0.4 fusion.9
  58.1 0.6 %fusion.3 = f32[256,4,128]{0,2,1:T(8,128)S(1)} fusion(f32[4,128,256]{2,1,0:T(8,128)S(1)} %fusion.9, f32[4,256,128]{2,1,0:T(8,128)S(1)} %broadcast_multiply_fusion, f32[4,256,256]{2,1,0:T(8,128)S(1)} %fusion.2), kind=kOutput, calls=%fused_computation.8 | convolution fusion | flops 201457664 | bytes 2621440 | tf_op jit(solution)/shard_map/hji,hjd->ihd/dot_general | solution.py:15
  58.8 0.4 copy-done.2
  59.5 1.0 %copy.72 = bf16[128,2,4,128]{3,2,1,0:T(4,128)(2,1)} copy(bf16[128,2,4,128]{3,1,0,2:T(2,128)(2,1)S(1)} %bitcast.224) | data formatting | bytes 524288
  60.7 1.0 %copy.73 = bf16[128,2,4,128]{3,2,1,0:T(4,128)(2,1)} copy(bf16[128,2,4,128]{3,1,0,2:T(2,128)(2,1)S(1)} %bitcast.225) | data formatting | bytes 524288
  (46 shorter events, 2.0 us)
Async XLA Ops:
  0.6 22.5 %copy-start = (bf16[128,4,128]{2,1,0:T(4,128)(2,1)S(1)}, bf16[128,4,128]{2,1,0:T(4,128)(2,1)}, u32[]{:S(2)}) copy-start(bf16[128,4,128]{2,1,0:T(4,128)(2,1)} %param.7) | copy-start | bytes 393220
  11.8 9.0 %copy-start.6 = (f32[4,1,128,128]{3,2,0,1:T(8,128)}, f32[4,1,128,128]{3,2,0,1:T(8,128)S(1)}, u32[]{:S(2)}) copy-start(f32[4,1,128,128]{3,2,0,1:T(8,128)S(1)} %get-tuple-element.12) | copy-start | bytes 786436
  11.8 9.0 %copy-start.8 = (f32[4,1,128,128]{3,2,0,1:T(8,128)}, f32[4,1,128,128]{3,2,0,1:T(8,128)S(1)}, u32[]{:S(2)}) copy-start(f32[4,1,128,128]{3,2,0,1:T(8,128)S(1)} %get-tuple-element.13) | copy-start | bytes 786436
  13.1 1.0 %copy-start.11 = (bf16[128,2,4,128]{3,2,1,0:T(4,128)(2,1)S(1)}, bf16[128,2,4,128]{3,2,1,0:T(4,128)(2,1)}, u32[]{:S(2)}) copy-start(bf16[128,2,4,128]{3,2,1,0:T(4,128)(2,1)} %param.6) | copy-start | bytes 786436
  13.8 7.0 %copy-start.4 = (f32[4,1,128,128]{3,2,0,1:T(8,128)}, f32[4,1,128,128]{3,2,0,1:T(8,128)S(1)}, u32[]{:S(2)}) copy-start(f32[4,1,128,128]{3,2,0,1:T(8,128)S(1)} %fusion.19) | copy-start | bytes 786436
  15.1 11.5 %collective-permute-start = (f32[4,128,128]{2,1,0:T(8,128)S(1)}, f32[4,128,128]{2,1,0:T(8,128)}, u32[]{:S(2)}, u32[]{:S(2)}) collective-permute-start(f32[4,128,128]{2,1,0:T(8,128)S(1)} %convolution_multiply_fusion.9), channel_id=1, source_target_pairs={{0,4},{4,8},{8,12},{1,5},{5,9},{9,13},{2,6},{6,10},{10,14},{3,7},{... | collective-permute-start | bytes 786440 | tf_op jit(solution)/shard_map/ppermute | solution.py:64
  20.8 0.9 %copy-start.10 = (bf16[128,4,128]{2,1,0:T(4,128)(2,1)S(1)}, bf16[128,4,128]{2,1,0:T(4,128)(2,1)}, u32[]{:S(2)}) copy-start(bf16[128,4,128]{2,1,0:T(4,128)(2,1)} %param.4) | copy-start | bytes 393220
  23.3 10.4 %collective-permute-start.3 = (f32[4,128,128]{2,1,0:T(8,128)S(1)}, f32[4,128,128]{2,1,0:T(8,128)S(1)}, u32[]{:S(2)}, u32[]{:S(2)}) collective-permute-start(f32[4,128,128]{2,1,0:T(8,128)S(1)} %fusion.54), channel_id=1, source_target_pairs={{4,0},{8,4},{12,8},{5,1},{9,5},{13,9},{6,2},{10,6},{14,10},{7,3},{... | collective-permute-start | bytes 786440 | tf_op jit(solution)/shard_map/ppermute | solution.py:65
  28.0 9.5 %collective-permute-start.1 = (f32[4,128,128]{2,1,0:T(8,128)S(1)}, f32[4,128,128]{2,1,0:T(8,128)S(1)}, u32[]{:S(2)}, u32[]{:S(2)}) collective-permute-start(f32[4,128,128]{2,1,0:T(8,128)S(1)} %convolution_add_fusion.9), channel_id=1, source_target_pairs={{0,4},{4,8},{8,12},{1,5},{5,9},{9,13},{2,6},{6,10},{10,14},{3,7},{... | collective-permute-start | bytes 786440 | tf_op jit(solution)/shard_map/ppermute | solution.py:64
  35.0 9.4 %collective-permute-start.4 = (f32[4,128,128]{2,1,0:T(8,128)}, f32[4,128,128]{2,1,0:T(8,128)}, u32[]{:S(2)}, u32[]{:S(2)}) collective-permute-start(f32[4,128,128]{2,1,0:T(8,128)} %convolution_add_fusion.6), channel_id=1, source_target_pairs={{4,0},{8,4},{12,8},{5,1},{9,5},{13,9},{6,2},{10,6},{14,10},{7,3},{... | collective-permute-start | bytes 786440 | tf_op jit(solution)/shard_map/ppermute | solution.py:65
  38.6 9.5 %collective-permute-start.2 = (f32[4,128,128]{2,1,0:T(8,128)}, f32[4,128,128]{2,1,0:T(8,128)S(1)}, u32[]{:S(2)}, u32[]{:S(2)}) collective-permute-start(f32[4,128,128]{2,1,0:T(8,128)} %convolution_add_fusion.8), channel_id=1, source_target_pairs={{0,4},{4,8},{8,12},{1,5},{5,9},{9,13},{2,6},{6,10},{10,14},{3,7},{... | collective-permute-start | bytes 786440 | tf_op jit(solution)/shard_map/ppermute | solution.py:64
  46.6 8.5 %collective-permute-start.5 = (f32[4,128,128]{2,1,0:T(8,128)}, f32[4,128,128]{2,1,0:T(8,128)S(1)}, u32[]{:S(2)}, u32[]{:S(2)}) collective-permute-start(f32[4,128,128]{2,1,0:T(8,128)} %convolution_add_fusion.5), channel_id=1, source_target_pairs={{4,0},{8,4},{12,8},{5,1},{9,5},{13,9},{6,2},{10,6},{14,10},{7,3},{... | collective-permute-start | bytes 786440 | tf_op jit(solution)/shard_map/ppermute | solution.py:65
  48.9 1.0 %copy-start.3 = (f32[128,4,128]{0,2,1:T(8,128)S(1)}, f32[128,4,128]{0,2,1:T(8,128)}, u32[]{:S(2)}) copy-start(f32[128,4,128]{0,2,1:T(8,128)} %convolution_bitcast_fusion.2) | copy-start | bytes 786436
  52.2 2.9 %copy-start.1 = (f32[4,256,128]{1,2,0:T(8,128)S(1)}, f32[4,256,128]{1,2,0:T(8,128)}, u32[]{:S(2)}) copy-start(f32[4,256,128]{1,2,0:T(8,128)} %fusion.57) | copy-start | bytes 1572868
  52.6 3.0 %copy-start.5 = (f32[4,1,128,128]{3,2,0,1:T(8,128)S(1)}, f32[4,1,128,128]{3,2,0,1:T(8,128)}, u32[]{:S(2)}) copy-start(f32[4,1,128,128]{3,2,0,1:T(8,128)} %copy-done.4) | copy-start | bytes 786436
  52.6 3.0 %copy-start.7 = (f32[4,1,128,128]{3,2,0,1:T(8,128)S(1)}, f32[4,1,128,128]{3,2,0,1:T(8,128)}, u32[]{:S(2)}) copy-start(f32[4,1,128,128]{3,2,0,1:T(8,128)} %copy-done.6) | copy-start | bytes 786436
  52.6 3.0 %copy-start.9 = (f32[4,1,128,128]{3,2,0,1:T(8,128)S(1)}, f32[4,1,128,128]{3,2,0,1:T(8,128)}, u32[]{:S(2)}) copy-start(f32[4,1,128,128]{3,2,0,1:T(8,128)} %copy-done.8) | copy-start | bytes 786436
  58.1 1.0 %copy-start.2 = (f32[256,4,128]{0,2,1:T(8,128)S(1)}, f32[256,4,128]{0,2,1:T(8,128)}, u32[]{:S(2)}) copy-start(f32[256,4,128]{0,2,1:T(8,128)} %copy.67) | copy-start | bytes 1572868

commit v15 on v7

--- a/solution.py
+++ b/solution.py
@@ -65,8 +65,8 @@
         got_cot = lax.ppermute(bwd_sum, "seq", left)
         if hop == count - 2:
             return got_sum, got_cot
-        fwd_sum = mm("hij,hjk->hik", transition, got_sum) + offset
-        bwd_sum = mm("hji,hjk->hik", transition, got_cot) + local_cot
+        fwd_sum = mh("hij,hjk->hik", transition, got_sum) + offset
+        bwd_sum = mh("hji,hjk->hik", transition, got_cot) + local_cot
     zero = jnp.zeros_like(offset)
     return zero, zero
 

time: 58.7 us -> 58.3 us (level)
  matrix products: 23.5 us -> 22.8 us
    dot_general x23 -> x19, matrix products: 12.6 us -> 10.6 us  [mm(): return jnp.einsum(spec, *operands, precision=highest)]
    dot_general x22 -> x26, matrix products: 10.9 us -> 12.2 us  [mh(): return jnp.einsum(spec, *operands, precision=lax.Precision.HIGH)]
  transfers between devices with their start and end apart: 6 -> 6, of which waited for: 6 -> 6; matrix products, arithmetic and copies ran while one was open for 16% -> 15% of each run, Pallas kernels for 0% -> 0%
where the time goes in v15:
time: 58.3 us; the launch traced here: 58 us
  matrix products  22.8 us (39%)
  starting transfers between devices  17.8 us (31%)
  waiting for transfers between devices  7.68 us (13%)
  local copies, waits for them, and re-layouts  5.45 us (9%)
  other arithmetic  3.12 us (5%)
  between operations  1.15 us (2%)
    ppermute x3, starting transfers between devices, chain_seq(): got_sum = lax.ppermute(fwd_sum, 'seq', right)  13.9 us
    dot_general x26, matrix products, mh(): return jnp.einsum(spec, *operands, precision=lax.Precision.HIGH)  12.2 us
    dot_general x19, matrix products, mm(): return jnp.einsum(spec, *operands, precision=highest)  10.6 us
    ppermute x3, waiting for transfers between devices, chain_seq(): got_cot = lax.ppermute(bwd_sum, 'seq', left)  5.33 us
    ppermute x3, starting transfers between devices, chain_seq(): got_cot = lax.ppermute(bwd_sum, 'seq', left)  3.88 us
    ppermute x3, waiting for transfers between devices, chain_seq(): got_sum = lax.ppermute(fwd_sum, 'seq', right)  2.36 us
    convert_element_type x2, local copies, waits for them, and re-layouts, pair_major(): return tensor.reshape(heads_here, tok_count, 2, head_size).transpose(1, 2...  2.09 us
    unnamed x8, local copies, waits for them, and re-layouts  2.02 us
  transfers between devices with their start and end apart: 6, of which 6 were waited for; matrix products, arithmetic and copies ran while one was open for 15% of the time, Pallas kernels for 0%

profile of v15, /device:TPU:0, one launch (start us, length us, event | category | flops | bytes accessed | tf_op | source)
XLA Modules:
  0.0 58.0 jit_solution(837219688557874765)
XLA Ops:
  0.7 1.2 %copy.9 = f32[128,2,4,128]{3,1,0,2:T(2,128)S(1)} copy(bf16[128,2,4,128]{3,2,1,0:T(4,128)(2,1)} %param.5) | data formatting | bytes 786432 | tf_op jit(solution)/shard_map/transpose | solution.py:107
  2.3 0.9 %fusion.3 = f32[4,16,16,16]{3,2,1,0:T(8,128)S(1)} fusion(f32[4,16,16,128]{3,2,1,0:T(8,128)S(1)} %bitcast.204, pred[16,16]{1,0:T(8,128)(4,1)S(1)} %iota_compare_fusion.7), kind=kOutput, calls=%fused_computation.10 | convolution fusion | flops 25198592 | bytes 590080 | tf_op jit(solution)/shard_map/hpid,hpjd->hpij/dot_general | solution.py:11
  3.2 0.6 %fusion.73 = f32[4,16,16,16]{3,2,1,0:T(8,128)S(1)} fusion(f32[4,16,16,16]{3,2,1,0:T(8,128)S(1)} %fusion.3), kind=kOutput, calls=%fused_computation.138 | convolution fusion | flops 3145728 | bytes 131072 | tf_op jit(solution)/shard_map/hpij,hpjk->hpik/dot_general | solution.py:11
  3.9 0.6 %fusion.74 = f32[4,16,16,16]{3,2,1,0:T(8,128)S(1)} fusion(f32[4,16,16,16]{3,2,1,0:T(8,128)S(1)} %fusion.73), kind=kOutput, calls=%fused_computation.139 | convolution fusion | flops 3145728 | bytes 131072 | tf_op jit(solution)/shard_map/hpij,hpjk->hpik/dot_general | solution.py:11
  4.5 0.7 %convolution_add_fusion.2 = f32[4,16,16,16]{3,2,1,0:T(8,128)S(1)} fusion(f32[4,16,16,16]{3,2,1,0:T(8,128)S(1)} %fusion.73, f32[4,16,16,16]{3,2,1,0:T(8,128)S(1)} %fusion.3, f32[16,16]{1,0:T(8,128)S(1)} %fusion.58), kind=kOutput, calls=%fused_computation.5 | convolution fusion | flops 3178496 | bytes 197632 | tf_op jit(solution)/shard_map/hpij,hpjk->hpik/dot_general | solution.py:11
  5.2 0.6 %fusion.75 = f32[4,16,16,16]{3,2,1,0:T(8,128)S(1)} fusion(f32[4,16,16,16]{3,2,1,0:T(8,128)S(1)} %fusion.74), kind=kOutput, calls=%fused_computation.140 | convolution fusion | flops 3145728 | bytes 131072 | tf_op jit(solution)/shard_map/hpij,hpjk->hpik/dot_general | solution.py:11
  5.8 0.6 %convolution_add_fusion.1 = f32[4,16,16,16]{3,2,1,0:T(8,128)S(1)} fusion(f32[4,16,16,16]{3,2,1,0:T(8,128)S(1)} %convolution_add_fusion.2, f32[4,16,16,16]{3,2,1,0:T(8,128)S(1)} %fusion.74), kind=kOutput, calls=%fused_computation.4 | convolution fusion | flops 3162112 | bytes 196608 | tf_op jit(solution)/shard_map/hpij,hpjk->hpik/dot_general | solution.py:11
  6.5 0.6 %convolution_add_fusion = f32[4,16,16,16]{3,2,1,0:T(8,128)S(1)} fusion(f32[4,16,16,16]{3,2,1,0:T(8,128)S(1)} %convolution_add_fusion.1, f32[4,16,16,16]{3,2,1,0:T(8,128)S(1)} %fusion.75), kind=kOutput, calls=%fused_computation.3 | convolution fusion | flops 3162112 | bytes 196608 | tf_op jit(solution)/shard_map/hpij,hpjk->hpik/dot_general | solution.py:11
  7.2 0.5 convolution_multiply_fusion.7
  7.7 0.4 fusion.69
  8.1 0.4 convolution_negate_fusion.3
  8.7 0.5 convolution_multiply_fusion.6
  9.2 0.4 fusion.70
  9.6 0.4 convolution_negate_fusion.2
  10.2 0.5 convolution_multiply_fusion.5
  10.7 0.4 fusion.71
  11.1 0.4 convolution_negate_fusion.1
  11.7 0.7 %convolution_multiply_fusion.4 = f32[4,128,128]{2,1,0:T(8,128)S(1)} fusion(f32[4,1,2,128,128]{4,3,2,0,1:T(8,128)S(1)} %bitcast.208), kind=kOutput, calls=%fused_computation.31 | convolution fusion | flops 100728832 | bytes 786432 | tf_op jit(solution)/shard_map/hpid,hpjd->hpij/dot_general | solution.py:11
  12.4 0.6 %fusion.38 = f32[4,128,128]{1,2,0:T(8,128)S(1)} fusion(f32[4,128,128]{2,1,0:T(8,128)S(1)} %convolution_multiply_fusion.4, f32[4,1,2,128,128]{4,3,2,0,1:T(8,128)S(1)} %fusion.17), kind=kOutput, calls=%fused_computation.88 | convolution fusion | flops 100663296 | bytes 786432 | tf_op jit(solution)/shard_map/hpij,hpjk->hpik/dot_general | solution.py:11
  13.0 0.7 %fusion.12 = f32[4,1,128,128]{3,2,0,1:T(8,128)S(1)} fusion(f32[4,128,128]{1,2,0:T(8,128)S(1)} %fusion.38, f32[4,1,2,128,128]{4,3,2,0,1:T(8,128)S(1)} %fusion.17), kind=kOutput, calls=%fused_computation.30 | convolution fusion | flops 100728832 | bytes 786432 | tf_op jit(solution)/shard_map/hpij,hpjk->hpik/dot_general | solution.py:11
  13.6 0.3 copy-done.2
  13.9 0.4 fusion.22
  14.4 0.6 %convolution_multiply_fusion.9 = f32[4,128,128]{2,1,0:T(8,128)S(1)} fusion(f32[4,256,128]{2,1,0:T(8,128)S(1)} %broadcast_multiply_fusion, f32[4,256,128]{2,1,0:T(8,128)S(1)} %fusion.22), kind=kOutput, calls=%fused_computation.39 | convolution fusion | flops 100728832 | bytes 1310720 | tf_op jit(solution)/shard_map/hjd,hjw->hdw/dot_general | solution.py:15
  15.0 5.1 %collective-permute-start = (f32[4,128,128]{2,1,0:T(8,128)S(1)}, f32[4,128,128]{2,1,0:T(8,128)S(1)}, u32[]{:S(2)}, u32[]{:S(2)}) collective-permute-start(f32[4,128,128]{2,1,0:T(8,128)S(1)} %convolution_multiply_fusion.9), channel_id=1, source_target_pairs={{0,4},{4,8},{8,12},{1,5},{5,9},{9,13},{2,6},{6,10},{10,14},{3,7},{... | collective-permute-start | bytes 786440 | tf_op jit(solution)/shard_map/ppermute | solution.py:64
  20.2 0.6 %fusion.24 = f32[4,256,128]{2,1,0:T(8,128)S(1)} fusion(f32[4,256,128]{2,1,0:T(8,128)S(1)} %broadcast_multiply_fusion, f32[4,1,128,128]{3,2,0,1:T(8,128)S(1)} %get-tuple-element.9, f32[4,1,128,128]{3,2,0,1:T(8,128)S(1)} %get-tuple-element.8, f32[4,1,128,128]{3,2,0,1:T(8,128)S(1)} %fusion.12), kind=kOutput, calls=%fused_computation.61 | convolution fusion | flops 202375168 | bytes 1835008 | tf_op jit(solution)/shard_map/hij,hjd->hid/dot_general | solution.py:15
  21.2 0.4 fusion.10
  21.7 0.4 convolution_subtract_fusion.2
  22.1 0.3 fusion.48
  22.4 1.3 %collective-permute-start.3 = (f32[4,128,128]{2,1,0:T(8,128)S(1)}, f32[4,128,128]{2,1,0:T(8,128)S(1)}, u32[]{:S(2)}, u32[]{:S(2)}) collective-permute-start(f32[4,128,128]{2,1,0:T(8,128)S(1)} %fusion.48), channel_id=1, source_target_pairs={{4,0},{8,4},{12,8},{5,1},{9,5},{13,9},{6,2},{10,6},{14,10},{7,3},{... | collective-permute-start | bytes 786440 | tf_op jit(solution)/shard_map/ppermute | solution.py:65
  23.7 0.4 fusion.76
  24.1 0.6 %fusion.13 = f32[4,128,128]{2,1,0:T(8,128)S(1)} fusion(f32[4,256,128]{2,1,0:T(8,128)S(1)} %broadcast_multiply_fusion, f32[4,256,128]{2,1,0:T(8,128)S(1)} %fusion.24, f32[128,128]{1,0:T(8,128)S(1)} %fusion.55), kind=kOutput, calls=%fused_computation.42 | convolution fusion | flops 100794368 | bytes 1376256 | tf_op jit(solution)/shard_map/hjd,hjw->hdw/dot_general | solution.py:15
  24.7 0.8 %collective-permute-done = f32[4,128,128]{2,1,0:T(8,128)S(1)} collective-permute-done((f32[4,128,128]{2,1,0:T(8,128)S(1)}, f32[4,128,128]{2,1,0:T(8,128)S(1)}, u32[]{:S(2)}, u32[]{:S(2)}) %collective-permute-start) | collective-permute-done | bytes 262176 | tf_op jit(solution)/shard_map/ppermute | solution.py:64
  25.5 0.3 convolution_add_fusion.9
  25.8 4.4 %collective-permute-start.1 = (f32[4,128,128]{2,1,0:T(8,128)S(1)}, f32[4,128,128]{2,1,0:T(8,128)S(1)}, u32[]{:S(2)}, u32[]{:S(2)}) collective-permute-start(f32[4,128,128]{2,1,0:T(8,128)S(1)} %convolution_add_fusion.9), channel_id=1, source_target_pairs={{0,4},{4,8},{8,12},{1,5},{5,9},{9,13},{2,6},{6,10},{10,14},{3,7},{... | collective-permute-start | bytes 786440 | tf_op jit(solution)/shard_map/ppermute | solution.py:64
  30.2 0.5 fusion.51
  30.6 1.4 %collective-permute-done.3 = f32[4,128,128]{2,1,0:T(8,128)S(1)} collective-permute-done((f32[4,128,128]{2,1,0:T(8,128)S(1)}, f32[4,128,128]{2,1,0:T(8,128)S(1)}, u32[]{:S(2)}, u32[]{:S(2)}) %collective-permute-start.3) | collective-permute-done | bytes 262176 | tf_op jit(solution)/shard_map/ppermute | solution.py:65
  32.0 0.4 convolution_add_fusion.6
  32.4 1.3 %collective-permute-start.4 = (f32[4,128,128]{2,1,0:T(8,128)S(1)}, f32[4,128,128]{2,1,0:T(8,128)S(1)}, u32[]{:S(2)}, u32[]{:S(2)}) collective-permute-start(f32[4,128,128]{2,1,0:T(8,128)S(1)} %convolution_add_fusion.6), channel_id=1, source_target_pairs={{4,0},{8,4},{12,8},{5,1},{9,5},{13,9},{6,2},{10,6},{14,10},{7,3},{... | collective-permute-start | bytes 786440 | tf_op jit(solution)/shard_map/ppermute | solution.py:65
  33.7 1.1 %collective-permute-done.1 = f32[4,128,128]{2,1,0:T(8,128)S(1)} collective-permute-done((f32[4,128,128]{2,1,0:T(8,128)S(1)}, f32[4,128,128]{2,1,0:T(8,128)S(1)}, u32[]{:S(2)}, u32[]{:S(2)}) %collective-permute-start.1) | collective-permute-done | bytes 262176 | tf_op jit(solution)/shard_map/ppermute | solution.py:64
  34.8 0.3 convolution_add_fusion.8
  35.1 4.4 %collective-permute-start.2 = (f32[4,128,128]{2,1,0:T(8,128)S(1)}, f32[4,128,128]{2,1,0:T(8,128)S(1)}, u32[]{:S(2)}, u32[]{:S(2)}) collective-permute-start(f32[4,128,128]{2,1,0:T(8,128)S(1)} %convolution_add_fusion.8), channel_id=1, source_target_pairs={{0,4},{4,8},{8,12},{1,5},{5,9},{9,13},{2,6},{6,10},{10,14},{3,7},{... | collective-permute-start | bytes 786440 | tf_op jit(solution)/shard_map/ppermute | solution.py:64
  39.5 1.6 %collective-permute-done.4 = f32[4,128,128]{2,1,0:T(8,128)S(1)} collective-permute-done((f32[4,128,128]{2,1,0:T(8,128)S(1)}, f32[4,128,128]{2,1,0:T(8,128)S(1)}, u32[]{:S(2)}, u32[]{:S(2)}) %collective-permute-start.4) | collective-permute-done | bytes 262176 | tf_op jit(solution)/shard_map/ppermute | solution.py:65
  41.2 0.4 convolution_add_fusion.5
  41.6 1.3 %collective-permute-start.5 = (f32[4,128,128]{2,1,0:T(8,128)S(1)}, f32[4,128,128]{2,1,0:T(8,128)S(1)}, u32[]{:S(2)}, u32[]{:S(2)}) collective-permute-start(f32[4,128,128]{2,1,0:T(8,128)S(1)} %convolution_add_fusion.5), channel_id=1, source_target_pairs={{4,0},{8,4},{12,8},{5,1},{9,5},{13,9},{6,2},{10,6},{14,10},{7,3},{... | collective-permute-start | bytes 786440 | tf_op jit(solution)/shard_map/ppermute | solution.py:65
  42.9 0.5 collective-permute-done.2
  43.4 0.4 convolution_subtract_fusion.1
  43.7 0.3 fusion.2
  44.1 0.3 fusion.53
  44.4 0.5 fusion.32
  44.8 0.3 fusion.15
  45.3 0.8 %copy.36 = bf16[128,4,128]{2,1,0:T(4,128)(2,1)} copy(bf16[128,4,128]{2,0,1:T(8,128)(2,1)S(1)} %fusion.15) | data formatting | bytes 262144
  46.1 0.8 %copy.37 = bf16[128,4,128]{2,1,0:T(4,128)(2,1)} copy(bf16[128,4,128]{2,0,1:T(8,128)(2,1)S(1)} %fusion.37) | data formatting | bytes 262144
  46.8 0.7 %fusion.28 = f32[4,256,128]{2,1,0:T(8,128)S(1)} fusion(f32[4,128,256]{2,1,0:T(8,128)S(1)} %fusion.2, f32[4,128]{1,0:T(4,128)S(1)} %get-tuple-element.17, bf16[128,4,128]{2,1,0:T(4,128)(2,1)S(1)} %copy-done.1), kind=kOutput, calls=%fused_computation.66 | convolution fusion | flops 100794368 | bytes 1181696 | tf_op jit(solution)/shard_map/hij,hid->hjd/dot_general | solution.py:15
  47.5 2.3 %collective-permute-done.5 = f32[4,128,128]{2,1,0:T(8,128)S(1)} collective-permute-done((f32[4,128,128]{2,1,0:T(8,128)S(1)}, f32[4,128,128]{2,1,0:T(8,128)S(1)}, u32[]{:S(2)}, u32[]{:S(2)}) %collective-permute-start.5) | collective-permute-done | bytes 262176 | tf_op jit(solution)/shard_map/ppermute | solution.py:65
  49.8 0.4 fusion.8
  50.2 0.9 %fusion.72 = (bf16[4,256,128]{2,1,0:T(8,128)(2,1)S(1)}, f32[4,256,128]{2,1,0:T(8,128)S(1)}) fusion(f32[4,256,128]{2,1,0:T(8,128)S(1)} %fusion.8, f32[4,1,128,128]{3,2,0,1:T(8,128)S(1)} %get-tuple-element.9, f32[4,1,128,128]{3,2,0,1:T(8,128)S(1)} %get-tuple-element.8, f32[4,1,128,128]{3,2,0,1:T(8,128)S(1)} %fusion.12), kind=kOutput, calls=%fused_computation.137 | convolution fusion | flops 202506240 | bytes 2097152 | tf_op jit(solution)/shard_map/hij,hiw->hjw/dot_general | solution.py:15
  51.1 0.6 %fusion.1 = f32[4,256,256]{2,1,0:T(8,128)S(1)} fusion(f32[4,256,128]{2,1,0:T(8,128)S(1)} %get-tuple-element.21, f32[4,256,128]{2,1,0:T(8,128)S(1)} %convolution_subtract_fusion.1, pred[256,256]{1,0:T(8,128)(4,1)S(1)} %iota_compare_fusion.4), kind=kOutput, calls=%fused_computation.2 | convolution fusion | flops 201850880 | bytes 2162688 | tf_op jit(solution)/shard_map/hiw,hjw->hij/dot_general | solution.py:15
  51.7 0.6 %fusion.77 = f32[4,256,128]{2,1,0:T(8,128)S(1)} fusion(f32[4,256,256]{2,1,0:T(8,128)S(1)} %fusion.1, f32[4,256,128]{2,1,0:T(8,128)S(1)} %broadcast_multiply_fusion), kind=kOutput, calls=%fused_computation.142 | convolution fusion | flops 201326592 | bytes 2097152 | tf_op jit(solution)/shard_map/hij,hjd->hid/dot_general | solution.py:15
  52.3 0.4 fusion.9
  52.7 0.4 fusion.7
  53.1 1.0 %convolution_add_fusion.3 = f32[4,256,128]{2,1,0:T(8,128)S(1)} fusion(f32[4,256,128]{2,1,0:T(8,128)S(1)} %fusion.7, f32[4,256,256]{2,1,0:T(8,128)S(1)} %fusion.1, f32[4,256,128]{2,1,0:T(8,128)S(1)} %broadcast_multiply_fusion), kind=kOutput, calls=%fused_computation.6 | convolution fusion | flops 201457664 | bytes 2621440 | tf_op jit(solution)/shard_map/hji,hjd->hid/dot_general | solution.py:15
  54.1 1.8 %fusion.11 = bf16[4,256,128]{2,1,0:T(8,128)(2,1)S(1)} fusion(f32[4,256,128]{2,1,0:T(8,128)S(1)} %convolution_add_fusion.3, f32[4,256,128]{2,1,0:T(8,128)S(1)} %broadcast_multiply_fusion, f32[4,256]{1,0:T(4,128)S(1)} %add_rsqrt_fusion), kind=kOutput, calls=%fused_computation.23 | output fusion | flops 656511 | bytes 1314816 | tf_op jit(solution)/shard_map/mul | solution.py:143
  55.9 1.0 %copy.84 = bf16[4,128,2,128]{3,0,2,1:T(4,128)(2,1)} copy(bf16[4,128,2,128]{3,2,1,0:T(2,128)(2,1)S(1)} %bitcast.220) | data formatting | bytes 524288 | tf_op jit(solution)/shard_map/convert_element_type | solution.py:152
  57.0 1.0 %copy.83 = bf16[4,128,2,128]{3,0,2,1:T(4,128)(2,1)} copy(bf16[4,128,2,128]{3,2,1,0:T(2,128)(2,1)S(1)} %bitcast.221) | data formatting | bytes 524288 | tf_op jit(solution)/shard_map/convert_element_type | solution.py:152
  (24 shorter events, 1.7 us)
Async XLA Ops:
  0.6 21.4 %copy-start = (bf16[128,4,128]{2,1,0:T(4,128)(2,1)S(1)}, bf16[128,4,128]{2,1,0:T(4,128)(2,1)}, u32[]{:S(2)}) copy-start(bf16[128,4,128]{2,1,0:T(4,128)(2,1)} %param.7) | copy-start | bytes 393220
  13.0 1.0 %copy-start.2 = (bf16[128,2,4,128]{3,2,1,0:T(4,128)(2,1)S(1)}, bf16[128,2,4,128]{3,2,1,0:T(4,128)(2,1)}, u32[]{:S(2)}) copy-start(bf16[128,2,4,128]{3,2,1,0:T(4,128)(2,1)} %param.6) | copy-start | bytes 786436
  15.0 10.5 %collective-permute-start = (f32[4,128,128]{2,1,0:T(8,128)S(1)}, f32[4,128,128]{2,1,0:T(8,128)S(1)}, u32[]{:S(2)}, u32[]{:S(2)}) collective-permute-start(f32[4,128,128]{2,1,0:T(8,128)S(1)} %convolution_multiply_fusion.9), channel_id=1, source_target_pairs={{0,4},{4,8},{8,12},{1,5},{5,9},{9,13},{2,6},{6,10},{10,14},{3,7},{... | collective-permute-start | bytes 786440 | tf_op jit(solution)/shard_map/ppermute | solution.py:64
  20.2 0.9 %copy-start.1 = (bf16[128,4,128]{2,1,0:T(4,128)(2,1)S(1)}, bf16[128,4,128]{2,1,0:T(4,128)(2,1)}, u32[]{:S(2)}) copy-start(bf16[128,4,128]{2,1,0:T(4,128)(2,1)} %param.4) | copy-start | bytes 393220
  22.4 9.7 %collective-permute-start.3 = (f32[4,128,128]{2,1,0:T(8,128)S(1)}, f32[4,128,128]{2,1,0:T(8,128)S(1)}, u32[]{:S(2)}, u32[]{:S(2)}) collective-permute-start(f32[4,128,128]{2,1,0:T(8,128)S(1)} %fusion.48), channel_id=1, source_target_pairs={{4,0},{8,4},{12,8},{5,1},{9,5},{13,9},{6,2},{10,6},{14,10},{7,3},{... | collective-permute-start | bytes 786440 | tf_op jit(solution)/shard_map/ppermute | solution.py:65
  25.8 9.1 %collective-permute-start.1 = (f32[4,128,128]{2,1,0:T(8,128)S(1)}, f32[4,128,128]{2,1,0:T(8,128)S(1)}, u32[]{:S(2)}, u32[]{:S(2)}) collective-permute-start(f32[4,128,128]{2,1,0:T(8,128)S(1)} %convolution_add_fusion.9), channel_id=1, source_target_pairs={{0,4},{4,8},{8,12},{1,5},{5,9},{9,13},{2,6},{6,10},{10,14},{3,7},{... | collective-permute-start | bytes 786440 | tf_op jit(solution)/shard_map/ppermute | solution.py:64
  32.4 8.7 %collective-permute-start.4 = (f32[4,128,128]{2,1,0:T(8,128)S(1)}, f32[4,128,128]{2,1,0:T(8,128)S(1)}, u32[]{:S(2)}, u32[]{:S(2)}) collective-permute-start(f32[4,128,128]{2,1,0:T(8,128)S(1)} %convolution_add_fusion.6), channel_id=1, source_target_pairs={{4,0},{8,4},{12,8},{5,1},{9,5},{13,9},{6,2},{10,6},{14,10},{7,3},{... | collective-permute-start | bytes 786440 | tf_op jit(solution)/shard_map/ppermute | solution.py:65
  35.1 8.3 %collective-permute-start.2 = (f32[4,128,128]{2,1,0:T(8,128)S(1)}, f32[4,128,128]{2,1,0:T(8,128)S(1)}, u32[]{:S(2)}, u32[]{:S(2)}) collective-permute-start(f32[4,128,128]{2,1,0:T(8,128)S(1)} %convolution_add_fusion.8), channel_id=1, source_target_pairs={{0,4},{4,8},{8,12},{1,5},{5,9},{9,13},{2,6},{6,10},{10,14},{3,7},{... | collective-permute-start | bytes 786440 | tf_op jit(solution)/shard_map/ppermute | solution.py:64
  41.6 8.3 %collective-permute-start.5 = (f32[4,128,128]{2,1,0:T(8,128)S(1)}, f32[4,128,128]{2,1,0:T(8,128)S(1)}, u32[]{:S(2)}, u32[]{:S(2)}) collective-permute-start(f32[4,128,128]{2,1,0:T(8,128)S(1)} %convolution_add_fusion.5), channel_id=1, source_target_pairs={{4,0},{8,4},{12,8},{5,1},{9,5},{13,9},{6,2},{10,6},{14,10},{7,3},{... | collective-permute-start | bytes 786440 | tf_op jit(solution)/shard_map/ppermute | solution.py:65

commit v16 on v15

--- a/solution.py
+++ b/solution.py
@@ -121,13 +121,14 @@
     eye = jnp.eye(head_size, dtype=jnp.float32)
     transition = eye - 2.0 * mh("hjd,hjw->hdw", kn, proj)
     offset = 2.0 * mh("hjd,hjw->hdw", kn, upd_v)
-    local_cot = mh("hld,hlw->hdw", read_map, cot)
+    seen_cot = mh("hij,hiw->hjw", scores, cot)
+    local_cot = mh("hld,hlw->hdw", qn, cot) - mh("hjd,hjw->hdw", proj, seen_cot)
 
     state_in, end_cot = scan_seq(transition, offset, local_cot)
 
     produced = mh("hld,hdw->hlw", read_map, state_in) + own_out
     updates = upd_v - mh("hjd,hdw->hjw", proj, state_in)
-    d_upd = mh("hij,hiw->hjw", scores, cot) + 2.0 * mh("hjd,hdw->hjw", kn, end_cot)
+    d_upd = seen_cot + 2.0 * mh("hjd,hdw->hjw", kn, end_cot)
     d_w = mh("hij,hiw->hjw", inverse, d_upd)
     touch = jnp.where(visible, mh("hiw,hjw->hij", cot, updates), 0.0)
     d_qn = mh("hiw,hdw->hid", cot, state_in) + 2.0 * mh("hij,hjd->hid", touch, kn)

time: 58.3 us -> 60.3 us (1.034)
  other arithmetic: 3.12 us -> 4.06 us
  matrix products: 22.8 us -> 23.7 us
    ppermute x3, waiting for transfers between devices: 2.36 us -> 0.34 us  [chain_seq(): got_sum = lax.ppermute(fwd_sum, 'seq', right)]
    ppermute x3, waiting for transfers between devices: 5.33 us -> 7.27 us  [chain_seq(): got_cot = lax.ppermute(bwd_sum, 'seq', left)]
    reduce_sum x2, other arithmetic: 0.35 us -> 1.29 us  [unit_rows(): scale = lax.rsqrt(jnp.sum(tensor * tensor, axis=-1, keepdims=True) + 1e-06)]
    dot_general x26 -> x27, matrix products: 12.2 us -> 13.1 us  [mh(): return jnp.einsum(spec, *operands, precision=lax.Precision.HIGH)]
  transfers between devices with their start and end apart: 6 -> 6, of which waited for: 6 -> 5; matrix products, arithmetic and copies ran while one was open for 15% -> 10% of each run, Pallas kernels for 0% -> 0%
where the time goes in v16:
time: 60.3 us; the launch traced here: 60 us
  matrix products  23.7 us (39%)
  starting transfers between devices  18.3 us (30%)
  waiting for transfers between devices  7.61 us (13%)
  local copies, waits for them, and re-layouts  5.17 us (9%)
  other arithmetic  4.06 us (7%)
  between operations  1.18 us (2%)
    ppermute x3, starting transfers between devices, chain_seq(): got_sum = lax.ppermute(fwd_sum, 'seq', right)  14.4 us
    dot_general x27, matrix products, mh(): return jnp.einsum(spec, *operands, precision=lax.Precision.HIGH)  13.1 us
    dot_general x19, matrix products, mm(): return jnp.einsum(spec, *operands, precision=highest)  10.6 us
    ppermute x3, waiting for transfers between devices, chain_seq(): got_cot = lax.ppermute(bwd_sum, 'seq', left)  7.27 us
    ppermute x3, starting transfers between devices, chain_seq(): got_cot = lax.ppermute(bwd_sum, 'seq', left)  3.88 us
    convert_element_type x2, local copies, waits for them, and re-layouts, pair_major(): return tensor.reshape(heads_here, tok_count, 2, head_size).transpose(1, 2...  2.09 us
    mul x1, other arithmetic, local(): d_k = k_scale * (d_kn - jnp.sum(kn * d_kn, axis=-1, keepdims=True) * kn)  1.79 us
    unnamed x8, local copies, waits for them, and re-layouts  1.77 us
  transfers between devices with their start and end apart: 6, of which 5 were waited for; matrix products, arithmetic and copies ran while one was open for 10% of the time, Pallas kernels for 0%

profile of v16, /device:TPU:0, one launch (start us, length us, event | category | flops | bytes accessed | tf_op | source)
XLA Modules:
  0.0 60.0 jit_solution(10261958712362700128)
XLA Ops:
  0.7 1.1 %fusion.34 = f32[4,128]{1,0:T(4,128)S(1)} fusion(bf16[128,4,128]{2,1,0:T(4,128)(2,1)} %param.4), kind=kLoop, calls=%fused_computation.70 | loop fusion | flops 196096 | bytes 133120 | tf_op jit(solution)/shard_map/reduce_sum | solution.py:19
  1.9 1.2 %copy.9 = f32[128,2,4,128]{3,1,0,2:T(2,128)S(1)} copy(bf16[128,2,4,128]{3,2,1,0:T(4,128)(2,1)} %param.5) | data formatting | bytes 786432 | tf_op jit(solution)/shard_map/transpose | solution.py:107
  3.0 0.2 multiply_reduce_fusion
  3.5 0.5 convolution_multiply_fusion.7
  4.0 0.5 convolution_multiply_fusion.6
  4.5 0.5 convolution_multiply_fusion.5
  5.1 0.7 %convolution_multiply_fusion.4 = f32[4,128,128]{2,1,0:T(8,128)S(1)} fusion(f32[4,1,2,128,128]{4,3,2,0,1:T(8,128)S(1)} %bitcast.209), kind=kOutput, calls=%fused_computation.32 | convolution fusion | flops 100728832 | bytes 786432 | tf_op jit(solution)/shard_map/hpid,hpjd->hpij/dot_general | solution.py:11
  5.8 0.9 %fusion.3 = f32[4,16,16,16]{3,2,1,0:T(8,128)S(1)} fusion(f32[4,16,16,128]{3,2,1,0:T(8,128)S(1)} %bitcast.210, pred[16,16]{1,0:T(8,128)(4,1)S(1)} %iota_compare_fusion.7), kind=kOutput, calls=%fused_computation.10 | convolution fusion | flops 25198592 | bytes 590080 | tf_op jit(solution)/shard_map/hpid,hpjd->hpij/dot_general | solution.py:11
  6.7 0.6 %fusion.75 = f32[4,16,16,16]{3,2,1,0:T(8,128)S(1)} fusion(f32[4,16,16,16]{3,2,1,0:T(8,128)S(1)} %fusion.3), kind=kOutput, calls=%fused_computation.140 | convolution fusion | flops 3145728 | bytes 131072 | tf_op jit(solution)/shard_map/hpij,hpjk->hpik/dot_general | solution.py:11
  7.3 0.6 %fusion.76 = f32[4,16,16,16]{3,2,1,0:T(8,128)S(1)} fusion(f32[4,16,16,16]{3,2,1,0:T(8,128)S(1)} %fusion.75), kind=kOutput, calls=%fused_computation.141 | convolution fusion | flops 3145728 | bytes 131072 | tf_op jit(solution)/shard_map/hpij,hpjk->hpik/dot_general | solution.py:11
  8.0 0.7 %convolution_add_fusion.2 = f32[4,16,16,16]{3,2,1,0:T(8,128)S(1)} fusion(f32[4,16,16,16]{3,2,1,0:T(8,128)S(1)} %fusion.75, f32[4,16,16,16]{3,2,1,0:T(8,128)S(1)} %fusion.3, f32[16,16]{1,0:T(8,128)S(1)} %fusion.60), kind=kOutput, calls=%fused_computation.5 | convolution fusion | flops 3178496 | bytes 197632 | tf_op jit(solution)/shard_map/hpij,hpjk->hpik/dot_general | solution.py:11
  8.7 0.6 %fusion.77 = f32[4,16,16,16]{3,2,1,0:T(8,128)S(1)} fusion(f32[4,16,16,16]{3,2,1,0:T(8,128)S(1)} %fusion.76), kind=kOutput, calls=%fused_computation.142 | convolution fusion | flops 3145728 | bytes 131072 | tf_op jit(solution)/shard_map/hpij,hpjk->hpik/dot_general | solution.py:11
  9.3 0.6 %convolution_add_fusion.1 = f32[4,16,16,16]{3,2,1,0:T(8,128)S(1)} fusion(f32[4,16,16,16]{3,2,1,0:T(8,128)S(1)} %convolution_add_fusion.2, f32[4,16,16,16]{3,2,1,0:T(8,128)S(1)} %fusion.76), kind=kOutput, calls=%fused_computation.4 | convolution fusion | flops 3162112 | bytes 196608 | tf_op jit(solution)/shard_map/hpij,hpjk->hpik/dot_general | solution.py:11
  9.9 0.6 %convolution_add_fusion = f32[4,16,16,16]{3,2,1,0:T(8,128)S(1)} fusion(f32[4,16,16,16]{3,2,1,0:T(8,128)S(1)} %convolution_add_fusion.1, f32[4,16,16,16]{3,2,1,0:T(8,128)S(1)} %fusion.77), kind=kOutput, calls=%fused_computation.3 | convolution fusion | flops 3162112 | bytes 196608 | tf_op jit(solution)/shard_map/hpij,hpjk->hpik/dot_general | solution.py:11
  10.6 0.4 fusion.71
  11.0 0.4 convolution_negate_fusion.3
  11.6 0.4 fusion.72
  12.0 0.4 convolution_negate_fusion.2
  12.6 0.4 fusion.73
  13.0 0.4 convolution_negate_fusion.1
  13.5 0.6 fusion.39
  14.1 0.7 %fusion.12 = f32[4,1,128,128]{3,2,0,1:T(8,128)S(1)} fusion(f32[4,128,128]{1,2,0:T(8,128)S(1)} %fusion.39, f32[4,1,2,128,128]{4,3,2,0,1:T(8,128)S(1)} %fusion.17), kind=kOutput, calls=%fused_computation.31 | convolution fusion | flops 100728832 | bytes 786432 | tf_op jit(solution)/shard_map/hpij,hpjk->hpik/dot_general | solution.py:11
  14.8 0.2 copy-done.1
  15.0 0.4 fusion.10
  15.5 0.5 fusion.50
  15.9 0.8 %fusion.24 = f32[4,256,128]{2,1,0:T(8,128)S(1)} fusion(f32[4,256,128]{2,1,0:T(8,128)S(1)} %broadcast_multiply_fusion, f32[4,1,128,128]{3,2,0,1:T(8,128)S(1)} %get-tuple-element.9, f32[4,1,128,128]{3,2,0,1:T(8,128)S(1)} %get-tuple-element.8, f32[4,1,128,128]{3,2,0,1:T(8,128)S(1)} %fusion.12), kind=kOutput, calls=%fused_computation.62 | convolution fusion | flops 202375168 | bytes 1835008 | tf_op jit(solution)/shard_map/hij,hjd->hid/dot_general | solution.py:15
  16.7 0.6 %fusion.79 = f32[4,128,128]{2,1,0:T(8,128)S(1)} fusion(f32[4,256,128]{2,1,0:T(8,128)S(1)} %fusion.24, f32[4,256,128]{2,1,0:T(8,128)S(1)} %fusion.50), kind=kOutput, calls=%fused_computation.144 | convolution fusion | flops 100663296 | bytes 1310720 | tf_op jit(solution)/shard_map/hjd,hjw->hdw/dot_general | solution.py:15
  17.4 0.4 convolution_subtract_fusion.2
  17.8 1.3 %collective-permute-start.3 = (f32[4,128,128]{2,1,0:T(8,128)S(1)}, f32[4,128,128]{2,1,0:T(8,128)S(1)}, u32[]{:S(2)}, u32[]{:S(2)}) collective-permute-start(f32[4,128,128]{2,1,0:T(8,128)S(1)} %convolution_subtract_fusion.2), channel_id=1, source_target_pairs={{4,0},{8,4},{12,8},{5,1},{9,5},{13,9},{6,2},{10,6},{14,10},{7,3},{... | collective-permute-start | bytes 786440 | tf_op jit(solution)/shard_map/ppermute | solution.py:65
  19.1 0.5 fusion.22
  19.6 0.6 %convolution_multiply_fusion.9 = f32[4,128,128]{2,1,0:T(8,128)S(1)} fusion(f32[4,256,128]{2,1,0:T(8,128)S(1)} %broadcast_multiply_fusion, f32[4,256,128]{2,1,0:T(8,128)S(1)} %fusion.22), kind=kOutput, calls=%fused_computation.40 | convolution fusion | flops 100728832 | bytes 1310720 | tf_op jit(solution)/shard_map/hjd,hjw->hdw/dot_general | solution.py:15
  20.2 5.6 %collective-permute-start = (f32[4,128,128]{2,1,0:T(8,128)S(1)}, f32[4,128,128]{2,1,0:T(8,128)S(1)}, u32[]{:S(2)}, u32[]{:S(2)}) collective-permute-start(f32[4,128,128]{2,1,0:T(8,128)S(1)} %convolution_multiply_fusion.9), channel_id=1, source_target_pairs={{0,4},{4,8},{8,12},{1,5},{5,9},{9,13},{2,6},{6,10},{10,14},{3,7},{... | collective-permute-start | bytes 786440 | tf_op jit(solution)/shard_map/ppermute | solution.py:64
  25.8 0.6 %fusion.13 = f32[4,128,128]{2,1,0:T(8,128)S(1)} fusion(f32[4,256,128]{2,1,0:T(8,128)S(1)} %broadcast_multiply_fusion, f32[4,256,128]{2,1,0:T(8,128)S(1)} %fusion.24, f32[128,128]{1,0:T(8,128)S(1)} %fusion.56), kind=kOutput, calls=%fused_computation.43 | convolution fusion | flops 100794368 | bytes 1376256 | tf_op jit(solution)/shard_map/hjd,hjw->hdw/dot_general | solution.py:15
  26.4 0.4 convolution_subtract_fusion.3
  26.8 2.2 %collective-permute-done.3 = f32[4,128,128]{2,1,0:T(8,128)S(1)} collective-permute-done((f32[4,128,128]{2,1,0:T(8,128)S(1)}, f32[4,128,128]{2,1,0:T(8,128)S(1)}, u32[]{:S(2)}, u32[]{:S(2)}) %collective-permute-start.3) | collective-permute-done | bytes 262176 | tf_op jit(solution)/shard_map/ppermute | solution.py:65
  29.0 0.4 convolution_add_fusion.6
  29.4 1.3 %collective-permute-start.4 = (f32[4,128,128]{2,1,0:T(8,128)S(1)}, f32[4,128,128]{2,1,0:T(8,128)S(1)}, u32[]{:S(2)}, u32[]{:S(2)}) collective-permute-start(f32[4,128,128]{2,1,0:T(8,128)S(1)} %convolution_add_fusion.6), channel_id=1, source_target_pairs={{4,0},{8,4},{12,8},{5,1},{9,5},{13,9},{6,2},{10,6},{14,10},{7,3},{... | collective-permute-start | bytes 786440 | tf_op jit(solution)/shard_map/ppermute | solution.py:65
  30.7 0.4 fusion.78
  31.3 0.3 convolution_add_fusion.9
  31.6 4.4 %collective-permute-start.1 = (f32[4,128,128]{2,1,0:T(8,128)S(1)}, f32[4,128,128]{2,1,0:T(8,128)S(1)}, u32[]{:S(2)}, u32[]{:S(2)}) collective-permute-start(f32[4,128,128]{2,1,0:T(8,128)S(1)} %convolution_add_fusion.9), channel_id=1, source_target_pairs={{0,4},{4,8},{8,12},{1,5},{5,9},{9,13},{2,6},{6,10},{10,14},{3,7},{... | collective-permute-start | bytes 786440 | tf_op jit(solution)/shard_map/ppermute | solution.py:64
  36.0 2.8 %collective-permute-done.4 = f32[4,128,128]{2,1,0:T(8,128)S(1)} collective-permute-done((f32[4,128,128]{2,1,0:T(8,128)S(1)}, f32[4,128,128]{2,1,0:T(8,128)S(1)}, u32[]{:S(2)}, u32[]{:S(2)}) %collective-permute-start.4) | collective-permute-done | bytes 262176 | tf_op jit(solution)/shard_map/ppermute | solution.py:65
  38.8 0.4 convolution_add_fusion.5
  39.2 1.3 %collective-permute-start.5 = (f32[4,128,128]{2,1,0:T(8,128)S(1)}, f32[4,128,128]{2,1,0:T(8,128)S(1)}, u32[]{:S(2)}, u32[]{:S(2)}) collective-permute-start(f32[4,128,128]{2,1,0:T(8,128)S(1)} %convolution_add_fusion.5), channel_id=1, source_target_pairs={{4,0},{8,4},{12,8},{5,1},{9,5},{13,9},{6,2},{10,6},{14,10},{7,3},{... | collective-permute-start | bytes 786440 | tf_op jit(solution)/shard_map/ppermute | solution.py:65
  40.7 0.3 convolution_add_fusion.8
  40.9 4.4 %collective-permute-start.2 = (f32[4,128,128]{2,1,0:T(8,128)S(1)}, f32[4,128,128]{2,1,0:T(8,128)S(1)}, u32[]{:S(2)}, u32[]{:S(2)}) collective-permute-start(f32[4,128,128]{2,1,0:T(8,128)S(1)} %convolution_add_fusion.8), channel_id=1, source_target_pairs={{0,4},{4,8},{8,12},{1,5},{5,9},{9,13},{2,6},{6,10},{10,14},{3,7},{... | collective-permute-start | bytes 786440 | tf_op jit(solution)/shard_map/ppermute | solution.py:64
  45.4 2.3 %collective-permute-done.5 = f32[4,128,128]{2,1,0:T(8,128)S(1)} collective-permute-done((f32[4,128,128]{2,1,0:T(8,128)S(1)}, f32[4,128,128]{2,1,0:T(8,128)S(1)}, u32[]{:S(2)}, u32[]{:S(2)}) %collective-permute-start.5) | collective-permute-done | bytes 262176 | tf_op jit(solution)/shard_map/ppermute | solution.py:65
  47.7 0.4 fusion.8
  48.0 0.9 %fusion.74 = (bf16[4,256,128]{2,1,0:T(8,128)(2,1)S(1)}, f32[4,256,128]{2,1,0:T(8,128)S(1)}) fusion(f32[4,256,128]{2,1,0:T(8,128)S(1)} %fusion.8, f32[4,1,128,128]{3,2,0,1:T(8,128)S(1)} %get-tuple-element.9, f32[4,1,128,128]{3,2,0,1:T(8,128)S(1)} %get-tuple-element.8, f32[4,1,128,128]{3,2,0,1:T(8,128)S(1)} %fusion.12), kind=kOutput, calls=%fused_computation.139 | convolution fusion | flops 202506240 | bytes 2097152 | tf_op jit(solution)/shard_map/hij,hiw->hjw/dot_general | solution.py:15
  48.9 1.0 %copy.92 = bf16[4,128,2,128]{3,0,2,1:T(4,128)(2,1)} copy(bf16[4,128,2,128]{3,2,1,0:T(2,128)(2,1)S(1)} %bitcast.225) | data formatting | bytes 524288 | tf_op jit(solution)/shard_map/convert_element_type | solution.py:153
  50.0 0.3 fusion.15
  50.2 0.8 %copy.39 = bf16[128,4,128]{2,1,0:T(4,128)(2,1)} copy(bf16[128,4,128]{2,0,1:T(8,128)(2,1)S(1)} %fusion.15) | data formatting | bytes 262144
  51.0 0.4 convolution_subtract_fusion.1
  51.4 0.3 fusion.2
  51.7 0.7 %fusion.29 = f32[4,256,128]{2,1,0:T(8,128)S(1)} fusion(f32[4,128,256]{2,1,0:T(8,128)S(1)} %fusion.2, f32[4,128]{1,0:T(4,128)S(1)} %get-tuple-element.17, bf16[128,4,128]{2,1,0:T(4,128)(2,1)S(1)} %copy-done.1), kind=kOutput, calls=%fused_computation.67 | convolution fusion | flops 100794368 | bytes 1181696 | tf_op jit(solution)/shard_map/hij,hid->hjd/dot_general | solution.py:15
  52.4 0.3 fusion.54
  52.7 0.5 fusion.33
  53.4 0.8 %copy.40 = bf16[128,4,128]{2,1,0:T(4,128)(2,1)} copy(bf16[128,4,128]{2,0,1:T(8,128)(2,1)S(1)} %fusion.38) | data formatting | bytes 262144
  54.1 0.6 %fusion.1 = f32[4,256,256]{2,1,0:T(8,128)S(1)} fusion(f32[4,256,128]{2,1,0:T(8,128)S(1)} %get-tuple-element.21, f32[4,256,128]{2,1,0:T(8,128)S(1)} %convolution_subtract_fusion.1, pred[256,256]{1,0:T(8,128)(4,1)S(1)} %iota_compare_fusion.4), kind=kOutput, calls=%fused_computation.2 | convolution fusion | flops 201850880 | bytes 2162688 | tf_op jit(solution)/shard_map/hiw,hjw->hij/dot_general | solution.py:15
  54.8 0.6 fusion.80
  55.4 0.4 fusion.9
  55.8 0.4 fusion.7
  56.1 1.0 %convolution_add_fusion.3 = f32[4,256,128]{2,1,0:T(8,128)S(1)} fusion(f32[4,256,128]{2,1,0:T(8,128)S(1)} %fusion.7, f32[4,256,256]{2,1,0:T(8,128)S(1)} %fusion.1, f32[4,256,128]{2,1,0:T(8,128)S(1)} %broadcast_multiply_fusion), kind=kOutput, calls=%fused_computation.6 | convolution fusion | flops 201457664 | bytes 2621440 | tf_op jit(solution)/shard_map/hji,hjd->hid/dot_general | solution.py:15
  57.2 1.8 %fusion.11 = bf16[4,256,128]{2,1,0:T(8,128)(2,1)S(1)} fusion(f32[4,256,128]{2,1,0:T(8,128)S(1)} %convolution_add_fusion.3, f32[4,256,128]{2,1,0:T(8,128)S(1)} %broadcast_multiply_fusion, f32[4,256]{1,0:T(4,128)S(1)} %add_rsqrt_fusion), kind=kOutput, calls=%fused_computation.23 | output fusion | flops 656511 | bytes 1314816 | tf_op jit(solution)/shard_map/mul | solution.py:144
  59.0 1.0 %copy.93 = bf16[4,128,2,128]{3,0,2,1:T(4,128)(2,1)} copy(bf16[4,128,2,128]{3,2,1,0:T(2,128)(2,1)S(1)} %bitcast.222) | data formatting | bytes 524288 | tf_op jit(solution)/shard_map/convert_element_type | solution.py:153
  (25 shorter events, 1.5 us)
Async XLA Ops:
  0.6 14.8 %copy-start = (bf16[128,4,128]{2,1,0:T(4,128)(2,1)S(1)}, bf16[128,4,128]{2,1,0:T(4,128)(2,1)}, u32[]{:S(2)}) copy-start(bf16[128,4,128]{2,1,0:T(4,128)(2,1)} %param.7) | copy-start | bytes 393220
  14.1 0.9 %copy-start.1 = (bf16[128,4,128]{2,1,0:T(4,128)(2,1)S(1)}, bf16[128,4,128]{2,1,0:T(4,128)(2,1)}, u32[]{:S(2)}) copy-start(bf16[128,4,128]{2,1,0:T(4,128)(2,1)} %param.4) | copy-start | bytes 393220
  17.4 1.7 %copy-start.2 = (bf16[128,2,4,128]{3,2,1,0:T(4,128)(2,1)S(1)}, bf16[128,2,4,128]{3,2,1,0:T(4,128)(2,1)}, u32[]{:S(2)}) copy-start(bf16[128,2,4,128]{3,2,1,0:T(4,128)(2,1)} %param.6) | copy-start | bytes 786436
  17.8 11.2 %collective-permute-start.3 = (f32[4,128,128]{2,1,0:T(8,128)S(1)}, f32[4,128,128]{2,1,0:T(8,128)S(1)}, u32[]{:S(2)}, u32[]{:S(2)}) collective-permute-start(f32[4,128,128]{2,1,0:T(8,128)S(1)} %convolution_subtract_fusion.2), channel_id=1, source_target_pairs={{4,0},{8,4},{12,8},{5,1},{9,5},{13,9},{6,2},{10,6},{14,10},{7,3},{... | collective-permute-start | bytes 786440 | tf_op jit(solution)/shard_map/ppermute | solution.py:65
  20.2 11.1 %collective-permute-start = (f32[4,128,128]{2,1,0:T(8,128)S(1)}, f32[4,128,128]{2,1,0:T(8,128)S(1)}, u32[]{:S(2)}, u32[]{:S(2)}) collective-permute-start(f32[4,128,128]{2,1,0:T(8,128)S(1)} %convolution_multiply_fusion.9), channel_id=1, source_target_pairs={{0,4},{4,8},{8,12},{1,5},{5,9},{9,13},{2,6},{6,10},{10,14},{3,7},{... | collective-permute-start | bytes 786440 | tf_op jit(solution)/shard_map/ppermute | solution.py:64
  29.4 9.4 %collective-permute-start.4 = (f32[4,128,128]{2,1,0:T(8,128)S(1)}, f32[4,128,128]{2,1,0:T(8,128)S(1)}, u32[]{:S(2)}, u32[]{:S(2)}) collective-permute-start(f32[4,128,128]{2,1,0:T(8,128)S(1)} %convolution_add_fusion.6), channel_id=1, source_target_pairs={{4,0},{8,4},{12,8},{5,1},{9,5},{13,9},{6,2},{10,6},{14,10},{7,3},{... | collective-permute-start | bytes 786440 | tf_op jit(solution)/shard_map/ppermute | solution.py:65
  31.6 9.1 %collective-permute-start.1 = (f32[4,128,128]{2,1,0:T(8,128)S(1)}, f32[4,128,128]{2,1,0:T(8,128)S(1)}, u32[]{:S(2)}, u32[]{:S(2)}) collective-permute-start(f32[4,128,128]{2,1,0:T(8,128)S(1)} %convolution_add_fusion.9), channel_id=1, source_target_pairs={{0,4},{4,8},{8,12},{1,5},{5,9},{9,13},{2,6},{6,10},{10,14},{3,7},{... | collective-permute-start | bytes 786440 | tf_op jit(solution)/shard_map/ppermute | solution.py:64
  39.2 8.5 %collective-permute-start.5 = (f32[4,128,128]{2,1,0:T(8,128)S(1)}, f32[4,128,128]{2,1,0:T(8,128)S(1)}, u32[]{:S(2)}, u32[]{:S(2)}) collective-permute-start(f32[4,128,128]{2,1,0:T(8,128)S(1)} %convolution_add_fusion.5), channel_id=1, source_target_pairs={{4,0},{8,4},{12,8},{5,1},{9,5},{13,9},{6,2},{10,6},{14,10},{7,3},{... | collective-permute-start | bytes 786440 | tf_op jit(solution)/shard_map/ppermute | solution.py:65
  40.9 9.0 %collective-permute-start.2 = (f32[4,128,128]{2,1,0:T(8,128)S(1)}, f32[4,128,128]{2,1,0:T(8,128)S(1)}, u32[]{:S(2)}, u32[]{:S(2)}) collective-permute-start(f32[4,128,128]{2,1,0:T(8,128)S(1)} %convolution_add_fusion.8), channel_id=1, source_target_pairs={{0,4},{4,8},{8,12},{1,5},{5,9},{9,13},{2,6},{6,10},{10,14},{3,7},{... | collective-permute-start | bytes 786440 | tf_op jit(solution)/shard_map/ppermute | solution.py:64

commit v17 on v15

--- a/solution.py
+++ b/solution.py
@@ -4,7 +4,7 @@
 from jax.sharding import PartitionSpec as P
 
 highest = lax.Precision.HIGHEST
-LEAF = 16
+LEAF = 8
 
 
 def mm(spec, *operands):

time: 58.3 us -> 60.2 us (1.033)
  matrix products: 22.8 us -> 24.7 us
    dot_general x19 -> x20, matrix products: 10.6 us -> 12.5 us  [mm(): return jnp.einsum(spec, *operands, precision=highest)]
where the time goes in v17:
time: 60.2 us; the launch traced here: 59.9 us
  matrix products  24.7 us (41%)
  starting transfers between devices  17.8 us (30%)
  waiting for transfers between devices  7.48 us (12%)
  local copies, waits for them, and re-layouts  5.49 us (9%)
  other arithmetic  3.25 us (5%)
  between operations  1.17 us (2%)
    ppermute x3, starting transfers between devices, chain_seq(): got_sum = lax.ppermute(fwd_sum, 'seq', right)  13.7 us
    dot_general x20, matrix products, mm(): return jnp.einsum(spec, *operands, precision=highest)  12.5 us
    dot_general x26, matrix products, mh(): return jnp.einsum(spec, *operands, precision=lax.Precision.HIGH)  12.2 us
    ppermute x3, waiting for transfers between devices, chain_seq(): got_cot = lax.ppermute(bwd_sum, 'seq', left)  4.77 us
    ppermute x3, starting transfers between devices, chain_seq(): got_cot = lax.ppermute(bwd_sum, 'seq', left)  4.1 us
    ppermute x3, waiting for transfers between devices, chain_seq(): got_sum = lax.ppermute(fwd_sum, 'seq', right)  2.71 us
    convert_element_type x2, local copies, waits for them, and re-layouts, pair_major(): return tensor.reshape(heads_here, tok_count, 2, head_size).transpose(1, 2...  2.09 us
    unnamed x8, local copies, waits for them, and re-layouts  2.02 us
  transfers between devices with their start and end apart: 6, of which 6 were waited for; matrix products, arithmetic and copies ran while one was open for 15% of the time, Pallas kernels for 0%

profile of v17, /device:TPU:0, one launch (start us, length us, event | category | flops | bytes accessed | tf_op | source)
XLA Modules:
  0.0 59.9 jit_solution(6232886533501815370)
XLA Ops:
  0.7 1.2 %copy.9 = f32[128,2,4,128]{3,1,0,2:T(2,128)S(1)} copy(bf16[128,2,4,128]{3,2,1,0:T(4,128)(2,1)} %param.5) | data formatting | bytes 786432 | tf_op jit(solution)/shard_map/transpose | solution.py:107
  2.3 1.0 %fusion.3 = f32[4,32,8,8]{3,2,1,0:T(8,128)S(1)} fusion(f32[4,256,128]{2,1,0:T(8,128)S(1)} %broadcast_multiply_fusion, pred[8,8]{1,0:T(8,128)(4,1)S(1)} %iota_compare_fusion.8), kind=kOutput, calls=%fused_computation.9 | convolution fusion | flops 12599296 | bytes 557120 | tf_op jit(solution)/shard_map/hpid,hpjd->hpij/dot_general | solution.py:11
  3.3 1.0 %fusion.75 = f32[4,32,8,8]{3,2,1,0:T(8,128)S(1)} fusion(f32[4,32,8,8]{3,2,1,0:T(8,128)S(1)} %fusion.3), kind=kOutput, calls=%fused_computation.147 | convolution fusion | flops 786432 | bytes 65536 | tf_op jit(solution)/shard_map/hpij,hpjk->hpik/dot_general | solution.py:11
  4.2 1.0 %fusion.76 = f32[4,32,8,8]{3,2,1,0:T(8,128)S(1)} fusion(f32[4,32,8,8]{3,2,1,0:T(8,128)S(1)} %fusion.75), kind=kOutput, calls=%fused_computation.148 | convolution fusion | flops 786432 | bytes 65536 | tf_op jit(solution)/shard_map/hpij,hpjk->hpik/dot_general | solution.py:11
  5.2 1.0 %convolution_add_fusion.1 = f32[4,32,8,8]{3,2,1,0:T(8,128)S(1)} fusion(f32[4,32,8,8]{3,2,1,0:T(8,128)S(1)} %fusion.75, f32[4,32,8,8]{3,2,1,0:T(8,128)S(1)} %fusion.3, f32[8,8]{1,0:T(8,128)S(1)} %fusion.59), kind=kOutput, calls=%fused_computation.4 | convolution fusion | flops 802816 | bytes 98560 | tf_op jit(solution)/shard_map/hpij,hpjk->hpik/dot_general | solution.py:11
  6.2 1.0 %convolution_add_fusion = f32[4,32,8,8]{3,2,1,0:T(8,128)S(1)} fusion(f32[4,32,8,8]{3,2,1,0:T(8,128)S(1)} %convolution_add_fusion.1, f32[4,32,8,8]{3,2,1,0:T(8,128)S(1)} %fusion.76), kind=kOutput, calls=%fused_computation.3 | convolution fusion | flops 794624 | bytes 98304 | tf_op jit(solution)/shard_map/hpij,hpjk->hpik/dot_general | solution.py:11
  7.2 0.6 convolution_multiply_fusion.8
  7.8 0.5 fusion.70
  8.3 0.6 convolution_negate_fusion.4
  9.1 0.5 convolution_multiply_fusion.7
  9.6 0.4 fusion.71
  10.0 0.4 convolution_negate_fusion.3
  10.6 0.5 convolution_multiply_fusion.6
  11.1 0.4 fusion.72
  11.5 0.4 convolution_negate_fusion.2
  12.1 0.5 convolution_multiply_fusion.5
  12.6 0.4 fusion.73
  13.0 0.4 convolution_negate_fusion.1
  13.6 0.7 %convolution_multiply_fusion.4 = f32[4,128,128]{2,1,0:T(8,128)S(1)} fusion(f32[4,1,2,128,128]{4,3,2,0,1:T(8,128)S(1)} %bitcast.224), kind=kOutput, calls=%fused_computation.30 | convolution fusion | flops 100728832 | bytes 786432 | tf_op jit(solution)/shard_map/hpid,hpjd->hpij/dot_general | solution.py:11
  14.3 0.8 %fusion.39 = f32[4,128,128]{1,2,0:T(8,128)S(1)} fusion(f32[4,128,128]{2,1,0:T(8,128)S(1)} %convolution_multiply_fusion.4, f32[4,1,2,128,128]{4,3,2,0,1:T(8,128)S(1)} %fusion.17), kind=kOutput, calls=%fused_computation.96 | convolution fusion | flops 100663296 | bytes 786432 | tf_op jit(solution)/shard_map/hpij,hpjk->hpik/dot_general | solution.py:11
  15.1 0.7 %fusion.12 = f32[4,1,128,128]{3,2,0,1:T(8,128)S(1)} fusion(f32[4,128,128]{1,2,0:T(8,128)S(1)} %fusion.39, f32[4,1,2,128,128]{4,3,2,0,1:T(8,128)S(1)} %fusion.17), kind=kOutput, calls=%fused_computation.29 | convolution fusion | flops 100728832 | bytes 786432 | tf_op jit(solution)/shard_map/hpij,hpjk->hpik/dot_general | solution.py:11
  15.7 0.3 copy-done.2
  16.0 0.4 fusion.23
  16.5 0.6 %convolution_multiply_fusion.10 = f32[4,128,128]{2,1,0:T(8,128)S(1)} fusion(f32[4,256,128]{2,1,0:T(8,128)S(1)} %broadcast_multiply_fusion, f32[4,256,128]{2,1,0:T(8,128)S(1)} %fusion.23), kind=kOutput, calls=%fused_computation.40 | convolution fusion | flops 100728832 | bytes 1310720 | tf_op jit(solution)/shard_map/hjd,hjw->hdw/dot_general | solution.py:15
  17.1 4.9 %collective-permute-start = (f32[4,128,128]{2,1,0:T(8,128)S(1)}, f32[4,128,128]{2,1,0:T(8,128)S(1)}, u32[]{:S(2)}, u32[]{:S(2)}) collective-permute-start(f32[4,128,128]{2,1,0:T(8,128)S(1)} %convolution_multiply_fusion.10), channel_id=1, source_target_pairs={{0,4},{4,8},{8,12},{1,5},{5,9},{9,13},{2,6},{6,10},{10,14},{3,7},{... | collective-permute-start | bytes 786440 | tf_op jit(solution)/shard_map/ppermute | solution.py:64
  22.1 0.6 fusion.25
  23.1 0.4 fusion.10
  23.6 0.4 convolution_subtract_fusion.2
  24.0 0.3 fusion.49
  24.3 1.3 %collective-permute-start.3 = (f32[4,128,128]{2,1,0:T(8,128)S(1)}, f32[4,128,128]{2,1,0:T(8,128)S(1)}, u32[]{:S(2)}, u32[]{:S(2)}) collective-permute-start(f32[4,128,128]{2,1,0:T(8,128)S(1)} %fusion.49), channel_id=1, source_target_pairs={{4,0},{8,4},{12,8},{5,1},{9,5},{13,9},{6,2},{10,6},{14,10},{7,3},{... | collective-permute-start | bytes 786440 | tf_op jit(solution)/shard_map/ppermute | solution.py:65
  25.6 0.4 fusion.77
  26.0 0.6 %fusion.13 = f32[4,128,128]{2,1,0:T(8,128)S(1)} fusion(f32[4,256,128]{2,1,0:T(8,128)S(1)} %broadcast_multiply_fusion, f32[4,256,128]{2,1,0:T(8,128)S(1)} %fusion.25, f32[128,128]{1,0:T(8,128)S(1)} %fusion.56), kind=kOutput, calls=%fused_computation.43 | convolution fusion | flops 100794368 | bytes 1376256 | tf_op jit(solution)/shard_map/hjd,hjw->hdw/dot_general | solution.py:15
  26.6 1.0 %collective-permute-done = f32[4,128,128]{2,1,0:T(8,128)S(1)} collective-permute-done((f32[4,128,128]{2,1,0:T(8,128)S(1)}, f32[4,128,128]{2,1,0:T(8,128)S(1)}, u32[]{:S(2)}, u32[]{:S(2)}) %collective-permute-start) | collective-permute-done | bytes 262176 | tf_op jit(solution)/shard_map/ppermute | solution.py:64
  27.6 0.3 convolution_add_fusion.8
  27.9 4.4 %collective-permute-start.1 = (f32[4,128,128]{2,1,0:T(8,128)S(1)}, f32[4,128,128]{2,1,0:T(8,128)S(1)}, u32[]{:S(2)}, u32[]{:S(2)}) collective-permute-start(f32[4,128,128]{2,1,0:T(8,128)S(1)} %convolution_add_fusion.8), channel_id=1, source_target_pairs={{0,4},{4,8},{8,12},{1,5},{5,9},{9,13},{2,6},{6,10},{10,14},{3,7},{... | collective-permute-start | bytes 786440 | tf_op jit(solution)/shard_map/ppermute | solution.py:64
  32.3 0.5 fusion.52
  32.7 1.2 %collective-permute-done.3 = f32[4,128,128]{2,1,0:T(8,128)S(1)} collective-permute-done((f32[4,128,128]{2,1,0:T(8,128)S(1)}, f32[4,128,128]{2,1,0:T(8,128)S(1)}, u32[]{:S(2)}, u32[]{:S(2)}) %collective-permute-start.3) | collective-permute-done | bytes 262176 | tf_op jit(solution)/shard_map/ppermute | solution.py:65
  33.9 0.4 convolution_add_fusion.5
  34.3 1.3 %collective-permute-start.4 = (f32[4,128,128]{2,1,0:T(8,128)S(1)}, f32[4,128,128]{2,1,0:T(8,128)S(1)}, u32[]{:S(2)}, u32[]{:S(2)}) collective-permute-start(f32[4,128,128]{2,1,0:T(8,128)S(1)} %convolution_add_fusion.5), channel_id=1, source_target_pairs={{4,0},{8,4},{12,8},{5,1},{9,5},{13,9},{6,2},{10,6},{14,10},{7,3},{... | collective-permute-start | bytes 786440 | tf_op jit(solution)/shard_map/ppermute | solution.py:65
  35.6 1.3 %collective-permute-done.1 = f32[4,128,128]{2,1,0:T(8,128)S(1)} collective-permute-done((f32[4,128,128]{2,1,0:T(8,128)S(1)}, f32[4,128,128]{2,1,0:T(8,128)S(1)}, u32[]{:S(2)}, u32[]{:S(2)}) %collective-permute-start.1) | collective-permute-done | bytes 262176 | tf_op jit(solution)/shard_map/ppermute | solution.py:64
  37.2 4.4 %collective-permute-start.2 = (f32[4,128,128]{2,1,0:T(8,128)S(1)}, f32[4,128,128]{2,1,0:T(8,128)S(1)}, u32[]{:S(2)}, u32[]{:S(2)}) collective-permute-start(f32[4,128,128]{2,1,0:T(8,128)S(1)} %convolution_add_fusion.7), channel_id=1, source_target_pairs={{0,4},{4,8},{8,12},{1,5},{5,9},{9,13},{2,6},{6,10},{10,14},{3,7},{... | collective-permute-start | bytes 786440 | tf_op jit(solution)/shard_map/ppermute | solution.py:64
  41.6 1.4 %collective-permute-done.4 = f32[4,128,128]{2,1,0:T(8,128)S(1)} collective-permute-done((f32[4,128,128]{2,1,0:T(8,128)S(1)}, f32[4,128,128]{2,1,0:T(8,128)S(1)}, u32[]{:S(2)}, u32[]{:S(2)}) %collective-permute-start.4) | collective-permute-done | bytes 262176 | tf_op jit(solution)/shard_map/ppermute | solution.py:65
  43.1 0.4 convolution_add_fusion.4
  43.5 1.5 %collective-permute-start.5 = (f32[4,128,128]{2,1,0:T(8,128)S(1)}, f32[4,128,128]{2,1,0:T(8,128)S(1)}, u32[]{:S(2)}, u32[]{:S(2)}) collective-permute-start(f32[4,128,128]{2,1,0:T(8,128)S(1)} %convolution_add_fusion.4), channel_id=1, source_target_pairs={{4,0},{8,4},{12,8},{5,1},{9,5},{13,9},{6,2},{10,6},{14,10},{7,3},{... | collective-permute-start | bytes 786440 | tf_op jit(solution)/shard_map/ppermute | solution.py:65
  45.0 0.5 collective-permute-done.2
  45.5 0.4 convolution_subtract_fusion.1
  45.8 0.3 fusion.2
  46.2 0.3 fusion.54
  46.5 0.5 fusion.33
  46.9 0.3 fusion.15
  47.4 0.8 %copy.38 = bf16[128,4,128]{2,1,0:T(4,128)(2,1)} copy(bf16[128,4,128]{2,0,1:T(8,128)(2,1)S(1)} %fusion.15) | data formatting | bytes 262144
  48.2 0.8 %copy.39 = bf16[128,4,128]{2,1,0:T(4,128)(2,1)} copy(bf16[128,4,128]{2,0,1:T(8,128)(2,1)S(1)} %fusion.38) | data formatting | bytes 262144
  49.0 0.7 %fusion.29 = f32[4,256,128]{2,1,0:T(8,128)S(1)} fusion(f32[4,128,256]{2,1,0:T(8,128)S(1)} %fusion.2, f32[4,128]{1,0:T(4,128)S(1)} %get-tuple-element.19, bf16[128,4,128]{2,1,0:T(4,128)(2,1)S(1)} %copy-done.1), kind=kOutput, calls=%fused_computation.70 | convolution fusion | flops 100794368 | bytes 1181696 | tf_op jit(solution)/shard_map/hij,hid->hjd/dot_general | solution.py:15
  49.6 2.1 %collective-permute-done.5 = f32[4,128,128]{2,1,0:T(8,128)S(1)} collective-permute-done((f32[4,128,128]{2,1,0:T(8,128)S(1)}, f32[4,128,128]{2,1,0:T(8,128)S(1)}, u32[]{:S(2)}, u32[]{:S(2)}) %collective-permute-start.5) | collective-permute-done | bytes 262176 | tf_op jit(solution)/shard_map/ppermute | solution.py:65
  51.7 0.4 fusion.8
  52.1 0.9 %fusion.74 = (bf16[4,256,128]{2,1,0:T(8,128)(2,1)S(1)}, f32[4,256,128]{2,1,0:T(8,128)S(1)}) fusion(f32[4,256,128]{2,1,0:T(8,128)S(1)} %fusion.8, f32[4,1,128,128]{3,2,0,1:T(8,128)S(1)} %get-tuple-element.9, f32[4,1,128,128]{3,2,0,1:T(8,128)S(1)} %get-tuple-element.8, f32[4,1,128,128]{3,2,0,1:T(8,128)S(1)} %fusion.12), kind=kOutput, calls=%fused_computation.146 | convolution fusion | flops 202506240 | bytes 2097152 | tf_op jit(solution)/shard_map/hij,hiw->hjw/dot_general | solution.py:15
  53.0 0.6 %fusion.1 = f32[4,256,256]{2,1,0:T(8,128)S(1)} fusion(f32[4,256,128]{2,1,0:T(8,128)S(1)} %get-tuple-element.23, f32[4,256,128]{2,1,0:T(8,128)S(1)} %convolution_subtract_fusion.1, pred[256,256]{1,0:T(8,128)(4,1)S(1)} %iota_compare_fusion.5), kind=kOutput, calls=%fused_computation.2 | convolution fusion | flops 201850880 | bytes 2162688 | tf_op jit(solution)/shard_map/hiw,hjw->hij/dot_general | solution.py:15
  53.6 0.6 fusion.78
  54.2 0.4 fusion.9
  54.6 0.4 fusion.7
  55.0 1.0 %convolution_add_fusion.2 = f32[4,256,128]{2,1,0:T(8,128)S(1)} fusion(f32[4,256,128]{2,1,0:T(8,128)S(1)} %fusion.7, f32[4,256,256]{2,1,0:T(8,128)S(1)} %fusion.1, f32[4,256,128]{2,1,0:T(8,128)S(1)} %broadcast_multiply_fusion), kind=kOutput, calls=%fused_computation.5 | convolution fusion | flops 201457664 | bytes 2621440 | tf_op jit(solution)/shard_map/hji,hjd->hid/dot_general | solution.py:15
  56.1 1.8 %fusion.11 = bf16[4,256,128]{2,1,0:T(8,128)(2,1)S(1)} fusion(f32[4,256,128]{2,1,0:T(8,128)S(1)} %convolution_add_fusion.2, f32[4,256,128]{2,1,0:T(8,128)S(1)} %broadcast_multiply_fusion, f32[4,256]{1,0:T(4,128)S(1)} %add_rsqrt_fusion), kind=kOutput, calls=%fused_computation.22 | output fusion | flops 656511 | bytes 1314816 | tf_op jit(solution)/shard_map/mul | solution.py:143
  57.8 1.0 %copy.88 = bf16[4,128,2,128]{3,0,2,1:T(4,128)(2,1)} copy(bf16[4,128,2,128]{3,2,1,0:T(2,128)(2,1)S(1)} %bitcast.239) | data formatting | bytes 524288 | tf_op jit(solution)/shard_map/convert_element_type | solution.py:152
  58.9 1.0 %copy.87 = bf16[4,128,2,128]{3,0,2,1:T(4,128)(2,1)} copy(bf16[4,128,2,128]{3,2,1,0:T(2,128)(2,1)S(1)} %bitcast.240) | data formatting | bytes 524288 | tf_op jit(solution)/shard_map/convert_element_type | solution.py:152
  (27 shorter events, 2.2 us)
Async XLA Ops:
  0.6 23.3 %copy-start = (bf16[128,4,128]{2,1,0:T(4,128)(2,1)S(1)}, bf16[128,4,128]{2,1,0:T(4,128)(2,1)}, u32[]{:S(2)}) copy-start(bf16[128,4,128]{2,1,0:T(4,128)(2,1)} %param.7) | copy-start | bytes 393220
  15.0 1.0 %copy-start.2 = (bf16[128,2,4,128]{3,2,1,0:T(4,128)(2,1)S(1)}, bf16[128,2,4,128]{3,2,1,0:T(4,128)(2,1)}, u32[]{:S(2)}) copy-start(bf16[128,2,4,128]{3,2,1,0:T(4,128)(2,1)} %param.6) | copy-start | bytes 786436
  17.1 10.5 %collective-permute-start = (f32[4,128,128]{2,1,0:T(8,128)S(1)}, f32[4,128,128]{2,1,0:T(8,128)S(1)}, u32[]{:S(2)}, u32[]{:S(2)}) collective-permute-start(f32[4,128,128]{2,1,0:T(8,128)S(1)} %convolution_multiply_fusion.10), channel_id=1, source_target_pairs={{0,4},{4,8},{8,12},{1,5},{5,9},{9,13},{2,6},{6,10},{10,14},{3,7},{... | collective-permute-start | bytes 786440 | tf_op jit(solution)/shard_map/ppermute | solution.py:64
  22.1 0.9 %copy-start.1 = (bf16[128,4,128]{2,1,0:T(4,128)(2,1)S(1)}, bf16[128,4,128]{2,1,0:T(4,128)(2,1)}, u32[]{:S(2)}) copy-start(bf16[128,4,128]{2,1,0:T(4,128)(2,1)} %param.4) | copy-start | bytes 393220
  24.3 9.7 %collective-permute-start.3 = (f32[4,128,128]{2,1,0:T(8,128)S(1)}, f32[4,128,128]{2,1,0:T(8,128)S(1)}, u32[]{:S(2)}, u32[]{:S(2)}) collective-permute-start(f32[4,128,128]{2,1,0:T(8,128)S(1)} %fusion.49), channel_id=1, source_target_pairs={{4,0},{8,4},{12,8},{5,1},{9,5},{13,9},{6,2},{10,6},{14,10},{7,3},{... | collective-permute-start | bytes 786440 | tf_op jit(solution)/shard_map/ppermute | solution.py:65
  27.9 9.1 %collective-permute-start.1 = (f32[4,128,128]{2,1,0:T(8,128)S(1)}, f32[4,128,128]{2,1,0:T(8,128)S(1)}, u32[]{:S(2)}, u32[]{:S(2)}) collective-permute-start(f32[4,128,128]{2,1,0:T(8,128)S(1)} %convolution_add_fusion.8), channel_id=1, source_target_pairs={{0,4},{4,8},{8,12},{1,5},{5,9},{9,13},{2,6},{6,10},{10,14},{3,7},{... | collective-permute-start | bytes 786440 | tf_op jit(solution)/shard_map/ppermute | solution.py:64
  34.3 8.8 %collective-permute-start.4 = (f32[4,128,128]{2,1,0:T(8,128)S(1)}, f32[4,128,128]{2,1,0:T(8,128)S(1)}, u32[]{:S(2)}, u32[]{:S(2)}) collective-permute-start(f32[4,128,128]{2,1,0:T(8,128)S(1)} %convolution_add_fusion.5), channel_id=1, source_target_pairs={{4,0},{8,4},{12,8},{5,1},{9,5},{13,9},{6,2},{10,6},{14,10},{7,3},{... | collective-permute-start | bytes 786440 | tf_op jit(solution)/shard_map/ppermute | solution.py:65
  37.2 8.3 %collective-permute-start.2 = (f32[4,128,128]{2,1,0:T(8,128)S(1)}, f32[4,128,128]{2,1,0:T(8,128)S(1)}, u32[]{:S(2)}, u32[]{:S(2)}) collective-permute-start(f32[4,128,128]{2,1,0:T(8,128)S(1)} %convolution_add_fusion.7), channel_id=1, source_target_pairs={{0,4},{4,8},{8,12},{1,5},{5,9},{9,13},{2,6},{6,10},{10,14},{3,7},{... | collective-permute-start | bytes 786440 | tf_op jit(solution)/shard_map/ppermute | solution.py:64
  43.5 8.3 %collective-permute-start.5 = (f32[4,128,128]{2,1,0:T(8,128)S(1)}, f32[4,128,128]{2,1,0:T(8,128)S(1)}, u32[]{:S(2)}, u32[]{:S(2)}) collective-permute-start(f32[4,128,128]{2,1,0:T(8,128)S(1)} %convolution_add_fusion.4), channel_id=1, source_target_pairs={{4,0},{8,4},{12,8},{5,1},{9,5},{13,9},{6,2},{10,6},{14,10},{7,3},{... | collective-permute-start | bytes 786440 | tf_op jit(solution)/shard_map/ppermute | solution.py:65

commit v18 on v15

--- a/solution.py
+++ b/solution.py
@@ -36,8 +36,8 @@
     inverse = eye + power
     reach = 2
     while reach < LEAF:
-        power = mm("hpij,hpjk->hpik", power, power)
-        inverse = inverse + mm("hpij,hpjk->hpik", inverse, power)
+        power = mh("hpij,hpjk->hpik", power, power)
+        inverse = inverse + mh("hpij,hpjk->hpik", inverse, power)
         reach *= 2
     span = LEAF
     while span < rows:

time: 58.3 us -> 56.5 us (0.969)
  matrix products: 22.8 us -> 21.1 us
    dot_general x19 -> x13, matrix products: 10.6 us -> 6.73 us  [mm(): return jnp.einsum(spec, *operands, precision=highest)]
    dot_general x26 -> x32, matrix products: 12.2 us -> 14.4 us  [mh(): return jnp.einsum(spec, *operands, precision=lax.Precision.HIGH)]
    ppermute x3, waiting for transfers between devices: 5.33 us -> 4.74 us  [chain_seq(): got_cot = lax.ppermute(bwd_sum, 'seq', left)]
  transfers between devices with their start and end apart: 6 -> 6, of which waited for: 6 -> 6; matrix products, arithmetic and copies ran while one was open for 15% -> 16% of each run, Pallas kernels for 0% -> 0%
where the time goes in v18:
time: 56.5 us; the launch traced here: 56.2 us
  matrix products  21.1 us (37%)
  starting transfers between devices  17.8 us (32%)
  waiting for transfers between devices  7.5 us (13%)
  local copies, waits for them, and re-layouts  5.45 us (10%)
  other arithmetic  3.12 us (6%)
  between operations  1.16 us (2%)
    dot_general x32, matrix products, mh(): return jnp.einsum(spec, *operands, precision=lax.Precision.HIGH)  14.4 us
    ppermute x3, starting transfers between devices, chain_seq(): got_sum = lax.ppermute(fwd_sum, 'seq', right)  13.7 us
    dot_general x13, matrix products, mm(): return jnp.einsum(spec, *operands, precision=highest)  6.73 us
    ppermute x3, waiting for transfers between devices, chain_seq(): got_cot = lax.ppermute(bwd_sum, 'seq', left)  4.74 us
    ppermute x3, starting transfers between devices, chain_seq(): got_cot = lax.ppermute(bwd_sum, 'seq', left)  4.06 us
    ppermute x3, waiting for transfers between devices, chain_seq(): got_sum = lax.ppermute(fwd_sum, 'seq', right)  2.76 us
    convert_element_type x2, local copies, waits for them, and re-layouts, pair_major(): return tensor.reshape(heads_here, tok_count, 2, head_size).transpose(1, 2...  2.09 us
    unnamed x8, local copies, waits for them, and re-layouts  2.02 us
  transfers between devices with their start and end apart: 6, of which 6 were waited for; matrix products, arithmetic and copies ran while one was open for 16% of the time, Pallas kernels for 0%

profile of v18, /device:TPU:0, one launch (start us, length us, event | category | flops | bytes accessed | tf_op | source)
XLA Modules:
  0.0 56.2 jit_solution(6329086735993195768)
XLA Ops:
  0.7 1.2 %copy.9 = f32[128,2,4,128]{3,1,0,2:T(2,128)S(1)} copy(bf16[128,2,4,128]{3,2,1,0:T(4,128)(2,1)} %param.5) | data formatting | bytes 786432 | tf_op jit(solution)/shard_map/transpose | solution.py:107
  2.3 0.9 %fusion.3 = f32[4,16,16,16]{3,2,1,0:T(8,128)S(1)} fusion(f32[4,16,16,128]{3,2,1,0:T(8,128)S(1)} %bitcast.204, pred[16,16]{1,0:T(8,128)(4,1)S(1)} %iota_compare_fusion.7), kind=kOutput, calls=%fused_computation.10 | convolution fusion | flops 25198592 | bytes 590080 | tf_op jit(solution)/shard_map/hpid,hpjd->hpij/dot_general | solution.py:11
  3.2 0.4 fusion.73
  3.6 0.4 fusion.74
  4.0 0.4 convolution_add_fusion.2
  4.3 0.4 fusion.75
  4.7 0.4 convolution_add_fusion.1
  5.1 0.4 convolution_add_fusion
  5.5 0.5 convolution_multiply_fusion.7
  6.0 0.4 fusion.69
  6.4 0.4 convolution_negate_fusion.3
  7.0 0.5 convolution_multiply_fusion.6
  7.5 0.4 fusion.70
  7.9 0.4 convolution_negate_fusion.2
  8.5 0.5 convolution_multiply_fusion.5
  9.0 0.4 fusion.71
  9.4 0.4 convolution_negate_fusion.1
  10.0 0.7 %convolution_multiply_fusion.4 = f32[4,128,128]{2,1,0:T(8,128)S(1)} fusion(f32[4,1,2,128,128]{4,3,2,0,1:T(8,128)S(1)} %bitcast.208), kind=kOutput, calls=%fused_computation.31 | convolution fusion | flops 100728832 | bytes 786432 | tf_op jit(solution)/shard_map/hpid,hpjd->hpij/dot_general | solution.py:11
  10.7 0.6 %fusion.38 = f32[4,128,128]{1,2,0:T(8,128)S(1)} fusion(f32[4,128,128]{2,1,0:T(8,128)S(1)} %convolution_multiply_fusion.4, f32[4,1,2,128,128]{4,3,2,0,1:T(8,128)S(1)} %fusion.17), kind=kOutput, calls=%fused_computation.88 | convolution fusion | flops 100663296 | bytes 786432 | tf_op jit(solution)/shard_map/hpij,hpjk->hpik/dot_general | solution.py:11
  11.3 0.7 %fusion.12 = f32[4,1,128,128]{3,2,0,1:T(8,128)S(1)} fusion(f32[4,128,128]{1,2,0:T(8,128)S(1)} %fusion.38, f32[4,1,2,128,128]{4,3,2,0,1:T(8,128)S(1)} %fusion.17), kind=kOutput, calls=%fused_computation.30 | convolution fusion | flops 100728832 | bytes 786432 | tf_op jit(solution)/shard_map/hpij,hpjk->hpik/dot_general | solution.py:11
  11.9 0.3 copy-done.2
  12.2 0.4 fusion.22
  12.7 0.6 %convolution_multiply_fusion.9 = f32[4,128,128]{2,1,0:T(8,128)S(1)} fusion(f32[4,256,128]{2,1,0:T(8,128)S(1)} %broadcast_multiply_fusion, f32[4,256,128]{2,1,0:T(8,128)S(1)} %fusion.22), kind=kOutput, calls=%fused_computation.39 | convolution fusion | flops 100728832 | bytes 1310720 | tf_op jit(solution)/shard_map/hjd,hjw->hdw/dot_general | solution.py:15
  13.3 4.9 %collective-permute-start = (f32[4,128,128]{2,1,0:T(8,128)S(1)}, f32[4,128,128]{2,1,0:T(8,128)S(1)}, u32[]{:S(2)}, u32[]{:S(2)}) collective-permute-start(f32[4,128,128]{2,1,0:T(8,128)S(1)} %convolution_multiply_fusion.9), channel_id=1, source_target_pairs={{0,4},{4,8},{8,12},{1,5},{5,9},{9,13},{2,6},{6,10},{10,14},{3,7},{... | collective-permute-start | bytes 786440 | tf_op jit(solution)/shard_map/ppermute | solution.py:64
  18.3 0.6 %fusion.24 = f32[4,256,128]{2,1,0:T(8,128)S(1)} fusion(f32[4,256,128]{2,1,0:T(8,128)S(1)} %broadcast_multiply_fusion, f32[4,1,128,128]{3,2,0,1:T(8,128)S(1)} %get-tuple-element.9, f32[4,1,128,128]{3,2,0,1:T(8,128)S(1)} %get-tuple-element.8, f32[4,1,128,128]{3,2,0,1:T(8,128)S(1)} %fusion.12), kind=kOutput, calls=%fused_computation.61 | convolution fusion | flops 202375168 | bytes 1835008 | tf_op jit(solution)/shard_map/hij,hjd->hid/dot_general | solution.py:15
  19.3 0.4 fusion.10
  19.8 0.4 convolution_subtract_fusion.2
  20.2 0.3 fusion.48
  20.5 1.5 %collective-permute-start.3 = (f32[4,128,128]{2,1,0:T(8,128)S(1)}, f32[4,128,128]{2,1,0:T(8,128)S(1)}, u32[]{:S(2)}, u32[]{:S(2)}) collective-permute-start(f32[4,128,128]{2,1,0:T(8,128)S(1)} %fusion.48), channel_id=1, source_target_pairs={{4,0},{8,4},{12,8},{5,1},{9,5},{13,9},{6,2},{10,6},{14,10},{7,3},{... | collective-permute-start | bytes 786440 | tf_op jit(solution)/shard_map/ppermute | solution.py:65
  22.0 0.4 fusion.76
  22.4 0.6 %fusion.13 = f32[4,128,128]{2,1,0:T(8,128)S(1)} fusion(f32[4,256,128]{2,1,0:T(8,128)S(1)} %broadcast_multiply_fusion, f32[4,256,128]{2,1,0:T(8,128)S(1)} %fusion.24, f32[128,128]{1,0:T(8,128)S(1)} %fusion.55), kind=kOutput, calls=%fused_computation.42 | convolution fusion | flops 100794368 | bytes 1376256 | tf_op jit(solution)/shard_map/hjd,hjw->hdw/dot_general | solution.py:15
  23.0 0.8 %collective-permute-done = f32[4,128,128]{2,1,0:T(8,128)S(1)} collective-permute-done((f32[4,128,128]{2,1,0:T(8,128)S(1)}, f32[4,128,128]{2,1,0:T(8,128)S(1)}, u32[]{:S(2)}, u32[]{:S(2)}) %collective-permute-start) | collective-permute-done | bytes 262176 | tf_op jit(solution)/shard_map/ppermute | solution.py:64
  23.8 0.3 convolution_add_fusion.9
  24.1 4.4 %collective-permute-start.1 = (f32[4,128,128]{2,1,0:T(8,128)S(1)}, f32[4,128,128]{2,1,0:T(8,128)S(1)}, u32[]{:S(2)}, u32[]{:S(2)}) collective-permute-start(f32[4,128,128]{2,1,0:T(8,128)S(1)} %convolution_add_fusion.9), channel_id=1, source_target_pairs={{0,4},{4,8},{8,12},{1,5},{5,9},{9,13},{2,6},{6,10},{10,14},{3,7},{... | collective-permute-start | bytes 786440 | tf_op jit(solution)/shard_map/ppermute | solution.py:64
  28.5 0.5 fusion.51
  28.9 1.2 %collective-permute-done.3 = f32[4,128,128]{2,1,0:T(8,128)S(1)} collective-permute-done((f32[4,128,128]{2,1,0:T(8,128)S(1)}, f32[4,128,128]{2,1,0:T(8,128)S(1)}, u32[]{:S(2)}, u32[]{:S(2)}) %collective-permute-start.3) | collective-permute-done | bytes 262176 | tf_op jit(solution)/shard_map/ppermute | solution.py:65
  30.2 0.4 convolution_add_fusion.6
  30.6 1.3 %collective-permute-start.4 = (f32[4,128,128]{2,1,0:T(8,128)S(1)}, f32[4,128,128]{2,1,0:T(8,128)S(1)}, u32[]{:S(2)}, u32[]{:S(2)}) collective-permute-start(f32[4,128,128]{2,1,0:T(8,128)S(1)} %convolution_add_fusion.6), channel_id=1, source_target_pairs={{4,0},{8,4},{12,8},{5,1},{9,5},{13,9},{6,2},{10,6},{14,10},{7,3},{... | collective-permute-start | bytes 786440 | tf_op jit(solution)/shard_map/ppermute | solution.py:65
  31.9 1.3 %collective-permute-done.1 = f32[4,128,128]{2,1,0:T(8,128)S(1)} collective-permute-done((f32[4,128,128]{2,1,0:T(8,128)S(1)}, f32[4,128,128]{2,1,0:T(8,128)S(1)}, u32[]{:S(2)}, u32[]{:S(2)}) %collective-permute-start.1) | collective-permute-done | bytes 262176 | tf_op jit(solution)/shard_map/ppermute | solution.py:64
  33.1 0.3 convolution_add_fusion.8
  33.4 4.4 %collective-permute-start.2 = (f32[4,128,128]{2,1,0:T(8,128)S(1)}, f32[4,128,128]{2,1,0:T(8,128)S(1)}, u32[]{:S(2)}, u32[]{:S(2)}) collective-permute-start(f32[4,128,128]{2,1,0:T(8,128)S(1)} %convolution_add_fusion.8), channel_id=1, source_target_pairs={{0,4},{4,8},{8,12},{1,5},{5,9},{9,13},{2,6},{6,10},{10,14},{3,7},{... | collective-permute-start | bytes 786440 | tf_op jit(solution)/shard_map/ppermute | solution.py:64
  37.9 1.4 %collective-permute-done.4 = f32[4,128,128]{2,1,0:T(8,128)S(1)} collective-permute-done((f32[4,128,128]{2,1,0:T(8,128)S(1)}, f32[4,128,128]{2,1,0:T(8,128)S(1)}, u32[]{:S(2)}, u32[]{:S(2)}) %collective-permute-start.4) | collective-permute-done | bytes 262176 | tf_op jit(solution)/shard_map/ppermute | solution.py:65
  39.3 0.4 convolution_add_fusion.5
  39.7 1.3 %collective-permute-start.5 = (f32[4,128,128]{2,1,0:T(8,128)S(1)}, f32[4,128,128]{2,1,0:T(8,128)S(1)}, u32[]{:S(2)}, u32[]{:S(2)}) collective-permute-start(f32[4,128,128]{2,1,0:T(8,128)S(1)} %convolution_add_fusion.5), channel_id=1, source_target_pairs={{4,0},{8,4},{12,8},{5,1},{9,5},{13,9},{6,2},{10,6},{14,10},{7,3},{... | collective-permute-start | bytes 786440 | tf_op jit(solution)/shard_map/ppermute | solution.py:65
  41.0 0.7 %collective-permute-done.2 = f32[4,128,128]{2,1,0:T(8,128)S(1)} collective-permute-done((f32[4,128,128]{2,1,0:T(8,128)S(1)}, f32[4,128,128]{2,1,0:T(8,128)S(1)}, u32[]{:S(2)}, u32[]{:S(2)}) %collective-permute-start.2) | collective-permute-done | bytes 262176 | tf_op jit(solution)/shard_map/ppermute | solution.py:64
  41.7 0.4 convolution_subtract_fusion.1
  42.1 0.3 fusion.2
  42.4 0.3 fusion.53
  42.7 0.5 fusion.32
  43.2 0.3 fusion.15
  43.7 0.8 %copy.36 = bf16[128,4,128]{2,1,0:T(4,128)(2,1)} copy(bf16[128,4,128]{2,0,1:T(8,128)(2,1)S(1)} %fusion.15) | data formatting | bytes 262144
  44.4 0.8 %copy.37 = bf16[128,4,128]{2,1,0:T(4,128)(2,1)} copy(bf16[128,4,128]{2,0,1:T(8,128)(2,1)S(1)} %fusion.37) | data formatting | bytes 262144
  45.2 0.7 %fusion.28 = f32[4,256,128]{2,1,0:T(8,128)S(1)} fusion(f32[4,128,256]{2,1,0:T(8,128)S(1)} %fusion.2, f32[4,128]{1,0:T(4,128)S(1)} %get-tuple-element.17, bf16[128,4,128]{2,1,0:T(4,128)(2,1)S(1)} %copy-done.1), kind=kOutput, calls=%fused_computation.66 | convolution fusion | flops 100794368 | bytes 1181696 | tf_op jit(solution)/shard_map/hij,hid->hjd/dot_general | solution.py:15
  45.9 2.1 %collective-permute-done.5 = f32[4,128,128]{2,1,0:T(8,128)S(1)} collective-permute-done((f32[4,128,128]{2,1,0:T(8,128)S(1)}, f32[4,128,128]{2,1,0:T(8,128)S(1)}, u32[]{:S(2)}, u32[]{:S(2)}) %collective-permute-start.5) | collective-permute-done | bytes 262176 | tf_op jit(solution)/shard_map/ppermute | solution.py:65
  48.0 0.4 fusion.8
  48.3 0.9 %fusion.72 = (bf16[4,256,128]{2,1,0:T(8,128)(2,1)S(1)}, f32[4,256,128]{2,1,0:T(8,128)S(1)}) fusion(f32[4,256,128]{2,1,0:T(8,128)S(1)} %fusion.8, f32[4,1,128,128]{3,2,0,1:T(8,128)S(1)} %get-tuple-element.9, f32[4,1,128,128]{3,2,0,1:T(8,128)S(1)} %get-tuple-element.8, f32[4,1,128,128]{3,2,0,1:T(8,128)S(1)} %fusion.12), kind=kOutput, calls=%fused_computation.137 | convolution fusion | flops 202506240 | bytes 2097152 | tf_op jit(solution)/shard_map/hij,hiw->hjw/dot_general | solution.py:15
  49.2 0.6 %fusion.1 = f32[4,256,256]{2,1,0:T(8,128)S(1)} fusion(f32[4,256,128]{2,1,0:T(8,128)S(1)} %get-tuple-element.21, f32[4,256,128]{2,1,0:T(8,128)S(1)} %convolution_subtract_fusion.1, pred[256,256]{1,0:T(8,128)(4,1)S(1)} %iota_compare_fusion.4), kind=kOutput, calls=%fused_computation.2 | convolution fusion | flops 201850880 | bytes 2162688 | tf_op jit(solution)/shard_map/hiw,hjw->hij/dot_general | solution.py:15
  49.8 0.6 %fusion.77 = f32[4,256,128]{2,1,0:T(8,128)S(1)} fusion(f32[4,256,256]{2,1,0:T(8,128)S(1)} %fusion.1, f32[4,256,128]{2,1,0:T(8,128)S(1)} %broadcast_multiply_fusion), kind=kOutput, calls=%fused_computation.142 | convolution fusion | flops 201326592 | bytes 2097152 | tf_op jit(solution)/shard_map/hij,hjd->hid/dot_general | solution.py:15
  50.4 0.4 fusion.9
  50.8 0.4 fusion.7
  51.2 1.0 %convolution_add_fusion.3 = f32[4,256,128]{2,1,0:T(8,128)S(1)} fusion(f32[4,256,128]{2,1,0:T(8,128)S(1)} %fusion.7, f32[4,256,256]{2,1,0:T(8,128)S(1)} %fusion.1, f32[4,256,128]{2,1,0:T(8,128)S(1)} %broadcast_multiply_fusion), kind=kOutput, calls=%fused_computation.6 | convolution fusion | flops 201457664 | bytes 2621440 | tf_op jit(solution)/shard_map/hji,hjd->hid/dot_general | solution.py:15
  52.3 1.8 %fusion.11 = bf16[4,256,128]{2,1,0:T(8,128)(2,1)S(1)} fusion(f32[4,256,128]{2,1,0:T(8,128)S(1)} %convolution_add_fusion.3, f32[4,256,128]{2,1,0:T(8,128)S(1)} %broadcast_multiply_fusion, f32[4,256]{1,0:T(4,128)S(1)} %add_rsqrt_fusion), kind=kOutput, calls=%fused_computation.23 | output fusion | flops 656511 | bytes 1314816 | tf_op jit(solution)/shard_map/mul | solution.py:143
  54.1 1.0 %copy.84 = bf16[4,128,2,128]{3,0,2,1:T(4,128)(2,1)} copy(bf16[4,128,2,128]{3,2,1,0:T(2,128)(2,1)S(1)} %bitcast.220) | data formatting | bytes 524288 | tf_op jit(solution)/shard_map/convert_element_type | solution.py:152
  55.1 1.0 %copy.83 = bf16[4,128,2,128]{3,0,2,1:T(4,128)(2,1)} copy(bf16[4,128,2,128]{3,2,1,0:T(2,128)(2,1)S(1)} %bitcast.221) | data formatting | bytes 524288 | tf_op jit(solution)/shard_map/convert_element_type | solution.py:152
  (24 shorter events, 1.7 us)
Async XLA Ops:
  0.6 19.5 %copy-start = (bf16[128,4,128]{2,1,0:T(4,128)(2,1)S(1)}, bf16[128,4,128]{2,1,0:T(4,128)(2,1)}, u32[]{:S(2)}) copy-start(bf16[128,4,128]{2,1,0:T(4,128)(2,1)} %param.7) | copy-start | bytes 393220
  11.3 1.0 %copy-start.2 = (bf16[128,2,4,128]{3,2,1,0:T(4,128)(2,1)S(1)}, bf16[128,2,4,128]{3,2,1,0:T(4,128)(2,1)}, u32[]{:S(2)}) copy-start(bf16[128,2,4,128]{3,2,1,0:T(4,128)(2,1)} %param.6) | copy-start | bytes 786436
  13.3 10.5 %collective-permute-start = (f32[4,128,128]{2,1,0:T(8,128)S(1)}, f32[4,128,128]{2,1,0:T(8,128)S(1)}, u32[]{:S(2)}, u32[]{:S(2)}) collective-permute-start(f32[4,128,128]{2,1,0:T(8,128)S(1)} %convolution_multiply_fusion.9), channel_id=1, source_target_pairs={{0,4},{4,8},{8,12},{1,5},{5,9},{9,13},{2,6},{6,10},{10,14},{3,7},{... | collective-permute-start | bytes 786440 | tf_op jit(solution)/shard_map/ppermute | solution.py:64
  18.3 0.9 %copy-start.1 = (bf16[128,4,128]{2,1,0:T(4,128)(2,1)S(1)}, bf16[128,4,128]{2,1,0:T(4,128)(2,1)}, u32[]{:S(2)}) copy-start(bf16[128,4,128]{2,1,0:T(4,128)(2,1)} %param.4) | copy-start | bytes 393220
  20.5 9.7 %collective-permute-start.3 = (f32[4,128,128]{2,1,0:T(8,128)S(1)}, f32[4,128,128]{2,1,0:T(8,128)S(1)}, u32[]{:S(2)}, u32[]{:S(2)}) collective-permute-start(f32[4,128,128]{2,1,0:T(8,128)S(1)} %fusion.48), channel_id=1, source_target_pairs={{4,0},{8,4},{12,8},{5,1},{9,5},{13,9},{6,2},{10,6},{14,10},{7,3},{... | collective-permute-start | bytes 786440 | tf_op jit(solution)/shard_map/ppermute | solution.py:65
  24.1 9.1 %collective-permute-start.1 = (f32[4,128,128]{2,1,0:T(8,128)S(1)}, f32[4,128,128]{2,1,0:T(8,128)S(1)}, u32[]{:S(2)}, u32[]{:S(2)}) collective-permute-start(f32[4,128,128]{2,1,0:T(8,128)S(1)} %convolution_add_fusion.9), channel_id=1, source_target_pairs={{0,4},{4,8},{8,12},{1,5},{5,9},{9,13},{2,6},{6,10},{10,14},{3,7},{... | collective-permute-start | bytes 786440 | tf_op jit(solution)/shard_map/ppermute | solution.py:64
  30.6 8.7 %collective-permute-start.4 = (f32[4,128,128]{2,1,0:T(8,128)S(1)}, f32[4,128,128]{2,1,0:T(8,128)S(1)}, u32[]{:S(2)}, u32[]{:S(2)}) collective-permute-start(f32[4,128,128]{2,1,0:T(8,128)S(1)} %convolution_add_fusion.6), channel_id=1, source_target_pairs={{4,0},{8,4},{12,8},{5,1},{9,5},{13,9},{6,2},{10,6},{14,10},{7,3},{... | collective-permute-start | bytes 786440 | tf_op jit(solution)/shard_map/ppermute | solution.py:65
  33.4 8.3 %collective-permute-start.2 = (f32[4,128,128]{2,1,0:T(8,128)S(1)}, f32[4,128,128]{2,1,0:T(8,128)S(1)}, u32[]{:S(2)}, u32[]{:S(2)}) collective-permute-start(f32[4,128,128]{2,1,0:T(8,128)S(1)} %convolution_add_fusion.8), channel_id=1, source_target_pairs={{0,4},{4,8},{8,12},{1,5},{5,9},{9,13},{2,6},{6,10},{10,14},{3,7},{... | collective-permute-start | bytes 786440 | tf_op jit(solution)/shard_map/ppermute | solution.py:64
  39.7 8.3 %collective-permute-start.5 = (f32[4,128,128]{2,1,0:T(8,128)S(1)}, f32[4,128,128]{2,1,0:T(8,128)S(1)}, u32[]{:S(2)}, u32[]{:S(2)}) collective-permute-start(f32[4,128,128]{2,1,0:T(8,128)S(1)} %convolution_add_fusion.5), channel_id=1, source_target_pairs={{4,0},{8,4},{12,8},{5,1},{9,5},{13,9},{6,2},{10,6},{14,10},{7,3},{... | collective-permute-start | bytes 786440 | tf_op jit(solution)/shard_map/ppermute | solution.py:65

commit v19 on v18

--- a/solution.py
+++ b/solution.py
@@ -30,7 +30,7 @@
     heads, rows, size = keys.shape
     leaves = rows // LEAF
     leaf_keys = keys.reshape(heads, leaves, LEAF, size)
-    gram = mm("hpid,hpjd->hpij", leaf_keys, leaf_keys)
+    gram = mh("hpid,hpjd->hpij", leaf_keys, leaf_keys)
     power = jnp.where(strict_lower(LEAF, LEAF), -2.0 * gram, 0.0)
     eye = jnp.eye(LEAF, dtype=jnp.float32)
     inverse = eye + power

time: 56.5 us -> 56.1 us (level)
    dot_general x13 -> x12, matrix products: 6.73 us -> 5.8 us  [mm(): return jnp.einsum(spec, *operands, precision=highest)]
    dot_general x32 -> x33, matrix products: 14.4 us -> 14.9 us  [mh(): return jnp.einsum(spec, *operands, precision=lax.Precision.HIGH)]
where the time goes in v19:
time: 56.1 us; the launch traced here: 55.8 us
  matrix products  20.7 us (37%)
  starting transfers between devices  17.8 us (32%)
  waiting for transfers between devices  7.5 us (13%)
  local copies, waits for them, and re-layouts  5.45 us (10%)
  other arithmetic  3.12 us (6%)
  between operations  1.16 us (2%)
    dot_general x33, matrix products, mh(): return jnp.einsum(spec, *operands, precision=lax.Precision.HIGH)  14.9 us
    ppermute x3, starting transfers between devices, chain_seq(): got_sum = lax.ppermute(fwd_sum, 'seq', right)  13.7 us
    dot_general x12, matrix products, mm(): return jnp.einsum(spec, *operands, precision=highest)  5.8 us
    ppermute x3, waiting for transfers between devices, chain_seq(): got_cot = lax.ppermute(bwd_sum, 'seq', left)  4.74 us
    ppermute x3, starting transfers between devices, chain_seq(): got_cot = lax.ppermute(bwd_sum, 'seq', left)  4.06 us
    ppermute x3, waiting for transfers between devices, chain_seq(): got_sum = lax.ppermute(fwd_sum, 'seq', right)  2.76 us
    convert_element_type x2, local copies, waits for them, and re-layouts, pair_major(): return tensor.reshape(heads_here, tok_count, 2, head_size).transpose(1, 2...  2.09 us
    unnamed x8, local copies, waits for them, and re-layouts  2.02 us
  transfers between devices with their start and end apart: 6, of which 6 were waited for; matrix products, arithmetic and copies ran while one was open for 16% of the time, Pallas kernels for 0%

profile of v19, /device:TPU:0, one launch (start us, length us, event | category | flops | bytes accessed | tf_op | source)
XLA Modules:
  0.0 55.8 jit_solution(18049891612209239754)
XLA Ops:
  0.7 1.2 %copy.9 = f32[128,2,4,128]{3,1,0,2:T(2,128)S(1)} copy(bf16[128,2,4,128]{3,2,1,0:T(4,128)(2,1)} %param.5) | data formatting | bytes 786432 | tf_op jit(solution)/shard_map/transpose | solution.py:107
  2.3 0.5 fusion.3
  2.8 0.4 fusion.73
  3.2 0.4 fusion.74
  3.6 0.4 convolution_add_fusion.2
  3.9 0.4 fusion.75
  4.3 0.4 convolution_add_fusion.1
  4.7 0.4 convolution_add_fusion
  5.1 0.5 convolution_multiply_fusion.7
  5.6 0.4 fusion.69
  6.0 0.4 convolution_negate_fusion.3
  6.6 0.5 convolution_multiply_fusion.6
  7.1 0.4 fusion.70
  7.5 0.4 convolution_negate_fusion.2
  8.1 0.5 convolution_multiply_fusion.5
  8.6 0.4 fusion.71
  9.0 0.4 convolution_negate_fusion.1
  9.6 0.7 %convolution_multiply_fusion.4 = f32[4,128,128]{2,1,0:T(8,128)S(1)} fusion(f32[4,1,2,128,128]{4,3,2,0,1:T(8,128)S(1)} %bitcast.208), kind=kOutput, calls=%fused_computation.31 | convolution fusion | flops 100728832 | bytes 786432 | tf_op jit(solution)/shard_map/hpid,hpjd->hpij/dot_general | solution.py:11
  10.3 0.6 %fusion.38 = f32[4,128,128]{1,2,0:T(8,128)S(1)} fusion(f32[4,128,128]{2,1,0:T(8,128)S(1)} %convolution_multiply_fusion.4, f32[4,1,2,128,128]{4,3,2,0,1:T(8,128)S(1)} %fusion.17), kind=kOutput, calls=%fused_computation.88 | convolution fusion | flops 100663296 | bytes 786432 | tf_op jit(solution)/shard_map/hpij,hpjk->hpik/dot_general | solution.py:11
  10.9 0.7 %fusion.12 = f32[4,1,128,128]{3,2,0,1:T(8,128)S(1)} fusion(f32[4,128,128]{1,2,0:T(8,128)S(1)} %fusion.38, f32[4,1,2,128,128]{4,3,2,0,1:T(8,128)S(1)} %fusion.17), kind=kOutput, calls=%fused_computation.30 | convolution fusion | flops 100728832 | bytes 786432 | tf_op jit(solution)/shard_map/hpij,hpjk->hpik/dot_general | solution.py:11
  11.5 0.3 copy-done.2
  11.8 0.4 fusion.22
  12.3 0.6 %convolution_multiply_fusion.9 = f32[4,128,128]{2,1,0:T(8,128)S(1)} fusion(f32[4,256,128]{2,1,0:T(8,128)S(1)} %broadcast_multiply_fusion, f32[4,256,128]{2,1,0:T(8,128)S(1)} %fusion.22), kind=kOutput, calls=%fused_computation.39 | convolution fusion | flops 100728832 | bytes 1310720 | tf_op jit(solution)/shard_map/hjd,hjw->hdw/dot_general | solution.py:15
  12.9 4.9 %collective-permute-start = (f32[4,128,128]{2,1,0:T(8,128)S(1)}, f32[4,128,128]{2,1,0:T(8,128)S(1)}, u32[]{:S(2)}, u32[]{:S(2)}) collective-permute-start(f32[4,128,128]{2,1,0:T(8,128)S(1)} %convolution_multiply_fusion.9), channel_id=1, source_target_pairs={{0,4},{4,8},{8,12},{1,5},{5,9},{9,13},{2,6},{6,10},{10,14},{3,7},{... | collective-permute-start | bytes 786440 | tf_op jit(solution)/shard_map/ppermute | solution.py:64
  17.9 0.6 %fusion.24 = f32[4,256,128]{2,1,0:T(8,128)S(1)} fusion(f32[4,256,128]{2,1,0:T(8,128)S(1)} %broadcast_multiply_fusion, f32[4,1,128,128]{3,2,0,1:T(8,128)S(1)} %get-tuple-element.9, f32[4,1,128,128]{3,2,0,1:T(8,128)S(1)} %get-tuple-element.8, f32[4,1,128,128]{3,2,0,1:T(8,128)S(1)} %fusion.12), kind=kOutput, calls=%fused_computation.61 | convolution fusion | flops 202375168 | bytes 1835008 | tf_op jit(solution)/shard_map/hij,hjd->hid/dot_general | solution.py:15
  18.9 0.4 fusion.10
  19.4 0.4 convolution_subtract_fusion.2
  19.8 0.3 fusion.48
  20.1 1.5 %collective-permute-start.3 = (f32[4,128,128]{2,1,0:T(8,128)S(1)}, f32[4,128,128]{2,1,0:T(8,128)S(1)}, u32[]{:S(2)}, u32[]{:S(2)}) collective-permute-start(f32[4,128,128]{2,1,0:T(8,128)S(1)} %fusion.48), channel_id=1, source_target_pairs={{4,0},{8,4},{12,8},{5,1},{9,5},{13,9},{6,2},{10,6},{14,10},{7,3},{... | collective-permute-start | bytes 786440 | tf_op jit(solution)/shard_map/ppermute | solution.py:65
  21.6 0.4 fusion.76
  22.0 0.6 %fusion.13 = f32[4,128,128]{2,1,0:T(8,128)S(1)} fusion(f32[4,256,128]{2,1,0:T(8,128)S(1)} %broadcast_multiply_fusion, f32[4,256,128]{2,1,0:T(8,128)S(1)} %fusion.24, f32[128,128]{1,0:T(8,128)S(1)} %fusion.55), kind=kOutput, calls=%fused_computation.42 | convolution fusion | flops 100794368 | bytes 1376256 | tf_op jit(solution)/shard_map/hjd,hjw->hdw/dot_general | solution.py:15
  22.6 0.8 %collective-permute-done = f32[4,128,128]{2,1,0:T(8,128)S(1)} collective-permute-done((f32[4,128,128]{2,1,0:T(8,128)S(1)}, f32[4,128,128]{2,1,0:T(8,128)S(1)}, u32[]{:S(2)}, u32[]{:S(2)}) %collective-permute-start) | collective-permute-done | bytes 262176 | tf_op jit(solution)/shard_map/ppermute | solution.py:64
  23.4 0.3 convolution_add_fusion.9
  23.7 4.4 %collective-permute-start.1 = (f32[4,128,128]{2,1,0:T(8,128)S(1)}, f32[4,128,128]{2,1,0:T(8,128)S(1)}, u32[]{:S(2)}, u32[]{:S(2)}) collective-permute-start(f32[4,128,128]{2,1,0:T(8,128)S(1)} %convolution_add_fusion.9), channel_id=1, source_target_pairs={{0,4},{4,8},{8,12},{1,5},{5,9},{9,13},{2,6},{6,10},{10,14},{3,7},{... | collective-permute-start | bytes 786440 | tf_op jit(solution)/shard_map/ppermute | solution.py:64
  28.1 0.5 fusion.51
  28.5 1.2 %collective-permute-done.3 = f32[4,128,128]{2,1,0:T(8,128)S(1)} collective-permute-done((f32[4,128,128]{2,1,0:T(8,128)S(1)}, f32[4,128,128]{2,1,0:T(8,128)S(1)}, u32[]{:S(2)}, u32[]{:S(2)}) %collective-permute-start.3) | collective-permute-done | bytes 262176 | tf_op jit(solution)/shard_map/ppermute | solution.py:65
  29.8 0.4 convolution_add_fusion.6
  30.1 1.3 %collective-permute-start.4 = (f32[4,128,128]{2,1,0:T(8,128)S(1)}, f32[4,128,128]{2,1,0:T(8,128)S(1)}, u32[]{:S(2)}, u32[]{:S(2)}) collective-permute-start(f32[4,128,128]{2,1,0:T(8,128)S(1)} %convolution_add_fusion.6), channel_id=1, source_target_pairs={{4,0},{8,4},{12,8},{5,1},{9,5},{13,9},{6,2},{10,6},{14,10},{7,3},{... | collective-permute-start | bytes 786440 | tf_op jit(solution)/shard_map/ppermute | solution.py:65
  31.4 1.3 %collective-permute-done.1 = f32[4,128,128]{2,1,0:T(8,128)S(1)} collective-permute-done((f32[4,128,128]{2,1,0:T(8,128)S(1)}, f32[4,128,128]{2,1,0:T(8,128)S(1)}, u32[]{:S(2)}, u32[]{:S(2)}) %collective-permute-start.1) | collective-permute-done | bytes 262176 | tf_op jit(solution)/shard_map/ppermute | solution.py:64
  32.7 0.3 convolution_add_fusion.8
  33.0 4.4 %collective-permute-start.2 = (f32[4,128,128]{2,1,0:T(8,128)S(1)}, f32[4,128,128]{2,1,0:T(8,128)S(1)}, u32[]{:S(2)}, u32[]{:S(2)}) collective-permute-start(f32[4,128,128]{2,1,0:T(8,128)S(1)} %convolution_add_fusion.8), channel_id=1, source_target_pairs={{0,4},{4,8},{8,12},{1,5},{5,9},{9,13},{2,6},{6,10},{10,14},{3,7},{... | collective-permute-start | bytes 786440 | tf_op jit(solution)/shard_map/ppermute | solution.py:64
  37.5 1.4 %collective-permute-done.4 = f32[4,128,128]{2,1,0:T(8,128)S(1)} collective-permute-done((f32[4,128,128]{2,1,0:T(8,128)S(1)}, f32[4,128,128]{2,1,0:T(8,128)S(1)}, u32[]{:S(2)}, u32[]{:S(2)}) %collective-permute-start.4) | collective-permute-done | bytes 262176 | tf_op jit(solution)/shard_map/ppermute | solution.py:65
  38.9 0.4 convolution_add_fusion.5
  39.3 1.3 %collective-permute-start.5 = (f32[4,128,128]{2,1,0:T(8,128)S(1)}, f32[4,128,128]{2,1,0:T(8,128)S(1)}, u32[]{:S(2)}, u32[]{:S(2)}) collective-permute-start(f32[4,128,128]{2,1,0:T(8,128)S(1)} %convolution_add_fusion.5), channel_id=1, source_target_pairs={{4,0},{8,4},{12,8},{5,1},{9,5},{13,9},{6,2},{10,6},{14,10},{7,3},{... | collective-permute-start | bytes 786440 | tf_op jit(solution)/shard_map/ppermute | solution.py:65
  40.6 0.7 %collective-permute-done.2 = f32[4,128,128]{2,1,0:T(8,128)S(1)} collective-permute-done((f32[4,128,128]{2,1,0:T(8,128)S(1)}, f32[4,128,128]{2,1,0:T(8,128)S(1)}, u32[]{:S(2)}, u32[]{:S(2)}) %collective-permute-start.2) | collective-permute-done | bytes 262176 | tf_op jit(solution)/shard_map/ppermute | solution.py:64
  41.3 0.4 convolution_subtract_fusion.1
  41.7 0.3 fusion.2
  42.0 0.3 fusion.53
  42.3 0.5 fusion.32
  42.8 0.3 fusion.15
  43.3 0.8 %copy.36 = bf16[128,4,128]{2,1,0:T(4,128)(2,1)} copy(bf16[128,4,128]{2,0,1:T(8,128)(2,1)S(1)} %fusion.15) | data formatting | bytes 262144
  44.0 0.8 %copy.37 = bf16[128,4,128]{2,1,0:T(4,128)(2,1)} copy(bf16[128,4,128]{2,0,1:T(8,128)(2,1)S(1)} %fusion.37) | data formatting | bytes 262144
  44.8 0.7 %fusion.28 = f32[4,256,128]{2,1,0:T(8,128)S(1)} fusion(f32[4,128,256]{2,1,0:T(8,128)S(1)} %fusion.2, f32[4,128]{1,0:T(4,128)S(1)} %get-tuple-element.17, bf16[128,4,128]{2,1,0:T(4,128)(2,1)S(1)} %copy-done.1), kind=kOutput, calls=%fused_computation.66 | convolution fusion | flops 100794368 | bytes 1181696 | tf_op jit(solution)/shard_map/hij,hid->hjd/dot_general | solution.py:15
  45.5 2.1 %collective-permute-done.5 = f32[4,128,128]{2,1,0:T(8,128)S(1)} collective-permute-done((f32[4,128,128]{2,1,0:T(8,128)S(1)}, f32[4,128,128]{2,1,0:T(8,128)S(1)}, u32[]{:S(2)}, u32[]{:S(2)}) %collective-permute-start.5) | collective-permute-done | bytes 262176 | tf_op jit(solution)/shard_map/ppermute | solution.py:65
  47.6 0.4 fusion.8
  47.9 0.9 %fusion.72 = (bf16[4,256,128]{2,1,0:T(8,128)(2,1)S(1)}, f32[4,256,128]{2,1,0:T(8,128)S(1)}) fusion(f32[4,256,128]{2,1,0:T(8,128)S(1)} %fusion.8, f32[4,1,128,128]{3,2,0,1:T(8,128)S(1)} %get-tuple-element.9, f32[4,1,128,128]{3,2,0,1:T(8,128)S(1)} %get-tuple-element.8, f32[4,1,128,128]{3,2,0,1:T(8,128)S(1)} %fusion.12), kind=kOutput, calls=%fused_computation.137 | convolution fusion | flops 202506240 | bytes 2097152 | tf_op jit(solution)/shard_map/hij,hiw->hjw/dot_general | solution.py:15
  48.8 0.6 %fusion.1 = f32[4,256,256]{2,1,0:T(8,128)S(1)} fusion(f32[4,256,128]{2,1,0:T(8,128)S(1)} %get-tuple-element.21, f32[4,256,128]{2,1,0:T(8,128)S(1)} %convolution_subtract_fusion.1, pred[256,256]{1,0:T(8,128)(4,1)S(1)} %iota_compare_fusion.4), kind=kOutput, calls=%fused_computation.2 | convolution fusion | flops 201850880 | bytes 2162688 | tf_op jit(solution)/shard_map/hiw,hjw->hij/dot_general | solution.py:15
  49.4 0.6 %fusion.77 = f32[4,256,128]{2,1,0:T(8,128)S(1)} fusion(f32[4,256,256]{2,1,0:T(8,128)S(1)} %fusion.1, f32[4,256,128]{2,1,0:T(8,128)S(1)} %broadcast_multiply_fusion), kind=kOutput, calls=%fused_computation.142 | convolution fusion | flops 201326592 | bytes 2097152 | tf_op jit(solution)/shard_map/hij,hjd->hid/dot_general | solution.py:15
  50.0 0.4 fusion.9
  50.4 0.4 fusion.7
  50.8 1.0 %convolution_add_fusion.3 = f32[4,256,128]{2,1,0:T(8,128)S(1)} fusion(f32[4,256,128]{2,1,0:T(8,128)S(1)} %fusion.7, f32[4,256,256]{2,1,0:T(8,128)S(1)} %fusion.1, f32[4,256,128]{2,1,0:T(8,128)S(1)} %broadcast_multiply_fusion), kind=kOutput, calls=%fused_computation.6 | convolution fusion | flops 201457664 | bytes 2621440 | tf_op jit(solution)/shard_map/hji,hjd->hid/dot_general | solution.py:15
  51.9 1.8 %fusion.11 = bf16[4,256,128]{2,1,0:T(8,128)(2,1)S(1)} fusion(f32[4,256,128]{2,1,0:T(8,128)S(1)} %convolution_add_fusion.3, f32[4,256,128]{2,1,0:T(8,128)S(1)} %broadcast_multiply_fusion, f32[4,256]{1,0:T(4,128)S(1)} %add_rsqrt_fusion), kind=kOutput, calls=%fused_computation.23 | output fusion | flops 656511 | bytes 1314816 | tf_op jit(solution)/shard_map/mul | solution.py:143
  53.7 1.0 %copy.84 = bf16[4,128,2,128]{3,0,2,1:T(4,128)(2,1)} copy(bf16[4,128,2,128]{3,2,1,0:T(2,128)(2,1)S(1)} %bitcast.220) | data formatting | bytes 524288 | tf_op jit(solution)/shard_map/convert_element_type | solution.py:152
  54.7 1.0 %copy.83 = bf16[4,128,2,128]{3,0,2,1:T(4,128)(2,1)} copy(bf16[4,128,2,128]{3,2,1,0:T(2,128)(2,1)S(1)} %bitcast.221) | data formatting | bytes 524288 | tf_op jit(solution)/shard_map/convert_element_type | solution.py:152
  (24 shorter events, 1.7 us)
Async XLA Ops:
  0.6 19.1 %copy-start = (bf16[128,4,128]{2,1,0:T(4,128)(2,1)S(1)}, bf16[128,4,128]{2,1,0:T(4,128)(2,1)}, u32[]{:S(2)}) copy-start(bf16[128,4,128]{2,1,0:T(4,128)(2,1)} %param.7) | copy-start | bytes 393220
  10.9 1.0 %copy-start.2 = (bf16[128,2,4,128]{3,2,1,0:T(4,128)(2,1)S(1)}, bf16[128,2,4,128]{3,2,1,0:T(4,128)(2,1)}, u32[]{:S(2)}) copy-start(bf16[128,2,4,128]{3,2,1,0:T(4,128)(2,1)} %param.6) | copy-start | bytes 786436
  12.9 10.5 %collective-permute-start = (f32[4,128,128]{2,1,0:T(8,128)S(1)}, f32[4,128,128]{2,1,0:T(8,128)S(1)}, u32[]{:S(2)}, u32[]{:S(2)}) collective-permute-start(f32[4,128,128]{2,1,0:T(8,128)S(1)} %convolution_multiply_fusion.9), channel_id=1, source_target_pairs={{0,4},{4,8},{8,12},{1,5},{5,9},{9,13},{2,6},{6,10},{10,14},{3,7},{... | collective-permute-start | bytes 786440 | tf_op jit(solution)/shard_map/ppermute | solution.py:64
  17.9 0.9 %copy-start.1 = (bf16[128,4,128]{2,1,0:T(4,128)(2,1)S(1)}, bf16[128,4,128]{2,1,0:T(4,128)(2,1)}, u32[]{:S(2)}) copy-start(bf16[128,4,128]{2,1,0:T(4,128)(2,1)} %param.4) | copy-start | bytes 393220
  20.1 9.7 %collective-permute-start.3 = (f32[4,128,128]{2,1,0:T(8,128)S(1)}, f32[4,128,128]{2,1,0:T(8,128)S(1)}, u32[]{:S(2)}, u32[]{:S(2)}) collective-permute-start(f32[4,128,128]{2,1,0:T(8,128)S(1)} %fusion.48), channel_id=1, source_target_pairs={{4,0},{8,4},{12,8},{5,1},{9,5},{13,9},{6,2},{10,6},{14,10},{7,3},{... | collective-permute-start | bytes 786440 | tf_op jit(solution)/shard_map/ppermute | solution.py:65
  23.7 9.1 %collective-permute-start.1 = (f32[4,128,128]{2,1,0:T(8,128)S(1)}, f32[4,128,128]{2,1,0:T(8,128)S(1)}, u32[]{:S(2)}, u32[]{:S(2)}) collective-permute-start(f32[4,128,128]{2,1,0:T(8,128)S(1)} %convolution_add_fusion.9), channel_id=1, source_target_pairs={{0,4},{4,8},{8,12},{1,5},{5,9},{9,13},{2,6},{6,10},{10,14},{3,7},{... | collective-permute-start | bytes 786440 | tf_op jit(solution)/shard_map/ppermute | solution.py:64
  30.1 8.7 %collective-permute-start.4 = (f32[4,128,128]{2,1,0:T(8,128)S(1)}, f32[4,128,128]{2,1,0:T(8,128)S(1)}, u32[]{:S(2)}, u32[]{:S(2)}) collective-permute-start(f32[4,128,128]{2,1,0:T(8,128)S(1)} %convolution_add_fusion.6), channel_id=1, source_target_pairs={{4,0},{8,4},{12,8},{5,1},{9,5},{13,9},{6,2},{10,6},{14,10},{7,3},{... | collective-permute-start | bytes 786440 | tf_op jit(solution)/shard_map/ppermute | solution.py:65
  33.0 8.3 %collective-permute-start.2 = (f32[4,128,128]{2,1,0:T(8,128)S(1)}, f32[4,128,128]{2,1,0:T(8,128)S(1)}, u32[]{:S(2)}, u32[]{:S(2)}) collective-permute-start(f32[4,128,128]{2,1,0:T(8,128)S(1)} %convolution_add_fusion.8), channel_id=1, source_target_pairs={{0,4},{4,8},{8,12},{1,5},{5,9},{9,13},{2,6},{6,10},{10,14},{3,7},{... | collective-permute-start | bytes 786440 | tf_op jit(solution)/shard_map/ppermute | solution.py:64
  39.3 8.3 %collective-permute-start.5 = (f32[4,128,128]{2,1,0:T(8,128)S(1)}, f32[4,128,128]{2,1,0:T(8,128)S(1)}, u32[]{:S(2)}, u32[]{:S(2)}) collective-permute-start(f32[4,128,128]{2,1,0:T(8,128)S(1)} %convolution_add_fusion.5), channel_id=1, source_target_pairs={{4,0},{8,4},{12,8},{5,1},{9,5},{13,9},{6,2},{10,6},{14,10},{7,3},{... | collective-permute-start | bytes 786440 | tf_op jit(solution)/shard_map/ppermute | solution.py:65
